TPU v7x, 128 devices: a whole 4x4x4 slice. The times are simulated.
128 devices in a mesh: ctx: 4 (over x_hi, core), exp: 32 (over z, y, x_lo).
Axes of the slice: x: 4 (x_hi: 2, x_lo: 2; x = x_hi * 2 + x_lo), y: 4, z: 4, core: 2. Of those that a mesh axis runs over, the one named last changes fastest.
Arguments:
- queries: bfloat16 [4096, 8192], P('ctx', 'exp'), may hold values from -32 to 32
- keys: bfloat16 [4096, 8192], P('ctx', 'exp'), may hold values from -4 to 4
- values: bfloat16 [4096, 8192], P('ctx', 'exp'), may hold values from -6 to 6
- out_proj: bfloat16 [8192, 3584], P('exp'), may hold values from -0.5 to 0.5
- residual: bfloat16 [4096, 3584], P(('ctx', 'exp')), may hold values from -6 to 6
- norm_gain: float32 [3584], replicated, may hold values from 0.25 to 1.75
- routes: int32 [4096, 8], P(('ctx', 'exp')), may hold values from 0 to 31, all different within a row; in each aligned block of 32 rows (0 to 31, 32 to 63, ...) at most 10 rows name the same one
- combine: float32 [4096, 8], P(('ctx', 'exp')), may hold values from 0.1 to 0.5
- w_gate: bfloat16 [32, 3584, 1024], P('exp', None, 'ctx'), may hold values from -0.09375 to 0.09375
- w_up: bfloat16 [32, 3584, 1024], P('exp', None, 'ctx'), may hold values from -0.09375 to 0.09375
- w_down: bfloat16 [32, 1024, 3584], P('exp', 'ctx'), may hold values from -0.1875 to 0.1875
Outputs:
- layer_out: bfloat16 [4096, 3584], P(('ctx', 'exp'))
Inputs may be any that keep to these rules, and one draw needn't show every extreme that they name: `routes`: each row names 8 different experts. Within each aligned block of 32 rows no expert is named by more than 10 rows, and some block names some expert exactly 10 times.
All inputs are finite; a program needn't handle non-finite values.
Results may differ from a plain program's by a relative error of at most 0.023.
Values may be sent and summed in bfloat16 or wider, within the bound.
No kernel may reach another device: no remote copies, remote signals or barrier semaphores. Data moves between devices by JAX's collectives and lax.ppermute only.
A program may use at most 128 MiB of HBM per device.

v0:
```python
import math

import jax
import jax.numpy as jnp
from jax import lax
from jax.sharding import PartitionSpec as P

HD = 128


masked_score = -1e30
norm_eps = 1e-06


def from_behind(shard, axis, by):
    peers = lax.axis_size(axis)
    pairs = [(i, i + by) for i in range(peers) if 0 <= i + by < peers]
    return lax.ppermute(shard, axis, pairs)


def per_device(
    queries, keys, values, out_proj, residual, norm_gain, routes, combine, w_gate, w_up, w_down
):
    query_rows = queries.shape[0]
    head_count = queries.shape[1] // HD
    scaling = 1.0 / math.sqrt(HD)
    ctx_where = lax.axis_index("ctx")
    ctx_count = lax.axis_size("ctx")

    def attend(carried, query_heads, pair_block, visible):
        key_count = pair_block.shape[1]
        key_heads = pair_block[0].reshape(key_count, head_count, HD)
        value_heads = pair_block[1].reshape(key_count, head_count, HD)
        scores = (
            jnp.einsum("qhd,khd->hqk", query_heads, key_heads, preferred_element_type=jnp.float32)
            * scaling
        )
        scores = jnp.where(visible, scores, masked_score)
        peak_old, total_old, weighted_old = carried
        peak_new = jnp.maximum(peak_old, jnp.max(scores, axis=2))
        expo_block = jnp.exp(scores - peak_new[:, :, None])
        factor = jnp.exp(peak_old - peak_new)
        total_new = total_old * factor + jnp.sum(expo_block, axis=2)
        weighted_new = weighted_old * factor.T[:, :, None] + jnp.einsum(
            "hqk,khd->qhd",
            expo_block.astype(jnp.bfloat16),
            value_heads,
            preferred_element_type=jnp.float32,
        )
        return (peak_new, total_new, weighted_new)

    initial = (
        jnp.full((head_count, query_rows), masked_score, jnp.float32),
        jnp.zeros((head_count, query_rows), jnp.float32),
        jnp.zeros((query_rows, head_count, HD), jnp.float32),
    )
    query_heads = queries.reshape(query_rows, head_count, HD)
    row_ids = jnp.arange(query_rows)
    diag_mask = row_ids[:, None] >= row_ids[None, :]
    pair_block = jnp.stack([keys, values])
    carried = attend(initial, query_heads, pair_block, diag_mask)
    for step_index in range(1, ctx_count):
        pair_block = from_behind(pair_block, "ctx", 1)
        carried = attend(carried, query_heads, pair_block, ctx_where >= step_index)
    attended = (
        (carried[2] / carried[1].T[:, :, None])
        .astype(jnp.bfloat16)
        .reshape(query_rows, head_count * HD)
    )
    tok_count = residual.shape[0]
    term = jnp.dot(attended, out_proj, preferred_element_type=jnp.float32)
    mixed = lax.psum_scatter(
        lax.optimization_barrier(term.astype(jnp.bfloat16))
        .astype(jnp.float32)
        .astype(jnp.bfloat16),
        "exp",
        scatter_dimension=0,
        tiled=True,
    ).astype(jnp.float32)
    stream = residual.astype(jnp.float32) + mixed
    normed = (
        stream * lax.rsqrt(jnp.mean(stream * stream, axis=1, keepdims=True) + norm_eps) * norm_gain
    ).astype(jnp.bfloat16)
    width = normed.shape[1]
    per_token = routes.shape[1]
    experts = lax.axis_size("exp")
    capacity = min(tok_count, max(2, tok_count * per_token * 5 // (4 * experts)))
    pair_count = tok_count * per_token
    flat_routes = routes.reshape(pair_count)
    expert_hot = (flat_routes[:, None] == jnp.arange(experts)[None, :]).astype(jnp.int32)
    earlier = jnp.cumsum(expert_hot, axis=0) - expert_hot
    slot_index = jnp.sum(earlier * expert_hot, axis=1)
    position = flat_routes * capacity + slot_index
    position_hot = (position[:, None] == jnp.arange(experts * capacity)[None, :]).astype(
        jnp.float32
    )
    token_hot = (
        (jnp.arange(pair_count) // per_token)[:, None] == jnp.arange(tok_count)[None, :]
    ).astype(jnp.float32)
    pick_rows = jnp.einsum("pr,pt->rt", position_hot, token_hot).astype(jnp.bfloat16)
    outgoing = (
        jnp.dot(pick_rows, normed, preferred_element_type=jnp.float32)
        .astype(jnp.bfloat16)
        .reshape(experts, capacity, width)
    )
    received = lax.all_to_all(outgoing, "exp", split_axis=0, concat_axis=0, tiled=True)
    gate_local = w_gate[0]
    up_local = w_up[0]
    down_local = w_down[0]
    piece = lax.all_gather(received, "ctx", axis=0, tiled=True)
    gate = jnp.einsum("smd,df->smf", piece, gate_local, preferred_element_type=jnp.float32)
    upper = jnp.einsum("smd,df->smf", piece, up_local, preferred_element_type=jnp.float32)
    act_all = (jax.nn.silu(gate) * upper).astype(jnp.bfloat16)
    expert_out = lax.psum_scatter(
        jnp.einsum("smf,fd->smd", act_all, down_local, preferred_element_type=jnp.float32).astype(
            jnp.bfloat16
        ),
        "ctx",
        scatter_dimension=0,
        tiled=True,
    )
    returned = lax.all_to_all(expert_out, "exp", split_axis=0, concat_axis=0, tiled=True)
    weigh_rows = jnp.einsum(
        "pr,pt->tr", position_hot, token_hot * combine.reshape(pair_count)[:, None]
    )
    moe_sum = jnp.dot(
        weigh_rows,
        returned.reshape(experts * capacity, width).astype(jnp.float32),
        precision=lax.Precision.HIGHEST,
    )
    return (stream + moe_sum).astype(jnp.bfloat16)


def solution(mesh):
    in_specs = (
        P("ctx", "exp"),
        P("ctx", "exp"),
        P("ctx", "exp"),
        P("exp", None),
        P(("ctx", "exp"), None),
        P(),
        P(("ctx", "exp"), None),
        P(("ctx", "exp"), None),
        P("exp", None, "ctx"),
        P("exp", None, "ctx"),
        P("exp", "ctx", None),
    )
    out_specs = P(("ctx", "exp"), None)
    return jax.shard_map(
        per_device, mesh=mesh, in_specs=in_specs, out_specs=out_specs, check_vma=False
    )
```

profile of v0, /device:TPU:1, one launch (start us, length us, event | category | flops | bytes accessed | tf_op | source)
XLA Modules:
  0.0 577.0 jit_solution(9103200832604221513)
XLA Ops:
  6.5 0.0 copy-start
  6.5 1.4 copy.75
  7.9 1.2 copy.51
  9.2 0.0 copy-start.1
  9.2 0.1 pad_maximum_fusion
  9.3 6.2 %collective-permute-start = (bf16[2,1024,256]{1,2,0:T(8,128)(2,1)S(1)}, bf16[2,1024,256]{1,2,0:T(8,128)(2,1)}, u32[]{:S(2)}, u32[]{:S(2)}) collective-permute-start(bf16[2,1024,256]{1,2,0:T(8,128)(2,1)S(1)} %pad_maximum_fusion), channel_id=1, source_target_pairs={{0,32},{32,64},{64,96},{1,33},{33,65},{65,97},{2,34},{34,66},{66,9... | collective-permute-start | bytes 3145736 | tf_op jit(solution)/shard_map/ppermute | solution.py:18
  15.5 11.7 %collective-permute-done = bf16[2,1024,256]{1,2,0:T(8,128)(2,1)} collective-permute-done((bf16[2,1024,256]{1,2,0:T(8,128)(2,1)S(1)}, bf16[2,1024,256]{1,2,0:T(8,128)(2,1)}, u32[]{:S(2)}, u32[]{:S(2)}) %collective-permute-start) | collective-permute-done | bytes 1048608 | tf_op jit(solution)/shard_map/ppermute | solution.py:18
  27.2 6.0 %collective-permute-start.1 = (bf16[2,1024,256]{1,2,0:T(8,128)(2,1)}, bf16[2,1024,256]{1,2,0:T(8,128)(2,1)}, u32[]{:S(2)}, u32[]{:S(2)}) collective-permute-start(bf16[2,1024,256]{1,2,0:T(8,128)(2,1)} %collective-permute-done), channel_id=1, source_target_pairs={{0,32},{32,64},{64,96},{1,33},{33,65},{65,97},{2,34},{34,66},{66,9... | collective-permute-start | bytes 3145736 | tf_op jit(solution)/shard_map/ppermute | solution.py:18
  33.2 0.3 iota_compare_fusion
  33.5 6.3 %fusion.3 = (f32[2,1024]{1,0:T(2,128)S(1)}, f32[2,1024,1024]{1,2,0:T(8,128)}) fusion(pred[1024,1024]{0,1:T(8,128)(4,1)S(1)} %iota_compare_fusion, bf16[1024,256]{1,0:T(8,128)(2,1)} %param.12, bf16[1024,256]{1,0:T(8,128)(2,1)} %param.11), kind=kOutput, calls=%fused_computation.16 | convolution fusion | flops 543160320 | bytes 10493952 | tf_op jit(solution)/shard_map/qhd,khd->hqk/dot_general | solution.py:35
  39.8 1.3 fusion.127
  41.1 4.2 collective-permute-done.1
  45.2 5.9 %collective-permute-start.2 = (bf16[2,1024,256]{1,2,0:T(8,128)(2,1)}, bf16[2,1024,256]{1,2,0:T(8,128)(2,1)S(1)}, u32[]{:S(2)}, u32[]{:S(2)}) collective-permute-start(bf16[2,1024,256]{1,2,0:T(8,128)(2,1)} %collective-permute-done.1), channel_id=1, source_target_pairs={{0,32},{32,64},{64,96},{1,33},{33,65},{65,97},{2,34},{34,66},{66,9... | collective-permute-start | bytes 3145736 | tf_op jit(solution)/shard_map/ppermute | solution.py:18
  51.1 1.4 bitcast_reduce_fusion.2
  52.6 1.3 fusion.126
  53.8 1.4 bitcast_reduce_fusion.1
  55.3 7.9 %collective-permute-done.2 = bf16[2,1024,256]{1,2,0:T(8,128)(2,1)S(1)} collective-permute-done((bf16[2,1024,256]{1,2,0:T(8,128)(2,1)}, bf16[2,1024,256]{1,2,0:T(8,128)(2,1)S(1)}, u32[]{:S(2)}, u32[]{:S(2)}) %collective-permute-start.2) | collective-permute-done | bytes 1048608 | tf_op jit(solution)/shard_map/ppermute | solution.py:18
  63.1 0.1 fusion.125
  63.2 1.4 bitcast_reduce_fusion
  64.7 2.3 fusion.10
  67.0 4.5 fusion.4
  71.5 4.0 fusion.6
  75.5 4.9 fusion.66
  80.4 2.6 fusion.57
  83.0 2.6 fusion.60
  85.7 0.0 copy-start.4
  85.7 2.4 divide_convert_fusion
  88.1 0.0 copy-start.6
  88.1 0.0 copy-start.2
  88.1 0.0 copy-start.5
  88.1 5.1 convolution_convert_fusion.1
  93.2 0.0 reduce-scatter.3.cloned.1.call-update
  93.2 0.0 all-gather.2.cloned.1.call-start
  93.3 0.1 copy.63
  93.4 0.1 eq.61
  93.4 0.1 reshape.94
  93.5 0.6 reduce-window.6
  94.1 0.2 slice_reduce_fusion
  94.4 0.1 fusion.102
  94.5 167.9 %reduce-scatter.3.cloned.1.call-done = bf16[32,3584]{1,0:T(8,128)(2,1)} async-done(((bf16[1024,3584]{1,0:T(8,128)(2,1)}), bf16[32,3584]{1,0:T(8,128)(2,1)}) %reduce-scatter.3.cloned.1.call-update) | async-done | bytes 229392 | tf_op jit(solution)/shard_map/reduce_scatter | solution.py:72
  262.4 1.1 multiply_reduce_fusion
  263.5 0.0 copy-done.5
  263.6 3.4 convolution_convert_fusion.2
  266.9 4.4 reshape.96
  271.4 32.3 %all_to_all.10 = bf16[32,10,3584]{2,1,0:T(8,128)(2,1)S(1)} all-to-all(bf16[32,10,3584]{2,1,0:T(8,128)(2,1)} %reshape.96), channel_id=1, replica_groups=mesh['ctx'=4,'exp'=32] {'exp'}, dimensions={0} | all-to-all | bytes 4587520 | tf_op jit(solution)/shard_map/all_to_all | solution.py:106
  303.7 2.7 copy.66
  306.3 0.0 all-gather.2.cloned.1.call-update
  306.3 0.0 reduce-scatter.5.cloned.1.call-start
  306.4 87.2 %all-gather.2.cloned.1.call-done = bf16[128,10,3584]{2,0,1:T(8,128)(2,1)} async-done(((bf16[32,10,3584]{2,0,1:T(8,128)(2,1)}), bf16[128,10,3584]{2,0,1:T(8,128)(2,1)}) %all-gather.2.cloned.1.call-update) | async-done | bytes 9175056 | tf_op jit(solution)/shard_map/all_gather | solution.py:110
  393.6 7.7 %fusion.28 = f32[128,10,256]{2,0,1:T(8,128)} fusion(bf16[128,10,3584]{2,0,1:T(8,128)(2,1)} %all-gather.2.cloned.1.call-done, bf16[1,3584,256]{2,1,0:T(8,128)(2,1)} %param.19), kind=kOutput, calls=%fused_computation.40 | convolution fusion | flops 2348810240 | bytes 12320768 | tf_op jit(solution)/shard_map/smd,df->smf/dot_general | solution.py:111
  401.3 18.5 %convolution_convert_fusion = bf16[128,10,3584]{2,0,1:T(8,128)(2,1)} fusion(bf16[1,256,3584]{2,1,0:T(8,128)(2,1)S(1)} %copy-done, bf16[128,10,3584]{2,0,1:T(8,128)(2,1)} %all-gather.2.cloned.1.call-done, bf16[1,3584,256]{2,1,0:T(8,128)(2,1)} %param.20, f32[128,10,256]{2,0,1:T(8,128)} %fusion.28), kind=kOutput, calls=%fused_computation.14 | convolution fusion | flops 4704174080 | bytes 23330816 | tf_op jit(solution)/shard_map/smf,fd->smd/dot_general | solution.py:115
  419.7 0.0 reduce-scatter.5.cloned.1.call-update
  419.8 0.0 copy-start.7
  419.8 0.0 copy-start.3
  419.8 82.0 %reduce-scatter.5.cloned.1.call-done = bf16[32,10,3584]{2,0,1:T(8,128)(2,1)} async-done(((bf16[128,10,3584]{2,0,1:T(8,128)(2,1)}), bf16[32,10,3584]{2,0,1:T(8,128)(2,1)}) %reduce-scatter.5.cloned.1.call-update) | async-done | bytes 2293776 | tf_op jit(solution)/shard_map/reduce_scatter | solution.py:114
  501.8 4.9 copy.67
  506.7 7.1 %all-to-all-start.1 = ((bf16[32,10,3584]{2,1,0:T(8,128)(2,1)}), bf16[32,10,3584]{2,1,0:T(8,128)(2,1)}, u32[]{:S(2)}, u32[]{:S(2)}) async-start(bf16[32,10,3584]{2,1,0:T(8,128)(2,1)} %copy.67), calls=%async_computation.3 | async-start | bytes 7340032 | tf_op jit(solution)/shard_map/all_to_all | solution.py:122
  513.8 0.0 copy-done.7
  513.8 0.1 copy.62
  513.9 0.1 mul.119
  514.0 0.3 fusion.84
  514.3 48.1 %all-to-all-done.1 = bf16[32,10,3584]{2,1,0:T(8,128)(2,1)} async-done(((bf16[32,10,3584]{2,1,0:T(8,128)(2,1)}), bf16[32,10,3584]{2,1,0:T(8,128)(2,1)}, u32[]{:S(2)}, u32[]{:S(2)}) %all-to-all-start.1) | async-done | bytes 2293792 | tf_op jit(solution)/shard_map/all_to_all | solution.py:122
  562.4 4.5 reshape.97
  566.9 3.6 fusion.12
  (14 shorter events, 0.1 us)
Async XLA Ops:
  6.5 394.7 %copy-start = (bf16[1,256,3584]{2,1,0:T(8,128)(2,1)S(1)}, bf16[1,256,3584]{2,1,0:T(8,128)(2,1)}, u32[]{:S(2)}) copy-start(bf16[1,256,3584]{2,1,0:T(8,128)(2,1)} %param.21) | copy-start | bytes 5505028
  6.5 255.9 %reduce-scatter.3.cloned.1.call-start = ((), (), s32[]{:S(2)}) async-start(), calls=%async_computation.4 | async-start | bytes 7569408 | tf_op jit(solution)/shard_map/reduce_scatter | solution.py:72
  9.2 41.9 %copy-start.1 = (bf16[1024,256]{1,0:T(8,128)(2,1)S(1)}, bf16[1024,256]{1,0:T(8,128)(2,1)}, u32[]{:S(2)}) copy-start(bf16[1024,256]{1,0:T(8,128)(2,1)} %param.11) | copy-start | bytes 1572868
  9.3 17.9 %collective-permute-start = (bf16[2,1024,256]{1,2,0:T(8,128)(2,1)S(1)}, bf16[2,1024,256]{1,2,0:T(8,128)(2,1)}, u32[]{:S(2)}, u32[]{:S(2)}) collective-permute-start(bf16[2,1024,256]{1,2,0:T(8,128)(2,1)S(1)} %pad_maximum_fusion), channel_id=1, source_target_pairs={{0,32},{32,64},{64,96},{1,33},{33,65},{65,97},{2,34},{34,66},{66,9... | collective-permute-start | bytes 3145736 | tf_op jit(solution)/shard_map/ppermute | solution.py:18
  27.2 18.0 %collective-permute-start.1 = (bf16[2,1024,256]{1,2,0:T(8,128)(2,1)}, bf16[2,1024,256]{1,2,0:T(8,128)(2,1)}, u32[]{:S(2)}, u32[]{:S(2)}) collective-permute-start(bf16[2,1024,256]{1,2,0:T(8,128)(2,1)} %collective-permute-done), channel_id=1, source_target_pairs={{0,32},{32,64},{64,96},{1,33},{33,65},{65,97},{2,34},{34,66},{66,9... | collective-permute-start | bytes 3145736 | tf_op jit(solution)/shard_map/ppermute | solution.py:18
  45.2 17.9 %collective-permute-start.2 = (bf16[2,1024,256]{1,2,0:T(8,128)(2,1)}, bf16[2,1024,256]{1,2,0:T(8,128)(2,1)S(1)}, u32[]{:S(2)}, u32[]{:S(2)}) collective-permute-start(bf16[2,1024,256]{1,2,0:T(8,128)(2,1)} %collective-permute-done.1), channel_id=1, source_target_pairs={{0,32},{32,64},{64,96},{1,33},{33,65},{65,97},{2,34},{34,66},{66,9... | collective-permute-start | bytes 3145736 | tf_op jit(solution)/shard_map/ppermute | solution.py:18
  85.7 2.4 copy-start.4
  88.1 5.2 copy-start.6
  88.1 174.3 %copy-start.2 = (bf16[32,3584]{1,0:T(8,128)(2,1)S(1)}, bf16[32,3584]{1,0:T(8,128)(2,1)}, u32[]{:S(2)}) copy-start(bf16[32,3584]{1,0:T(8,128)(2,1)} %param.15) | copy-start | bytes 688132
  88.1 175.4 %copy-start.5 = (f32[3584]{0:T(1024)S(1)}, f32[3584]{0:T(1024)}, u32[]{:S(2)}) copy-start(f32[3584]{0:T(1024)} %param.16) | copy-start | bytes 43012
  93.2 300.3 %all-gather.2.cloned.1.call-start = ((), (), s32[]{:S(2)}) async-start(), calls=%async_computation.5 | async-start | bytes 11468800 | tf_op jit(solution)/shard_map/all_gather | solution.py:110
  306.3 195.5 %reduce-scatter.5.cloned.1.call-start = ((), (), s32[]{:S(2)}) async-start(), calls=%async_computation.6 | async-start | bytes 11468800 | tf_op jit(solution)/shard_map/reduce_scatter | solution.py:114
  419.8 94.0 %copy-start.7 = (f32[32,8]{0,1:T(8,128)S(1)}, f32[32,8]{0,1:T(8,128)}, u32[]{:S(2)}) copy-start(f32[32,8]{0,1:T(8,128)} %param.18) | copy-start | bytes 3076
  419.8 147.1 %copy-start.3 = (bf16[32,3584]{1,0:T(8,128)(2,1)S(1)}, bf16[32,3584]{1,0:T(8,128)(2,1)}, u32[]{:S(2)}) copy-start(bf16[32,3584]{1,0:T(8,128)(2,1)} %reduce-scatter.3.cloned.1.call-done) | copy-start | bytes 688132
  506.7 55.7 %all-to-all-start.1 = ((bf16[32,10,3584]{2,1,0:T(8,128)(2,1)}), bf16[32,10,3584]{2,1,0:T(8,128)(2,1)}, u32[]{:S(2)}, u32[]{:S(2)}) async-start(bf16[32,10,3584]{2,1,0:T(8,128)(2,1)} %copy.67), calls=%async_computation.3 | async-start | bytes 7340032 | tf_op jit(solution)/shard_map/all_to_all | solution.py:122
Sparse Core Ops, SparseCore 0:
  93.3 169.0 reduce-scatter.2
  306.5 87.0 all-gather.1
  419.9 81.8 reduce-scatter.4
where the time goes:
time: 579 us; the launch traced here: 577 us
  waiting for transfers between devices  409 us (71%)
  matrix products  61.7 us (11%)
  blocking collectives  32.3 us (6%)
  starting transfers between devices  25.2 us (4%)
  local copies, waits for them, and re-layouts  22.3 us (4%)
  between operations  13.4 us (2%)
  other arithmetic  13.1 us (2%)
    reduce_scatter x1, waiting for transfers between devices, per_device(): lax.psum_scatter(lax.optimization_barrier(term.astype(jnp.bfloat16)).asty...  168 us
    all_gather x1, waiting for transfers between devices, per_device(): piece = lax.all_gather(received, 'ctx', axis=0, tiled=True)  87.2 us
    reduce_scatter x1, waiting for transfers between devices, per_device(): lax.psum_scatter(jnp.einsum('smf,fd->smd', act_all, down_local, preferred...  82 us
    all_to_all x1, waiting for transfers between devices, per_device(): lax.all_to_all(expert_out, 'exp', split_axis=0, concat_axis=0, tiled=True)  48.1 us
    all_to_all x1, blocking collectives, per_device(): lax.all_to_all(outgoing, 'exp', split_axis=0, concat_axis=0, tiled=True)  32.3 us
    ppermute x3, waiting for transfers between devices, from_behind(): return lax.ppermute(shard, axis, pairs)  23.8 us
    dot_general x1, matrix products, per_device(): jnp.einsum('smf,fd->smd', act_all, down_local, preferred_element_type=jnp...  18.5 us
    ppermute x3, starting transfers between devices, from_behind(): return lax.ppermute(shard, axis, pairs)  18 us
  transfers between devices with their start and end apart: 7, of which 7 were waited for; matrix products, arithmetic and copies ran while one was open for 2% of the time, Pallas kernels for 0%

commit v1 on v0

--- a/solution.py
+++ b/solution.py
@@ -69,14 +69,15 @@
     )
     tok_count = residual.shape[0]
     term = jnp.dot(attended, out_proj, preferred_element_type=jnp.float32)
-    mixed = lax.psum_scatter(
-        lax.optimization_barrier(term.astype(jnp.bfloat16))
-        .astype(jnp.float32)
-        .astype(jnp.bfloat16),
+    exp_count = lax.axis_size("exp")
+    group_terms = lax.all_to_all(
+        term.astype(jnp.bfloat16).reshape(exp_count, query_rows // exp_count, term.shape[1]),
         "exp",
-        scatter_dimension=0,
+        split_axis=0,
+        concat_axis=0,
         tiled=True,
-    ).astype(jnp.float32)
+    )
+    mixed = jnp.sum(group_terms.astype(jnp.float32), axis=0)
     stream = residual.astype(jnp.float32) + mixed
     normed = (
         stream * lax.rsqrt(jnp.mean(stream * stream, axis=1, keepdims=True) + norm_eps) * norm_gain

time: 579 us -> 504 us (0.87)
  waiting for transfers between devices: 409 us -> 306 us
  blocking collectives: 32.3 us -> 49.3 us
  starting transfers between devices: 25.2 us -> 33.5 us
    reduce_scatter x1 -> x0, waiting for transfers between devices: 168 us -> none  [per_device(): lax.psum_scatter(lax.optimization_barrier(term.astype(jnp.bfloat16)).asty...]
    all_to_all x0 -> x1, waiting for transfers between devices: none -> 87.6 us  [per_device(): lax.all_to_all(term.astype(jnp.bfloat16).reshape(exp_count, query_rows //...]
    all_gather x1, waiting for transfers between devices: 87.2 us -> 64.7 us  [per_device(): piece = lax.all_gather(received, 'ctx', axis=0, tiled=True)]
    all_to_all x1, blocking collectives: 32.3 us -> 49.3 us  [per_device(): lax.all_to_all(outgoing, 'exp', split_axis=0, concat_axis=0, tiled=True)]
    all_to_all x0 -> x1, starting transfers between devices: none -> 8.33 us  [per_device(): lax.all_to_all(term.astype(jnp.bfloat16).reshape(exp_count, query_rows //...]
  transfers between devices with their start and end apart: 7 -> 7, of which waited for: 7 -> 7; matrix products, arithmetic and copies ran while one was open for 2% -> 3% of each run, Pallas kernels for 0% -> 0%
where the time goes in v1:
time: 504 us; the launch traced here: 502 us
  waiting for transfers between devices  306 us (61%)
  matrix products  60.8 us (12%)
  blocking collectives  49.3 us (10%)
  starting transfers between devices  33.5 us (7%)
  local copies, waits for them, and re-layouts  22.3 us (4%)
  other arithmetic  16.5 us (3%)
  between operations  13.7 us (3%)
    all_to_all x1, waiting for transfers between devices, per_device(): lax.all_to_all(term.astype(jnp.bfloat16).reshape(exp_count, query_rows //...  87.6 us
    reduce_scatter x1, waiting for transfers between devices, per_device(): lax.psum_scatter(jnp.einsum('smf,fd->smd', act_all, down_local, preferred...  82 us
    all_gather x1, waiting for transfers between devices, per_device(): piece = lax.all_gather(received, 'ctx', axis=0, tiled=True)  64.7 us
    all_to_all x1, blocking collectives, per_device(): lax.all_to_all(outgoing, 'exp', split_axis=0, concat_axis=0, tiled=True)  49.3 us
    all_to_all x1, waiting for transfers between devices, per_device(): lax.all_to_all(expert_out, 'exp', split_axis=0, concat_axis=0, tiled=True)  48.1 us
    ppermute x3, waiting for transfers between devices, from_behind(): return lax.ppermute(shard, axis, pairs)  23.8 us
    dot_general x1, matrix products, per_device(): jnp.einsum('smf,fd->smd', act_all, down_local, preferred_element_type=jnp...  18.5 us
    ppermute x3, starting transfers between devices, from_behind(): return lax.ppermute(shard, axis, pairs)  18 us
  transfers between devices with their start and end apart: 7, of which 7 were waited for; matrix products, arithmetic and copies ran while one was open for 3% of the time, Pallas kernels for 0%

profile of v1, /device:TPU:1, one launch (start us, length us, event | category | flops | bytes accessed | tf_op | source)
XLA Modules:
  0.0 502.3 jit_solution(3049779965349512212)
XLA Ops:
  6.5 0.0 copy-start
  6.5 1.4 copy.75
  7.9 1.2 copy.51
  9.2 0.0 copy-start.1
  9.2 0.1 pad_maximum_fusion
  9.3 6.2 %collective-permute-start = (bf16[2,1024,256]{1,2,0:T(8,128)(2,1)S(1)}, bf16[2,1024,256]{1,2,0:T(8,128)(2,1)}, u32[]{:S(2)}, u32[]{:S(2)}) collective-permute-start(bf16[2,1024,256]{1,2,0:T(8,128)(2,1)S(1)} %pad_maximum_fusion), channel_id=1, source_target_pairs={{0,32},{32,64},{64,96},{1,33},{33,65},{65,97},{2,34},{34,66},{66,9... | collective-permute-start | bytes 3145736 | tf_op jit(solution)/shard_map/ppermute | solution.py:18
  15.5 11.7 %collective-permute-done = bf16[2,1024,256]{1,2,0:T(8,128)(2,1)} collective-permute-done((bf16[2,1024,256]{1,2,0:T(8,128)(2,1)S(1)}, bf16[2,1024,256]{1,2,0:T(8,128)(2,1)}, u32[]{:S(2)}, u32[]{:S(2)}) %collective-permute-start) | collective-permute-done | bytes 1048608 | tf_op jit(solution)/shard_map/ppermute | solution.py:18
  27.2 6.0 %collective-permute-start.1 = (bf16[2,1024,256]{1,2,0:T(8,128)(2,1)}, bf16[2,1024,256]{1,2,0:T(8,128)(2,1)}, u32[]{:S(2)}, u32[]{:S(2)}) collective-permute-start(bf16[2,1024,256]{1,2,0:T(8,128)(2,1)} %collective-permute-done), channel_id=1, source_target_pairs={{0,32},{32,64},{64,96},{1,33},{33,65},{65,97},{2,34},{34,66},{66,9... | collective-permute-start | bytes 3145736 | tf_op jit(solution)/shard_map/ppermute | solution.py:18
  33.2 0.3 iota_compare_fusion
  33.5 6.3 %fusion.3 = (f32[2,1024]{1,0:T(2,128)S(1)}, f32[2,1024,1024]{1,2,0:T(8,128)}) fusion(pred[1024,1024]{0,1:T(8,128)(4,1)S(1)} %iota_compare_fusion, bf16[1024,256]{1,0:T(8,128)(2,1)} %param.12, bf16[1024,256]{1,0:T(8,128)(2,1)} %param.11), kind=kOutput, calls=%fused_computation.17 | convolution fusion | flops 543160320 | bytes 10493952 | tf_op jit(solution)/shard_map/qhd,khd->hqk/dot_general | solution.py:35
  39.8 1.3 fusion.127
  41.1 4.2 collective-permute-done.1
  45.2 5.9 %collective-permute-start.2 = (bf16[2,1024,256]{1,2,0:T(8,128)(2,1)}, bf16[2,1024,256]{1,2,0:T(8,128)(2,1)S(1)}, u32[]{:S(2)}, u32[]{:S(2)}) collective-permute-start(bf16[2,1024,256]{1,2,0:T(8,128)(2,1)} %collective-permute-done.1), channel_id=1, source_target_pairs={{0,32},{32,64},{64,96},{1,33},{33,65},{65,97},{2,34},{34,66},{66,9... | collective-permute-start | bytes 3145736 | tf_op jit(solution)/shard_map/ppermute | solution.py:18
  51.1 0.0 copy-done.1
  51.1 1.4 bitcast_reduce_fusion.2
  52.6 1.3 fusion.126
  53.8 1.4 bitcast_reduce_fusion.1
  55.3 7.9 %collective-permute-done.2 = bf16[2,1024,256]{1,2,0:T(8,128)(2,1)S(1)} collective-permute-done((bf16[2,1024,256]{1,2,0:T(8,128)(2,1)}, bf16[2,1024,256]{1,2,0:T(8,128)(2,1)S(1)}, u32[]{:S(2)}, u32[]{:S(2)}) %collective-permute-start.2) | collective-permute-done | bytes 1048608 | tf_op jit(solution)/shard_map/ppermute | solution.py:18
  63.1 0.1 fusion.125
  63.2 1.4 bitcast_reduce_fusion
  64.7 2.3 fusion.10
  66.9 4.5 fusion.4
  71.5 4.0 fusion.6
  75.5 4.9 fusion.66
  80.4 2.6 fusion.57
  83.0 2.6 fusion.60
  85.7 0.0 copy-start.3
  85.7 2.4 divide_convert_fusion
  88.1 0.0 copy-done.3
  88.1 5.1 %convolution_convert_fusion.1 = bf16[1024,3584]{1,0:T(8,128)(2,1)} fusion(bf16[1024,256]{0,1:T(8,128)(2,1)S(1)} %bitcast.244, bf16[256,3584]{1,0:T(8,128)(2,1)S(1)} %copy-done.3), kind=kOutput, calls=%fused_computation.16 | convolution fusion | flops 1882718208 | bytes 9699328 | tf_op jit(solution)/shard_map/dot_general | solution.py:71
  93.2 8.3 %all-to-all-start = ((bf16[32,32,3584]{2,1,0:T(8,128)(2,1)}), bf16[32,32,3584]{2,1,0:T(8,128)(2,1)}, u32[]{:S(2)}, u32[]{:S(2)}) async-start(bf16[32,32,3584]{2,1,0:T(8,128)(2,1)} %bitcast.237), calls=%async_computation | async-start | bytes 14680064 | tf_op jit(solution)/shard_map/all_to_all | solution.py:73
  101.6 0.0 all-gather.2.cloned.1.call-start
  101.6 0.0 copy-done.5
  101.6 0.1 copy.63
  101.7 0.1 eq.61
  101.8 0.1 reshape.98
  101.9 0.8 reduce-window.6
  102.7 0.2 slice_reduce_fusion
  102.9 0.1 fusion.102
  103.0 87.6 %all-to-all-done = bf16[32,32,3584]{2,1,0:T(8,128)(2,1)} async-done(((bf16[32,32,3584]{2,1,0:T(8,128)(2,1)}), bf16[32,32,3584]{2,1,0:T(8,128)(2,1)}, u32[]{:S(2)}, u32[]{:S(2)}) %all-to-all-start) | async-done | bytes 7340064 | tf_op jit(solution)/shard_map/all_to_all | solution.py:73
  190.6 4.2 convert_reduce_fusion
  194.8 0.0 copy-done.2
  194.8 0.2 multiply_reduce_fusion
  195.0 2.4 convolution_convert_fusion.2
  197.4 4.4 reshape.100
  201.8 49.3 %all_to_all.15 = bf16[32,10,3584]{2,1,0:T(8,128)(2,1)S(1)} all-to-all(bf16[32,10,3584]{2,1,0:T(8,128)(2,1)} %reshape.100), channel_id=1, replica_groups=mesh['ctx'=4,'exp'=32] {'exp'}, dimensions={0} | all-to-all | bytes 4587520 | tf_op jit(solution)/shard_map/all_to_all | solution.py:107
  251.1 2.7 copy.66
  253.8 0.0 all-gather.2.cloned.1.call-update
  253.8 0.0 reduce-scatter.2.cloned.1.call-start
  253.8 64.7 %all-gather.2.cloned.1.call-done = bf16[128,10,3584]{2,0,1:T(8,128)(2,1)} async-done(((bf16[32,10,3584]{2,0,1:T(8,128)(2,1)}), bf16[128,10,3584]{2,0,1:T(8,128)(2,1)}) %all-gather.2.cloned.1.call-update) | async-done | bytes 9175056 | tf_op jit(solution)/shard_map/all_gather | solution.py:111
  318.6 7.7 %fusion.28 = f32[128,10,256]{2,0,1:T(8,128)} fusion(bf16[128,10,3584]{2,0,1:T(8,128)(2,1)} %all-gather.2.cloned.1.call-done, bf16[1,3584,256]{2,1,0:T(8,128)(2,1)} %param.19), kind=kOutput, calls=%fused_computation.41 | convolution fusion | flops 2348810240 | bytes 12320768 | tf_op jit(solution)/shard_map/smd,df->smf/dot_general | solution.py:112
  326.3 18.5 %convolution_convert_fusion = bf16[128,10,3584]{2,0,1:T(8,128)(2,1)} fusion(bf16[1,256,3584]{2,1,0:T(8,128)(2,1)S(1)} %copy-done, bf16[128,10,3584]{2,0,1:T(8,128)(2,1)} %all-gather.2.cloned.1.call-done, bf16[1,3584,256]{2,1,0:T(8,128)(2,1)} %param.20, f32[128,10,256]{2,0,1:T(8,128)} %fusion.28), kind=kOutput, calls=%fused_computation.15 | convolution fusion | flops 4704174080 | bytes 23330816 | tf_op jit(solution)/shard_map/smf,fd->smd/dot_general | solution.py:116
  344.8 0.0 reduce-scatter.2.cloned.1.call-update
  344.8 0.0 copy-start.6
  344.8 82.0 %reduce-scatter.2.cloned.1.call-done = bf16[32,10,3584]{2,0,1:T(8,128)(2,1)} async-done(((bf16[128,10,3584]{2,0,1:T(8,128)(2,1)}), bf16[32,10,3584]{2,0,1:T(8,128)(2,1)}) %reduce-scatter.2.cloned.1.call-update) | async-done | bytes 2293776 | tf_op jit(solution)/shard_map/reduce_scatter | solution.py:115
  426.9 4.9 copy.67
  431.7 7.1 %all-to-all-start.2 = ((bf16[32,10,3584]{2,1,0:T(8,128)(2,1)}), bf16[32,10,3584]{2,1,0:T(8,128)(2,1)}, u32[]{:S(2)}, u32[]{:S(2)}) async-start(bf16[32,10,3584]{2,1,0:T(8,128)(2,1)} %copy.67), calls=%async_computation.3 | async-start | bytes 7340032 | tf_op jit(solution)/shard_map/all_to_all | solution.py:123
  438.8 0.0 copy-done.6
  438.8 0.1 copy.62
  438.9 0.1 mul.119
  439.0 0.3 fusion.84
  439.3 48.1 %all-to-all-done.2 = bf16[32,10,3584]{2,1,0:T(8,128)(2,1)} async-done(((bf16[32,10,3584]{2,1,0:T(8,128)(2,1)}), bf16[32,10,3584]{2,1,0:T(8,128)(2,1)}, u32[]{:S(2)}, u32[]{:S(2)}) %all-to-all-start.2) | async-done | bytes 2293792 | tf_op jit(solution)/shard_map/all_to_all | solution.py:123
  487.4 4.5 reshape.101
  491.9 3.6 fusion.12
  (12 shorter events, 0.1 us)
Async XLA Ops:
  6.5 319.8 %copy-start = (bf16[1,256,3584]{2,1,0:T(8,128)(2,1)S(1)}, bf16[1,256,3584]{2,1,0:T(8,128)(2,1)}, u32[]{:S(2)}) copy-start(bf16[1,256,3584]{2,1,0:T(8,128)(2,1)} %param.21) | copy-start | bytes 5505028
  9.2 41.9 %copy-start.1 = (bf16[1024,256]{1,0:T(8,128)(2,1)S(1)}, bf16[1024,256]{1,0:T(8,128)(2,1)}, u32[]{:S(2)}) copy-start(bf16[1024,256]{1,0:T(8,128)(2,1)} %param.11) | copy-start | bytes 1572868
  9.3 17.9 %collective-permute-start = (bf16[2,1024,256]{1,2,0:T(8,128)(2,1)S(1)}, bf16[2,1024,256]{1,2,0:T(8,128)(2,1)}, u32[]{:S(2)}, u32[]{:S(2)}) collective-permute-start(bf16[2,1024,256]{1,2,0:T(8,128)(2,1)S(1)} %pad_maximum_fusion), channel_id=1, source_target_pairs={{0,32},{32,64},{64,96},{1,33},{33,65},{65,97},{2,34},{34,66},{66,9... | collective-permute-start | bytes 3145736 | tf_op jit(solution)/shard_map/ppermute | solution.py:18
  27.2 18.0 %collective-permute-start.1 = (bf16[2,1024,256]{1,2,0:T(8,128)(2,1)}, bf16[2,1024,256]{1,2,0:T(8,128)(2,1)}, u32[]{:S(2)}, u32[]{:S(2)}) collective-permute-start(bf16[2,1024,256]{1,2,0:T(8,128)(2,1)} %collective-permute-done), channel_id=1, source_target_pairs={{0,32},{32,64},{64,96},{1,33},{33,65},{65,97},{2,34},{34,66},{66,9... | collective-permute-start | bytes 3145736 | tf_op jit(solution)/shard_map/ppermute | solution.py:18
  45.2 17.9 %collective-permute-start.2 = (bf16[2,1024,256]{1,2,0:T(8,128)(2,1)}, bf16[2,1024,256]{1,2,0:T(8,128)(2,1)S(1)}, u32[]{:S(2)}, u32[]{:S(2)}) collective-permute-start(bf16[2,1024,256]{1,2,0:T(8,128)(2,1)} %collective-permute-done.1), channel_id=1, source_target_pairs={{0,32},{32,64},{64,96},{1,33},{33,65},{65,97},{2,34},{34,66},{66,9... | collective-permute-start | bytes 3145736 | tf_op jit(solution)/shard_map/ppermute | solution.py:18
  85.7 2.4 copy-start.3
  93.2 8.4 %copy-start.5 = (s32[32,8]{0,1:T(8,128)S(1)}, s32[32,8]{0,1:T(8,128)}, u32[]{:S(2)}) copy-start(s32[32,8]{0,1:T(8,128)} %param.17) | copy-start | bytes 3076
  93.2 101.6 %copy-start.2 = (bf16[32,3584]{1,0:T(8,128)(2,1)S(1)}, bf16[32,3584]{1,0:T(8,128)(2,1)}, u32[]{:S(2)}) copy-start(bf16[32,3584]{1,0:T(8,128)(2,1)} %param.15) | copy-start | bytes 688132
  93.2 101.7 %copy-start.4 = (f32[3584]{0:T(1024)S(1)}, f32[3584]{0:T(1024)}, u32[]{:S(2)}) copy-start(f32[3584]{0:T(1024)} %param.16) | copy-start | bytes 43012
  93.2 97.4 %all-to-all-start = ((bf16[32,32,3584]{2,1,0:T(8,128)(2,1)}), bf16[32,32,3584]{2,1,0:T(8,128)(2,1)}, u32[]{:S(2)}, u32[]{:S(2)}) async-start(bf16[32,32,3584]{2,1,0:T(8,128)(2,1)} %bitcast.237), calls=%async_computation | async-start | bytes 14680064 | tf_op jit(solution)/shard_map/all_to_all | solution.py:73
  101.6 217.0 %all-gather.2.cloned.1.call-start = ((), (), s32[]{:S(2)}) async-start(), calls=%async_computation.4 | async-start | bytes 11468800 | tf_op jit(solution)/shard_map/all_gather | solution.py:111
  253.8 173.1 %reduce-scatter.2.cloned.1.call-start = ((), (), s32[]{:S(2)}) async-start(), calls=%async_computation.5 | async-start | bytes 11468800 | tf_op jit(solution)/shard_map/reduce_scatter | solution.py:115
  344.8 94.0 %copy-start.6 = (f32[32,8]{0,1:T(8,128)S(1)}, f32[32,8]{0,1:T(8,128)}, u32[]{:S(2)}) copy-start(f32[32,8]{0,1:T(8,128)} %param.18) | copy-start | bytes 3076
  431.7 55.7 %all-to-all-start.2 = ((bf16[32,10,3584]{2,1,0:T(8,128)(2,1)}), bf16[32,10,3584]{2,1,0:T(8,128)(2,1)}, u32[]{:S(2)}, u32[]{:S(2)}) async-start(bf16[32,10,3584]{2,1,0:T(8,128)(2,1)} %copy.67), calls=%async_computation.3 | async-start | bytes 7340032 | tf_op jit(solution)/shard_map/all_to_all | solution.py:123
Sparse Core Ops, SparseCore 0:
  253.9 64.6 all-gather.1
  344.9 81.8 reduce-scatter.1

commit v2 on v1

--- a/solution.py
+++ b/solution.py
@@ -105,20 +105,24 @@
         .reshape(experts, capacity, width)
     )
     received = lax.all_to_all(outgoing, "exp", split_axis=0, concat_axis=0, tiled=True)
-    gate_local = w_gate[0]
-    up_local = w_up[0]
-    down_local = w_down[0]
-    piece = lax.all_gather(received, "ctx", axis=0, tiled=True)
-    gate = jnp.einsum("smd,df->smf", piece, gate_local, preferred_element_type=jnp.float32)
-    upper = jnp.einsum("smd,df->smf", piece, up_local, preferred_element_type=jnp.float32)
+    gate_full = lax.all_gather(w_gate[0], "ctx", axis=1, tiled=True)
+    up_full = lax.all_gather(w_up[0], "ctx", axis=1, tiled=True)
+    down_full = lax.all_gather(w_down[0], "ctx", axis=0, tiled=True)
+    rows = received.reshape(experts * capacity, width)
+    gate = jnp.dot(rows, gate_full, preferred_element_type=jnp.float32)
+    upper = jnp.dot(rows, up_full, preferred_element_type=jnp.float32)
     act_all = (jax.nn.silu(gate) * upper).astype(jnp.bfloat16)
-    expert_out = lax.psum_scatter(
-        jnp.einsum("smf,fd->smd", act_all, down_local, preferred_element_type=jnp.float32).astype(
-            jnp.bfloat16
-        ),
-        "ctx",
-        scatter_dimension=0,
-        tiled=True,
+    quarter = w_down.shape[1]
+    quarter_terms = jnp.einsum(
+        "rqf,qfd->qrd",
+        act_all.reshape(experts * capacity, ctx_count, quarter),
+        down_full.reshape(ctx_count, quarter, width),
+        preferred_element_type=jnp.float32,
+    ).astype(jnp.bfloat16)
+    expert_out = (
+        jnp.sum(quarter_terms.astype(jnp.float32), axis=0)
+        .astype(jnp.bfloat16)
+        .reshape(experts, capacity, width)
     )
     returned = lax.all_to_all(expert_out, "exp", split_axis=0, concat_axis=0, tiled=True)
     weigh_rows = jnp.einsum(

time: 504 us -> 434 us (0.86)
  waiting for transfers between devices: 306 us -> 234 us
    reduce_scatter x1 -> x0, waiting for transfers between devices: 82 us -> none  [per_device(): lax.psum_scatter(jnp.einsum('smf,fd->smd', act_all, down_local, preferred...]
    all_gather x1 -> x3, waiting for transfers between devices: 64.7 us -> 0.02 us  [the longest x1 0.02 us: per_device(): down_full = lax.all_gather(w_down[0], 'ctx', axis=0, tiled=True)]
    all_to_all x1, waiting for transfers between devices: 87.6 us -> 125 us  [per_device(): lax.all_to_all(term.astype(jnp.bfloat16).reshape(exp_count, query_rows //...]
    ppermute x3, waiting for transfers between devices: 23.8 us -> 56 us  [from_behind(): return lax.ppermute(shard, axis, pairs)]
    reshape x0 -> x2, local copies, waits for them, and re-layouts: none -> 9.03 us  [the longest x1 4.55 us: per_device(): expert_out = jnp.sum(quarter_terms.astype(jnp.float32), axis=0).astype(jn...]
    dot_general x2 -> x3, matrix products: 26.2 us -> 21.7 us  [the longest x1 7.55 us: per_device(): jnp.einsum('rqf,qfd->qrd', act_all.reshape(experts * capacity, ctx_count,...]
  transfers between devices with their start and end apart: 7 -> 8, of which waited for: 7 -> 5; matrix products, arithmetic and copies ran while one was open for 3% -> 18% of each run, Pallas kernels for 0% -> 0%
where the time goes in v2:
time: 434 us; the launch traced here: 430 us
  waiting for transfers between devices  234 us (54%)
  matrix products  56.2 us (13%)
  blocking collectives  52.4 us (12%)
  starting transfers between devices  31.7 us (7%)
  local copies, waits for them, and re-layouts  23.8 us (5%)
  other arithmetic  17.7 us (4%)
  between operations  13.4 us (3%)
    all_to_all x1, waiting for transfers between devices, per_device(): lax.all_to_all(term.astype(jnp.bfloat16).reshape(exp_count, query_rows //...  125 us
    ppermute x3, waiting for transfers between devices, from_behind(): return lax.ppermute(shard, axis, pairs)  56 us
    all_to_all x1, blocking collectives, per_device(): lax.all_to_all(outgoing, 'exp', split_axis=0, concat_axis=0, tiled=True)  52.4 us
    all_to_all x1, waiting for transfers between devices, per_device(): lax.all_to_all(expert_out, 'exp', split_axis=0, concat_axis=0, tiled=True)  52.2 us
    ppermute x3, starting transfers between devices, from_behind(): return lax.ppermute(shard, axis, pairs)  17.8 us
    dot_general x4, matrix products, attend(): jnp.einsum('hqk,khd->qhd', expo_block.astype(jnp.bfloat16), value_heads,...  12.5 us
    reduce_sum x3, other arithmetic, attend(): total_new = total_old * factor + jnp.sum(expo_block, axis=2)  11 us
    dot_general x4, matrix products, attend(): jnp.einsum('qhd,khd->hqk', query_heads, key_heads, preferred_element_type...  10.5 us
  transfers between devices with their start and end apart: 8, of which 5 were waited for; matrix products, arithmetic and copies ran while one was open for 18% of the time, Pallas kernels for 0%

profile of v2, /device:TPU:1, one launch (start us, length us, event | category | flops | bytes accessed | tf_op | source)
XLA Modules:
  0.0 429.7 jit_solution(5110746708921329813)
XLA Ops:
  6.5 0.0 copy-start
  6.5 0.0 all-gather.7.cloned.1.call-start
  6.5 0.7 all-gather.7.cloned.1.call-update
  7.3 0.0 all-gather.9.cloned.1.call-start
  7.3 1.2 copy.53
  8.6 1.2 copy.30
  9.8 1.1 pad_maximum_fusion
  10.9 6.0 %collective-permute-start = (bf16[2,1024,256]{1,2,0:T(8,128)(2,1)}, bf16[2,1024,256]{1,2,0:T(8,128)(2,1)}, u32[]{:S(2)}, u32[]{:S(2)}) collective-permute-start(bf16[2,1024,256]{1,2,0:T(8,128)(2,1)} %pad_maximum_fusion), channel_id=1, source_target_pairs={{0,32},{32,64},{64,96},{1,33},{33,65},{65,97},{2,34},{34,66},{66,9... | collective-permute-start | bytes 3145736 | tf_op jit(solution)/shard_map/ppermute | solution.py:18
  16.9 0.0 all-gather.9.cloned.1.call-update
  17.0 21.3 %collective-permute-done = bf16[2,1024,256]{1,2,0:T(8,128)(2,1)} collective-permute-done((bf16[2,1024,256]{1,2,0:T(8,128)(2,1)}, bf16[2,1024,256]{1,2,0:T(8,128)(2,1)}, u32[]{:S(2)}, u32[]{:S(2)}) %collective-permute-start) | collective-permute-done | bytes 1048608 | tf_op jit(solution)/shard_map/ppermute | solution.py:18
  38.3 5.9 %collective-permute-start.1 = (bf16[2,1024,256]{1,2,0:T(8,128)(2,1)}, bf16[2,1024,256]{1,2,0:T(8,128)(2,1)}, u32[]{:S(2)}, u32[]{:S(2)}) collective-permute-start(bf16[2,1024,256]{1,2,0:T(8,128)(2,1)} %collective-permute-done), channel_id=1, source_target_pairs={{0,32},{32,64},{64,96},{1,33},{33,65},{65,97},{2,34},{34,66},{66,9... | collective-permute-start | bytes 3145736 | tf_op jit(solution)/shard_map/ppermute | solution.py:18
  44.2 0.3 iota_compare_fusion
  44.5 0.0 copy-done.2
  44.5 6.2 %fusion.3 = (f32[2,1024]{1,0:T(2,128)S(1)}, f32[2,1024,1024]{1,2,0:T(8,128)}) fusion(pred[1024,1024]{0,1:T(8,128)(4,1)S(1)} %iota_compare_fusion, bf16[1024,256]{1,0:T(8,128)(2,1)} %param.12, bf16[1024,256]{1,0:T(8,128)(2,1)S(1)} %copy-done.2), kind=kOutput, calls=%fused_computation.17 | convolution fusion | flops 543160320 | bytes 10493952 | tf_op jit(solution)/shard_map/qhd,khd->hqk/dot_general | solution.py:35
  50.6 1.3 fusion.124
  51.9 26.9 %collective-permute-done.1 = bf16[2,1024,256]{1,2,0:T(8,128)(2,1)} collective-permute-done((bf16[2,1024,256]{1,2,0:T(8,128)(2,1)}, bf16[2,1024,256]{1,2,0:T(8,128)(2,1)}, u32[]{:S(2)}, u32[]{:S(2)}) %collective-permute-start.1) | collective-permute-done | bytes 1048608 | tf_op jit(solution)/shard_map/ppermute | solution.py:18
  78.8 5.9 %collective-permute-start.2 = (bf16[2,1024,256]{1,2,0:T(8,128)(2,1)}, bf16[2,1024,256]{1,2,0:T(8,128)(2,1)S(1)}, u32[]{:S(2)}, u32[]{:S(2)}) collective-permute-start(bf16[2,1024,256]{1,2,0:T(8,128)(2,1)} %collective-permute-done.1), channel_id=1, source_target_pairs={{0,32},{32,64},{64,96},{1,33},{33,65},{65,97},{2,34},{34,66},{66,9... | collective-permute-start | bytes 3145736 | tf_op jit(solution)/shard_map/ppermute | solution.py:18
  84.7 1.4 bitcast_reduce_fusion.2
  86.1 1.3 fusion.123
  87.4 1.4 bitcast_reduce_fusion.1
  88.8 7.9 %collective-permute-done.2 = bf16[2,1024,256]{1,2,0:T(8,128)(2,1)S(1)} collective-permute-done((bf16[2,1024,256]{1,2,0:T(8,128)(2,1)}, bf16[2,1024,256]{1,2,0:T(8,128)(2,1)S(1)}, u32[]{:S(2)}, u32[]{:S(2)}) %collective-permute-start.2) | collective-permute-done | bytes 1048608 | tf_op jit(solution)/shard_map/ppermute | solution.py:18
  96.7 0.1 fusion.122
  96.8 1.4 bitcast_reduce_fusion
  98.2 2.3 fusion.14
  100.5 4.7 %fusion.8 = f32[2,1024]{1,0:T(2,128)S(1)} fusion(f32[2,1024,1024]{1,2,0:T(8,128)} %get-tuple-element.27, f32[2,1024]{1,0:T(2,128)S(1)} %get-tuple-element.19, pred[1024,1024]{0,1:T(8,128)(4,1)S(1)} %iota_compare_fusion), kind=kLoop, calls=%fused_computation.22 | loop fusion | flops 8386560 | bytes 9453568 | tf_op jit(solution)/shard_map/reduce_sum | solution.py:43
  105.2 4.0 fusion.10
  109.3 4.9 %fusion.65 = f32[1024,2,128]{0,2,1:T(8,128)S(1)} fusion(bf16[1024,2,128]{0,2,1:T(8,128)(2,1)S(1)} %bitcast.240, f32[2,1024,1024]{1,2,0:T(8,128)} %get-tuple-element.27, f32[2,1024]{1,0:T(2,128)S(1)} %get-tuple-element.19, pred[1024,1024]{0,1:T(8,128)(4,1)S(1)} %iota_compare_fusion, f32[1024,2]{0,1:T(2,128)S(1)} %get-tuple-element.17, ...), kind=kOutput, calls=%fused_computation.54 | convolution fusion | flops 545783808 | bytes 11034624 | tf_op jit(solution)/shard_map/hqk,khd->qhd/dot_general | solution.py:44
  114.2 2.6 fusion.56
  116.8 2.6 fusion.59
  119.4 2.4 divide_convert_fusion
  121.8 0.0 copy-done
  121.8 5.1 %convolution_convert_fusion = bf16[1024,3584]{1,0:T(8,128)(2,1)} fusion(bf16[1024,256]{0,1:T(8,128)(2,1)S(1)} %bitcast.242, bf16[256,3584]{1,0:T(8,128)(2,1)S(1)} %copy-done), kind=kOutput, calls=%fused_computation.16 | convolution fusion | flops 1882718208 | bytes 9699328 | tf_op jit(solution)/shard_map/dot_general | solution.py:71
  126.9 9.0 %all-to-all-start = ((bf16[32,32,3584]{2,1,0:T(8,128)(2,1)}), bf16[32,32,3584]{2,1,0:T(8,128)(2,1)}, u32[]{:S(2)}, u32[]{:S(2)}) async-start(bf16[32,32,3584]{2,1,0:T(8,128)(2,1)} %bitcast.235), calls=%async_computation | async-start | bytes 14680064 | tf_op jit(solution)/shard_map/all_to_all | solution.py:73
  135.9 0.0 copy-start.3
  135.9 0.0 copy-start.4
  135.9 0.0 all-gather.11.cloned.1.call-start
  136.0 0.7 all-gather.11.cloned.1.call-update
  136.7 0.0 copy-done.5
  136.7 0.1 copy.42
  136.8 0.1 eq.61
  136.9 0.1 reshape.110
  137.0 0.8 reduce-window.6
  137.8 0.2 slice_reduce_fusion
  138.0 0.1 fusion.100
  138.1 124.8 %all-to-all-done = bf16[32,32,3584]{2,1,0:T(8,128)(2,1)} async-done(((bf16[32,32,3584]{2,1,0:T(8,128)(2,1)}), bf16[32,32,3584]{2,1,0:T(8,128)(2,1)}, u32[]{:S(2)}, u32[]{:S(2)}) %all-to-all-start) | async-done | bytes 7340064 | tf_op jit(solution)/shard_map/all_to_all | solution.py:73
  263.0 4.2 convert_reduce_fusion
  267.1 0.0 copy-done.3
  267.1 0.2 multiply_reduce_fusion
  267.3 2.5 convolution_convert_fusion.1
  269.9 4.5 %reshape.112 = bf16[32,10,3584]{2,1,0:T(8,128)(2,1)} reshape(bf16[320,3584]{1,0:T(8,128)(2,1)} %convolution_convert_fusion.1) | data formatting | bytes 4587520 | tf_op jit(solution)/shard_map/reshape | solution.py:105
  274.4 52.4 %all_to_all.15 = bf16[32,10,3584]{2,1,0:T(8,128)(2,1)} all-to-all(bf16[32,10,3584]{2,1,0:T(8,128)(2,1)} %reshape.112), channel_id=1, replica_groups=mesh['ctx'=4,'exp'=32] {'exp'}, dimensions={0} | all-to-all | bytes 4587520 | tf_op jit(solution)/shard_map/all_to_all | solution.py:107
  326.8 4.5 %reshape.113 = bf16[320,3584]{1,0:T(8,128)(2,1)} reshape(bf16[32,10,3584]{2,1,0:T(8,128)(2,1)} %all_to_all.15) | data formatting | bytes 4587520 | tf_op jit(solution)/shard_map/reshape | solution.py:111
  331.2 7.5 %fusion.6 = f32[320,1024]{1,0:T(8,128)} fusion(bf16[320,3584]{1,0:T(8,128)(2,1)} %reshape.113, bf16[1,3584,1024]{2,1,0:T(8,128)(2,1)} %all-gather.7.cloned.1.call-done), kind=kOutput, calls=%fused_computation.20 | convolution fusion | flops 2348810240 | bytes 10944512 | tf_op jit(solution)/shard_map/dot_general | solution.py:112
  338.7 6.7 %fusion.44 = bf16[320,1024]{1,0:T(8,128)(2,1)S(1)} fusion(bf16[320,3584]{1,0:T(8,128)(2,1)} %reshape.113, bf16[1,3584,1024]{2,1,0:T(8,128)(2,1)} %all-gather.9.cloned.1.call-done, f32[320,1024]{1,0:T(8,128)} %fusion.6), kind=kOutput, calls=%fused_computation.47 | convolution fusion | flops 2350776320 | bytes 11599872 | tf_op jit(solution)/shard_map/dot_general | solution.py:113
  345.4 0.0 all-gather.11.cloned.1.call-done
  345.4 7.5 %convert_reduce_fusion.1 = bf16[320,3584]{1,0:T(8,128)(2,1)} fusion(bf16[4,256,3584]{2,1,0:T(8,128)(2,1)} %bitcast.246, bf16[40,4,8,256]{3,2,1,0:T(8,128)(2,1)S(1)} %bitcast.247), kind=kOutput, calls=%fused_computation.1 | convolution fusion | flops 2356838400 | bytes 10289152 | tf_op jit(solution)/shard_map/rqf,qfd->qrd/dot_general | solution.py:116
  353.0 4.6 %reshape.116 = bf16[32,10,3584]{2,1,0:T(8,128)(2,1)} reshape(bf16[320,3584]{1,0:T(8,128)(2,1)} %convert_reduce_fusion.1) | data formatting | bytes 4587520 | tf_op jit(solution)/shard_map/reshape | solution.py:125
  357.6 4.8 %all-to-all-start.2 = ((bf16[32,10,3584]{2,1,0:T(8,128)(2,1)}), bf16[32,10,3584]{2,1,0:T(8,128)(2,1)}, u32[]{:S(2)}, u32[]{:S(2)}) async-start(bf16[32,10,3584]{2,1,0:T(8,128)(2,1)} %reshape.116), calls=%async_computation.2 | async-start | bytes 7340032 | tf_op jit(solution)/shard_map/all_to_all | solution.py:127
  362.4 0.1 copy.41
  362.5 0.1 mul.119
  362.6 0.3 fusion.82
  362.9 52.2 %all-to-all-done.2 = bf16[32,10,3584]{2,1,0:T(8,128)(2,1)} async-done(((bf16[32,10,3584]{2,1,0:T(8,128)(2,1)}), bf16[32,10,3584]{2,1,0:T(8,128)(2,1)}, u32[]{:S(2)}, u32[]{:S(2)}) %all-to-all-start.2) | async-done | bytes 2293792 | tf_op jit(solution)/shard_map/all_to_all | solution.py:127
  415.1 4.5 %reshape.117 = bf16[320,3584]{1,0:T(8,128)(2,1)} reshape(bf16[32,10,3584]{2,1,0:T(8,128)(2,1)} %all-to-all-done.2) | data formatting | bytes 4587520 | tf_op jit(solution)/shard_map/reshape | solution.py:133
  419.5 3.6 fusion.16
  (16 shorter events, 0.1 us)
Async XLA Ops:
  6.5 115.3 %copy-start = (bf16[256,3584]{1,0:T(8,128)(2,1)S(1)}, bf16[256,3584]{1,0:T(8,128)(2,1)}, u32[]{:S(2)}) copy-start(bf16[256,3584]{1,0:T(8,128)(2,1)} %param.14) | copy-start | bytes 5505028
  6.5 37.9 %copy-start.2 = (bf16[1024,256]{1,0:T(8,128)(2,1)S(1)}, bf16[1024,256]{1,0:T(8,128)(2,1)}, u32[]{:S(2)}) copy-start(bf16[1024,256]{1,0:T(8,128)(2,1)} %param.11) | copy-start | bytes 1572868
  6.5 324.7 %all-gather.7.cloned.1.call-start = ((), (), s32[]{:S(2)}) async-start(), calls=%async_computation.3 | async-start | bytes 9175040 | tf_op jit(solution)/shard_map/all_gather | solution.py:108
  7.3 331.5 %all-gather.9.cloned.1.call-start = ((), (), s32[]{:S(2)}) async-start(), calls=%async_computation.4 | async-start | bytes 9175040 | tf_op jit(solution)/shard_map/all_gather | solution.py:109
  10.9 27.3 %collective-permute-start = (bf16[2,1024,256]{1,2,0:T(8,128)(2,1)}, bf16[2,1024,256]{1,2,0:T(8,128)(2,1)}, u32[]{:S(2)}, u32[]{:S(2)}) collective-permute-start(bf16[2,1024,256]{1,2,0:T(8,128)(2,1)} %pad_maximum_fusion), channel_id=1, source_target_pairs={{0,32},{32,64},{64,96},{1,33},{33,65},{65,97},{2,34},{34,66},{66,9... | collective-permute-start | bytes 3145736 | tf_op jit(solution)/shard_map/ppermute | solution.py:18
  38.3 40.5 %collective-permute-start.1 = (bf16[2,1024,256]{1,2,0:T(8,128)(2,1)}, bf16[2,1024,256]{1,2,0:T(8,128)(2,1)}, u32[]{:S(2)}, u32[]{:S(2)}) collective-permute-start(bf16[2,1024,256]{1,2,0:T(8,128)(2,1)} %collective-permute-done), channel_id=1, source_target_pairs={{0,32},{32,64},{64,96},{1,33},{33,65},{65,97},{2,34},{34,66},{66,9... | collective-permute-start | bytes 3145736 | tf_op jit(solution)/shard_map/ppermute | solution.py:18
  78.8 17.9 %collective-permute-start.2 = (bf16[2,1024,256]{1,2,0:T(8,128)(2,1)}, bf16[2,1024,256]{1,2,0:T(8,128)(2,1)S(1)}, u32[]{:S(2)}, u32[]{:S(2)}) collective-permute-start(bf16[2,1024,256]{1,2,0:T(8,128)(2,1)} %collective-permute-done.1), channel_id=1, source_target_pairs={{0,32},{32,64},{64,96},{1,33},{33,65},{65,97},{2,34},{34,66},{66,9... | collective-permute-start | bytes 3145736 | tf_op jit(solution)/shard_map/ppermute | solution.py:18
  126.9 9.8 %copy-start.5 = (s32[32,8]{0,1:T(8,128)S(1)}, s32[32,8]{0,1:T(8,128)}, u32[]{:S(2)}) copy-start(s32[32,8]{0,1:T(8,128)} %param.17) | copy-start | bytes 3076
  126.9 136.0 %all-to-all-start = ((bf16[32,32,3584]{2,1,0:T(8,128)(2,1)}), bf16[32,32,3584]{2,1,0:T(8,128)(2,1)}, u32[]{:S(2)}, u32[]{:S(2)}) async-start(bf16[32,32,3584]{2,1,0:T(8,128)(2,1)} %bitcast.235), calls=%async_computation | async-start | bytes 14680064 | tf_op jit(solution)/shard_map/all_to_all | solution.py:73
  135.9 131.2 %copy-start.3 = (bf16[32,3584]{1,0:T(8,128)(2,1)S(1)}, bf16[32,3584]{1,0:T(8,128)(2,1)}, u32[]{:S(2)}) copy-start(bf16[32,3584]{1,0:T(8,128)(2,1)} %param.15) | copy-start | bytes 688132
  135.9 131.4 %copy-start.4 = (f32[3584]{0:T(1024)S(1)}, f32[3584]{0:T(1024)}, u32[]{:S(2)}) copy-start(f32[3584]{0:T(1024)} %param.16) | copy-start | bytes 43012
  135.9 209.5 %all-gather.11.cloned.1.call-start = ((), (), s32[]{:S(2)}) async-start(), calls=%async_computation.5 | async-start | bytes 9175040 | tf_op jit(solution)/shard_map/all_gather | solution.py:110
  353.0 9.4 %copy-start.6 = (f32[32,8]{0,1:T(8,128)S(1)}, f32[32,8]{0,1:T(8,128)}, u32[]{:S(2)}) copy-start(f32[32,8]{0,1:T(8,128)} %param.18) | copy-start | bytes 3076
  353.0 70.1 %copy-start.1 = (bf16[256,3584]{1,0:T(8,128)(2,1)S(1)}, bf16[256,3584]{1,0:T(8,128)(2,1)}, u32[]{:S(2)}) copy-start(bf16[256,3584]{1,0:T(8,128)(2,1)} %param.14) | copy-start | bytes 5505028
  357.6 57.5 %all-to-all-start.2 = ((bf16[32,10,3584]{2,1,0:T(8,128)(2,1)}), bf16[32,10,3584]{2,1,0:T(8,128)(2,1)}, u32[]{:S(2)}, u32[]{:S(2)}) async-start(bf16[32,10,3584]{2,1,0:T(8,128)(2,1)} %reshape.116), calls=%async_computation.2 | async-start | bytes 7340032 | tf_op jit(solution)/shard_map/all_to_all | solution.py:127
Sparse Core Ops, SparseCore 0:
  9.0 70.2 all-gather.6
  81.0 72.8 all-gather.8
  155.5 95.6 all-gather.10

commit v3 on v2

--- a/solution.py
+++ b/solution.py
@@ -3,10 +3,12 @@
 import jax
 import jax.numpy as jnp
 from jax import lax
-from jax.sharding import PartitionSpec as P
+from jax.sharding import Mesh, PartitionSpec as P
 
 HD = 128
 
+
+CTX = ("ctx_hi", "ctx_lo")
 
 masked_score = -1e30
 norm_eps = 1e-06
@@ -24,8 +26,8 @@
     query_rows = queries.shape[0]
     head_count = queries.shape[1] // HD
     scaling = 1.0 / math.sqrt(HD)
-    ctx_where = lax.axis_index("ctx")
-    ctx_count = lax.axis_size("ctx")
+    ctx_where = lax.axis_index(CTX)
+    ctx_count = lax.axis_size(CTX)
 
     def attend(carried, query_heads, pair_block, visible):
         key_count = pair_block.shape[1]
@@ -60,7 +62,7 @@
     pair_block = jnp.stack([keys, values])
     carried = attend(initial, query_heads, pair_block, diag_mask)
     for step_index in range(1, ctx_count):
-        pair_block = from_behind(pair_block, "ctx", 1)
+        pair_block = from_behind(pair_block, CTX, 1)
         carried = attend(carried, query_heads, pair_block, ctx_where >= step_index)
     attended = (
         (carried[2] / carried[1].T[:, :, None])
@@ -105,9 +107,13 @@
         .reshape(experts, capacity, width)
     )
     received = lax.all_to_all(outgoing, "exp", split_axis=0, concat_axis=0, tiled=True)
-    gate_full = lax.all_gather(w_gate[0], "ctx", axis=1, tiled=True)
-    up_full = lax.all_gather(w_up[0], "ctx", axis=1, tiled=True)
-    down_full = lax.all_gather(w_down[0], "ctx", axis=0, tiled=True)
+    def gather_quarters(local, axis):
+        across = lax.all_gather(local, "ctx_hi", axis=axis, tiled=True)
+        return lax.all_gather(across, "ctx_lo", axis=axis, tiled=True)
+
+    gate_full = gather_quarters(w_gate[0], 1)
+    up_full = gather_quarters(w_up[0], 1)
+    down_full = gather_quarters(w_down[0], 0)
     rows = received.reshape(experts * capacity, width)
     gate = jnp.dot(rows, gate_full, preferred_element_type=jnp.float32)
     upper = jnp.dot(rows, up_full, preferred_element_type=jnp.float32)
@@ -138,19 +144,20 @@
 
 def solution(mesh):
     in_specs = (
-        P("ctx", "exp"),
-        P("ctx", "exp"),
-        P("ctx", "exp"),
+        P(CTX, "exp"),
+        P(CTX, "exp"),
+        P(CTX, "exp"),
         P("exp", None),
-        P(("ctx", "exp"), None),
+        P((*CTX, "exp"), None),
         P(),
-        P(("ctx", "exp"), None),
-        P(("ctx", "exp"), None),
-        P("exp", None, "ctx"),
-        P("exp", None, "ctx"),
-        P("exp", "ctx", None),
+        P((*CTX, "exp"), None),
+        P((*CTX, "exp"), None),
+        P("exp", None, CTX),
+        P("exp", None, CTX),
+        P("exp", CTX, None),
     )
-    out_specs = P(("ctx", "exp"), None)
+    out_specs = P((*CTX, "exp"), None)
+    split_mesh = Mesh(mesh.devices.reshape(2, 2, -1), (*CTX, "exp"))
     return jax.shard_map(
-        per_device, mesh=mesh, in_specs=in_specs, out_specs=out_specs, check_vma=False
+        per_device, mesh=split_mesh, in_specs=in_specs, out_specs=out_specs, check_vma=False
     )

time: 434 us -> 444 us (1.023)
  waiting for transfers between devices: 234 us -> 244 us
  local copies, waits for them, and re-layouts: 23.8 us -> 30.1 us
  blocking collectives: 52.4 us -> 47.9 us
    all_gather x3 -> x6, waiting for transfers between devices: 0.02 us -> 94.4 us  [the longest x3 94.4 us: gather_quarters(): across = lax.all_gather(local, 'ctx_hi', axis=axis, tiled=True)]
    all_to_all x1, waiting for transfers between devices: 125 us -> 59.9 us  [per_device(): lax.all_to_all(term.astype(jnp.bfloat16).reshape(exp_count, query_rows //...]
    ppermute x3, waiting for transfers between devices: 56 us -> 38.3 us  [from_behind(): return lax.ppermute(shard, axis, pairs)]
    dot_general x4, matrix products: 12.5 us -> 17.2 us  [attend(): jnp.einsum('hqk,khd->qhd', expo_block.astype(jnp.bfloat16), value_heads,...]
    all_to_all x1, blocking collectives: 52.4 us -> 47.9 us  [per_device(): lax.all_to_all(outgoing, 'exp', split_axis=0, concat_axis=0, tiled=True)]
  transfers between devices with their start and end apart: 8 -> 11, of which waited for: 5 -> 6; matrix products, arithmetic and copies ran while one was open for 18% -> 18% of each run, Pallas kernels for 0% -> 0%
where the time goes in v3:
time: 444 us; the launch traced here: 443 us
  waiting for transfers between devices  244 us (55%)
  matrix products  57.7 us (13%)
  blocking collectives  47.9 us (11%)
  starting transfers between devices  33.8 us (8%)
  local copies, waits for them, and re-layouts  30.1 us (7%)
  other arithmetic  16.1 us (4%)
  between operations  13.8 us (3%)
    all_gather x3, waiting for transfers between devices, gather_quarters(): across = lax.all_gather(local, 'ctx_hi', axis=axis, tiled=True)  94.4 us
    all_to_all x1, waiting for transfers between devices, per_device(): lax.all_to_all(term.astype(jnp.bfloat16).reshape(exp_count, query_rows //...  59.9 us
    all_to_all x1, waiting for transfers between devices, per_device(): lax.all_to_all(expert_out, 'exp', split_axis=0, concat_axis=0, tiled=True)  49 us
    all_to_all x1, blocking collectives, per_device(): lax.all_to_all(outgoing, 'exp', split_axis=0, concat_axis=0, tiled=True)  47.9 us
    ppermute x3, waiting for transfers between devices, from_behind(): return lax.ppermute(shard, axis, pairs)  38.3 us
    ppermute x3, starting transfers between devices, from_behind(): return lax.ppermute(shard, axis, pairs)  18.1 us
    dot_general x4, matrix products, attend(): jnp.einsum('hqk,khd->qhd', expo_block.astype(jnp.bfloat16), value_heads,...  17.2 us
    all_to_all x1, starting transfers between devices, per_device(): lax.all_to_all(term.astype(jnp.bfloat16).reshape(exp_count, query_rows //...  10.6 us
  transfers between devices with their start and end apart: 11, of which 6 were waited for; matrix products, arithmetic and copies ran while one was open for 18% of the time, Pallas kernels for 0%

profile of v3, /device:TPU:1, one launch (start us, length us, event | category | flops | bytes accessed | tf_op | source)
XLA Modules:
  0.0 443.1 jit_solution(7619810947074779426)
XLA Ops:
  6.5 0.7 all-gather.13.cloned.1.call-update
  7.3 0.0 all-gather.17.cloned.1.call-start
  7.3 0.7 all-gather.17.cloned.1.call-update
  8.0 0.0 all-gather.21.cloned.1.call-start
  8.1 0.7 all-gather.21.cloned.1.call-update
  8.7 0.0 all-gather.15.cloned.1.call-start
  8.8 1.2 copy.53
  10.0 1.2 copy.30
  11.3 1.1 pad_maximum_fusion
  12.4 6.0 %collective-permute-start = (bf16[2,1024,256]{1,2,0:T(8,128)(2,1)}, bf16[2,1024,256]{1,2,0:T(8,128)(2,1)}, u32[]{:S(2)}, u32[]{:S(2)}) collective-permute-start(bf16[2,1024,256]{1,2,0:T(8,128)(2,1)} %pad_maximum_fusion), channel_id=1, source_target_pairs={{0,32},{32,64},{64,96},{1,33},{33,65},{65,97},{2,34},{34,66},{66,9... | collective-permute-start | bytes 3145736 | tf_op jit(solution)/shard_map/ppermute | solution.py:20
  18.4 51.1 %all-gather.13.cloned.1.call-done = bf16[1,3584,512]{2,1,0:T(8,128)(2,1)} async-done(((bf16[1,3584,256]{2,1,0:T(8,128)(2,1)}), bf16[1,3584,512]{2,1,0:T(8,128)(2,1)}) %all-gather.13.cloned.1.call-update) | async-done | bytes 3670032 | tf_op jit(solution)/shard_map/all_gather | solution.py:111
  69.5 0.0 all-gather.15.cloned.1.call-update
  69.6 0.0 all-gather.19.cloned.1.call-start
  69.6 6.2 %collective-permute-start.1 = (bf16[2,1024,256]{1,2,0:T(8,128)(2,1)}, bf16[2,1024,256]{1,2,0:T(8,128)(2,1)}, u32[]{:S(2)}, u32[]{:S(2)}) collective-permute-start(bf16[2,1024,256]{1,2,0:T(8,128)(2,1)} %collective-permute-done), channel_id=1, source_target_pairs={{0,32},{32,64},{64,96},{1,33},{33,65},{65,97},{2,34},{34,66},{66,9... | collective-permute-start | bytes 3145736 | tf_op jit(solution)/shard_map/ppermute | solution.py:20
  75.9 0.3 iota_compare_fusion
  76.2 2.9 fusion.3
  79.1 1.3 fusion.124
  80.4 9.9 %collective-permute-done.1 = bf16[2,1024,256]{1,2,0:T(8,128)(2,1)} collective-permute-done((bf16[2,1024,256]{1,2,0:T(8,128)(2,1)}, bf16[2,1024,256]{1,2,0:T(8,128)(2,1)}, u32[]{:S(2)}, u32[]{:S(2)}) %collective-permute-start.1) | collective-permute-done | bytes 1048608 | tf_op jit(solution)/shard_map/ppermute | solution.py:20
  90.3 5.9 %collective-permute-start.2 = (bf16[2,1024,256]{1,2,0:T(8,128)(2,1)}, bf16[2,1024,256]{1,2,0:T(8,128)(2,1)S(1)}, u32[]{:S(2)}, u32[]{:S(2)}) collective-permute-start(bf16[2,1024,256]{1,2,0:T(8,128)(2,1)} %collective-permute-done.1), channel_id=1, source_target_pairs={{0,32},{32,64},{64,96},{1,33},{33,65},{65,97},{2,34},{34,66},{66,9... | collective-permute-start | bytes 3145736 | tf_op jit(solution)/shard_map/ppermute | solution.py:20
  96.2 1.4 bitcast_reduce_fusion.2
  97.6 3.4 fusion.123
  101.0 1.4 bitcast_reduce_fusion.1
  102.4 28.4 %collective-permute-done.2 = bf16[2,1024,256]{1,2,0:T(8,128)(2,1)S(1)} collective-permute-done((bf16[2,1024,256]{1,2,0:T(8,128)(2,1)}, bf16[2,1024,256]{1,2,0:T(8,128)(2,1)S(1)}, u32[]{:S(2)}, u32[]{:S(2)}) %collective-permute-start.2) | collective-permute-done | bytes 1048608 | tf_op jit(solution)/shard_map/ppermute | solution.py:20
  130.8 0.9 fusion.122
  131.7 1.4 bitcast_reduce_fusion
  133.1 3.2 copy-done.4
  136.3 2.1 fusion.14
  138.4 2.0 fusion.8
  140.4 4.0 fusion.10
  144.5 3.6 fusion.65
  148.1 0.0 all-gather.19.cloned.1.call-update
  148.1 5.8 %fusion.56 = f32[1024,2,128]{0,2,1:T(8,128)S(1)} fusion(f32[1024,2,128]{0,2,1:T(8,128)} %fusion.65, bf16[1024,2,128]{0,2,1:T(8,128)(2,1)S(1)} %bitcast.245, f32[2,1024,1024]{1,2,0:T(8,128)} %copy-done.3, f32[2,1024]{1,0:T(2,128)S(1)} %get-tuple-element.10, pred[]{:T(512)S(6)} %ge.25, f32[1024,2]{0,1:T(2,128)S(1)} %get-tuple-element.7), kind=kOutput, calls=%fused_computation.51 | convolution fusion | flops 545783808 | bytes 11026433 | tf_op jit(solution)/shard_map/hqk,khd->qhd/dot_general | solution.py:46
  154.0 5.5 %fusion.59 = f32[1024,2,128]{0,2,1:T(8,128)S(1)} fusion(f32[1024,2,128]{0,2,1:T(8,128)S(1)} %fusion.56, bf16[1024,2,128]{0,2,1:T(8,128)(2,1)S(1)} %bitcast.246, f32[2,1024,1024]{1,2,0:T(8,128)} %copy-done.2, f32[2,1024]{1,0:T(2,128)S(1)} %get-tuple-element.9, pred[]{:T(512)S(6)} %ge.26, f32[1024,2]{0,1:T(2,128)S(1)} %get-tuple-element.6), kind=kOutput, calls=%fused_computation.52 | convolution fusion | flops 545783808 | bytes 11026433 | tf_op jit(solution)/shard_map/hqk,khd->qhd/dot_general | solution.py:46
  159.5 0.3 slice-done.1
  159.8 2.3 divide_convert_fusion
  162.1 5.1 %convolution_convert_fusion = bf16[1024,3584]{1,0:T(8,128)(2,1)} fusion(bf16[1024,256]{0,1:T(8,128)(2,1)S(1)} %bitcast.244, bf16[256,3584]{1,0:T(8,128)(2,1)S(1)} %copy-done), kind=kOutput, calls=%fused_computation.16 | convolution fusion | flops 1882718208 | bytes 9699328 | tf_op jit(solution)/shard_map/dot_general | solution.py:73
  167.2 10.6 %all-to-all-start = ((bf16[32,32,3584]{2,1,0:T(8,128)(2,1)}), bf16[32,32,3584]{2,1,0:T(8,128)(2,1)}, u32[]{:S(2)}, u32[]{:S(2)}) async-start(bf16[32,32,3584]{2,1,0:T(8,128)(2,1)} %bitcast.235), calls=%async_computation | async-start | bytes 14680064 | tf_op jit(solution)/shard_map/all_to_all | solution.py:75
  177.8 0.0 all-gather.23.cloned.1.call-start
  177.9 43.3 %all-gather.21.cloned.1.call-done = bf16[1,512,3584]{2,1,0:T(8,128)(2,1)} async-done(((bf16[1,256,3584]{2,1,0:T(8,128)(2,1)}), bf16[1,512,3584]{2,1,0:T(8,128)(2,1)}) %all-gather.21.cloned.1.call-update) | async-done | bytes 3670032 | tf_op jit(solution)/shard_map/all_gather | solution.py:111
  221.2 0.1 copy.42
  221.3 0.1 eq.61
  221.4 0.1 reshape.110
  221.5 0.8 reduce-window.6
  222.3 0.2 slice_reduce_fusion
  222.5 0.1 fusion.100
  222.6 59.9 %all-to-all-done = bf16[32,32,3584]{2,1,0:T(8,128)(2,1)} async-done(((bf16[32,32,3584]{2,1,0:T(8,128)(2,1)}), bf16[32,32,3584]{2,1,0:T(8,128)(2,1)}, u32[]{:S(2)}, u32[]{:S(2)}) %all-to-all-start) | async-done | bytes 7340064 | tf_op jit(solution)/shard_map/all_to_all | solution.py:75
  282.5 5.5 %convert_reduce_fusion = f32[32,3584]{1,0:T(8,128)S(1)} fusion(bf16[32,32,3584]{2,1,0:T(8,128)(2,1)} %all-to-all-done), kind=kLoop, calls=%fused_computation | loop fusion | flops 7225344 | bytes 7798784 | tf_op jit(solution)/shard_map/reduce_sum | solution.py:82
  287.9 0.2 multiply_reduce_fusion
  288.1 2.6 convolution_convert_fusion.1
  290.7 4.4 reshape.112
  295.1 47.9 %all_to_all.15 = bf16[32,10,3584]{2,1,0:T(8,128)(2,1)} all-to-all(bf16[32,10,3584]{2,1,0:T(8,128)(2,1)} %reshape.112), channel_id=1, replica_groups=mesh['ctx_hi'=2,'ctx_lo'=2,'exp'=32] {'exp'}, dimensions={0} | all-to-all | bytes 4587520 | tf_op jit(solution)/shard_map/all_to_all | solution.py:109
  343.0 4.5 %reshape.113 = bf16[320,3584]{1,0:T(8,128)(2,1)} reshape(bf16[32,10,3584]{2,1,0:T(8,128)(2,1)} %all_to_all.15) | data formatting | bytes 4587520 | tf_op jit(solution)/shard_map/reshape | solution.py:117
  347.5 7.4 %fusion.6 = f32[320,1024]{1,0:T(8,128)} fusion(bf16[320,3584]{1,0:T(8,128)(2,1)} %reshape.113, bf16[1,3584,1024]{2,1,0:T(8,128)(2,1)} %all-gather.15.cloned.1.call-done), kind=kOutput, calls=%fused_computation.20 | convolution fusion | flops 2348810240 | bytes 10944512 | tf_op jit(solution)/shard_map/dot_general | solution.py:118
  354.9 6.7 %fusion.44 = bf16[320,1024]{1,0:T(8,128)(2,1)S(1)} fusion(bf16[320,3584]{1,0:T(8,128)(2,1)} %reshape.113, bf16[1,3584,1024]{2,1,0:T(8,128)(2,1)} %all-gather.19.cloned.1.call-done, f32[320,1024]{1,0:T(8,128)} %fusion.6), kind=kOutput, calls=%fused_computation.47 | convolution fusion | flops 2350776320 | bytes 11599872 | tf_op jit(solution)/shard_map/dot_general | solution.py:119
  361.7 0.0 all-gather.23.cloned.1.call-done
  361.7 7.6 %convert_reduce_fusion.1 = bf16[320,3584]{1,0:T(8,128)(2,1)} fusion(bf16[4,256,3584]{2,1,0:T(8,128)(2,1)} %bitcast.248, bf16[40,4,8,256]{3,2,1,0:T(8,128)(2,1)S(1)} %bitcast.249), kind=kOutput, calls=%fused_computation.1 | convolution fusion | flops 2356838400 | bytes 10289152 | tf_op jit(solution)/shard_map/rqf,qfd->qrd/dot_general | solution.py:122
  369.3 4.5 %reshape.116 = bf16[32,10,3584]{2,1,0:T(8,128)(2,1)} reshape(bf16[320,3584]{1,0:T(8,128)(2,1)} %convert_reduce_fusion.1) | data formatting | bytes 4587520 | tf_op jit(solution)/shard_map/reshape | solution.py:131
  373.8 4.8 %all-to-all-start.2 = ((bf16[32,10,3584]{2,1,0:T(8,128)(2,1)}), bf16[32,10,3584]{2,1,0:T(8,128)(2,1)}, u32[]{:S(2)}, u32[]{:S(2)}) async-start(bf16[32,10,3584]{2,1,0:T(8,128)(2,1)} %reshape.116), calls=%async_computation.2 | async-start | bytes 7340032 | tf_op jit(solution)/shard_map/all_to_all | solution.py:133
  378.7 0.1 copy.41
  378.8 0.1 mul.123
  378.9 0.3 fusion.82
  379.2 49.0 %all-to-all-done.2 = bf16[32,10,3584]{2,1,0:T(8,128)(2,1)} async-done(((bf16[32,10,3584]{2,1,0:T(8,128)(2,1)}), bf16[32,10,3584]{2,1,0:T(8,128)(2,1)}, u32[]{:S(2)}, u32[]{:S(2)}) %all-to-all-start.2) | async-done | bytes 2293792 | tf_op jit(solution)/shard_map/all_to_all | solution.py:133
  428.2 4.5 %reshape.117 = bf16[320,3584]{1,0:T(8,128)(2,1)} reshape(bf16[32,10,3584]{2,1,0:T(8,128)(2,1)} %all-to-all-done.2) | data formatting | bytes 4587520 | tf_op jit(solution)/shard_map/reshape | solution.py:139
  432.7 3.6 fusion.16
  (40 shorter events, 0.2 us)
Async XLA Ops:
  6.5 155.6 %copy-start = (bf16[256,3584]{1,0:T(8,128)(2,1)S(1)}, bf16[256,3584]{1,0:T(8,128)(2,1)}, u32[]{:S(2)}) copy-start(bf16[256,3584]{1,0:T(8,128)(2,1)} %param.14) | copy-start | bytes 5505028
  6.5 69.7 %copy-start.5 = (bf16[1024,256]{1,0:T(8,128)(2,1)S(1)}, bf16[1024,256]{1,0:T(8,128)(2,1)}, u32[]{:S(2)}) copy-start(bf16[1024,256]{1,0:T(8,128)(2,1)} %param.11) | copy-start | bytes 1572868
  6.5 63.0 %all-gather.13.cloned.1.call-start = ((), (), s32[]{:S(2)}) async-start(), calls=%async_computation.3 | async-start | bytes 5505024 | tf_op jit(solution)/shard_map/all_gather | solution.py:111
  7.3 140.8 %all-gather.17.cloned.1.call-start = ((), (), s32[]{:S(2)}) async-start(), calls=%async_computation.5 | async-start | bytes 5505024 | tf_op jit(solution)/shard_map/all_gather | solution.py:111
  8.0 213.1 %all-gather.21.cloned.1.call-start = ((), (), s32[]{:S(2)}) async-start(), calls=%async_computation.7 | async-start | bytes 5505024 | tf_op jit(solution)/shard_map/all_gather | solution.py:111
  8.7 338.8 %all-gather.15.cloned.1.call-start = ((), (), s32[]{:S(2)}) async-start(), calls=%async_computation.4 | async-start | bytes 11010048 | tf_op jit(solution)/shard_map/all_gather | solution.py:112
  12.4 57.2 %collective-permute-start = (bf16[2,1024,256]{1,2,0:T(8,128)(2,1)}, bf16[2,1024,256]{1,2,0:T(8,128)(2,1)}, u32[]{:S(2)}, u32[]{:S(2)}) collective-permute-start(bf16[2,1024,256]{1,2,0:T(8,128)(2,1)} %pad_maximum_fusion), channel_id=1, source_target_pairs={{0,32},{32,64},{64,96},{1,33},{33,65},{65,97},{2,34},{34,66},{66,9... | collective-permute-start | bytes 3145736 | tf_op jit(solution)/shard_map/ppermute | solution.py:20
  69.6 285.3 %all-gather.19.cloned.1.call-start = ((), (), s32[]{:S(2)}) async-start(), calls=%async_computation.6 | async-start | bytes 11010048 | tf_op jit(solution)/shard_map/all_gather | solution.py:112
  69.6 20.6 %collective-permute-start.1 = (bf16[2,1024,256]{1,2,0:T(8,128)(2,1)}, bf16[2,1024,256]{1,2,0:T(8,128)(2,1)}, u32[]{:S(2)}, u32[]{:S(2)}) collective-permute-start(bf16[2,1024,256]{1,2,0:T(8,128)(2,1)} %collective-permute-done), channel_id=1, source_target_pairs={{0,32},{32,64},{64,96},{1,33},{33,65},{65,97},{2,34},{34,66},{66,9... | collective-permute-start | bytes 3145736 | tf_op jit(solution)/shard_map/ppermute | solution.py:20
  90.3 40.5 %collective-permute-start.2 = (bf16[2,1024,256]{1,2,0:T(8,128)(2,1)}, bf16[2,1024,256]{1,2,0:T(8,128)(2,1)S(1)}, u32[]{:S(2)}, u32[]{:S(2)}) collective-permute-start(bf16[2,1024,256]{1,2,0:T(8,128)(2,1)} %collective-permute-done.1), channel_id=1, source_target_pairs={{0,32},{32,64},{64,96},{1,33},{33,65},{65,97},{2,34},{34,66},{66,9... | collective-permute-start | bytes 3145736 | tf_op jit(solution)/shard_map/ppermute | solution.py:20
  97.6 42.8 %copy-start.3 = (f32[2,1024,1024]{1,2,0:T(8,128)}, f32[2,1024,1024]{1,2,0:T(8,128)S(1)}, u32[]{:S(2)}) copy-start(f32[2,1024,1024]{1,2,0:T(8,128)S(1)} %get-tuple-element.25) | copy-start | bytes 25165828
  102.4 38.0 %copy-start.2 = (f32[2,1024,1024]{1,2,0:T(8,128)}, f32[2,1024,1024]{1,2,0:T(8,128)S(1)}, u32[]{:S(2)}) copy-start(f32[2,1024,1024]{1,2,0:T(8,128)S(1)} %get-tuple-element.23) | copy-start | bytes 25165828
  133.1 3.2 copy-start.4
  148.1 5.9 %copy-start.7 = (bf16[1,1024,256]{1,2,0:T(8,128)(2,1)S(1)}, bf16[1,1024,256]{1,2,0:T(8,128)(2,1)}, u32[]{:S(2)}) copy-start(bf16[1,1024,256]{1,2,0:T(8,128)(2,1)} %get-tuple-element.13) | copy-start | bytes 1572868
  148.1 11.4 %slice-start = ((s8[8388608]{0:T(1024)(128)(4,1)}), s8[4194304]{0:T(1024)(128)(4,1)S(1)}, s32[]{:S(2)}) async-start(s8[8388608]{0:T(1024)(128)(4,1)} %bitcast.236), calls=%async_computation.9 | async-start | bytes 8388608
  153.9 5.5 %copy-start.8 = (bf16[1,1024,256]{1,2,0:T(8,128)(2,1)S(1)}, bf16[1,1024,256]{1,2,0:T(8,128)(2,1)}, u32[]{:S(2)}) copy-start(bf16[1,1024,256]{1,2,0:T(8,128)(2,1)} %get-tuple-element.11) | copy-start | bytes 1572868
  154.0 5.8 %slice-start.1 = ((s8[8388608]{0:T(1024)(128)(4,1)}), s8[4194304]{0:T(1024)(128)(4,1)S(1)}, s32[]{:S(2)}) async-start(s8[8388608]{0:T(1024)(128)(4,1)} %bitcast.236), calls=%async_computation.10 | async-start | bytes 8388608
  167.2 54.0 %copy-start.10 = (s32[32,8]{0,1:T(8,128)S(1)}, s32[32,8]{0,1:T(8,128)}, u32[]{:S(2)}) copy-start(s32[32,8]{0,1:T(8,128)} %param.17) | copy-start | bytes 3076
  167.2 115.3 %all-to-all-start = ((bf16[32,32,3584]{2,1,0:T(8,128)(2,1)}), bf16[32,32,3584]{2,1,0:T(8,128)(2,1)}, u32[]{:S(2)}, u32[]{:S(2)}) async-start(bf16[32,32,3584]{2,1,0:T(8,128)(2,1)} %bitcast.235), calls=%async_computation | async-start | bytes 14680064 | tf_op jit(solution)/shard_map/all_to_all | solution.py:75
  177.8 110.1 %copy-start.6 = (bf16[32,3584]{1,0:T(8,128)(2,1)S(1)}, bf16[32,3584]{1,0:T(8,128)(2,1)}, u32[]{:S(2)}) copy-start(bf16[32,3584]{1,0:T(8,128)(2,1)} %param.15) | copy-start | bytes 688132
  177.8 110.3 %copy-start.9 = (f32[3584]{0:T(1024)S(1)}, f32[3584]{0:T(1024)}, u32[]{:S(2)}) copy-start(f32[3584]{0:T(1024)} %param.16) | copy-start | bytes 43012
  177.8 183.8 %all-gather.23.cloned.1.call-start = ((), (), s32[]{:S(2)}) async-start(), calls=%async_computation.8 | async-start | bytes 11010048 | tf_op jit(solution)/shard_map/all_gather | solution.py:112
  369.3 9.4 %copy-start.11 = (f32[32,8]{0,1:T(8,128)S(1)}, f32[32,8]{0,1:T(8,128)}, u32[]{:S(2)}) copy-start(f32[32,8]{0,1:T(8,128)} %param.18) | copy-start | bytes 3076
  369.3 67.0 %copy-start.1 = (bf16[256,3584]{1,0:T(8,128)(2,1)S(1)}, bf16[256,3584]{1,0:T(8,128)(2,1)}, u32[]{:S(2)}) copy-start(bf16[256,3584]{1,0:T(8,128)(2,1)} %param.14) | copy-start | bytes 5505028
  373.8 54.4 %all-to-all-start.2 = ((bf16[32,10,3584]{2,1,0:T(8,128)(2,1)}), bf16[32,10,3584]{2,1,0:T(8,128)(2,1)}, u32[]{:S(2)}, u32[]{:S(2)}) async-start(bf16[32,10,3584]{2,1,0:T(8,128)(2,1)} %reshape.116), calls=%async_computation.2 | async-start | bytes 7340032 | tf_op jit(solution)/shard_map/all_to_all | solution.py:133
Sparse Core Ops, SparseCore 0:
  9.0 60.5 all-gather.12
  71.2 67.0 all-gather.16
  139.9 81.2 all-gather.20
  222.7 22.3 all-gather.14
  246.6 22.3 all-gather.18
  270.5 22.3 all-gather.22

commit v4 on v3

--- a/solution.py
+++ b/solution.py
@@ -108,8 +108,9 @@
     )
     received = lax.all_to_all(outgoing, "exp", split_axis=0, concat_axis=0, tiled=True)
     def gather_quarters(local, axis):
-        across = lax.all_gather(local, "ctx_hi", axis=axis, tiled=True)
-        return lax.all_gather(across, "ctx_lo", axis=axis, tiled=True)
+        swap = [(0, 1), (1, 0)]
+        across = jnp.concatenate([local, lax.ppermute(local, "ctx_hi", swap)], axis=axis)
+        return jnp.concatenate([across, lax.ppermute(across, "ctx_lo", swap)], axis=axis)
 
     gate_full = gather_quarters(w_gate[0], 1)
     up_full = gather_quarters(w_up[0], 1)

time: 444 us -> 462 us (1.041)
  waiting for transfers between devices: 244 us -> 309 us
  blocking collectives: 47.9 us -> 0 us
  other arithmetic: 16.1 us -> 33 us
  between operations: 13.8 us -> 0.37 us
  starting transfers between devices: 33.8 us -> 42.5 us
  matrix products: 57.7 us -> 50.8 us
  local copies, waits for them, and re-layouts: 30.1 us -> 23.8 us
    ppermute x0 -> x6, waiting for transfers between devices: none -> 194 us  [the longest x3 194 us: gather_quarters(): lax.ppermute(local, 'ctx_hi', swap)]
    all_gather x6 -> x0, waiting for transfers between devices: 94.4 us -> none  [the longest x3 94.4 us: gather_quarters(): across = lax.all_gather(local, 'ctx_hi', axis=axis, tiled=True)]
    all_to_all x1, waiting for transfers between devices: 59.9 us -> 0.01 us  [per_device(): lax.all_to_all(term.astype(jnp.bfloat16).reshape(exp_count, query_rows //...]
    all_to_all x1 -> x0, blocking collectives: 47.9 us -> none  [per_device(): lax.all_to_all(outgoing, 'exp', split_axis=0, concat_axis=0, tiled=True)]
    all_to_all x0 -> x1, waiting for transfers between devices: none -> 43.7 us  [per_device(): lax.all_to_all(outgoing, 'exp', split_axis=0, concat_axis=0, tiled=True)]
    concatenate x0 -> x4, other arithmetic: none -> 16.7 us  [the longest x3 10.7 us: gather_quarters(): jnp.concatenate([local, lax.ppermute(local, 'ctx_hi', swap)], axis=axis)]
    ppermute x3, waiting for transfers between devices: 38.3 us -> 23.8 us  [from_behind(): return lax.ppermute(shard, axis, pairs)]
    all_to_all x0 -> x1, starting transfers between devices: none -> 4.84 us  [per_device(): lax.all_to_all(outgoing, 'exp', split_axis=0, concat_axis=0, tiled=True)]
  transfers between devices with their start and end apart: 11 -> 12, of which waited for: 6 -> 8; matrix products, arithmetic and copies ran while one was open for 18% -> 11% of each run, Pallas kernels for 0% -> 0%
where the time goes in v4:
time: 462 us; the launch traced here: 459 us
  waiting for transfers between devices  309 us (67%)
  matrix products  50.8 us (11%)
  starting transfers between devices  42.5 us (9%)
  other arithmetic  33 us (7%)
  local copies, waits for them, and re-layouts  23.8 us (5%)
    ppermute x3, waiting for transfers between devices, gather_quarters(): lax.ppermute(local, 'ctx_hi', swap)  194 us
    all_to_all x1, waiting for transfers between devices, per_device(): lax.all_to_all(expert_out, 'exp', split_axis=0, concat_axis=0, tiled=True)  47.3 us
    all_to_all x1, waiting for transfers between devices, per_device(): lax.all_to_all(outgoing, 'exp', split_axis=0, concat_axis=0, tiled=True)  43.7 us
    ppermute x3, waiting for transfers between devices, from_behind(): return lax.ppermute(shard, axis, pairs)  23.8 us
    ppermute x3, starting transfers between devices, from_behind(): return lax.ppermute(shard, axis, pairs)  18 us
    dot_general x4, matrix products, attend(): jnp.einsum('hqk,khd->qhd', expo_block.astype(jnp.bfloat16), value_heads,...  12.5 us
    reduce_sum x3, other arithmetic, attend(): total_new = total_old * factor + jnp.sum(expo_block, axis=2)  10.8 us
    concatenate x3, other arithmetic, gather_quarters(): jnp.concatenate([local, lax.ppermute(local, 'ctx_hi', swap)], axis=axis)  10.7 us
  transfers between devices with their start and end apart: 12, of which 8 were waited for; matrix products, arithmetic and copies ran while one was open for 11% of the time, Pallas kernels for 0%

profile of v4, /device:TPU:1, one launch (start us, length us, event | category | flops | bytes accessed | tf_op | source)
XLA Modules:
  0.0 459.4 jit_solution(14677116424015142785)
XLA Ops:
  0.0 1.4 copy.53
  1.4 1.2 copy.30
  2.6 0.1 pad_maximum_fusion.4
  2.7 0.0 copy-start.3
  2.8 6.2 %collective-permute-start = (bf16[2,1024,256]{1,2,0:T(8,128)(2,1)S(1)}, bf16[2,1024,256]{1,2,0:T(8,128)(2,1)}, u32[]{:S(2)}, u32[]{:S(2)}) collective-permute-start(bf16[2,1024,256]{1,2,0:T(8,128)(2,1)S(1)} %pad_maximum_fusion.4), channel_id=1, source_target_pairs={{0,32},{32,64},{64,96},{1,33},{33,65},{65,97},{2,34},{34,66},{66,9... | collective-permute-start | bytes 3145736 | tf_op jit(solution)/shard_map/ppermute | solution.py:20
  8.9 11.7 %collective-permute-done = bf16[2,1024,256]{1,2,0:T(8,128)(2,1)} collective-permute-done((bf16[2,1024,256]{1,2,0:T(8,128)(2,1)S(1)}, bf16[2,1024,256]{1,2,0:T(8,128)(2,1)}, u32[]{:S(2)}, u32[]{:S(2)}) %collective-permute-start) | collective-permute-done | bytes 1048608 | tf_op jit(solution)/shard_map/ppermute | solution.py:20
  20.7 6.0 %collective-permute-start.1 = (bf16[2,1024,256]{1,2,0:T(8,128)(2,1)}, bf16[2,1024,256]{1,2,0:T(8,128)(2,1)}, u32[]{:S(2)}, u32[]{:S(2)}) collective-permute-start(bf16[2,1024,256]{1,2,0:T(8,128)(2,1)} %collective-permute-done), channel_id=1, source_target_pairs={{0,32},{32,64},{64,96},{1,33},{33,65},{65,97},{2,34},{34,66},{66,9... | collective-permute-start | bytes 3145736 | tf_op jit(solution)/shard_map/ppermute | solution.py:20
  26.7 0.3 iota_compare_fusion
  27.0 6.3 %fusion.3 = (f32[2,1024]{1,0:T(2,128)S(1)}, f32[2,1024,1024]{1,2,0:T(8,128)}) fusion(pred[1024,1024]{0,1:T(8,128)(4,1)S(1)} %iota_compare_fusion, bf16[1024,256]{1,0:T(8,128)(2,1)} %param.12, bf16[1024,256]{1,0:T(8,128)(2,1)} %param.11), kind=kOutput, calls=%fused_computation.17 | convolution fusion | flops 543160320 | bytes 10493952 | tf_op jit(solution)/shard_map/qhd,khd->hqk/dot_general | solution.py:37
  33.2 1.3 fusion.130
  34.5 4.2 collective-permute-done.1
  38.7 5.9 %collective-permute-start.2 = (bf16[2,1024,256]{1,2,0:T(8,128)(2,1)}, bf16[2,1024,256]{1,2,0:T(8,128)(2,1)S(1)}, u32[]{:S(2)}, u32[]{:S(2)}) collective-permute-start(bf16[2,1024,256]{1,2,0:T(8,128)(2,1)} %collective-permute-done.1), channel_id=1, source_target_pairs={{0,32},{32,64},{64,96},{1,33},{33,65},{65,97},{2,34},{34,66},{66,9... | collective-permute-start | bytes 3145736 | tf_op jit(solution)/shard_map/ppermute | solution.py:20
  44.6 1.4 bitcast_reduce_fusion.2
  46.0 1.3 fusion.129
  47.3 1.4 bitcast_reduce_fusion.1
  48.8 7.9 %collective-permute-done.2 = bf16[2,1024,256]{1,2,0:T(8,128)(2,1)S(1)} collective-permute-done((bf16[2,1024,256]{1,2,0:T(8,128)(2,1)}, bf16[2,1024,256]{1,2,0:T(8,128)(2,1)S(1)}, u32[]{:S(2)}, u32[]{:S(2)}) %collective-permute-start.2) | collective-permute-done | bytes 1048608 | tf_op jit(solution)/shard_map/ppermute | solution.py:20
  56.6 0.1 fusion.128
  56.7 1.4 bitcast_reduce_fusion
  58.1 2.3 fusion.22
  60.4 4.5 fusion.16
  64.9 4.0 fusion.18
  69.0 4.9 %fusion.67 = f32[1024,2,128]{0,2,1:T(8,128)S(1)} fusion(bf16[1024,2,128]{0,2,1:T(8,128)(2,1)S(1)} %bitcast.239, f32[2,1024,1024]{1,2,0:T(8,128)} %get-tuple-element.27, f32[2,1024]{1,0:T(2,128)S(1)} %get-tuple-element.19, pred[1024,1024]{0,1:T(8,128)(4,1)S(1)} %iota_compare_fusion, f32[1024,2]{0,1:T(2,128)S(1)} %get-tuple-element.17, ...), kind=kOutput, calls=%fused_computation.64 | convolution fusion | flops 545783808 | bytes 11034624 | tf_op jit(solution)/shard_map/hqk,khd->qhd/dot_general | solution.py:46
  73.9 2.6 fusion.58
  76.5 2.6 fusion.61
  79.1 2.4 divide_convert_fusion
  81.5 5.1 %convolution_convert_fusion = bf16[1024,3584]{1,0:T(8,128)(2,1)} fusion(bf16[1024,256]{0,1:T(8,128)(2,1)S(1)} %bitcast.247, bf16[256,3584]{1,0:T(8,128)(2,1)S(1)} %copy-done), kind=kOutput, calls=%fused_computation.16 | convolution fusion | flops 1882718208 | bytes 9699328 | tf_op jit(solution)/shard_map/dot_general | solution.py:73
  86.7 8.3 %all-to-all-start = ((bf16[32,32,3584]{2,1,0:T(8,128)(2,1)}), bf16[32,32,3584]{2,1,0:T(8,128)(2,1)}, u32[]{:S(2)}, u32[]{:S(2)}) async-start(bf16[32,32,3584]{2,1,0:T(8,128)(2,1)} %bitcast.228), calls=%async_computation | async-start | bytes 14680064 | tf_op jit(solution)/shard_map/all_to_all | solution.py:75
  95.0 0.1 collective-permute-start.7
  95.1 3.0 collective-permute-start.3
  98.1 0.1 collective-permute-start.5
  98.2 0.1 copy.42
  98.2 0.1 eq.61
  98.3 0.1 reshape.110
  98.4 0.6 reduce-window.6
  99.0 0.2 slice_reduce_fusion
  99.3 0.1 fusion.102
  99.4 0.0 copy-start.7
  99.4 132.1 %collective-permute-done.7 = bf16[256,3584]{1,0:T(8,128)(2,1)} collective-permute-done((bf16[256,3584]{1,0:T(8,128)(2,1)S(1)}, bf16[256,3584]{1,0:T(8,128)(2,1)}, u32[]{:S(2)}, u32[]{:S(2)}) %collective-permute-start.7) | collective-permute-done | bytes 1835040 | tf_op jit(solution)/shard_map/ppermute | solution.py:112
  231.5 3.5 pad_maximum_fusion.3
  235.0 35.9 %collective-permute-done.3 = bf16[3584,256]{1,0:T(8,128)(2,1)} collective-permute-done((bf16[3584,256]{1,0:T(8,128)(2,1)}, bf16[3584,256]{1,0:T(8,128)(2,1)}, u32[]{:S(2)}, u32[]{:S(2)}) %collective-permute-start.3) | collective-permute-done | bytes 1835040 | tf_op jit(solution)/shard_map/ppermute | solution.py:112
  270.9 3.5 pad_maximum_fusion.1
  274.5 0.0 collective-permute-start.4
  274.5 26.0 %collective-permute-done.5 = bf16[3584,256]{1,0:T(8,128)(2,1)} collective-permute-done((bf16[3584,256]{1,0:T(8,128)(2,1)}, bf16[3584,256]{1,0:T(8,128)(2,1)}, u32[]{:S(2)}, u32[]{:S(2)}) %collective-permute-start.5) | collective-permute-done | bytes 1835040 | tf_op jit(solution)/shard_map/ppermute | solution.py:112
  300.5 3.6 pad_maximum_fusion.2
  304.2 4.2 convert_reduce_fusion
  308.3 0.2 multiply_reduce_fusion
  308.5 2.5 convolution_convert_fusion.1
  311.0 4.4 reshape.112
  315.4 4.8 %all-to-all-start.1 = ((bf16[32,10,3584]{2,1,0:T(8,128)(2,1)}), bf16[32,10,3584]{2,1,0:T(8,128)(2,1)}, u32[]{:S(2)}, u32[]{:S(2)}) async-start(bf16[32,10,3584]{2,1,0:T(8,128)(2,1)} %reshape.112), calls=%async_computation.1 | async-start | bytes 7340032 | tf_op jit(solution)/shard_map/all_to_all | solution.py:109
  320.2 0.0 collective-permute-done.8
  320.3 6.0 %pad_maximum_fusion = bf16[1024,3584]{1,0:T(8,128)(2,1)} fusion(bf16[512,3584]{1,0:T(8,128)(2,1)} %collective-permute-done.8, bf16[256,3584]{1,0:T(8,128)(2,1)} %collective-permute-done.7, bf16[256,3584]{1,0:T(8,128)(2,1)S(1)} %bitcast.231), kind=kLoop, calls=%fused_computation.30 | loop fusion | flops 22020096 | bytes 14680064 | tf_op jit(solution)/shard_map/concatenate | solution.py:113
  326.3 43.7 %all-to-all-done.1 = bf16[32,10,3584]{2,1,0:T(8,128)(2,1)} async-done(((bf16[32,10,3584]{2,1,0:T(8,128)(2,1)}), bf16[32,10,3584]{2,1,0:T(8,128)(2,1)}, u32[]{:S(2)}, u32[]{:S(2)}) %all-to-all-start.1) | async-done | bytes 2293792 | tf_op jit(solution)/shard_map/all_to_all | solution.py:109
  370.0 4.5 reshape.113
  374.5 6.5 %fusion.4 = f32[320,1024]{1,0:T(8,128)S(1)} fusion(bf16[320,3584]{1,0:T(8,128)(2,1)} %reshape.113, bf16[3584,512]{1,0:T(8,128)(2,1)} %collective-permute-done.4, bf16[3584,256]{1,0:T(8,128)(2,1)} %collective-permute-done.3, bf16[3584,256]{1,0:T(8,128)(2,1)} %bitcast.242), kind=kOutput, calls=%fused_computation.18 | convolution fusion | flops 2370830336 | bytes 10944512 | tf_op jit(solution)/shard_map/dot_general | solution.py:119
  381.0 5.5 %multiply_convert_fusion = bf16[320,1024]{1,0:T(8,128)(2,1)S(1)} fusion(f32[320,1024]{1,0:T(8,128)S(1)} %fusion.4, bf16[320,3584]{1,0:T(8,128)(2,1)S(1)} %copy-done.4, bf16[3584,512]{1,0:T(8,128)(2,1)} %collective-permute-done.6, bf16[3584,256]{1,0:T(8,128)(2,1)} %collective-permute-done.5, bf16[3584,256]{1,0:T(8,128)(2,1)S(1)} %bitcast.246), kind=kOutput, calls=%fused_computation.65 | convolution fusion | flops 2372796416 | bytes 11599872 | tf_op jit(solution)/shard_map/dot_general | solution.py:120
  386.5 4.2 convert_reduce_fusion.1
  390.7 4.6 reshape.116
  395.3 8.2 %all-to-all-start.2 = ((bf16[32,10,3584]{2,1,0:T(8,128)(2,1)}), bf16[32,10,3584]{2,1,0:T(8,128)(2,1)}, u32[]{:S(2)}, u32[]{:S(2)}) async-start(bf16[32,10,3584]{2,1,0:T(8,128)(2,1)} %reshape.116), calls=%async_computation.2 | async-start | bytes 7340032 | tf_op jit(solution)/shard_map/all_to_all | solution.py:134
  403.5 0.1 copy.41
  403.6 0.1 mul.123
  403.7 0.3 fusion.84
  404.0 47.3 %all-to-all-done.2 = bf16[32,10,3584]{2,1,0:T(8,128)(2,1)} async-done(((bf16[32,10,3584]{2,1,0:T(8,128)(2,1)}), bf16[32,10,3584]{2,1,0:T(8,128)(2,1)}, u32[]{:S(2)}, u32[]{:S(2)}) %all-to-all-start.2) | async-done | bytes 2293792 | tf_op jit(solution)/shard_map/all_to_all | solution.py:134
  451.3 4.5 reshape.117
  455.8 3.6 fusion.24
  (39 shorter events, 0.2 us)
Async XLA Ops:
  0.0 81.5 %copy-start = (bf16[256,3584]{1,0:T(8,128)(2,1)S(1)}, bf16[256,3584]{1,0:T(8,128)(2,1)}, u32[]{:S(2)}) copy-start(bf16[256,3584]{1,0:T(8,128)(2,1)} %param.14) | copy-start | bytes 5505028
  2.7 41.8 %copy-start.3 = (bf16[1024,256]{1,0:T(8,128)(2,1)S(1)}, bf16[1024,256]{1,0:T(8,128)(2,1)}, u32[]{:S(2)}) copy-start(bf16[1024,256]{1,0:T(8,128)(2,1)} %param.11) | copy-start | bytes 1572868
  2.8 17.9 %collective-permute-start = (bf16[2,1024,256]{1,2,0:T(8,128)(2,1)S(1)}, bf16[2,1024,256]{1,2,0:T(8,128)(2,1)}, u32[]{:S(2)}, u32[]{:S(2)}) collective-permute-start(bf16[2,1024,256]{1,2,0:T(8,128)(2,1)S(1)} %pad_maximum_fusion.4), channel_id=1, source_target_pairs={{0,32},{32,64},{64,96},{1,33},{33,65},{65,97},{2,34},{34,66},{66,9... | collective-permute-start | bytes 3145736 | tf_op jit(solution)/shard_map/ppermute | solution.py:20
  20.7 18.0 %collective-permute-start.1 = (bf16[2,1024,256]{1,2,0:T(8,128)(2,1)}, bf16[2,1024,256]{1,2,0:T(8,128)(2,1)}, u32[]{:S(2)}, u32[]{:S(2)}) collective-permute-start(bf16[2,1024,256]{1,2,0:T(8,128)(2,1)} %collective-permute-done), channel_id=1, source_target_pairs={{0,32},{32,64},{64,96},{1,33},{33,65},{65,97},{2,34},{34,66},{66,9... | collective-permute-start | bytes 3145736 | tf_op jit(solution)/shard_map/ppermute | solution.py:20
  38.7 17.9 %collective-permute-start.2 = (bf16[2,1024,256]{1,2,0:T(8,128)(2,1)}, bf16[2,1024,256]{1,2,0:T(8,128)(2,1)S(1)}, u32[]{:S(2)}, u32[]{:S(2)}) collective-permute-start(bf16[2,1024,256]{1,2,0:T(8,128)(2,1)} %collective-permute-done.1), channel_id=1, source_target_pairs={{0,32},{32,64},{64,96},{1,33},{33,65},{65,97},{2,34},{34,66},{66,9... | collective-permute-start | bytes 3145736 | tf_op jit(solution)/shard_map/ppermute | solution.py:20
  86.7 8.3 %copy-start.2 = (bf16[1,256,3584]{2,1,0:T(8,128)(2,1)S(1)}, bf16[1,256,3584]{2,1,0:T(8,128)(2,1)}, u32[]{:S(2)}) copy-start(bf16[1,256,3584]{2,1,0:T(8,128)(2,1)} %param.21) | copy-start | bytes 5505028
  86.7 11.5 %copy-start.10 = (s32[32,8]{0,1:T(8,128)S(1)}, s32[32,8]{0,1:T(8,128)}, u32[]{:S(2)}) copy-start(s32[32,8]{0,1:T(8,128)} %param.17) | copy-start | bytes 3076
  86.7 217.5 %all-to-all-start = ((bf16[32,32,3584]{2,1,0:T(8,128)(2,1)}), bf16[32,32,3584]{2,1,0:T(8,128)(2,1)}, u32[]{:S(2)}, u32[]{:S(2)}) async-start(bf16[32,32,3584]{2,1,0:T(8,128)(2,1)} %bitcast.228), calls=%async_computation | async-start | bytes 14680064 | tf_op jit(solution)/shard_map/all_to_all | solution.py:75
  95.0 136.5 %collective-permute-start.7 = (bf16[256,3584]{1,0:T(8,128)(2,1)S(1)}, bf16[256,3584]{1,0:T(8,128)(2,1)}, u32[]{:S(2)}, u32[]{:S(2)}) collective-permute-start(bf16[256,3584]{1,0:T(8,128)(2,1)S(1)} %bitcast.229), channel_id=1, source_target_pairs={{0,64},{64,0},{1,65},{65,1},{2,66},{66,2},{3,67},{67,3},{4,68},{68... | collective-permute-start | bytes 5505032 | tf_op jit(solution)/shard_map/ppermute | solution.py:112
  95.1 175.8 %collective-permute-start.3 = (bf16[3584,256]{1,0:T(8,128)(2,1)}, bf16[3584,256]{1,0:T(8,128)(2,1)}, u32[]{:S(2)}, u32[]{:S(2)}) collective-permute-start(bf16[3584,256]{1,0:T(8,128)(2,1)} %bitcast.241), channel_id=1, source_target_pairs={{0,64},{64,0},{1,65},{65,1},{2,66},{66,2},{3,67},{67,3},{4,68},{68... | collective-permute-start | bytes 5505032 | tf_op jit(solution)/shard_map/ppermute | solution.py:112
  98.1 202.5 %collective-permute-start.5 = (bf16[3584,256]{1,0:T(8,128)(2,1)}, bf16[3584,256]{1,0:T(8,128)(2,1)}, u32[]{:S(2)}, u32[]{:S(2)}) collective-permute-start(bf16[3584,256]{1,0:T(8,128)(2,1)} %bitcast.244), channel_id=1, source_target_pairs={{0,64},{64,0},{1,65},{65,1},{2,66},{66,2},{3,67},{67,3},{4,68},{68... | collective-permute-start | bytes 5505032 | tf_op jit(solution)/shard_map/ppermute | solution.py:112
  99.2 171.7 %copy-start.6 = (bf16[1,3584,256]{2,1,0:T(8,128)(2,1)S(1)}, bf16[1,3584,256]{2,1,0:T(8,128)(2,1)}, u32[]{:S(2)}) copy-start(bf16[1,3584,256]{2,1,0:T(8,128)(2,1)} %param.19) | copy-start | bytes 5505028
  99.4 201.2 %copy-start.7 = (bf16[1,3584,256]{2,1,0:T(8,128)(2,1)S(1)}, bf16[1,3584,256]{2,1,0:T(8,128)(2,1)}, u32[]{:S(2)}) copy-start(bf16[1,3584,256]{2,1,0:T(8,128)(2,1)} %param.20) | copy-start | bytes 5505028
  235.0 85.2 %collective-permute-start.8 = (bf16[512,3584]{1,0:T(8,128)(2,1)}, bf16[512,3584]{1,0:T(8,128)(2,1)}, u32[]{:S(2)}, u32[]{:S(2)}) collective-permute-start(bf16[512,3584]{1,0:T(8,128)(2,1)} %pad_maximum_fusion.3), channel_id=1, source_target_pairs={{0,32},{32,0},{1,33},{33,1},{2,34},{34,2},{3,35},{35,3},{4,36},{36... | collective-permute-start | bytes 11010056 | tf_op jit(solution)/shard_map/ppermute | solution.py:113
  274.5 33.8 %copy-start.5 = (bf16[32,3584]{1,0:T(8,128)(2,1)S(1)}, bf16[32,3584]{1,0:T(8,128)(2,1)}, u32[]{:S(2)}) copy-start(bf16[32,3584]{1,0:T(8,128)(2,1)} %param.15) | copy-start | bytes 688132
  274.5 34.0 %copy-start.9 = (f32[3584]{0:T(1024)S(1)}, f32[3584]{0:T(1024)}, u32[]{:S(2)}) copy-start(f32[3584]{0:T(1024)} %param.16) | copy-start | bytes 43012
  274.5 100.0 %collective-permute-start.4 = (bf16[3584,512]{1,0:T(8,128)(2,1)}, bf16[3584,512]{1,0:T(8,128)(2,1)}, u32[]{:S(2)}, u32[]{:S(2)}) collective-permute-start(bf16[3584,512]{1,0:T(8,128)(2,1)} %pad_maximum_fusion.1), channel_id=1, source_target_pairs={{0,32},{32,0},{1,33},{33,1},{2,34},{34,2},{3,35},{35,3},{4,36},{36... | collective-permute-start | bytes 11010056 | tf_op jit(solution)/shard_map/ppermute | solution.py:113
  304.1 76.8 %collective-permute-start.6 = (bf16[3584,512]{1,0:T(8,128)(2,1)}, bf16[3584,512]{1,0:T(8,128)(2,1)}, u32[]{:S(2)}, u32[]{:S(2)}) collective-permute-start(bf16[3584,512]{1,0:T(8,128)(2,1)} %pad_maximum_fusion.2), channel_id=1, source_target_pairs={{0,32},{32,0},{1,33},{33,1},{2,34},{34,2},{3,35},{35,3},{4,36},{36... | collective-permute-start | bytes 11010056 | tf_op jit(solution)/shard_map/ppermute | solution.py:113
  315.4 54.6 %all-to-all-start.1 = ((bf16[32,10,3584]{2,1,0:T(8,128)(2,1)}), bf16[32,10,3584]{2,1,0:T(8,128)(2,1)}, u32[]{:S(2)}, u32[]{:S(2)}) async-start(bf16[32,10,3584]{2,1,0:T(8,128)(2,1)} %reshape.112), calls=%async_computation.1 | async-start | bytes 7340032 | tf_op jit(solution)/shard_map/all_to_all | solution.py:109
  374.5 6.5 %copy-start.4 = (bf16[320,3584]{1,0:T(8,128)(2,1)S(1)}, bf16[320,3584]{1,0:T(8,128)(2,1)}, u32[]{:S(2)}) copy-start(bf16[320,3584]{1,0:T(8,128)(2,1)} %reshape.113) | copy-start | bytes 6881284
  374.5 6.5 %copy-start.8 = (bf16[1,3584,256]{2,1,0:T(8,128)(2,1)S(1)}, bf16[1,3584,256]{2,1,0:T(8,128)(2,1)}, u32[]{:S(2)}) copy-start(bf16[1,3584,256]{2,1,0:T(8,128)(2,1)} %param.20) | copy-start | bytes 5505028
  374.5 12.0 %slice-start = ((s8[7340032]{0:T(1024)(128)(4,1)}), s8[4194304]{0:T(1024)(128)(4,1)S(1)}, s32[]{:S(2)}) async-start(s8[7340032]{0:T(1024)(128)(4,1)} %bitcast.232), calls=%async_computation.3 | async-start | bytes 8388608
  381.0 5.6 %slice-start.1 = ((s8[7340032]{0:T(1024)(128)(4,1)}), s8[3145728]{0:T(1024)(128)(4,1)S(1)}, s32[]{:S(2)}) async-start(s8[7340032]{0:T(1024)(128)(4,1)} %bitcast.232), calls=%async_computation.4 | async-start | bytes 6291456
  390.7 12.7 %copy-start.11 = (f32[32,8]{0,1:T(8,128)S(1)}, f32[32,8]{0,1:T(8,128)}, u32[]{:S(2)}) copy-start(f32[32,8]{0,1:T(8,128)} %param.18) | copy-start | bytes 3076
  390.7 68.6 %copy-start.1 = (bf16[256,3584]{1,0:T(8,128)(2,1)S(1)}, bf16[256,3584]{1,0:T(8,128)(2,1)}, u32[]{:S(2)}) copy-start(bf16[256,3584]{1,0:T(8,128)(2,1)} %param.14) | copy-start | bytes 5505028
  395.3 56.0 %all-to-all-start.2 = ((bf16[32,10,3584]{2,1,0:T(8,128)(2,1)}), bf16[32,10,3584]{2,1,0:T(8,128)(2,1)}, u32[]{:S(2)}, u32[]{:S(2)}) async-start(bf16[32,10,3584]{2,1,0:T(8,128)(2,1)} %reshape.116), calls=%async_computation.2 | async-start | bytes 7340032 | tf_op jit(solution)/shard_map/all_to_all | solution.py:134

commit v5 on v2

--- a/solution.py
+++ b/solution.py
@@ -102,7 +102,7 @@
     outgoing = (
         jnp.dot(pick_rows, normed, preferred_element_type=jnp.float32)
         .astype(jnp.bfloat16)
-        .reshape(experts, capacity, width)
+        .reshape(experts, 8, capacity * width // 8)
     )
     received = lax.all_to_all(outgoing, "exp", split_axis=0, concat_axis=0, tiled=True)
     gate_full = lax.all_gather(w_gate[0], "ctx", axis=1, tiled=True)
@@ -122,7 +122,7 @@
     expert_out = (
         jnp.sum(quarter_terms.astype(jnp.float32), axis=0)
         .astype(jnp.bfloat16)
-        .reshape(experts, capacity, width)
+        .reshape(experts, 8, capacity * width // 8)
     )
     returned = lax.all_to_all(expert_out, "exp", split_axis=0, concat_axis=0, tiled=True)
     weigh_rows = jnp.einsum(

time: 434 us -> 396 us (0.912)
  waiting for transfers between devices: 234 us -> 214 us
  blocking collectives: 52.4 us -> 37.7 us
    all_to_all x1, waiting for transfers between devices: 52.2 us -> 31.7 us  [per_device(): lax.all_to_all(expert_out, 'exp', split_axis=0, concat_axis=0, tiled=True)]
    all_to_all x1, blocking collectives: 52.4 us -> 37.7 us  [per_device(): lax.all_to_all(outgoing, 'exp', split_axis=0, concat_axis=0, tiled=True)]
  transfers between devices with their start and end apart: 8 -> 8, of which waited for: 5 -> 5; matrix products, arithmetic and copies ran while one was open for 18% -> 20% of each run, Pallas kernels for 0% -> 0%
where the time goes in v5:
time: 396 us; the launch traced here: 395 us
  waiting for transfers between devices  214 us (54%)
  matrix products  54.9 us (14%)
  blocking collectives  37.7 us (10%)
  starting transfers between devices  31.6 us (8%)
  local copies, waits for them, and re-layouts  25.8 us (7%)
  other arithmetic  17.7 us (4%)
  between operations  13.4 us (3%)
    all_to_all x1, waiting for transfers between devices, per_device(): lax.all_to_all(term.astype(jnp.bfloat16).reshape(exp_count, query_rows //...  125 us
    ppermute x3, waiting for transfers between devices, from_behind(): return lax.ppermute(shard, axis, pairs)  56 us
    all_to_all x1, blocking collectives, per_device(): lax.all_to_all(outgoing, 'exp', split_axis=0, concat_axis=0, tiled=True)  37.7 us
    all_to_all x1, waiting for transfers between devices, per_device(): lax.all_to_all(expert_out, 'exp', split_axis=0, concat_axis=0, tiled=True)  31.7 us
    ppermute x3, starting transfers between devices, from_behind(): return lax.ppermute(shard, axis, pairs)  17.8 us
    dot_general x4, matrix products, attend(): jnp.einsum('hqk,khd->qhd', expo_block.astype(jnp.bfloat16), value_heads,...  12.5 us
    reduce_sum x3, other arithmetic, attend(): total_new = total_old * factor + jnp.sum(expo_block, axis=2)  11 us
    dot_general x4, matrix products, attend(): jnp.einsum('qhd,khd->hqk', query_heads, key_heads, preferred_element_type...  10.5 us
  transfers between devices with their start and end apart: 8, of which 5 were waited for; matrix products, arithmetic and copies ran while one was open for 20% of the time, Pallas kernels for 0%

profile of v5, /device:TPU:1, one launch (start us, length us, event | category | flops | bytes accessed | tf_op | source)
XLA Modules:
  0.0 395.2 jit_solution(11546213702327123510)
XLA Ops:
  6.5 0.0 copy-start
  6.5 0.0 all-gather.7.cloned.1.call-start
  6.5 0.7 all-gather.7.cloned.1.call-update
  7.3 0.0 all-gather.9.cloned.1.call-start
  7.3 1.2 copy.53
  8.6 1.2 copy.30
  9.8 1.1 pad_maximum_fusion
  10.9 6.0 %collective-permute-start = (bf16[2,1024,256]{1,2,0:T(8,128)(2,1)}, bf16[2,1024,256]{1,2,0:T(8,128)(2,1)}, u32[]{:S(2)}, u32[]{:S(2)}) collective-permute-start(bf16[2,1024,256]{1,2,0:T(8,128)(2,1)} %pad_maximum_fusion), channel_id=1, source_target_pairs={{0,32},{32,64},{64,96},{1,33},{33,65},{65,97},{2,34},{34,66},{66,9... | collective-permute-start | bytes 3145736 | tf_op jit(solution)/shard_map/ppermute | solution.py:18
  16.9 0.0 all-gather.9.cloned.1.call-update
  17.0 21.3 %collective-permute-done = bf16[2,1024,256]{1,2,0:T(8,128)(2,1)} collective-permute-done((bf16[2,1024,256]{1,2,0:T(8,128)(2,1)}, bf16[2,1024,256]{1,2,0:T(8,128)(2,1)}, u32[]{:S(2)}, u32[]{:S(2)}) %collective-permute-start) | collective-permute-done | bytes 1048608 | tf_op jit(solution)/shard_map/ppermute | solution.py:18
  38.3 5.9 %collective-permute-start.1 = (bf16[2,1024,256]{1,2,0:T(8,128)(2,1)}, bf16[2,1024,256]{1,2,0:T(8,128)(2,1)}, u32[]{:S(2)}, u32[]{:S(2)}) collective-permute-start(bf16[2,1024,256]{1,2,0:T(8,128)(2,1)} %collective-permute-done), channel_id=1, source_target_pairs={{0,32},{32,64},{64,96},{1,33},{33,65},{65,97},{2,34},{34,66},{66,9... | collective-permute-start | bytes 3145736 | tf_op jit(solution)/shard_map/ppermute | solution.py:18
  44.2 0.3 iota_compare_fusion
  44.5 0.0 copy-done.2
  44.5 6.2 %fusion.3 = (f32[2,1024]{1,0:T(2,128)S(1)}, f32[2,1024,1024]{1,2,0:T(8,128)}) fusion(pred[1024,1024]{0,1:T(8,128)(4,1)S(1)} %iota_compare_fusion, bf16[1024,256]{1,0:T(8,128)(2,1)} %param.12, bf16[1024,256]{1,0:T(8,128)(2,1)S(1)} %copy-done.2), kind=kOutput, calls=%fused_computation.17 | convolution fusion | flops 543160320 | bytes 10493952 | tf_op jit(solution)/shard_map/qhd,khd->hqk/dot_general | solution.py:35
  50.6 1.3 fusion.124
  51.9 26.9 %collective-permute-done.1 = bf16[2,1024,256]{1,2,0:T(8,128)(2,1)} collective-permute-done((bf16[2,1024,256]{1,2,0:T(8,128)(2,1)}, bf16[2,1024,256]{1,2,0:T(8,128)(2,1)}, u32[]{:S(2)}, u32[]{:S(2)}) %collective-permute-start.1) | collective-permute-done | bytes 1048608 | tf_op jit(solution)/shard_map/ppermute | solution.py:18
  78.8 5.9 %collective-permute-start.2 = (bf16[2,1024,256]{1,2,0:T(8,128)(2,1)}, bf16[2,1024,256]{1,2,0:T(8,128)(2,1)S(1)}, u32[]{:S(2)}, u32[]{:S(2)}) collective-permute-start(bf16[2,1024,256]{1,2,0:T(8,128)(2,1)} %collective-permute-done.1), channel_id=1, source_target_pairs={{0,32},{32,64},{64,96},{1,33},{33,65},{65,97},{2,34},{34,66},{66,9... | collective-permute-start | bytes 3145736 | tf_op jit(solution)/shard_map/ppermute | solution.py:18
  84.7 1.4 bitcast_reduce_fusion.2
  86.1 1.3 fusion.123
  87.4 1.4 bitcast_reduce_fusion.1
  88.8 7.9 %collective-permute-done.2 = bf16[2,1024,256]{1,2,0:T(8,128)(2,1)S(1)} collective-permute-done((bf16[2,1024,256]{1,2,0:T(8,128)(2,1)}, bf16[2,1024,256]{1,2,0:T(8,128)(2,1)S(1)}, u32[]{:S(2)}, u32[]{:S(2)}) %collective-permute-start.2) | collective-permute-done | bytes 1048608 | tf_op jit(solution)/shard_map/ppermute | solution.py:18
  96.7 0.1 fusion.122
  96.8 1.4 bitcast_reduce_fusion
  98.2 2.3 fusion.14
  100.5 4.7 %fusion.8 = f32[2,1024]{1,0:T(2,128)S(1)} fusion(f32[2,1024,1024]{1,2,0:T(8,128)} %get-tuple-element.27, f32[2,1024]{1,0:T(2,128)S(1)} %get-tuple-element.19, pred[1024,1024]{0,1:T(8,128)(4,1)S(1)} %iota_compare_fusion), kind=kLoop, calls=%fused_computation.22 | loop fusion | flops 8386560 | bytes 9453568 | tf_op jit(solution)/shard_map/reduce_sum | solution.py:43
  105.2 4.0 %fusion.10 = (f32[2,1024]{1,0:T(2,128)S(1)}, f32[2,1024]{1,0:T(2,128)S(1)}) fusion(f32[2,1024,1024]{1,2,0:T(8,128)S(1)} %get-tuple-element.25, f32[2,1024]{1,0:T(2,128)S(1)} %get-tuple-element.10, pred[]{:T(512)S(6)} %ge.25, f32[2,1024]{1,0:T(2,128)S(1)} %get-tuple-element.9, f32[2,1024,1024]{1,2,0:T(8,128)S(1)} %get-tuple-element.23, pred[]{:T(512)S(6)} %ge.26), kind=kLoop, calls=%fused_computation.24 | loop fusion | flops 16773120 | bytes 16809986 | tf_op jit(solution)/shard_map/reduce_sum | solution.py:43
  109.3 4.9 %fusion.65 = f32[1024,2,128]{0,2,1:T(8,128)S(1)} fusion(bf16[1024,2,128]{0,2,1:T(8,128)(2,1)S(1)} %bitcast.240, f32[2,1024,1024]{1,2,0:T(8,128)} %get-tuple-element.27, f32[2,1024]{1,0:T(2,128)S(1)} %get-tuple-element.19, pred[1024,1024]{0,1:T(8,128)(4,1)S(1)} %iota_compare_fusion, f32[1024,2]{0,1:T(2,128)S(1)} %get-tuple-element.17, ...), kind=kOutput, calls=%fused_computation.54 | convolution fusion | flops 545783808 | bytes 11034624 | tf_op jit(solution)/shard_map/hqk,khd->qhd/dot_general | solution.py:44
  114.2 2.6 fusion.56
  116.8 2.6 fusion.59
  119.4 2.4 divide_convert_fusion
  121.8 5.1 %convolution_convert_fusion = bf16[1024,3584]{1,0:T(8,128)(2,1)} fusion(bf16[1024,256]{0,1:T(8,128)(2,1)S(1)} %bitcast.242, bf16[256,3584]{1,0:T(8,128)(2,1)S(1)} %copy-done), kind=kOutput, calls=%fused_computation.16 | convolution fusion | flops 1882718208 | bytes 9699328 | tf_op jit(solution)/shard_map/dot_general | solution.py:71
  126.9 9.0 %all-to-all-start = ((bf16[32,32,3584]{2,1,0:T(8,128)(2,1)}), bf16[32,32,3584]{2,1,0:T(8,128)(2,1)}, u32[]{:S(2)}, u32[]{:S(2)}) async-start(bf16[32,32,3584]{2,1,0:T(8,128)(2,1)} %bitcast.235), calls=%async_computation | async-start | bytes 14680064 | tf_op jit(solution)/shard_map/all_to_all | solution.py:73
  135.9 0.0 copy-start.3
  135.9 0.0 copy-start.4
  135.9 0.0 all-gather.11.cloned.1.call-start
  136.0 0.7 all-gather.11.cloned.1.call-update
  136.7 0.1 copy.42
  136.8 0.1 eq.61
  136.9 0.1 reshape.110
  137.0 0.8 reduce-window.6
  137.8 0.2 slice_reduce_fusion
  138.0 0.1 fusion.100
  138.1 124.8 %all-to-all-done = bf16[32,32,3584]{2,1,0:T(8,128)(2,1)} async-done(((bf16[32,32,3584]{2,1,0:T(8,128)(2,1)}), bf16[32,32,3584]{2,1,0:T(8,128)(2,1)}, u32[]{:S(2)}, u32[]{:S(2)}) %all-to-all-start) | async-done | bytes 7340064 | tf_op jit(solution)/shard_map/all_to_all | solution.py:73
  263.0 4.2 %convert_reduce_fusion = f32[32,3584]{1,0:T(8,128)S(1)} fusion(bf16[32,32,3584]{2,1,0:T(8,128)(2,1)} %all-to-all-done), kind=kLoop, calls=%fused_computation | loop fusion | flops 7225344 | bytes 7798784 | tf_op jit(solution)/shard_map/reduce_sum | solution.py:80
  267.1 0.2 multiply_reduce_fusion
  267.3 2.5 convolution_convert_fusion.1
  269.9 5.0 %reshape.112 = bf16[32,8,4480]{2,1,0:T(8,128)(2,1)} reshape(bf16[320,3584]{1,0:T(8,128)(2,1)} %convolution_convert_fusion.1) | data formatting | bytes 4587520 | tf_op jit(solution)/shard_map/reshape | solution.py:105
  274.9 37.7 %all_to_all.15 = bf16[32,8,4480]{2,1,0:T(8,128)(2,1)} all-to-all(bf16[32,8,4480]{2,1,0:T(8,128)(2,1)} %reshape.112), channel_id=1, replica_groups=mesh['ctx'=4,'exp'=32] {'exp'}, dimensions={0} | all-to-all | bytes 4587520 | tf_op jit(solution)/shard_map/all_to_all | solution.py:107
  312.6 5.0 %reshape.113 = bf16[320,3584]{1,0:T(8,128)(2,1)} reshape(bf16[32,8,4480]{2,1,0:T(8,128)(2,1)} %all_to_all.15) | data formatting | bytes 4587520 | tf_op jit(solution)/shard_map/reshape | solution.py:111
  317.6 6.3 %fusion.6 = f32[320,1024]{1,0:T(8,128)S(1)} fusion(bf16[320,3584]{1,0:T(8,128)(2,1)} %reshape.113, bf16[1,3584,1024]{2,1,0:T(8,128)(2,1)} %all-gather.7.cloned.1.call-done), kind=kOutput, calls=%fused_computation.20 | convolution fusion | flops 2348810240 | bytes 10944512 | tf_op jit(solution)/shard_map/dot_general | solution.py:112
  323.9 0.0 all-gather.9.cloned.1.call-done
  323.9 6.4 %fusion.44 = bf16[320,1024]{1,0:T(8,128)(2,1)S(1)} fusion(bf16[320,3584]{1,0:T(8,128)(2,1)} %reshape.113, bf16[1,3584,1024]{2,1,0:T(8,128)(2,1)} %all-gather.9.cloned.1.call-done, f32[320,1024]{1,0:T(8,128)S(1)} %fusion.6), kind=kOutput, calls=%fused_computation.47 | convolution fusion | flops 2350776320 | bytes 11599872 | tf_op jit(solution)/shard_map/dot_general | solution.py:113
  330.3 0.0 all-gather.11.cloned.1.call-done
  330.4 0.0 copy-start.6
  330.4 0.0 copy-start.1
  330.4 7.7 %convert_reduce_fusion.1 = bf16[320,3584]{1,0:T(8,128)(2,1)} fusion(bf16[4,256,3584]{2,1,0:T(8,128)(2,1)} %bitcast.246, bf16[40,4,8,256]{3,2,1,0:T(8,128)(2,1)S(1)} %bitcast.247), kind=kOutput, calls=%fused_computation.1 | convolution fusion | flops 2356838400 | bytes 10289152 | tf_op jit(solution)/shard_map/rqf,qfd->qrd/dot_general | solution.py:116
  338.1 5.0 %reshape.116 = bf16[32,8,4480]{2,1,0:T(8,128)(2,1)} reshape(bf16[320,3584]{1,0:T(8,128)(2,1)} %convert_reduce_fusion.1) | data formatting | bytes 4587520 | tf_op jit(solution)/shard_map/reshape | solution.py:125
  343.1 4.8 %all-to-all-start.2 = ((bf16[32,8,4480]{2,1,0:T(8,128)(2,1)}), bf16[32,8,4480]{2,1,0:T(8,128)(2,1)}, u32[]{:S(2)}, u32[]{:S(2)}) async-start(bf16[32,8,4480]{2,1,0:T(8,128)(2,1)} %reshape.116), calls=%async_computation.2 | async-start | bytes 4587520 | tf_op jit(solution)/shard_map/all_to_all | solution.py:127
  347.9 0.1 copy.41
  348.0 0.1 mul.119
  348.1 0.3 fusion.82
  348.4 31.7 %all-to-all-done.2 = bf16[32,8,4480]{2,1,0:T(8,128)(2,1)} async-done(((bf16[32,8,4480]{2,1,0:T(8,128)(2,1)}), bf16[32,8,4480]{2,1,0:T(8,128)(2,1)}, u32[]{:S(2)}, u32[]{:S(2)}) %all-to-all-start.2) | async-done | bytes 2293792 | tf_op jit(solution)/shard_map/all_to_all | solution.py:127
  380.1 5.0 %reshape.117 = bf16[320,3584]{1,0:T(8,128)(2,1)} reshape(bf16[32,8,4480]{2,1,0:T(8,128)(2,1)} %all-to-all-done.2) | data formatting | bytes 4587520 | tf_op jit(solution)/shard_map/reshape | solution.py:133
  385.1 3.6 fusion.16
  (16 shorter events, 0.1 us)
Async XLA Ops:
  6.5 115.3 %copy-start = (bf16[256,3584]{1,0:T(8,128)(2,1)S(1)}, bf16[256,3584]{1,0:T(8,128)(2,1)}, u32[]{:S(2)}) copy-start(bf16[256,3584]{1,0:T(8,128)(2,1)} %param.14) | copy-start | bytes 5505028
  6.5 37.9 %copy-start.2 = (bf16[1024,256]{1,0:T(8,128)(2,1)S(1)}, bf16[1024,256]{1,0:T(8,128)(2,1)}, u32[]{:S(2)}) copy-start(bf16[1024,256]{1,0:T(8,128)(2,1)} %param.11) | copy-start | bytes 1572868
  6.5 311.0 %all-gather.7.cloned.1.call-start = ((), (), s32[]{:S(2)}) async-start(), calls=%async_computation.3 | async-start | bytes 9175040 | tf_op jit(solution)/shard_map/all_gather | solution.py:108
  7.3 316.6 %all-gather.9.cloned.1.call-start = ((), (), s32[]{:S(2)}) async-start(), calls=%async_computation.4 | async-start | bytes 9175040 | tf_op jit(solution)/shard_map/all_gather | solution.py:109
  10.9 27.3 %collective-permute-start = (bf16[2,1024,256]{1,2,0:T(8,128)(2,1)}, bf16[2,1024,256]{1,2,0:T(8,128)(2,1)}, u32[]{:S(2)}, u32[]{:S(2)}) collective-permute-start(bf16[2,1024,256]{1,2,0:T(8,128)(2,1)} %pad_maximum_fusion), channel_id=1, source_target_pairs={{0,32},{32,64},{64,96},{1,33},{33,65},{65,97},{2,34},{34,66},{66,9... | collective-permute-start | bytes 3145736 | tf_op jit(solution)/shard_map/ppermute | solution.py:18
  38.3 40.5 %collective-permute-start.1 = (bf16[2,1024,256]{1,2,0:T(8,128)(2,1)}, bf16[2,1024,256]{1,2,0:T(8,128)(2,1)}, u32[]{:S(2)}, u32[]{:S(2)}) collective-permute-start(bf16[2,1024,256]{1,2,0:T(8,128)(2,1)} %collective-permute-done), channel_id=1, source_target_pairs={{0,32},{32,64},{64,96},{1,33},{33,65},{65,97},{2,34},{34,66},{66,9... | collective-permute-start | bytes 3145736 | tf_op jit(solution)/shard_map/ppermute | solution.py:18
  78.8 17.9 %collective-permute-start.2 = (bf16[2,1024,256]{1,2,0:T(8,128)(2,1)}, bf16[2,1024,256]{1,2,0:T(8,128)(2,1)S(1)}, u32[]{:S(2)}, u32[]{:S(2)}) collective-permute-start(bf16[2,1024,256]{1,2,0:T(8,128)(2,1)} %collective-permute-done.1), channel_id=1, source_target_pairs={{0,32},{32,64},{64,96},{1,33},{33,65},{65,97},{2,34},{34,66},{66,9... | collective-permute-start | bytes 3145736 | tf_op jit(solution)/shard_map/ppermute | solution.py:18
  126.9 9.8 %copy-start.5 = (s32[32,8]{0,1:T(8,128)S(1)}, s32[32,8]{0,1:T(8,128)}, u32[]{:S(2)}) copy-start(s32[32,8]{0,1:T(8,128)} %param.17) | copy-start | bytes 3076
  126.9 136.0 %all-to-all-start = ((bf16[32,32,3584]{2,1,0:T(8,128)(2,1)}), bf16[32,32,3584]{2,1,0:T(8,128)(2,1)}, u32[]{:S(2)}, u32[]{:S(2)}) async-start(bf16[32,32,3584]{2,1,0:T(8,128)(2,1)} %bitcast.235), calls=%async_computation | async-start | bytes 14680064 | tf_op jit(solution)/shard_map/all_to_all | solution.py:73
  135.9 131.2 %copy-start.3 = (bf16[32,3584]{1,0:T(8,128)(2,1)S(1)}, bf16[32,3584]{1,0:T(8,128)(2,1)}, u32[]{:S(2)}) copy-start(bf16[32,3584]{1,0:T(8,128)(2,1)} %param.15) | copy-start | bytes 688132
  135.9 131.4 %copy-start.4 = (f32[3584]{0:T(1024)S(1)}, f32[3584]{0:T(1024)}, u32[]{:S(2)}) copy-start(f32[3584]{0:T(1024)} %param.16) | copy-start | bytes 43012
  135.9 194.4 %all-gather.11.cloned.1.call-start = ((), (), s32[]{:S(2)}) async-start(), calls=%async_computation.5 | async-start | bytes 9175040 | tf_op jit(solution)/shard_map/all_gather | solution.py:110
  330.4 17.6 %copy-start.6 = (f32[32,8]{0,1:T(8,128)S(1)}, f32[32,8]{0,1:T(8,128)}, u32[]{:S(2)}) copy-start(f32[32,8]{0,1:T(8,128)} %param.18) | copy-start | bytes 3076
  330.4 58.3 %copy-start.1 = (bf16[256,3584]{1,0:T(8,128)(2,1)S(1)}, bf16[256,3584]{1,0:T(8,128)(2,1)}, u32[]{:S(2)}) copy-start(bf16[256,3584]{1,0:T(8,128)(2,1)} %param.14) | copy-start | bytes 5505028
  343.1 37.0 %all-to-all-start.2 = ((bf16[32,8,4480]{2,1,0:T(8,128)(2,1)}), bf16[32,8,4480]{2,1,0:T(8,128)(2,1)}, u32[]{:S(2)}, u32[]{:S(2)}) async-start(bf16[32,8,4480]{2,1,0:T(8,128)(2,1)} %reshape.116), calls=%async_computation.2 | async-start | bytes 4587520 | tf_op jit(solution)/shard_map/all_to_all | solution.py:127
Sparse Core Ops, SparseCore 0:
  9.0 70.2 all-gather.6
  81.0 72.8 all-gather.8
  155.5 95.6 all-gather.10

commit v6 on v5

--- a/solution.py
+++ b/solution.py
@@ -58,10 +58,12 @@
     row_ids = jnp.arange(query_rows)
     diag_mask = row_ids[:, None] >= row_ids[None, :]
     pair_block = jnp.stack([keys, values])
+    earlier_blocks = [from_behind(pair_block, "ctx", step) for step in range(1, ctx_count)]
     carried = attend(initial, query_heads, pair_block, diag_mask)
     for step_index in range(1, ctx_count):
-        pair_block = from_behind(pair_block, "ctx", 1)
-        carried = attend(carried, query_heads, pair_block, ctx_where >= step_index)
+        carried = attend(
+            carried, query_heads, earlier_blocks[step_index - 1], ctx_where >= step_index
+        )
     attended = (
         (carried[2] / carried[1].T[:, :, None])
         .astype(jnp.bfloat16)

time: 396 us -> 429 us (1.083)
  waiting for transfers between devices: 214 us -> 247 us
  starting transfers between devices: 31.6 us -> 22.8 us
  blocking collectives: 37.7 us -> 44.9 us
    all_to_all x1, waiting for transfers between devices: 125 us -> 144 us  [per_device(): lax.all_to_all(term.astype(jnp.bfloat16).reshape(exp_count, query_rows //...]
    ppermute x3, waiting for transfers between devices: 56 us -> 71.2 us  [from_behind(): return lax.ppermute(shard, axis, pairs)]
    ppermute x3, starting transfers between devices: 17.8 us -> 9.67 us  [from_behind(): return lax.ppermute(shard, axis, pairs)]
    all_to_all x1, blocking collectives: 37.7 us -> 44.9 us  [per_device(): lax.all_to_all(outgoing, 'exp', split_axis=0, concat_axis=0, tiled=True)]
  transfers between devices with their start and end apart: 8 -> 8, of which waited for: 5 -> 4; matrix products, arithmetic and copies ran while one was open for 20% -> 18% of each run, Pallas kernels for 0% -> 0%
where the time goes in v6:
time: 429 us; the launch traced here: 427 us
  waiting for transfers between devices  247 us (58%)
  matrix products  53.8 us (13%)
  blocking collectives  44.9 us (10%)
  local copies, waits for them, and re-layouts  29.8 us (7%)
  starting transfers between devices  22.8 us (5%)
  other arithmetic  15.1 us (4%)
  between operations  13.5 us (3%)
    all_to_all x1, waiting for transfers between devices, per_device(): lax.all_to_all(term.astype(jnp.bfloat16).reshape(exp_count, query_rows //...  144 us
    ppermute x3, waiting for transfers between devices, from_behind(): return lax.ppermute(shard, axis, pairs)  71.2 us
    all_to_all x1, blocking collectives, per_device(): lax.all_to_all(outgoing, 'exp', split_axis=0, concat_axis=0, tiled=True)  44.9 us
    all_to_all x1, waiting for transfers between devices, per_device(): lax.all_to_all(expert_out, 'exp', split_axis=0, concat_axis=0, tiled=True)  29 us
    dot_general x4, matrix products, attend(): jnp.einsum('hqk,khd->qhd', expo_block.astype(jnp.bfloat16), value_heads,...  11 us
    dot_general x4, matrix products, attend(): jnp.einsum('qhd,khd->hqk', query_heads, key_heads, preferred_element_type...  10.9 us
    ppermute x3, starting transfers between devices, from_behind(): return lax.ppermute(shard, axis, pairs)  9.67 us
  transfers between devices with their start and end apart: 8, of which 4 were waited for; matrix products, arithmetic and copies ran while one was open for 18% of the time, Pallas kernels for 0%

profile of v6, /device:TPU:1, one launch (start us, length us, event | category | flops | bytes accessed | tf_op | source)
XLA Modules:
  0.0 426.6 jit_solution(4889013684373228181)
XLA Ops:
  6.5 0.7 all-gather.7.cloned.1.call-update
  7.3 0.0 all-gather.9.cloned.1.call-start
  7.3 0.7 all-gather.9.cloned.1.call-update
  8.0 1.2 copy.53
  9.3 1.4 copy.30
  10.7 1.2 pad_maximum_fusion
  11.9 1.6 collective-permute-start.2
  13.5 6.1 %collective-permute-start.1 = (bf16[2,1024,256]{1,2,0:T(8,128)(2,1)}, bf16[2,1024,256]{1,2,0:T(8,128)(2,1)}, u32[]{:S(2)}, u32[]{:S(2)}) collective-permute-start(bf16[2,1024,256]{1,2,0:T(8,128)(2,1)} %pad_maximum_fusion), channel_id=1, source_target_pairs={{0,64},{32,96},{1,65},{33,97},{2,66},{34,98},{3,67},{35,99},{4,68}... | collective-permute-start | bytes 3145736 | tf_op jit(solution)/shard_map/ppermute | solution.py:18
  19.7 1.9 collective-permute-start
  21.6 0.3 iota_compare_fusion
  21.9 6.6 %fusion.3 = (f32[2,1024]{1,0:T(2,128)S(1)}, f32[2,1024,1024]{1,2,0:T(8,128)}) fusion(pred[1024,1024]{0,1:T(8,128)(4,1)S(1)} %iota_compare_fusion, bf16[1024,256]{1,0:T(8,128)(2,1)} %param.12, bf16[1024,256]{1,0:T(8,128)(2,1)S(1)} %copy-done.2), kind=kOutput, calls=%fused_computation.17 | convolution fusion | flops 543160320 | bytes 10493952 | tf_op jit(solution)/shard_map/qhd,khd->hqk/dot_general | solution.py:35
  28.5 0.0 collective-permute-done.2
  28.5 1.3 fusion.124
  29.8 29.8 %collective-permute-done.1 = bf16[2,1024,256]{1,2,0:T(8,128)(2,1)} collective-permute-done((bf16[2,1024,256]{1,2,0:T(8,128)(2,1)}, bf16[2,1024,256]{1,2,0:T(8,128)(2,1)}, u32[]{:S(2)}, u32[]{:S(2)}) %collective-permute-start.1) | collective-permute-done | bytes 1048608 | tf_op jit(solution)/shard_map/ppermute | solution.py:18
  59.5 2.1 fusion.123
  61.6 41.4 %collective-permute-done = bf16[2,1024,256]{1,2,0:T(8,128)(2,1)} collective-permute-done((bf16[2,1024,256]{1,2,0:T(8,128)(2,1)}, bf16[2,1024,256]{1,2,0:T(8,128)(2,1)}, u32[]{:S(2)}, u32[]{:S(2)}) %collective-permute-start) | collective-permute-done | bytes 1048608 | tf_op jit(solution)/shard_map/ppermute | solution.py:18
  103.0 2.1 fusion.122
  105.1 1.4 bitcast_reduce_fusion
  106.5 1.4 bitcast_reduce_fusion.1
  108.0 0.0 slice-start.1
  108.0 1.4 bitcast_reduce_fusion.2
  109.5 2.3 fusion.14
  111.8 2.0 fusion.8
  113.8 4.0 fusion.10
  117.8 0.0 slice-start.2
  117.9 3.1 fusion.35
  121.0 2.6 fusion.38
  123.7 0.9 slice-done.3
  124.6 2.8 fusion.65
  127.3 2.5 divide_convert_fusion
  129.8 5.1 %convolution_convert_fusion = bf16[1024,3584]{1,0:T(8,128)(2,1)} fusion(bf16[1024,256]{0,1:T(8,128)(2,1)S(1)} %bitcast.246, bf16[256,3584]{1,0:T(8,128)(2,1)S(1)} %copy-done), kind=kOutput, calls=%fused_computation.16 | convolution fusion | flops 1882718208 | bytes 9699328 | tf_op jit(solution)/shard_map/dot_general | solution.py:73
  134.9 8.3 %all-to-all-start = ((bf16[32,32,3584]{2,1,0:T(8,128)(2,1)}), bf16[32,32,3584]{2,1,0:T(8,128)(2,1)}, u32[]{:S(2)}, u32[]{:S(2)}) async-start(bf16[32,32,3584]{2,1,0:T(8,128)(2,1)} %bitcast.235), calls=%async_computation | async-start | bytes 14680064 | tf_op jit(solution)/shard_map/all_to_all | solution.py:75
  143.2 0.0 copy-start.7
  143.2 0.0 copy-start.10
  143.2 0.0 all-gather.11.cloned.1.call-start
  143.3 0.7 all-gather.11.cloned.1.call-update
  144.0 0.1 copy.42
  144.0 0.1 eq.61
  144.1 0.1 reshape.110
  144.2 0.8 reduce-window.6
  145.0 0.2 slice_reduce_fusion
  145.3 0.1 fusion.100
  145.4 144.4 %all-to-all-done = bf16[32,32,3584]{2,1,0:T(8,128)(2,1)} async-done(((bf16[32,32,3584]{2,1,0:T(8,128)(2,1)}), bf16[32,32,3584]{2,1,0:T(8,128)(2,1)}, u32[]{:S(2)}, u32[]{:S(2)}) %all-to-all-start) | async-done | bytes 7340064 | tf_op jit(solution)/shard_map/all_to_all | solution.py:75
  289.8 4.2 convert_reduce_fusion
  293.9 0.2 multiply_reduce_fusion
  294.1 2.5 convolution_convert_fusion.1
  296.7 5.0 %reshape.112 = bf16[32,8,4480]{2,1,0:T(8,128)(2,1)} reshape(bf16[320,3584]{1,0:T(8,128)(2,1)} %convolution_convert_fusion.1) | data formatting | bytes 4587520 | tf_op jit(solution)/shard_map/reshape | solution.py:107
  301.7 44.9 %all_to_all.15 = bf16[32,8,4480]{2,1,0:T(8,128)(2,1)} all-to-all(bf16[32,8,4480]{2,1,0:T(8,128)(2,1)} %reshape.112), channel_id=1, replica_groups=mesh['ctx'=4,'exp'=32] {'exp'}, dimensions={0} | all-to-all | bytes 4587520 | tf_op jit(solution)/shard_map/all_to_all | solution.py:109
  346.6 5.0 %reshape.113 = bf16[320,3584]{1,0:T(8,128)(2,1)} reshape(bf16[32,8,4480]{2,1,0:T(8,128)(2,1)} %all_to_all.15) | data formatting | bytes 4587520 | tf_op jit(solution)/shard_map/reshape | solution.py:113
  351.6 6.3 %fusion.6 = f32[320,1024]{1,0:T(8,128)S(1)} fusion(bf16[320,3584]{1,0:T(8,128)(2,1)} %reshape.113, bf16[1,3584,1024]{2,1,0:T(8,128)(2,1)} %all-gather.7.cloned.1.call-done), kind=kOutput, calls=%fused_computation.20 | convolution fusion | flops 2348810240 | bytes 10944512 | tf_op jit(solution)/shard_map/dot_general | solution.py:114
  357.9 0.0 all-gather.9.cloned.1.call-done
  358.0 6.4 %fusion.44 = bf16[320,1024]{1,0:T(8,128)(2,1)S(1)} fusion(bf16[320,3584]{1,0:T(8,128)(2,1)} %reshape.113, bf16[1,3584,1024]{2,1,0:T(8,128)(2,1)} %all-gather.9.cloned.1.call-done, f32[320,1024]{1,0:T(8,128)S(1)} %fusion.6), kind=kOutput, calls=%fused_computation.47 | convolution fusion | flops 2350776320 | bytes 11599872 | tf_op jit(solution)/shard_map/dot_general | solution.py:115
  364.4 0.0 all-gather.11.cloned.1.call-done
  364.4 0.0 copy-start.12
  364.4 0.0 copy-start.1
  364.4 7.7 %convert_reduce_fusion.1 = bf16[320,3584]{1,0:T(8,128)(2,1)} fusion(bf16[4,256,3584]{2,1,0:T(8,128)(2,1)} %bitcast.250, bf16[40,4,8,256]{3,2,1,0:T(8,128)(2,1)S(1)} %bitcast.251), kind=kOutput, calls=%fused_computation.1 | convolution fusion | flops 2356838400 | bytes 10289152 | tf_op jit(solution)/shard_map/rqf,qfd->qrd/dot_general | solution.py:118
  372.1 5.0 %reshape.116 = bf16[32,8,4480]{2,1,0:T(8,128)(2,1)} reshape(bf16[320,3584]{1,0:T(8,128)(2,1)} %convert_reduce_fusion.1) | data formatting | bytes 4587520 | tf_op jit(solution)/shard_map/reshape | solution.py:127
  377.2 4.8 %all-to-all-start.2 = ((bf16[32,8,4480]{2,1,0:T(8,128)(2,1)}), bf16[32,8,4480]{2,1,0:T(8,128)(2,1)}, u32[]{:S(2)}, u32[]{:S(2)}) async-start(bf16[32,8,4480]{2,1,0:T(8,128)(2,1)} %reshape.116), calls=%async_computation.2 | async-start | bytes 4587520 | tf_op jit(solution)/shard_map/all_to_all | solution.py:129
  382.0 0.1 copy.41
  382.0 0.1 mul.119
  382.1 0.3 fusion.82
  382.5 29.0 %all-to-all-done.2 = bf16[32,8,4480]{2,1,0:T(8,128)(2,1)} async-done(((bf16[32,8,4480]{2,1,0:T(8,128)(2,1)}), bf16[32,8,4480]{2,1,0:T(8,128)(2,1)}, u32[]{:S(2)}, u32[]{:S(2)}) %all-to-all-start.2) | async-done | bytes 2293792 | tf_op jit(solution)/shard_map/all_to_all | solution.py:129
  411.5 5.0 %reshape.117 = bf16[320,3584]{1,0:T(8,128)(2,1)} reshape(bf16[32,8,4480]{2,1,0:T(8,128)(2,1)} %all-to-all-done.2) | data formatting | bytes 4587520 | tf_op jit(solution)/shard_map/reshape | solution.py:135
  416.4 3.6 fusion.16
  (40 shorter events, 0.2 us)
Async XLA Ops:
  6.5 123.3 %copy-start = (bf16[256,3584]{1,0:T(8,128)(2,1)S(1)}, bf16[256,3584]{1,0:T(8,128)(2,1)}, u32[]{:S(2)}) copy-start(bf16[256,3584]{1,0:T(8,128)(2,1)} %param.14) | copy-start | bytes 5505028
  6.5 15.4 %copy-start.2 = (bf16[1024,256]{1,0:T(8,128)(2,1)S(1)}, bf16[1024,256]{1,0:T(8,128)(2,1)}, u32[]{:S(2)}) copy-start(bf16[1024,256]{1,0:T(8,128)(2,1)} %param.11) | copy-start | bytes 1572868
  6.5 345.1 %all-gather.7.cloned.1.call-start = ((), (), s32[]{:S(2)}) async-start(), calls=%async_computation.3 | async-start | bytes 9175040 | tf_op jit(solution)/shard_map/all_gather | solution.py:110
  7.3 350.7 %all-gather.9.cloned.1.call-start = ((), (), s32[]{:S(2)}) async-start(), calls=%async_computation.4 | async-start | bytes 9175040 | tf_op jit(solution)/shard_map/all_gather | solution.py:111
  9.3 10.4 %copy-start.5 = (bf16[1024,256]{0,1:T(8,128)(2,1)}, bf16[1024,256]{0,1:T(8,128)(2,1)S(1)}, u32[]{:S(2)}) copy-start(bf16[1024,256]{0,1:T(8,128)(2,1)S(1)} %copy.53) | copy-start | bytes 1572868
  11.9 16.6 %collective-permute-start.2 = (bf16[2,1024,256]{1,2,0:T(8,128)(2,1)}, bf16[2,1024,256]{1,2,0:T(8,128)(2,1)}, u32[]{:S(2)}, u32[]{:S(2)}) collective-permute-start(bf16[2,1024,256]{1,2,0:T(8,128)(2,1)} %pad_maximum_fusion), channel_id=1, source_target_pairs={{0,96},{1,97},{2,98},{3,99},{4,100},{5,101},{6,102},{7,103},{8,104... | collective-permute-start | bytes 3145736 | tf_op jit(solution)/shard_map/ppermute | solution.py:18
  13.5 46.0 %collective-permute-start.1 = (bf16[2,1024,256]{1,2,0:T(8,128)(2,1)}, bf16[2,1024,256]{1,2,0:T(8,128)(2,1)}, u32[]{:S(2)}, u32[]{:S(2)}) collective-permute-start(bf16[2,1024,256]{1,2,0:T(8,128)(2,1)} %pad_maximum_fusion), channel_id=1, source_target_pairs={{0,64},{32,96},{1,65},{33,97},{2,66},{34,98},{3,67},{35,99},{4,68}... | collective-permute-start | bytes 3145736 | tf_op jit(solution)/shard_map/ppermute | solution.py:18
  19.7 83.3 %collective-permute-start = (bf16[2,1024,256]{1,2,0:T(8,128)(2,1)}, bf16[2,1024,256]{1,2,0:T(8,128)(2,1)}, u32[]{:S(2)}, u32[]{:S(2)}) collective-permute-start(bf16[2,1024,256]{1,2,0:T(8,128)(2,1)} %pad_maximum_fusion), channel_id=1, source_target_pairs={{0,32},{32,64},{64,96},{1,33},{33,65},{65,97},{2,34},{34,66},{66,9... | collective-permute-start | bytes 3145736 | tf_op jit(solution)/shard_map/ppermute | solution.py:18
  21.9 89.9 %copy-start.3 = (pred[1024,1024]{0,1:T(8,128)(4,1)}, pred[1024,1024]{0,1:T(8,128)(4,1)S(1)}, u32[]{:S(2)}) copy-start(pred[1024,1024]{0,1:T(8,128)(4,1)S(1)} %iota_compare_fusion) | copy-start | bytes 3145732
  108.0 3.8 slice-start
  108.0 3.8 slice-start.1
  113.8 4.1 copy-start.9
  117.8 5.8 %slice-start.2 = ((s8[8388608]{0:T(1024)(128)(4,1)}), s8[4194304]{0:T(1024)(128)(4,1)S(1)}, s32[]{:S(2)}) async-start(s8[8388608]{0:T(1024)(128)(4,1)} %bitcast.238), calls=%async_computation.8 | async-start | bytes 8388608
  121.0 2.7 copy-start.4
  121.0 2.7 copy-start.6
  121.0 3.6 slice-start.3
  123.6 3.7 copy-start.8
  123.6 3.7 copy-start.13
  134.9 9.0 %copy-start.11 = (s32[32,8]{0,1:T(8,128)S(1)}, s32[32,8]{0,1:T(8,128)}, u32[]{:S(2)}) copy-start(s32[32,8]{0,1:T(8,128)} %param.17) | copy-start | bytes 3076
  134.9 154.8 %all-to-all-start = ((bf16[32,32,3584]{2,1,0:T(8,128)(2,1)}), bf16[32,32,3584]{2,1,0:T(8,128)(2,1)}, u32[]{:S(2)}, u32[]{:S(2)}) async-start(bf16[32,32,3584]{2,1,0:T(8,128)(2,1)} %bitcast.235), calls=%async_computation | async-start | bytes 14680064 | tf_op jit(solution)/shard_map/all_to_all | solution.py:75
  143.2 150.7 %copy-start.7 = (bf16[32,3584]{1,0:T(8,128)(2,1)S(1)}, bf16[32,3584]{1,0:T(8,128)(2,1)}, u32[]{:S(2)}) copy-start(bf16[32,3584]{1,0:T(8,128)(2,1)} %param.15) | copy-start | bytes 688132
  143.2 150.9 %copy-start.10 = (f32[3584]{0:T(1024)S(1)}, f32[3584]{0:T(1024)}, u32[]{:S(2)}) copy-start(f32[3584]{0:T(1024)} %param.16) | copy-start | bytes 43012
  143.2 221.2 %all-gather.11.cloned.1.call-start = ((), (), s32[]{:S(2)}) async-start(), calls=%async_computation.5 | async-start | bytes 9175040 | tf_op jit(solution)/shard_map/all_gather | solution.py:112
  364.4 17.6 %copy-start.12 = (f32[32,8]{0,1:T(8,128)S(1)}, f32[32,8]{0,1:T(8,128)}, u32[]{:S(2)}) copy-start(f32[32,8]{0,1:T(8,128)} %param.18) | copy-start | bytes 3076
  364.4 55.6 %copy-start.1 = (bf16[256,3584]{1,0:T(8,128)(2,1)S(1)}, bf16[256,3584]{1,0:T(8,128)(2,1)}, u32[]{:S(2)}) copy-start(bf16[256,3584]{1,0:T(8,128)(2,1)} %param.14) | copy-start | bytes 5505028
  377.2 34.3 %all-to-all-start.2 = ((bf16[32,8,4480]{2,1,0:T(8,128)(2,1)}), bf16[32,8,4480]{2,1,0:T(8,128)(2,1)}, u32[]{:S(2)}, u32[]{:S(2)}) async-start(bf16[32,8,4480]{2,1,0:T(8,128)(2,1)} %reshape.116), calls=%async_computation.2 | async-start | bytes 4587520 | tf_op jit(solution)/shard_map/all_to_all | solution.py:129
Sparse Core Ops, SparseCore 0:
  9.0 93.3 all-gather.6
  104.1 95.0 all-gather.8
  200.9 88.0 all-gather.10

commit v7 on v3

--- a/solution.py
+++ b/solution.py
@@ -104,12 +104,13 @@
     outgoing = (
         jnp.dot(pick_rows, normed, preferred_element_type=jnp.float32)
         .astype(jnp.bfloat16)
-        .reshape(experts, capacity, width)
+        .reshape(experts, 8, capacity * width // 8)
     )
     received = lax.all_to_all(outgoing, "exp", split_axis=0, concat_axis=0, tiled=True)
     def gather_quarters(local, axis):
-        across = lax.all_gather(local, "ctx_hi", axis=axis, tiled=True)
-        return lax.all_gather(across, "ctx_lo", axis=axis, tiled=True)
+        across = lax.ppermute(local, "ctx_hi", [(0, 1), (1, 0)])
+        pair = jnp.concatenate([local, across], axis=axis)
+        return lax.all_gather(pair, "ctx_lo", axis=axis, tiled=True)
 
     gate_full = gather_quarters(w_gate[0], 1)
     up_full = gather_quarters(w_up[0], 1)
@@ -128,7 +129,7 @@
     expert_out = (
         jnp.sum(quarter_terms.astype(jnp.float32), axis=0)
         .astype(jnp.bfloat16)
-        .reshape(experts, capacity, width)
+        .reshape(experts, 8, capacity * width // 8)
     )
     returned = lax.all_to_all(expert_out, "exp", split_axis=0, concat_axis=0, tiled=True)
     weigh_rows = jnp.einsum(

time: 444 us -> 443 us (level)
  other arithmetic: 16.1 us -> 28.4 us
  blocking collectives: 47.9 us -> 40.2 us
  waiting for transfers between devices: 244 us -> 237 us
    ppermute x0 -> x3, waiting for transfers between devices: none -> 161 us  [gather_quarters(): across = lax.ppermute(local, 'ctx_hi', [(0, 1), (1, 0)])]
    all_gather x6 -> x3, waiting for transfers between devices: 94.4 us -> 0.02 us  [gather_quarters(): return lax.all_gather(pair, 'ctx_lo', axis=axis, tiled=True)]
    all_to_all x1, waiting for transfers between devices: 59.9 us -> 0.01 us  [per_device(): lax.all_to_all(term.astype(jnp.bfloat16).reshape(exp_count, query_rows //...]
    all_to_all x1, waiting for transfers between devices: 49 us -> 27.1 us  [per_device(): lax.all_to_all(expert_out, 'exp', split_axis=0, concat_axis=0, tiled=True)]
    ppermute x3, waiting for transfers between devices: 38.3 us -> 48.9 us  [from_behind(): return lax.ppermute(shard, axis, pairs)]
    concatenate x0 -> x3, other arithmetic: none -> 9.39 us  [gather_quarters(): pair = jnp.concatenate([local, across], axis=axis)]
    all_to_all x1, blocking collectives: 47.9 us -> 40.2 us  [per_device(): lax.all_to_all(outgoing, 'exp', split_axis=0, concat_axis=0, tiled=True)]
    dot_general x4, matrix products: 7.21 us -> 13.7 us  [attend(): jnp.einsum('qhd,khd->hqk', query_heads, key_heads, preferred_element_type...]
  transfers between devices with their start and end apart: 11 -> 11, of which waited for: 6 -> 6; matrix products, arithmetic and copies ran while one was open for 18% -> 20% of each run, Pallas kernels for 0% -> 0%
where the time goes in v7:
time: 443 us; the launch traced here: 441 us
  waiting for transfers between devices  237 us (53%)
  matrix products  59.5 us (13%)
  blocking collectives  40.2 us (9%)
  starting transfers between devices  35.1 us (8%)
  other arithmetic  28.4 us (6%)
  local copies, waits for them, and re-layouts  27.7 us (6%)
  between operations  13.5 us (3%)
    ppermute x3, waiting for transfers between devices, gather_quarters(): across = lax.ppermute(local, 'ctx_hi', [(0, 1), (1, 0)])  161 us
    ppermute x3, waiting for transfers between devices, from_behind(): return lax.ppermute(shard, axis, pairs)  48.9 us
    all_to_all x1, blocking collectives, per_device(): lax.all_to_all(outgoing, 'exp', split_axis=0, concat_axis=0, tiled=True)  40.2 us
    all_to_all x1, waiting for transfers between devices, per_device(): lax.all_to_all(expert_out, 'exp', split_axis=0, concat_axis=0, tiled=True)  27.1 us
    ppermute x3, starting transfers between devices, from_behind(): return lax.ppermute(shard, axis, pairs)  18.2 us
    dot_general x4, matrix products, attend(): jnp.einsum('qhd,khd->hqk', query_heads, key_heads, preferred_element_type...  13.7 us
    dot_general x4, matrix products, attend(): jnp.einsum('hqk,khd->qhd', expo_block.astype(jnp.bfloat16), value_heads,...  12.6 us
    reduce_sum x3, other arithmetic, attend(): total_new = total_old * factor + jnp.sum(expo_block, axis=2)  12.2 us
  transfers between devices with their start and end apart: 11, of which 6 were waited for; matrix products, arithmetic and copies ran while one was open for 20% of the time, Pallas kernels for 0%

profile of v7, /device:TPU:1, one launch (start us, length us, event | category | flops | bytes accessed | tf_op | source)
XLA Modules:
  0.0 441.4 jit_solution(291137116958191233)
XLA Ops:
  6.5 3.6 collective-permute-start.3
  10.2 39.5 %collective-permute-done.3 = bf16[3584,256]{1,0:T(8,128)(2,1)S(1)} collective-permute-done((bf16[3584,256]{1,0:T(8,128)(2,1)}, bf16[3584,256]{1,0:T(8,128)(2,1)S(1)}, u32[]{:S(2)}, u32[]{:S(2)}) %collective-permute-start.3) | collective-permute-done | bytes 1835040 | tf_op jit(solution)/shard_map/ppermute | solution.py:111
  49.7 3.7 pad_maximum_fusion
  53.4 0.0 all-gather.4.cloned.1.call-update
  53.4 0.0 all-gather.6.cloned.1.call-start
  53.5 0.2 copy.53
  53.7 1.4 copy.30
  55.2 1.1 pad_maximum_fusion.3
  56.3 6.4 %collective-permute-start = (bf16[2,1024,256]{1,2,0:T(8,128)(2,1)}, bf16[2,1024,256]{1,2,0:T(8,128)(2,1)}, u32[]{:S(2)}, u32[]{:S(2)}) collective-permute-start(bf16[2,1024,256]{1,2,0:T(8,128)(2,1)} %pad_maximum_fusion.3), channel_id=1, source_target_pairs={{0,32},{32,64},{64,96},{1,33},{33,65},{65,97},{2,34},{34,66},{66,9... | collective-permute-start | bytes 3145736 | tf_op jit(solution)/shard_map/ppermute | solution.py:20
  62.7 0.1 collective-permute-start.4
  62.8 0.3 iota_compare_fusion
  63.1 22.1 %collective-permute-done = bf16[2,1024,256]{1,2,0:T(8,128)(2,1)} collective-permute-done((bf16[2,1024,256]{1,2,0:T(8,128)(2,1)}, bf16[2,1024,256]{1,2,0:T(8,128)(2,1)}, u32[]{:S(2)}, u32[]{:S(2)}) %collective-permute-start) | collective-permute-done | bytes 1048608 | tf_op jit(solution)/shard_map/ppermute | solution.py:20
  85.2 5.9 %collective-permute-start.1 = (bf16[2,1024,256]{1,2,0:T(8,128)(2,1)}, bf16[2,1024,256]{1,2,0:T(8,128)(2,1)}, u32[]{:S(2)}, u32[]{:S(2)}) collective-permute-start(bf16[2,1024,256]{1,2,0:T(8,128)(2,1)} %collective-permute-done), channel_id=1, source_target_pairs={{0,32},{32,64},{64,96},{1,33},{33,65},{65,97},{2,34},{34,66},{66,9... | collective-permute-start | bytes 3145736 | tf_op jit(solution)/shard_map/ppermute | solution.py:20
  91.1 6.2 %fusion.3 = (f32[2,1024]{1,0:T(2,128)S(1)}, f32[2,1024,1024]{1,2,0:T(8,128)}) fusion(pred[1024,1024]{0,1:T(8,128)(4,1)S(1)} %iota_compare_fusion, bf16[1024,256]{1,0:T(8,128)(2,1)} %param.12, bf16[1024,256]{1,0:T(8,128)(2,1)S(1)} %copy-done.2), kind=kOutput, calls=%fused_computation.17 | convolution fusion | flops 543160320 | bytes 10493952 | tf_op jit(solution)/shard_map/qhd,khd->hqk/dot_general | solution.py:37
  97.3 2.2 fusion.114
  99.5 4.6 %bitcast_reduce_fusion.2 = (f32[2,1024]{1,0:T(2,128)S(1)}, f32[2,1024,1024]{1,2,0:T(8,128)}) fusion(pred[]{:T(512)S(6)} %ge.25, bf16[1024,2,128]{0,2,1:T(8,128)(2,1)S(1)} %bitcast.234, bf16[1024,256]{1,0:T(8,128)(2,1)S(1)} %copy-done.2), kind=kOutput, calls=%fused_computation.9 | convolution fusion | flops 543160320 | bytes 9445377 | tf_op jit(solution)/shard_map/qhd,khd->hqk/dot_general | solution.py:37
  104.1 21.1 %collective-permute-done.1 = bf16[2,1024,256]{1,2,0:T(8,128)(2,1)} collective-permute-done((bf16[2,1024,256]{1,2,0:T(8,128)(2,1)}, bf16[2,1024,256]{1,2,0:T(8,128)(2,1)}, u32[]{:S(2)}, u32[]{:S(2)}) %collective-permute-start.1) | collective-permute-done | bytes 1048608 | tf_op jit(solution)/shard_map/ppermute | solution.py:20
  125.3 5.9 %collective-permute-start.2 = (bf16[2,1024,256]{1,2,0:T(8,128)(2,1)}, bf16[2,1024,256]{1,2,0:T(8,128)(2,1)}, u32[]{:S(2)}, u32[]{:S(2)}) collective-permute-start(bf16[2,1024,256]{1,2,0:T(8,128)(2,1)} %collective-permute-done.1), channel_id=1, source_target_pairs={{0,32},{32,64},{64,96},{1,33},{33,65},{65,97},{2,34},{34,66},{66,9... | collective-permute-start | bytes 3145736 | tf_op jit(solution)/shard_map/ppermute | solution.py:20
  131.2 3.7 pad_maximum_fusion.1
  134.8 0.0 all-gather.6.cloned.1.call-update
  134.9 1.3 fusion.113
  136.1 1.4 bitcast_reduce_fusion.1
  137.6 5.6 %collective-permute-done.2 = bf16[2,1024,256]{1,2,0:T(8,128)(2,1)} collective-permute-done((bf16[2,1024,256]{1,2,0:T(8,128)(2,1)}, bf16[2,1024,256]{1,2,0:T(8,128)(2,1)}, u32[]{:S(2)}, u32[]{:S(2)}) %collective-permute-start.2) | collective-permute-done | bytes 1048608 | tf_op jit(solution)/shard_map/ppermute | solution.py:20
  143.2 1.4 fusion.112
  144.6 1.4 bitcast_reduce_fusion
  146.1 2.3 fusion.10
  148.4 6.0 %fusion.4 = f32[2,1024]{1,0:T(2,128)S(1)} fusion(f32[2,1024,1024]{1,2,0:T(8,128)} %get-tuple-element.27, f32[2,1024]{1,0:T(2,128)S(1)} %get-tuple-element.19, pred[1024,1024]{0,1:T(8,128)(4,1)S(1)} %iota_compare_fusion), kind=kLoop, calls=%fused_computation.18 | loop fusion | flops 8386560 | bytes 9453568 | tf_op jit(solution)/shard_map/reduce_sum | solution.py:45
  154.4 0.2 slice-done.1
  154.6 4.0 fusion.6
  158.7 5.0 %fusion.55 = f32[1024,2,128]{0,2,1:T(8,128)S(1)} fusion(bf16[1024,2,128]{0,2,1:T(8,128)(2,1)S(1)} %bitcast.237, f32[2,1024,1024]{1,2,0:T(8,128)} %get-tuple-element.27, f32[2,1024]{1,0:T(2,128)S(1)} %get-tuple-element.19, pred[1024,1024]{0,1:T(8,128)(4,1)S(1)} %iota_compare_fusion, f32[1024,2]{0,1:T(2,128)S(1)} %get-tuple-element.17, ...), kind=kOutput, calls=%fused_computation.51 | convolution fusion | flops 545783808 | bytes 11034624 | tf_op jit(solution)/shard_map/hqk,khd->qhd/dot_general | solution.py:46
  163.7 2.7 fusion.46
  166.3 2.6 fusion.49
  169.0 2.4 divide_convert_fusion
  171.4 5.1 %convolution_convert_fusion = bf16[1024,3584]{1,0:T(8,128)(2,1)} fusion(bf16[1024,256]{0,1:T(8,128)(2,1)S(1)} %bitcast.245, bf16[256,3584]{1,0:T(8,128)(2,1)S(1)} %copy-done), kind=kOutput, calls=%fused_computation.16 | convolution fusion | flops 1882718208 | bytes 9699328 | tf_op jit(solution)/shard_map/dot_general | solution.py:73
  176.5 8.3 %all-to-all-start = ((bf16[32,32,3584]{2,1,0:T(8,128)(2,1)}), bf16[32,32,3584]{2,1,0:T(8,128)(2,1)}, u32[]{:S(2)}, u32[]{:S(2)}) async-start(bf16[32,32,3584]{2,1,0:T(8,128)(2,1)} %bitcast.230), calls=%async_computation | async-start | bytes 14680064 | tf_op jit(solution)/shard_map/all_to_all | solution.py:75
  184.8 0.0 all-gather.8.cloned.1.call-start
  184.8 0.1 collective-permute-start.5
  184.9 121.5 %collective-permute-done.5 = bf16[256,3584]{1,0:T(8,128)(2,1)S(1)} collective-permute-done((bf16[256,3584]{1,0:T(8,128)(2,1)S(1)}, bf16[256,3584]{1,0:T(8,128)(2,1)S(1)}, u32[]{:S(2)}, u32[]{:S(2)}) %collective-permute-start.5) | collective-permute-done | bytes 1835040 | tf_op jit(solution)/shard_map/ppermute | solution.py:111
  306.4 2.0 pad_maximum_fusion.2
  308.5 0.0 all-gather.8.cloned.1.call-update
  308.5 0.1 copy.42
  308.6 0.1 eq.61
  308.7 0.1 reshape.110
  308.8 0.8 reduce-window.6
  309.6 0.2 slice_reduce_fusion
  309.8 0.1 fusion.90
  309.9 4.2 convert_reduce_fusion
  314.1 0.2 multiply_reduce_fusion
  314.3 2.5 convolution_convert_fusion.1
  316.8 5.1 %reshape.112 = bf16[32,8,4480]{2,1,0:T(8,128)(2,1)} reshape(bf16[320,3584]{1,0:T(8,128)(2,1)} %convolution_convert_fusion.1) | data formatting | bytes 4587520 | tf_op jit(solution)/shard_map/reshape | solution.py:107
  321.9 40.2 %all_to_all.15 = bf16[32,8,4480]{2,1,0:T(8,128)(2,1)} all-to-all(bf16[32,8,4480]{2,1,0:T(8,128)(2,1)} %reshape.112), channel_id=1, replica_groups=mesh['ctx_hi'=2,'ctx_lo'=2,'exp'=32] {'exp'}, dimensions={0} | all-to-all | bytes 4587520 | tf_op jit(solution)/shard_map/all_to_all | solution.py:109
  362.1 5.0 %reshape.113 = bf16[320,3584]{1,0:T(8,128)(2,1)} reshape(bf16[32,8,4480]{2,1,0:T(8,128)(2,1)} %all_to_all.15) | data formatting | bytes 4587520 | tf_op jit(solution)/shard_map/reshape | solution.py:118
  367.1 7.4 %fusion.115 = f32[320,1024]{1,0:T(8,128)} fusion(bf16[320,3584]{1,0:T(8,128)(2,1)} %reshape.113, bf16[3584,1024]{1,0:T(8,128)(2,1)} %all-gather.4.cloned.1.call-done), kind=kOutput, calls=%fused_computation.134 | convolution fusion | flops 2348810240 | bytes 10944512 | tf_op jit(solution)/shard_map/dot_general | solution.py:119
  374.5 6.7 %multiply_convert_fusion = bf16[320,1024]{1,0:T(8,128)(2,1)S(1)} fusion(f32[320,1024]{1,0:T(8,128)} %fusion.115, bf16[320,3584]{1,0:T(8,128)(2,1)} %reshape.113, bf16[3584,1024]{1,0:T(8,128)(2,1)} %all-gather.6.cloned.1.call-done), kind=kOutput, calls=%fused_computation.52 | convolution fusion | flops 2350776320 | bytes 11599872 | tf_op jit(solution)/shard_map/dot_general | solution.py:120
  381.2 0.0 all-gather.8.cloned.1.call-done
  381.3 7.6 %convert_reduce_fusion.1 = bf16[320,3584]{1,0:T(8,128)(2,1)} fusion(bf16[4,256,3584]{2,1,0:T(8,128)(2,1)} %bitcast.249, bf16[40,4,8,256]{3,2,1,0:T(8,128)(2,1)S(1)} %bitcast.250), kind=kOutput, calls=%fused_computation.1 | convolution fusion | flops 2356838400 | bytes 10289152 | tf_op jit(solution)/shard_map/rqf,qfd->qrd/dot_general | solution.py:123
  388.8 5.1 %reshape.116 = bf16[32,8,4480]{2,1,0:T(8,128)(2,1)} reshape(bf16[320,3584]{1,0:T(8,128)(2,1)} %convert_reduce_fusion.1) | data formatting | bytes 4587520 | tf_op jit(solution)/shard_map/reshape | solution.py:132
  394.0 4.8 %all-to-all-start.2 = ((bf16[32,8,4480]{2,1,0:T(8,128)(2,1)}), bf16[32,8,4480]{2,1,0:T(8,128)(2,1)}, u32[]{:S(2)}, u32[]{:S(2)}) async-start(bf16[32,8,4480]{2,1,0:T(8,128)(2,1)} %reshape.116), calls=%async_computation.2 | async-start | bytes 4587520 | tf_op jit(solution)/shard_map/all_to_all | solution.py:134
  398.8 0.1 copy.41
  398.9 0.1 mul.123
  399.0 0.3 fusion.72
  399.3 27.1 %all-to-all-done.2 = bf16[32,8,4480]{2,1,0:T(8,128)(2,1)} async-done(((bf16[32,8,4480]{2,1,0:T(8,128)(2,1)}), bf16[32,8,4480]{2,1,0:T(8,128)(2,1)}, u32[]{:S(2)}, u32[]{:S(2)}) %all-to-all-start.2) | async-done | bytes 2293792 | tf_op jit(solution)/shard_map/all_to_all | solution.py:134
  426.3 5.0 %reshape.117 = bf16[320,3584]{1,0:T(8,128)(2,1)} reshape(bf16[32,8,4480]{2,1,0:T(8,128)(2,1)} %all-to-all-done.2) | data formatting | bytes 4587520 | tf_op jit(solution)/shard_map/reshape | solution.py:140
  431.3 3.6 fusion.12
  (42 shorter events, 0.2 us)
Async XLA Ops:
  6.5 164.8 %copy-start = (bf16[256,3584]{1,0:T(8,128)(2,1)S(1)}, bf16[256,3584]{1,0:T(8,128)(2,1)}, u32[]{:S(2)}) copy-start(bf16[256,3584]{1,0:T(8,128)(2,1)} %param.14) | copy-start | bytes 5505028
  6.5 47.0 %copy-start.8 = (bf16[1024,256]{1,0:T(8,128)(2,1)S(1)}, bf16[1024,256]{1,0:T(8,128)(2,1)}, u32[]{:S(2)}) copy-start(bf16[1024,256]{1,0:T(8,128)(2,1)} %param.13) | copy-start | bytes 1572868
  6.5 360.6 %all-gather.4.cloned.1.call-start = ((), (), s32[]{:S(2)}) async-start(), calls=%async_computation.3 | async-start | bytes 11010048 | tf_op jit(solution)/shard_map/all_gather | solution.py:113
  6.5 84.6 %copy-start.2 = (bf16[1024,256]{1,0:T(8,128)(2,1)S(1)}, bf16[1024,256]{1,0:T(8,128)(2,1)}, u32[]{:S(2)}) copy-start(bf16[1024,256]{1,0:T(8,128)(2,1)} %param.11) | copy-start | bytes 1572868
  6.5 43.2 %collective-permute-start.3 = (bf16[3584,256]{1,0:T(8,128)(2,1)}, bf16[3584,256]{1,0:T(8,128)(2,1)S(1)}, u32[]{:S(2)}, u32[]{:S(2)}) collective-permute-start(bf16[3584,256]{1,0:T(8,128)(2,1)} %bitcast.239), channel_id=1, source_target_pairs={{0,64},{64,0},{1,65},{65,1},{2,66},{66,2},{3,67},{67,3},{4,68},{68... | collective-permute-start | bytes 5505032 | tf_op jit(solution)/shard_map/ppermute | solution.py:111
  53.4 321.1 %all-gather.6.cloned.1.call-start = ((), (), s32[]{:S(2)}) async-start(), calls=%async_computation.4 | async-start | bytes 11010048 | tf_op jit(solution)/shard_map/all_gather | solution.py:113
  53.7 9.0 %copy-start.3 = (bf16[1024,256]{0,1:T(8,128)(2,1)}, bf16[1024,256]{0,1:T(8,128)(2,1)S(1)}, u32[]{:S(2)}) copy-start(bf16[1024,256]{0,1:T(8,128)(2,1)S(1)} %copy.53) | copy-start | bytes 1572868
  56.3 29.0 %collective-permute-start = (bf16[2,1024,256]{1,2,0:T(8,128)(2,1)}, bf16[2,1024,256]{1,2,0:T(8,128)(2,1)}, u32[]{:S(2)}, u32[]{:S(2)}) collective-permute-start(bf16[2,1024,256]{1,2,0:T(8,128)(2,1)} %pad_maximum_fusion.3), channel_id=1, source_target_pairs={{0,32},{32,64},{64,96},{1,33},{33,65},{65,97},{2,34},{34,66},{66,9... | collective-permute-start | bytes 3145736 | tf_op jit(solution)/shard_map/ppermute | solution.py:20
  62.7 68.5 %collective-permute-start.4 = (bf16[3584,256]{1,0:T(8,128)(2,1)}, bf16[3584,256]{1,0:T(8,128)(2,1)}, u32[]{:S(2)}, u32[]{:S(2)}) collective-permute-start(bf16[3584,256]{1,0:T(8,128)(2,1)} %bitcast.241), channel_id=1, source_target_pairs={{0,64},{64,0},{1,65},{65,1},{2,66},{66,2},{3,67},{67,3},{4,68},{68... | collective-permute-start | bytes 5505032 | tf_op jit(solution)/shard_map/ppermute | solution.py:111
  85.2 40.0 %collective-permute-start.1 = (bf16[2,1024,256]{1,2,0:T(8,128)(2,1)}, bf16[2,1024,256]{1,2,0:T(8,128)(2,1)}, u32[]{:S(2)}, u32[]{:S(2)}) collective-permute-start(bf16[2,1024,256]{1,2,0:T(8,128)(2,1)} %collective-permute-done), channel_id=1, source_target_pairs={{0,32},{32,64},{64,96},{1,33},{33,65},{65,97},{2,34},{34,66},{66,9... | collective-permute-start | bytes 3145736 | tf_op jit(solution)/shard_map/ppermute | solution.py:20
  97.3 33.8 %copy-start.6 = (bf16[1,3584,256]{2,1,0:T(8,128)(2,1)S(1)}, bf16[1,3584,256]{2,1,0:T(8,128)(2,1)}, u32[]{:S(2)}) copy-start(bf16[1,3584,256]{2,1,0:T(8,128)(2,1)} %param.20) | copy-start | bytes 5505028
  125.3 17.9 %collective-permute-start.2 = (bf16[2,1024,256]{1,2,0:T(8,128)(2,1)}, bf16[2,1024,256]{1,2,0:T(8,128)(2,1)}, u32[]{:S(2)}, u32[]{:S(2)}) collective-permute-start(bf16[2,1024,256]{1,2,0:T(8,128)(2,1)} %collective-permute-done.1), channel_id=1, source_target_pairs={{0,32},{32,64},{64,96},{1,33},{33,65},{65,97},{2,34},{34,66},{66,9... | collective-permute-start | bytes 3145736 | tf_op jit(solution)/shard_map/ppermute | solution.py:20
  146.1 8.3 %slice-start = ((s8[8388608]{0:T(1024)(128)(4,1)}), s8[4194304]{0:T(1024)(128)(4,1)S(1)}, s32[]{:S(2)}) async-start(s8[8388608]{0:T(1024)(128)(4,1)} %bitcast.231), calls=%async_computation.6 | async-start | bytes 8388608
  148.4 6.3 %slice-start.1 = ((s8[8388608]{0:T(1024)(128)(4,1)}), s8[4194304]{0:T(1024)(128)(4,1)S(1)}, s32[]{:S(2)}) async-start(s8[8388608]{0:T(1024)(128)(4,1)} %bitcast.231), calls=%async_computation.7 | async-start | bytes 8388608
  154.6 4.1 copy-start.4
  158.7 5.0 %copy-start.9 = (bf16[1,1024,256]{1,2,0:T(8,128)(2,1)S(1)}, bf16[1,1024,256]{1,2,0:T(8,128)(2,1)}, u32[]{:S(2)}) copy-start(bf16[1,1024,256]{1,2,0:T(8,128)(2,1)} %get-tuple-element.15) | copy-start | bytes 1572868
  176.5 8.3 %copy-start.7 = (bf16[1,256,3584]{2,1,0:T(8,128)(2,1)S(1)}, bf16[1,256,3584]{2,1,0:T(8,128)(2,1)}, u32[]{:S(2)}) copy-start(bf16[1,256,3584]{2,1,0:T(8,128)(2,1)} %param.21) | copy-start | bytes 5505028
  176.5 133.4 %all-to-all-start = ((bf16[32,32,3584]{2,1,0:T(8,128)(2,1)}), bf16[32,32,3584]{2,1,0:T(8,128)(2,1)}, u32[]{:S(2)}, u32[]{:S(2)}) async-start(bf16[32,32,3584]{2,1,0:T(8,128)(2,1)} %bitcast.230), calls=%async_computation | async-start | bytes 14680064 | tf_op jit(solution)/shard_map/all_to_all | solution.py:75
  184.8 123.7 %copy-start.11 = (s32[32,8]{0,1:T(8,128)S(1)}, s32[32,8]{0,1:T(8,128)}, u32[]{:S(2)}) copy-start(s32[32,8]{0,1:T(8,128)} %param.17) | copy-start | bytes 3076
  184.8 196.5 %all-gather.8.cloned.1.call-start = ((), (), s32[]{:S(2)}) async-start(), calls=%async_computation.5 | async-start | bytes 11010048 | tf_op jit(solution)/shard_map/all_gather | solution.py:113
  184.8 121.6 %collective-permute-start.5 = (bf16[256,3584]{1,0:T(8,128)(2,1)S(1)}, bf16[256,3584]{1,0:T(8,128)(2,1)S(1)}, u32[]{:S(2)}, u32[]{:S(2)}) collective-permute-start(bf16[256,3584]{1,0:T(8,128)(2,1)S(1)} %bitcast.243), channel_id=1, source_target_pairs={{0,64},{64,0},{1,65},{65,1},{2,66},{66,2},{3,67},{67,3},{4,68},{68... | collective-permute-start | bytes 5505032 | tf_op jit(solution)/shard_map/ppermute | solution.py:111
  308.5 5.6 %copy-start.5 = (bf16[32,3584]{1,0:T(8,128)(2,1)S(1)}, bf16[32,3584]{1,0:T(8,128)(2,1)}, u32[]{:S(2)}) copy-start(bf16[32,3584]{1,0:T(8,128)(2,1)} %param.15) | copy-start | bytes 688132
  308.5 5.8 %copy-start.10 = (f32[3584]{0:T(1024)S(1)}, f32[3584]{0:T(1024)}, u32[]{:S(2)}) copy-start(f32[3584]{0:T(1024)} %param.16) | copy-start | bytes 43012
  388.8 10.0 %copy-start.12 = (f32[32,8]{0,1:T(8,128)S(1)}, f32[32,8]{0,1:T(8,128)}, u32[]{:S(2)}) copy-start(f32[32,8]{0,1:T(8,128)} %param.18) | copy-start | bytes 3076
  388.8 46.1 %copy-start.1 = (bf16[256,3584]{1,0:T(8,128)(2,1)S(1)}, bf16[256,3584]{1,0:T(8,128)(2,1)}, u32[]{:S(2)}) copy-start(bf16[256,3584]{1,0:T(8,128)(2,1)} %param.14) | copy-start | bytes 5505028
  394.0 32.4 %all-to-all-start.2 = ((bf16[32,8,4480]{2,1,0:T(8,128)(2,1)}), bf16[32,8,4480]{2,1,0:T(8,128)(2,1)}, u32[]{:S(2)}, u32[]{:S(2)}) async-start(bf16[32,8,4480]{2,1,0:T(8,128)(2,1)} %reshape.116), calls=%async_computation.2 | async-start | bytes 4587520 | tf_op jit(solution)/shard_map/all_to_all | solution.py:134
Sparse Core Ops, SparseCore 0:
  53.6 24.9 all-gather.3
  135.0 20.8 all-gather.5
  308.6 29.8 all-gather.7

commit v8 on v5

--- a/solution.py
+++ b/solution.py
@@ -62,6 +62,9 @@
     for step_index in range(1, ctx_count):
         pair_block = from_behind(pair_block, "ctx", 1)
         carried = attend(carried, query_heads, pair_block, ctx_where >= step_index)
+    gate_local, up_local, down_local, _ = lax.optimization_barrier(
+        (w_gate[0], w_up[0], w_down[0], pair_block)
+    )
     attended = (
         (carried[2] / carried[1].T[:, :, None])
         .astype(jnp.bfloat16)
@@ -105,9 +108,9 @@
         .reshape(experts, 8, capacity * width // 8)
     )
     received = lax.all_to_all(outgoing, "exp", split_axis=0, concat_axis=0, tiled=True)
-    gate_full = lax.all_gather(w_gate[0], "ctx", axis=1, tiled=True)
-    up_full = lax.all_gather(w_up[0], "ctx", axis=1, tiled=True)
-    down_full = lax.all_gather(w_down[0], "ctx", axis=0, tiled=True)
+    gate_full = lax.all_gather(gate_local, "ctx", axis=1, tiled=True)
+    up_full = lax.all_gather(up_local, "ctx", axis=1, tiled=True)
+    down_full = lax.all_gather(down_local, "ctx", axis=0, tiled=True)
     rows = received.reshape(experts * capacity, width)
     gate = jnp.dot(rows, gate_full, preferred_element_type=jnp.float32)
     upper = jnp.dot(rows, up_full, preferred_element_type=jnp.float32)

time: 396 us -> 400 us (1.010)
  blocking collectives: 37.7 us -> 62.3 us
  waiting for transfers between devices: 214 us -> 193 us
    all_to_all x1, blocking collectives: 37.7 us -> 62.3 us  [per_device(): lax.all_to_all(outgoing, 'exp', split_axis=0, concat_axis=0, tiled=True)]
    ppermute x3, waiting for transfers between devices: 56 us -> 35.2 us  [from_behind(): return lax.ppermute(shard, axis, pairs)]
  transfers between devices with their start and end apart: 8 -> 8, of which waited for: 5 -> 5; matrix products, arithmetic and copies ran while one was open for 20% -> 18% of each run, Pallas kernels for 0% -> 0%
where the time goes in v8:
time: 400 us; the launch traced here: 399 us
  waiting for transfers between devices  193 us (48%)
  blocking collectives  62.3 us (16%)
  matrix products  55 us (14%)
  starting transfers between devices  30.9 us (8%)
  local copies, waits for them, and re-layouts  27 us (7%)
  other arithmetic  17.3 us (4%)
  between operations  13.4 us (3%)
    all_to_all x1, waiting for transfers between devices, per_device(): lax.all_to_all(term.astype(jnp.bfloat16).reshape(exp_count, query_rows //...  127 us
    all_to_all x1, blocking collectives, per_device(): lax.all_to_all(outgoing, 'exp', split_axis=0, concat_axis=0, tiled=True)  62.3 us
    ppermute x3, waiting for transfers between devices, from_behind(): return lax.ppermute(shard, axis, pairs)  35.2 us
    all_to_all x1, waiting for transfers between devices, per_device(): lax.all_to_all(expert_out, 'exp', split_axis=0, concat_axis=0, tiled=True)  30.2 us
    ppermute x3, starting transfers between devices, from_behind(): return lax.ppermute(shard, axis, pairs)  17.8 us
    dot_general x4, matrix products, attend(): jnp.einsum('hqk,khd->qhd', expo_block.astype(jnp.bfloat16), value_heads,...  12.6 us
    reduce_sum x3, other arithmetic, attend(): total_new = total_old * factor + jnp.sum(expo_block, axis=2)  11.4 us
    dot_general x4, matrix products, attend(): jnp.einsum('qhd,khd->hqk', query_heads, key_heads, preferred_element_type...  10.5 us
  transfers between devices with their start and end apart: 8, of which 5 were waited for; matrix products, arithmetic and copies ran while one was open for 18% of the time, Pallas kernels for 0%

profile of v8, /device:TPU:1, one launch (start us, length us, event | category | flops | bytes accessed | tf_op | source)
XLA Modules:
  0.0 399.4 jit_solution(13259591039778332623)
XLA Ops:
  6.5 0.0 all-gather.4.cloned.1.call-start
  6.5 1.4 copy.53
  7.9 1.2 copy.30
  9.2 0.1 pad_maximum_fusion
  9.3 6.0 %collective-permute-start = (bf16[2,1024,256]{1,2,0:T(8,128)(2,1)S(1)}, bf16[2,1024,256]{1,2,0:T(8,128)(2,1)S(1)}, u32[]{:S(2)}, u32[]{:S(2)}) collective-permute-start(bf16[2,1024,256]{1,2,0:T(8,128)(2,1)S(1)} %pad_maximum_fusion), channel_id=1, source_target_pairs={{0,32},{32,64},{64,96},{1,33},{33,65},{65,97},{2,34},{34,66},{66,9... | collective-permute-start | bytes 3145736 | tf_op jit(solution)/shard_map/ppermute | solution.py:18
  15.3 11.7 %collective-permute-done = bf16[2,1024,256]{1,2,0:T(8,128)(2,1)S(1)} collective-permute-done((bf16[2,1024,256]{1,2,0:T(8,128)(2,1)S(1)}, bf16[2,1024,256]{1,2,0:T(8,128)(2,1)S(1)}, u32[]{:S(2)}, u32[]{:S(2)}) %collective-permute-start) | collective-permute-done | bytes 1048608 | tf_op jit(solution)/shard_map/ppermute | solution.py:18
  27.1 1.0 copy-done.4
  28.1 5.9 %collective-permute-start.1 = (bf16[2,1024,256]{1,2,0:T(8,128)(2,1)S(1)}, bf16[2,1024,256]{1,2,0:T(8,128)(2,1)S(1)}, u32[]{:S(2)}, u32[]{:S(2)}) collective-permute-start(bf16[2,1024,256]{1,2,0:T(8,128)(2,1)S(1)} %collective-permute-done), channel_id=1, source_target_pairs={{0,32},{32,64},{64,96},{1,33},{33,65},{65,97},{2,34},{34,66},{66,9... | collective-permute-start | bytes 3145736 | tf_op jit(solution)/shard_map/ppermute | solution.py:18
  33.9 11.7 %collective-permute-done.1 = bf16[2,1024,256]{1,2,0:T(8,128)(2,1)S(1)} collective-permute-done((bf16[2,1024,256]{1,2,0:T(8,128)(2,1)S(1)}, bf16[2,1024,256]{1,2,0:T(8,128)(2,1)S(1)}, u32[]{:S(2)}, u32[]{:S(2)}) %collective-permute-start.1) | collective-permute-done | bytes 1048608 | tf_op jit(solution)/shard_map/ppermute | solution.py:18
  45.7 1.0 copy-done.6
  46.7 5.9 %collective-permute-start.2 = (bf16[2,1024,256]{1,2,0:T(8,128)(2,1)S(1)}, bf16[2,1024,256]{1,2,0:T(8,128)(2,1)}, u32[]{:S(2)}, u32[]{:S(2)}) collective-permute-start(bf16[2,1024,256]{1,2,0:T(8,128)(2,1)S(1)} %collective-permute-done.1), channel_id=1, source_target_pairs={{0,32},{32,64},{64,96},{1,33},{33,65},{65,97},{2,34},{34,66},{66,9... | collective-permute-start | bytes 3145736 | tf_op jit(solution)/shard_map/ppermute | solution.py:18
  52.6 11.7 %collective-permute-done.2 = bf16[2,1024,256]{1,2,0:T(8,128)(2,1)} collective-permute-done((bf16[2,1024,256]{1,2,0:T(8,128)(2,1)S(1)}, bf16[2,1024,256]{1,2,0:T(8,128)(2,1)}, u32[]{:S(2)}, u32[]{:S(2)}) %collective-permute-start.2) | collective-permute-done | bytes 1048608 | tf_op jit(solution)/shard_map/ppermute | solution.py:18
  64.3 0.0 all-gather.4.cloned.1.call-update
  64.3 0.0 all-gather.6.cloned.1.call-start
  64.4 0.7 all-gather.6.cloned.1.call-update
  65.1 0.3 iota_compare_fusion
  65.4 6.2 %fusion.3 = (f32[2,1024]{1,0:T(2,128)S(1)}, f32[2,1024,1024]{1,2,0:T(8,128)}) fusion(pred[1024,1024]{0,1:T(8,128)(4,1)S(1)} %iota_compare_fusion, bf16[1024,256]{1,0:T(8,128)(2,1)} %param.12, bf16[1024,256]{1,0:T(8,128)(2,1)S(1)} %copy-done.2), kind=kOutput, calls=%fused_computation.17 | convolution fusion | flops 543160320 | bytes 10493952 | tf_op jit(solution)/shard_map/qhd,khd->hqk/dot_general | solution.py:35
  71.6 0.1 fusion.115
  71.7 1.4 bitcast_reduce_fusion.2
  73.1 0.1 fusion.114
  73.2 1.4 bitcast_reduce_fusion.1
  74.6 1.3 fusion.113
  75.9 1.4 bitcast_reduce_fusion
  77.4 2.3 fusion.10
  79.6 5.2 %fusion.4 = f32[2,1024]{1,0:T(2,128)S(1)} fusion(f32[2,1024,1024]{1,2,0:T(8,128)} %get-tuple-element.33, f32[2,1024]{1,0:T(2,128)S(1)} %get-tuple-element.25, pred[1024,1024]{0,1:T(8,128)(4,1)S(1)} %iota_compare_fusion), kind=kLoop, calls=%fused_computation.18 | loop fusion | flops 8386560 | bytes 9453568 | tf_op jit(solution)/shard_map/reduce_sum | solution.py:43
  84.8 4.0 fusion.6
  88.9 4.9 %fusion.56 = f32[1024,2,128]{0,2,1:T(8,128)S(1)} fusion(bf16[1024,2,128]{0,2,1:T(8,128)(2,1)S(1)} %bitcast.235, f32[2,1024,1024]{1,2,0:T(8,128)} %get-tuple-element.33, f32[2,1024]{1,0:T(2,128)S(1)} %get-tuple-element.25, pred[1024,1024]{0,1:T(8,128)(4,1)S(1)} %iota_compare_fusion, f32[1024,2]{0,1:T(2,128)S(1)} %get-tuple-element.23, ...), kind=kOutput, calls=%fused_computation.50 | convolution fusion | flops 545783808 | bytes 11034624 | tf_op jit(solution)/shard_map/hqk,khd->qhd/dot_general | solution.py:44
  93.8 2.6 fusion.47
  96.4 2.6 fusion.50
  99.1 2.4 divide_convert_fusion
  101.4 5.1 %convolution_convert_fusion = bf16[1024,3584]{1,0:T(8,128)(2,1)} fusion(bf16[1024,256]{0,1:T(8,128)(2,1)S(1)} %bitcast.240, bf16[256,3584]{1,0:T(8,128)(2,1)S(1)} %copy-done), kind=kOutput, calls=%fused_computation.16 | convolution fusion | flops 1882718208 | bytes 9699328 | tf_op jit(solution)/shard_map/dot_general | solution.py:74
  106.5 8.3 %all-to-all-start = ((bf16[32,32,3584]{2,1,0:T(8,128)(2,1)}), bf16[32,32,3584]{2,1,0:T(8,128)(2,1)}, u32[]{:S(2)}, u32[]{:S(2)}) async-start(bf16[32,32,3584]{2,1,0:T(8,128)(2,1)} %bitcast.230), calls=%async_computation | async-start | bytes 14680064 | tf_op jit(solution)/shard_map/all_to_all | solution.py:76
  114.8 0.0 copy-start.3
  114.8 0.0 copy-start.8
  114.8 0.0 all-gather.8.cloned.1.call-start
  114.9 0.7 all-gather.8.cloned.1.call-update
  115.6 0.1 copy.42
  115.7 0.1 eq.61
  115.7 0.1 reshape.110
  115.8 0.8 reduce-window.6
  116.7 0.2 slice_reduce_fusion
  116.9 0.1 fusion.91
  117.0 126.7 %all-to-all-done = bf16[32,32,3584]{2,1,0:T(8,128)(2,1)} async-done(((bf16[32,32,3584]{2,1,0:T(8,128)(2,1)}), bf16[32,32,3584]{2,1,0:T(8,128)(2,1)}, u32[]{:S(2)}, u32[]{:S(2)}) %all-to-all-start) | async-done | bytes 7340064 | tf_op jit(solution)/shard_map/all_to_all | solution.py:76
  243.7 4.3 %convert_reduce_fusion = f32[32,3584]{1,0:T(8,128)S(1)} fusion(bf16[32,32,3584]{2,1,0:T(8,128)(2,1)} %all-to-all-done), kind=kLoop, calls=%fused_computation | loop fusion | flops 7225344 | bytes 7798784 | tf_op jit(solution)/shard_map/reduce_sum | solution.py:83
  248.0 0.2 multiply_reduce_fusion
  248.2 2.5 convolution_convert_fusion.1
  250.7 5.2 %reshape.112 = bf16[32,8,4480]{2,1,0:T(8,128)(2,1)} reshape(bf16[320,3584]{1,0:T(8,128)(2,1)} %convolution_convert_fusion.1) | data formatting | bytes 4587520 | tf_op jit(solution)/shard_map/reshape | solution.py:108
  255.9 62.3 %all_to_all.15 = bf16[32,8,4480]{2,1,0:T(8,128)(2,1)} all-to-all(bf16[32,8,4480]{2,1,0:T(8,128)(2,1)} %reshape.112), channel_id=1, replica_groups=mesh['ctx'=4,'exp'=32] {'exp'}, dimensions={0} | all-to-all | bytes 4587520 | tf_op jit(solution)/shard_map/all_to_all | solution.py:110
  318.3 5.0 %reshape.113 = bf16[320,3584]{1,0:T(8,128)(2,1)} reshape(bf16[32,8,4480]{2,1,0:T(8,128)(2,1)} %all_to_all.15) | data formatting | bytes 4587520 | tf_op jit(solution)/shard_map/reshape | solution.py:114
  323.3 6.3 %fusion.116 = f32[320,1024]{1,0:T(8,128)S(1)} fusion(bf16[320,3584]{1,0:T(8,128)(2,1)} %reshape.113, bf16[3584,1024]{1,0:T(8,128)(2,1)} %all-gather.4.cloned.1.call-done), kind=kOutput, calls=%fused_computation.132 | convolution fusion | flops 2348810240 | bytes 10944512 | tf_op jit(solution)/shard_map/dot_general | solution.py:115
  329.6 0.0 all-gather.6.cloned.1.call-done
  329.6 6.4 %fusion.37 = bf16[320,1024]{1,0:T(8,128)(2,1)S(1)} fusion(bf16[320,3584]{1,0:T(8,128)(2,1)} %reshape.113, bf16[3584,1024]{1,0:T(8,128)(2,1)} %all-gather.6.cloned.1.call-done, f32[320,1024]{1,0:T(8,128)S(1)} %fusion.116), kind=kOutput, calls=%fused_computation.43 | convolution fusion | flops 2350776320 | bytes 11599872 | tf_op jit(solution)/shard_map/dot_general | solution.py:116
  336.1 0.0 all-gather.8.cloned.1.call-done
  336.1 0.0 copy-start.10
  336.1 0.0 copy-start.1
  336.1 7.7 %convert_reduce_fusion.1 = bf16[320,3584]{1,0:T(8,128)(2,1)} fusion(bf16[4,256,3584]{2,1,0:T(8,128)(2,1)} %bitcast.244, bf16[40,4,8,256]{3,2,1,0:T(8,128)(2,1)S(1)} %bitcast.245), kind=kOutput, calls=%fused_computation.1 | convolution fusion | flops 2356838400 | bytes 10289152 | tf_op jit(solution)/shard_map/rqf,qfd->qrd/dot_general | solution.py:119
  343.8 5.0 %reshape.116 = bf16[32,8,4480]{2,1,0:T(8,128)(2,1)} reshape(bf16[320,3584]{1,0:T(8,128)(2,1)} %convert_reduce_fusion.1) | data formatting | bytes 4587520 | tf_op jit(solution)/shard_map/reshape | solution.py:128
  348.8 4.8 %all-to-all-start.2 = ((bf16[32,8,4480]{2,1,0:T(8,128)(2,1)}), bf16[32,8,4480]{2,1,0:T(8,128)(2,1)}, u32[]{:S(2)}, u32[]{:S(2)}) async-start(bf16[32,8,4480]{2,1,0:T(8,128)(2,1)} %reshape.116), calls=%async_computation.2 | async-start | bytes 4587520 | tf_op jit(solution)/shard_map/all_to_all | solution.py:130
  353.7 0.1 copy.41
  353.7 0.1 mul.119
  353.8 0.3 fusion.73
  354.1 30.2 %all-to-all-done.2 = bf16[32,8,4480]{2,1,0:T(8,128)(2,1)} async-done(((bf16[32,8,4480]{2,1,0:T(8,128)(2,1)}), bf16[32,8,4480]{2,1,0:T(8,128)(2,1)}, u32[]{:S(2)}, u32[]{:S(2)}) %all-to-all-start.2) | async-done | bytes 2293792 | tf_op jit(solution)/shard_map/all_to_all | solution.py:130
  384.3 5.0 %reshape.117 = bf16[320,3584]{1,0:T(8,128)(2,1)} reshape(bf16[32,8,4480]{2,1,0:T(8,128)(2,1)} %all-to-all-done.2) | data formatting | bytes 4587520 | tf_op jit(solution)/shard_map/reshape | solution.py:136
  389.3 3.6 fusion.12
  (24 shorter events, 0.2 us)
Async XLA Ops:
  6.5 94.9 %copy-start = (bf16[256,3584]{1,0:T(8,128)(2,1)S(1)}, bf16[256,3584]{1,0:T(8,128)(2,1)}, u32[]{:S(2)}) copy-start(bf16[256,3584]{1,0:T(8,128)(2,1)} %param.14) | copy-start | bytes 5505028
  6.5 58.9 %copy-start.2 = (bf16[1024,256]{1,0:T(8,128)(2,1)S(1)}, bf16[1024,256]{1,0:T(8,128)(2,1)}, u32[]{:S(2)}) copy-start(bf16[1024,256]{1,0:T(8,128)(2,1)} %param.11) | copy-start | bytes 1572868
  6.5 316.8 %all-gather.4.cloned.1.call-start = ((), (), s32[]{:S(2)}) async-start(), calls=%async_computation.3 | async-start | bytes 9175040 | tf_op jit(solution)/shard_map/all_gather | solution.py:111
  9.3 17.8 %collective-permute-start = (bf16[2,1024,256]{1,2,0:T(8,128)(2,1)S(1)}, bf16[2,1024,256]{1,2,0:T(8,128)(2,1)S(1)}, u32[]{:S(2)}, u32[]{:S(2)}) collective-permute-start(bf16[2,1024,256]{1,2,0:T(8,128)(2,1)S(1)} %pad_maximum_fusion), channel_id=1, source_target_pairs={{0,32},{32,64},{64,96},{1,33},{33,65},{65,97},{2,34},{34,66},{66,9... | collective-permute-start | bytes 3145736 | tf_op jit(solution)/shard_map/ppermute | solution.py:18
  27.1 1.0 copy-start.4
  28.1 17.6 %collective-permute-start.1 = (bf16[2,1024,256]{1,2,0:T(8,128)(2,1)S(1)}, bf16[2,1024,256]{1,2,0:T(8,128)(2,1)S(1)}, u32[]{:S(2)}, u32[]{:S(2)}) collective-permute-start(bf16[2,1024,256]{1,2,0:T(8,128)(2,1)S(1)} %collective-permute-done), channel_id=1, source_target_pairs={{0,32},{32,64},{64,96},{1,33},{33,65},{65,97},{2,34},{34,66},{66,9... | collective-permute-start | bytes 3145736 | tf_op jit(solution)/shard_map/ppermute | solution.py:18
  45.7 1.0 copy-start.6
  46.7 17.6 %collective-permute-start.2 = (bf16[2,1024,256]{1,2,0:T(8,128)(2,1)S(1)}, bf16[2,1024,256]{1,2,0:T(8,128)(2,1)}, u32[]{:S(2)}, u32[]{:S(2)}) collective-permute-start(bf16[2,1024,256]{1,2,0:T(8,128)(2,1)S(1)} %collective-permute-done.1), channel_id=1, source_target_pairs={{0,32},{32,64},{64,96},{1,33},{33,65},{65,97},{2,34},{34,66},{66,9... | collective-permute-start | bytes 3145736 | tf_op jit(solution)/shard_map/ppermute | solution.py:18
  64.3 265.3 %all-gather.6.cloned.1.call-start = ((), (), s32[]{:S(2)}) async-start(), calls=%async_computation.4 | async-start | bytes 9175040 | tf_op jit(solution)/shard_map/all_gather | solution.py:112
  65.1 6.5 %copy-start.5 = (bf16[2,1024,256]{1,2,0:T(8,128)(2,1)S(1)}, bf16[2,1024,256]{1,2,0:T(8,128)(2,1)}, u32[]{:S(2)}) copy-start(bf16[2,1024,256]{1,2,0:T(8,128)(2,1)} %copy-done.4) | copy-start | bytes 3145732
  71.6 1.5 copy-start.7
  106.5 9.0 %copy-start.9 = (s32[32,8]{0,1:T(8,128)S(1)}, s32[32,8]{0,1:T(8,128)}, u32[]{:S(2)}) copy-start(s32[32,8]{0,1:T(8,128)} %param.17) | copy-start | bytes 3076
  106.5 137.2 %all-to-all-start = ((bf16[32,32,3584]{2,1,0:T(8,128)(2,1)}), bf16[32,32,3584]{2,1,0:T(8,128)(2,1)}, u32[]{:S(2)}, u32[]{:S(2)}) async-start(bf16[32,32,3584]{2,1,0:T(8,128)(2,1)} %bitcast.230), calls=%async_computation | async-start | bytes 14680064 | tf_op jit(solution)/shard_map/all_to_all | solution.py:76
  114.8 133.2 %copy-start.3 = (bf16[32,3584]{1,0:T(8,128)(2,1)S(1)}, bf16[32,3584]{1,0:T(8,128)(2,1)}, u32[]{:S(2)}) copy-start(bf16[32,3584]{1,0:T(8,128)(2,1)} %param.15) | copy-start | bytes 688132
  114.8 133.4 %copy-start.8 = (f32[3584]{0:T(1024)S(1)}, f32[3584]{0:T(1024)}, u32[]{:S(2)}) copy-start(f32[3584]{0:T(1024)} %param.16) | copy-start | bytes 43012
  114.8 221.2 %all-gather.8.cloned.1.call-start = ((), (), s32[]{:S(2)}) async-start(), calls=%async_computation.5 | async-start | bytes 9175040 | tf_op jit(solution)/shard_map/all_gather | solution.py:113
  336.1 17.6 %copy-start.10 = (f32[32,8]{0,1:T(8,128)S(1)}, f32[32,8]{0,1:T(8,128)}, u32[]{:S(2)}) copy-start(f32[32,8]{0,1:T(8,128)} %param.18) | copy-start | bytes 3076
  336.1 56.8 %copy-start.1 = (bf16[256,3584]{1,0:T(8,128)(2,1)S(1)}, bf16[256,3584]{1,0:T(8,128)(2,1)}, u32[]{:S(2)}) copy-start(bf16[256,3584]{1,0:T(8,128)(2,1)} %param.14) | copy-start | bytes 5505028
  348.8 35.5 %all-to-all-start.2 = ((bf16[32,8,4480]{2,1,0:T(8,128)(2,1)}), bf16[32,8,4480]{2,1,0:T(8,128)(2,1)}, u32[]{:S(2)}, u32[]{:S(2)}) async-start(bf16[32,8,4480]{2,1,0:T(8,128)(2,1)} %reshape.116), calls=%async_computation.2 | async-start | bytes 4587520 | tf_op jit(solution)/shard_map/all_to_all | solution.py:130
Sparse Core Ops, SparseCore 0:
  64.4 71.4 all-gather.3
  137.6 97.4 all-gather.5
  236.8 82.2 all-gather.7

commit v9 on v5

--- a/solution.py
+++ b/solution.py
@@ -3,10 +3,12 @@
 import jax
 import jax.numpy as jnp
 from jax import lax
-from jax.sharding import PartitionSpec as P
+from jax.sharding import Mesh, PartitionSpec as P
 
 HD = 128
 
+
+EXP = ("exp_hi", "exp_lo")
 
 masked_score = -1e30
 norm_eps = 1e-06
@@ -68,11 +70,27 @@
         .reshape(query_rows, head_count * HD)
     )
     tok_count = residual.shape[0]
-    term = jnp.dot(attended, out_proj, preferred_element_type=jnp.float32)
-    exp_count = lax.axis_size("exp")
+    swap = [(0, 1), (1, 0)]
+    lo_where = lax.axis_index("exp_lo")
+    hi_count = lax.axis_size("exp_hi")
+    partner_proj = lax.ppermute(out_proj, "exp_lo", swap)
+    per_owner = query_rows // (hi_count * 2)
+    by_owner = attended.reshape(hi_count, 2, per_owner, head_count * HD)
+    mine = lax.dynamic_index_in_dim(by_owner, lo_where, axis=1, keepdims=False)
+    theirs = lax.ppermute(
+        lax.dynamic_index_in_dim(by_owner, 1 - lo_where, axis=1, keepdims=False), "exp_lo", swap
+    )
+    half_rows = hi_count * per_owner
+    own_term = jnp.dot(
+        mine.reshape(half_rows, head_count * HD), out_proj, preferred_element_type=jnp.float32
+    ).astype(jnp.bfloat16)
+    partner_term = jnp.dot(
+        theirs.reshape(half_rows, head_count * HD), partner_proj, preferred_element_type=jnp.float32
+    ).astype(jnp.bfloat16)
+    pair_term = (own_term.astype(jnp.float32) + partner_term.astype(jnp.float32)).astype(jnp.bfloat16)
     group_terms = lax.all_to_all(
-        term.astype(jnp.bfloat16).reshape(exp_count, query_rows // exp_count, term.shape[1]),
-        "exp",
+        pair_term.reshape(hi_count, per_owner, pair_term.shape[1]),
+        "exp_hi",
         split_axis=0,
         concat_axis=0,
         tiled=True,
@@ -84,7 +102,7 @@
     ).astype(jnp.bfloat16)
     width = normed.shape[1]
     per_token = routes.shape[1]
-    experts = lax.axis_size("exp")
+    experts = lax.axis_size(EXP)
     capacity = min(tok_count, max(2, tok_count * per_token * 5 // (4 * experts)))
     pair_count = tok_count * per_token
     flat_routes = routes.reshape(pair_count)
@@ -104,7 +122,7 @@
         .astype(jnp.bfloat16)
         .reshape(experts, 8, capacity * width // 8)
     )
-    received = lax.all_to_all(outgoing, "exp", split_axis=0, concat_axis=0, tiled=True)
+    received = lax.all_to_all(outgoing, EXP, split_axis=0, concat_axis=0, tiled=True)
     gate_full = lax.all_gather(w_gate[0], "ctx", axis=1, tiled=True)
     up_full = lax.all_gather(w_up[0], "ctx", axis=1, tiled=True)
     down_full = lax.all_gather(w_down[0], "ctx", axis=0, tiled=True)
@@ -124,7 +142,7 @@
         .astype(jnp.bfloat16)
         .reshape(experts, 8, capacity * width // 8)
     )
-    returned = lax.all_to_all(expert_out, "exp", split_axis=0, concat_axis=0, tiled=True)
+    returned = lax.all_to_all(expert_out, EXP, split_axis=0, concat_axis=0, tiled=True)
     weigh_rows = jnp.einsum(
         "pr,pt->tr", position_hot, token_hot * combine.reshape(pair_count)[:, None]
     )
@@ -138,19 +156,20 @@
 
 def solution(mesh):
     in_specs = (
-        P("ctx", "exp"),
-        P("ctx", "exp"),
-        P("ctx", "exp"),
-        P("exp", None),
-        P(("ctx", "exp"), None),
+        P("ctx", EXP),
+        P("ctx", EXP),
+        P("ctx", EXP),
+        P(EXP, None),
+        P(("ctx", *EXP), None),
         P(),
-        P(("ctx", "exp"), None),
-        P(("ctx", "exp"), None),
-        P("exp", None, "ctx"),
-        P("exp", None, "ctx"),
-        P("exp", "ctx", None),
+        P(("ctx", *EXP), None),
+        P(("ctx", *EXP), None),
+        P(EXP, None, "ctx"),
+        P(EXP, None, "ctx"),
+        P(EXP, "ctx", None),
     )
-    out_specs = P(("ctx", "exp"), None)
+    out_specs = P(("ctx", *EXP), None)
+    split_mesh = Mesh(mesh.devices.reshape(mesh.devices.shape[0], -1, 2), ("ctx", *EXP))
     return jax.shard_map(
-        per_device, mesh=mesh, in_specs=in_specs, out_specs=out_specs, check_vma=False
+        per_device, mesh=split_mesh, in_specs=in_specs, out_specs=out_specs, check_vma=False
     )

time: 396 us -> 369 us (0.932)
  the two profiles are of different devices: /device:TPU:1 before, /device:TPU:6 now
where the time goes in v9:
time: 369 us
  waiting for transfers between devices  197 us (53%)
  matrix products  53.2 us (14%)
  blocking collectives  38.1 us (10%)
  local copies, waits for them, and re-layouts  27.5 us (7%)
  starting transfers between devices  27 us (7%)
  between operations  13.5 us (4%)
  other arithmetic  12.1 us (3%)
    ppermute x3, waiting for transfers between devices, from_behind(): return lax.ppermute(shard, axis, pairs)  135 us
    all_to_all x1, blocking collectives, per_device(): lax.all_to_all(outgoing, EXP, split_axis=0, concat_axis=0, tiled=True)  38.1 us
    all_to_all x1, waiting for transfers between devices, per_device(): lax.all_to_all(pair_term.reshape(hi_count, per_owner, pair_term.shape[1])...  31.9 us
    all_to_all x1, waiting for transfers between devices, per_device(): lax.all_to_all(expert_out, EXP, split_axis=0, concat_axis=0, tiled=True)  18.5 us
    dot_general x4, matrix products, attend(): jnp.einsum('hqk,khd->qhd', expo_block.astype(jnp.bfloat16), value_heads,...  15.3 us
    ppermute x1, waiting for transfers between devices, per_device(): lax.ppermute(lax.dynamic_index_in_dim(by_owner, 1 - lo_where, axis=1, kee...  10.1 us
    all_to_all x1, starting transfers between devices, per_device(): lax.all_to_all(pair_term.reshape(hi_count, per_owner, pair_term.shape[1])...  9.51 us
    reduce_sum x3, other arithmetic, attend(): total_new = total_old * factor + jnp.sum(expo_block, axis=2)  8.05 us
  transfers between devices with their start and end apart: 10, of which 6 were waited for; matrix products, arithmetic and copies ran while one was open for 20% of the time, Pallas kernels for 0%

profile of v9, /device:TPU:6, one launch (start us, length us, event | category | flops | bytes accessed | tf_op | source)
XLA Modules:
  0.0 368.6 jit_solution(3395495216941359001)
XLA Ops:
  6.5 0.7 all-gather.7.cloned.1.call-update
  7.3 0.0 all-gather.9.cloned.1.call-start
  7.3 0.7 all-gather.9.cloned.1.call-update
  8.0 0.0 all-gather.11.cloned.1.call-start
  8.1 1.2 copy.33
  9.3 1.2 copy.34
  10.6 0.1 pad_maximum_fusion
  10.7 1.9 collective-permute-start
  12.6 22.1 %collective-permute-done = bf16[2,1024,256]{1,2,0:T(8,128)(2,1)} collective-permute-done((bf16[2,1024,256]{1,2,0:T(8,128)(2,1)S(1)}, bf16[2,1024,256]{1,2,0:T(8,128)(2,1)}, u32[]{:S(2)}, u32[]{:S(2)}) %collective-permute-start) | collective-permute-done | bytes 1048608 | tf_op jit(solution)/shard_map/ppermute | solution.py:20
  34.7 1.9 collective-permute-start.1
  36.6 3.0 collective-permute-start.4
  39.6 0.0 all-gather.11.cloned.1.call-update
  39.7 0.3 iota_compare_fusion
  40.0 1.8 fusion.3
  41.9 2.1 fusion.126
  43.9 42.2 %collective-permute-done.1 = bf16[2,1024,256]{1,2,0:T(8,128)(2,1)} collective-permute-done((bf16[2,1024,256]{1,2,0:T(8,128)(2,1)}, bf16[2,1024,256]{1,2,0:T(8,128)(2,1)}, u32[]{:S(2)}, u32[]{:S(2)}) %collective-permute-start.1) | collective-permute-done | bytes 1048608 | tf_op jit(solution)/shard_map/ppermute | solution.py:20
  86.1 1.9 collective-permute-start.2
  88.0 1.4 bitcast_reduce_fusion.2
  89.5 2.1 fusion.125
  91.6 1.4 bitcast_reduce_fusion.1
  93.0 71.0 %collective-permute-done.2 = bf16[2,1024,256]{1,2,0:T(8,128)(2,1)S(1)} collective-permute-done((bf16[2,1024,256]{1,2,0:T(8,128)(2,1)}, bf16[2,1024,256]{1,2,0:T(8,128)(2,1)S(1)}, u32[]{:S(2)}, u32[]{:S(2)}) %collective-permute-start.2) | collective-permute-done | bytes 1048608 | tf_op jit(solution)/shard_map/ppermute | solution.py:20
  164.1 0.9 fusion.124
  164.9 1.4 bitcast_reduce_fusion
  166.4 3.2 copy-done.2
  169.6 2.1 fusion.14
  171.7 2.0 fusion.8
  173.7 0.0 copy-start.7
  173.7 4.0 %fusion.10 = (f32[2,1024]{1,0:T(2,128)S(1)}, f32[2,1024]{1,0:T(2,128)S(1)}) fusion(f32[2,1024,1024]{1,2,0:T(8,128)S(1)} %get-tuple-element.27, f32[2,1024]{1,0:T(2,128)S(1)} %get-tuple-element.10, pred[]{:T(512)S(6)} %ge.25, f32[2,1024]{1,0:T(2,128)S(1)} %get-tuple-element.9, f32[2,1024,1024]{1,2,0:T(8,128)S(1)} %get-tuple-element.25, pred[]{:T(512)S(6)} %ge.26), kind=kLoop, calls=%fused_computation.24 | loop fusion | flops 16773120 | bytes 16809986 | tf_op jit(solution)/shard_map/reduce_sum | solution.py:45
  177.7 7.5 %fusion.65 = f32[1024,2,128]{2,0,1:T(8,128)} fusion(f32[2,1024,1024]{1,2,0:T(8,128)} %copy-done.3, f32[2,1024]{1,0:T(2,128)S(1)} %get-tuple-element.21, pred[1024,1024]{0,1:T(8,128)(4,1)S(1)} %iota_compare_fusion, f32[1024,2]{0,1:T(2,128)S(1)} %get-tuple-element.19, f32[1024,2]{0,1:T(2,128)S(1)} %get-tuple-element.20, bf16[1024,256]{1,0:T(8,128)(2,1)S(1)} %copy-done.7), kind=kOutput, calls=%fused_computation.56 | convolution fusion | flops 545783808 | bytes 11034624 | tf_op jit(solution)/shard_map/hqk,khd->qhd/dot_general | solution.py:46
  185.2 3.4 fusion.56
  188.6 2.2 fusion.59
  190.9 0.7 slice-done.1
  191.5 2.3 divide_convert_fusion
  193.8 0.5 copy.47
  194.4 0.3 reshape_reshape.3
  194.7 3.8 %collective-permute-start.3 = (bf16[16,32,256]{2,1,0:T(8,128)(2,1)S(1)}, bf16[16,32,256]{2,1,0:T(8,128)(2,1)S(1)}, u32[]{:S(2)}, u32[]{:S(2)}) collective-permute-start(bf16[16,32,256]{2,1,0:T(8,128)(2,1)S(1)} %get-tuple-element.17), channel_id=1, source_target_pairs={{0,1},{1,0},{2,3},{3,2},{4,5},{5,4},{6,7},{7,6},{8,9},{9,8},{10,11... | collective-permute-start | bytes 786440 | tf_op jit(solution)/shard_map/ppermute | solution.py:80
  198.5 2.6 convolution_convert_fusion.1
  201.1 10.1 %collective-permute-done.3 = bf16[16,32,256]{2,1,0:T(8,128)(2,1)S(1)} collective-permute-done((bf16[16,32,256]{2,1,0:T(8,128)(2,1)S(1)}, bf16[16,32,256]{2,1,0:T(8,128)(2,1)S(1)}, u32[]{:S(2)}, u32[]{:S(2)}) %collective-permute-start.3) | collective-permute-done | bytes 262176 | tf_op jit(solution)/shard_map/ppermute | solution.py:80
  211.3 3.0 add_convert_fusion
  214.2 9.5 %all-to-all-start = ((bf16[16,32,3584]{2,1,0:T(8,128)(2,1)}), bf16[16,32,3584]{2,1,0:T(8,128)(2,1)}, u32[]{:S(2)}, u32[]{:S(2)}) async-start(bf16[16,32,3584]{2,1,0:T(8,128)(2,1)} %bitcast.247), calls=%async_computation | async-start | bytes 7340032 | tf_op jit(solution)/shard_map/all_to_all | solution.py:91
  223.8 0.1 copy.49
  223.8 0.1 eq.61
  223.9 0.1 reshape.115
  224.0 0.6 reduce-window.6
  224.6 0.2 slice_reduce_fusion
  224.9 0.1 fusion.102
  225.0 31.9 %all-to-all-done = bf16[16,32,3584]{2,1,0:T(8,128)(2,1)} async-done(((bf16[16,32,3584]{2,1,0:T(8,128)(2,1)}), bf16[16,32,3584]{2,1,0:T(8,128)(2,1)}, u32[]{:S(2)}, u32[]{:S(2)}) %all-to-all-start) | async-done | bytes 3670048 | tf_op jit(solution)/shard_map/all_to_all | solution.py:91
  256.9 2.6 convert_reduce_fusion.1
  259.5 0.2 multiply_reduce_fusion
  259.7 1.1 convolution_convert_fusion.2
  260.8 3.5 reshape.117
  264.3 38.1 %all_to_all.15 = bf16[32,8,4480]{2,1,0:T(8,128)(2,1)S(1)} all-to-all(bf16[32,8,4480]{2,1,0:T(8,128)(2,1)} %reshape.117), channel_id=1, replica_groups=mesh['ctx'=4,'exp_hi'=16,'exp_lo'=2] {'exp_hi','exp_lo'}, dimensions={0} | all-to-all | bytes 4587520 | tf_op jit(solution)/shard_map/all_to_all | solution.py:125
  302.4 3.5 reshape.118
  305.9 7.5 %fusion.6 = f32[320,1024]{1,0:T(8,128)} fusion(bf16[320,3584]{1,0:T(8,128)(2,1)} %reshape.118, bf16[1,3584,1024]{2,1,0:T(8,128)(2,1)} %all-gather.7.cloned.1.call-done), kind=kOutput, calls=%fused_computation.18 | convolution fusion | flops 2348810240 | bytes 10944512 | tf_op jit(solution)/shard_map/dot_general | solution.py:130
  313.4 6.9 %fusion.44 = bf16[320,1024]{1,0:T(8,128)(2,1)} fusion(bf16[320,3584]{1,0:T(8,128)(2,1)S(1)} %copy-done.4, bf16[1,3584,1024]{2,1,0:T(8,128)(2,1)} %all-gather.9.cloned.1.call-done, f32[320,1024]{1,0:T(8,128)} %fusion.6), kind=kOutput, calls=%fused_computation.49 | convolution fusion | flops 2350776320 | bytes 11599872 | tf_op jit(solution)/shard_map/dot_general | solution.py:131
  320.3 6.1 %convert_reduce_fusion = bf16[320,3584]{1,0:T(8,128)(2,1)S(1)} fusion(bf16[4,256,3584]{2,1,0:T(8,128)(2,1)} %bitcast.258, bf16[40,4,8,256]{3,2,1,0:T(8,128)(2,1)} %bitcast.259), kind=kOutput, calls=%fused_computation | convolution fusion | flops 2356838400 | bytes 10289152 | tf_op jit(solution)/shard_map/rqf,qfd->qrd/dot_general | solution.py:134
  326.4 3.5 reshape.121
  329.9 4.9 %all-to-all-start.2 = ((bf16[32,8,4480]{2,1,0:T(8,128)(2,1)}), bf16[32,8,4480]{2,1,0:T(8,128)(2,1)S(1)}, u32[]{:S(2)}, u32[]{:S(2)}) async-start(bf16[32,8,4480]{2,1,0:T(8,128)(2,1)} %reshape.121), calls=%async_computation.2 | async-start | bytes 4587520 | tf_op jit(solution)/shard_map/all_to_all | solution.py:145
  334.8 0.1 copy.48
  334.9 0.6 mul.119
  335.6 1.0 fusion.84
  336.5 18.5 %all-to-all-done.2 = bf16[32,8,4480]{2,1,0:T(8,128)(2,1)S(1)} async-done(((bf16[32,8,4480]{2,1,0:T(8,128)(2,1)}), bf16[32,8,4480]{2,1,0:T(8,128)(2,1)S(1)}, u32[]{:S(2)}, u32[]{:S(2)}) %all-to-all-start.2) | async-done | bytes 2293792 | tf_op jit(solution)/shard_map/all_to_all | solution.py:145
  355.0 3.5 reshape.122
  358.5 3.6 fusion.16
  (45 shorter events, 0.2 us)
Async XLA Ops:
  6.5 33.5 %copy-start = (bf16[1024,256]{1,0:T(8,128)(2,1)S(1)}, bf16[1024,256]{1,0:T(8,128)(2,1)}, u32[]{:S(2)}) copy-start(bf16[1024,256]{1,0:T(8,128)(2,1)} %param.11) | copy-start | bytes 1572868
  6.5 33.5 %copy-start.6 = (bf16[1024,256]{1,0:T(8,128)(2,1)S(1)}, bf16[1024,256]{1,0:T(8,128)(2,1)}, u32[]{:S(2)}) copy-start(bf16[1024,256]{1,0:T(8,128)(2,1)} %param.12) | copy-start | bytes 1572868
  6.5 299.3 %all-gather.7.cloned.1.call-start = ((), (), s32[]{:S(2)}) async-start(), calls=%async_computation.3 | async-start | bytes 9175040 | tf_op jit(solution)/shard_map/all_gather | solution.py:126
  7.3 306.1 %all-gather.9.cloned.1.call-start = ((), (), s32[]{:S(2)}) async-start(), calls=%async_computation.4 | async-start | bytes 9175040 | tf_op jit(solution)/shard_map/all_gather | solution.py:127
  8.0 312.3 %all-gather.11.cloned.1.call-start = ((), (), s32[]{:S(2)}) async-start(), calls=%async_computation.5 | async-start | bytes 9175040 | tf_op jit(solution)/shard_map/all_gather | solution.py:128
  10.7 24.1 %collective-permute-start = (bf16[2,1024,256]{1,2,0:T(8,128)(2,1)S(1)}, bf16[2,1024,256]{1,2,0:T(8,128)(2,1)}, u32[]{:S(2)}, u32[]{:S(2)}) collective-permute-start(bf16[2,1024,256]{1,2,0:T(8,128)(2,1)S(1)} %pad_maximum_fusion), channel_id=1, source_target_pairs={{0,32},{32,64},{64,96},{1,33},{33,65},{65,97},{2,34},{34,66},{66,9... | collective-permute-start | bytes 3145736 | tf_op jit(solution)/shard_map/ppermute | solution.py:20
  34.7 51.4 %collective-permute-start.1 = (bf16[2,1024,256]{1,2,0:T(8,128)(2,1)}, bf16[2,1024,256]{1,2,0:T(8,128)(2,1)}, u32[]{:S(2)}, u32[]{:S(2)}) collective-permute-start(bf16[2,1024,256]{1,2,0:T(8,128)(2,1)} %collective-permute-done), channel_id=1, source_target_pairs={{0,32},{32,64},{64,96},{1,33},{33,65},{65,97},{2,34},{34,66},{66,9... | collective-permute-start | bytes 3145736 | tf_op jit(solution)/shard_map/ppermute | solution.py:20
  36.6 164.5 %collective-permute-start.4 = (bf16[256,3584]{1,0:T(8,128)(2,1)}, bf16[256,3584]{1,0:T(8,128)(2,1)S(1)}, u32[]{:S(2)}, u32[]{:S(2)}) collective-permute-start(bf16[256,3584]{1,0:T(8,128)(2,1)} %param.14), channel_id=1, source_target_pairs={{0,1},{1,0},{2,3},{3,2},{4,5},{5,4},{6,7},{7,6},{8,9},{9,8},{10,11... | collective-permute-start | bytes 5505032 | tf_op jit(solution)/shard_map/ppermute | solution.py:76
  41.9 129.8 %copy-start.3 = (f32[2,1024,1024]{1,2,0:T(8,128)}, f32[2,1024,1024]{1,2,0:T(8,128)S(1)}, u32[]{:S(2)}) copy-start(f32[2,1024,1024]{1,2,0:T(8,128)S(1)} %get-tuple-element.29) | copy-start | bytes 25165828
  86.1 77.9 %collective-permute-start.2 = (bf16[2,1024,256]{1,2,0:T(8,128)(2,1)}, bf16[2,1024,256]{1,2,0:T(8,128)(2,1)S(1)}, u32[]{:S(2)}, u32[]{:S(2)}) collective-permute-start(bf16[2,1024,256]{1,2,0:T(8,128)(2,1)} %collective-permute-done.1), channel_id=1, source_target_pairs={{0,32},{32,64},{64,96},{1,33},{33,65},{65,97},{2,34},{34,66},{66,9... | collective-permute-start | bytes 3145736 | tf_op jit(solution)/shard_map/ppermute | solution.py:20
  166.4 3.2 copy-start.2
  173.7 4.1 %copy-start.7 = (bf16[1024,256]{1,0:T(8,128)(2,1)S(1)}, bf16[1024,256]{1,0:T(8,128)(2,1)}, u32[]{:S(2)}) copy-start(bf16[1024,256]{1,0:T(8,128)(2,1)} %param.13) | copy-start | bytes 1572868
  185.2 3.4 copy-start.8
  185.2 5.6 %slice-start = ((s8[8388608]{0:T(1024)(128)(4,1)}), s8[4194304]{0:T(1024)(128)(4,1)S(1)}, s32[]{:S(2)}) async-start(s8[8388608]{0:T(1024)(128)(4,1)} %bitcast.245), calls=%async_computation.6 | async-start | bytes 8388608
  188.6 2.2 copy-start.9
  188.6 2.9 slice-start.1
  194.7 16.5 %collective-permute-start.3 = (bf16[16,32,256]{2,1,0:T(8,128)(2,1)S(1)}, bf16[16,32,256]{2,1,0:T(8,128)(2,1)S(1)}, u32[]{:S(2)}, u32[]{:S(2)}) collective-permute-start(bf16[16,32,256]{2,1,0:T(8,128)(2,1)S(1)} %get-tuple-element.17), channel_id=1, source_target_pairs={{0,1},{1,0},{2,3},{3,2},{4,5},{5,4},{6,7},{7,6},{8,9},{9,8},{10,11... | collective-permute-start | bytes 786440 | tf_op jit(solution)/shard_map/ppermute | solution.py:80
  211.3 12.5 %copy-start.13 = (s32[32,8]{0,1:T(8,128)S(1)}, s32[32,8]{0,1:T(8,128)}, u32[]{:S(2)}) copy-start(s32[32,8]{0,1:T(8,128)} %param.17) | copy-start | bytes 3076
  214.2 45.2 %copy-start.5 = (bf16[32,3584]{1,0:T(8,128)(2,1)S(1)}, bf16[32,3584]{1,0:T(8,128)(2,1)}, u32[]{:S(2)}) copy-start(bf16[32,3584]{1,0:T(8,128)(2,1)} %param.15) | copy-start | bytes 688132
  214.2 45.4 %copy-start.10 = (f32[3584]{0:T(1024)S(1)}, f32[3584]{0:T(1024)}, u32[]{:S(2)}) copy-start(f32[3584]{0:T(1024)} %param.16) | copy-start | bytes 43012
  214.2 42.6 %all-to-all-start = ((bf16[16,32,3584]{2,1,0:T(8,128)(2,1)}), bf16[16,32,3584]{2,1,0:T(8,128)(2,1)}, u32[]{:S(2)}, u32[]{:S(2)}) async-start(bf16[16,32,3584]{2,1,0:T(8,128)(2,1)} %bitcast.247), calls=%async_computation | async-start | bytes 7340032 | tf_op jit(solution)/shard_map/all_to_all | solution.py:91
  225.0 77.4 %copy-start.11 = (s32[256]{0:T(256)}, s32[256]{0:T(256)S(1)}, u32[]{:S(2)}) copy-start(s32[256]{0:T(256)S(1)} %get-tuple-element.30) | copy-start | bytes 3076
  225.0 77.4 %copy-start.12 = (s32[256]{0:T(256)}, s32[256]{0:T(256)S(1)}, u32[]{:S(2)}) copy-start(s32[256]{0:T(256)S(1)} %get-tuple-element.31) | copy-start | bytes 3076
  305.9 7.5 %copy-start.4 = (bf16[320,3584]{1,0:T(8,128)(2,1)S(1)}, bf16[320,3584]{1,0:T(8,128)(2,1)}, u32[]{:S(2)}) copy-start(bf16[320,3584]{1,0:T(8,128)(2,1)} %reshape.118) | copy-start | bytes 6881284
  320.3 14.6 %copy-start.14 = (f32[32,8]{0,1:T(8,128)S(1)}, f32[32,8]{0,1:T(8,128)}, u32[]{:S(2)}) copy-start(f32[32,8]{0,1:T(8,128)} %param.18) | copy-start | bytes 3076
  320.3 41.8 %copy-start.1 = (bf16[1024,256]{1,0:T(8,128)(2,1)S(1)}, bf16[1024,256]{1,0:T(8,128)(2,1)}, u32[]{:S(2)}) copy-start(bf16[1024,256]{1,0:T(8,128)(2,1)} %param.11) | copy-start | bytes 1572868
  329.9 25.1 %all-to-all-start.2 = ((bf16[32,8,4480]{2,1,0:T(8,128)(2,1)}), bf16[32,8,4480]{2,1,0:T(8,128)(2,1)S(1)}, u32[]{:S(2)}, u32[]{:S(2)}) async-start(bf16[32,8,4480]{2,1,0:T(8,128)(2,1)} %reshape.121), calls=%async_computation.2 | async-start | bytes 4587520 | tf_op jit(solution)/shard_map/all_to_all | solution.py:145
Sparse Core Ops, SparseCore 0:
  9.0 87.2 all-gather.6
  97.9 76.2 all-gather.8
  175.9 72.1 all-gather.10

commit v10 on v9

--- a/solution.py
+++ b/solution.py
@@ -64,6 +64,9 @@
     for step_index in range(1, ctx_count):
         pair_block = from_behind(pair_block, "ctx", 1)
         carried = attend(carried, query_heads, pair_block, ctx_where >= step_index)
+    gate_local, up_local, down_local, _ = lax.optimization_barrier(
+        (w_gate[0], w_up[0], w_down[0], pair_block)
+    )
     attended = (
         (carried[2] / carried[1].T[:, :, None])
         .astype(jnp.bfloat16)
@@ -123,9 +126,9 @@
         .reshape(experts, 8, capacity * width // 8)
     )
     received = lax.all_to_all(outgoing, EXP, split_axis=0, concat_axis=0, tiled=True)
-    gate_full = lax.all_gather(w_gate[0], "ctx", axis=1, tiled=True)
-    up_full = lax.all_gather(w_up[0], "ctx", axis=1, tiled=True)
-    down_full = lax.all_gather(w_down[0], "ctx", axis=0, tiled=True)
+    gate_full = lax.all_gather(gate_local, "ctx", axis=1, tiled=True)
+    up_full = lax.all_gather(up_local, "ctx", axis=1, tiled=True)
+    down_full = lax.all_gather(down_local, "ctx", axis=0, tiled=True)
     rows = received.reshape(experts * capacity, width)
     gate = jnp.dot(rows, gate_full, preferred_element_type=jnp.float32)
     upper = jnp.dot(rows, up_full, preferred_element_type=jnp.float32)

time: 369 us -> 357 us (0.967)
  the two profiles are of different devices: /device:TPU:6 before, /device:TPU:1 now
where the time goes in v10:
time: 357 us; the launch traced here: 356 us
  waiting for transfers between devices  179 us (50%)
  matrix products  55.9 us (16%)
  starting transfers between devices  36.6 us (10%)
  blocking collectives  31.4 us (9%)
  local copies, waits for them, and re-layouts  27.5 us (8%)
  between operations  13.5 us (4%)
  other arithmetic  12.1 us (3%)
    ppermute x3, waiting for transfers between devices, from_behind(): return lax.ppermute(shard, axis, pairs)  45.6 us
    all_gather x1, waiting for transfers between devices, per_device(): down_full = lax.all_gather(down_local, 'ctx', axis=0, tiled=True)  40.9 us
    all_to_all x1, waiting for transfers between devices, per_device(): lax.all_to_all(pair_term.reshape(hi_count, per_owner, pair_term.shape[1])...  40.7 us
    all_to_all x1, blocking collectives, per_device(): lax.all_to_all(outgoing, EXP, split_axis=0, concat_axis=0, tiled=True)  31.4 us
    all_to_all x1, waiting for transfers between devices, per_device(): lax.all_to_all(expert_out, EXP, split_axis=0, concat_axis=0, tiled=True)  29.3 us
    ppermute x3, starting transfers between devices, from_behind(): return lax.ppermute(shard, axis, pairs)  17.8 us
    dot_general x4, matrix products, attend(): jnp.einsum('hqk,khd->qhd', expo_block.astype(jnp.bfloat16), value_heads,...  16.9 us
    ppermute x1, waiting for transfers between devices, per_device(): partner_proj = lax.ppermute(out_proj, 'exp_lo', swap)  13.1 us
  transfers between devices with their start and end apart: 10, of which 8 were waited for; matrix products, arithmetic and copies ran while one was open for 20% of the time, Pallas kernels for 0%

profile of v10, /device:TPU:1, one launch (start us, length us, event | category | flops | bytes accessed | tf_op | source)
XLA Modules:
  0.0 355.7 jit_solution(10304448257620502222)
XLA Ops:
  6.5 1.3 copy.33
  7.9 1.2 copy.34
  9.1 0.1 pad_maximum_fusion
  9.2 6.0 %collective-permute-start = (bf16[2,1024,256]{1,2,0:T(8,128)(2,1)S(1)}, bf16[2,1024,256]{1,2,0:T(8,128)(2,1)S(1)}, u32[]{:S(2)}, u32[]{:S(2)}) collective-permute-start(bf16[2,1024,256]{1,2,0:T(8,128)(2,1)S(1)} %pad_maximum_fusion), channel_id=1, source_target_pairs={{0,32},{32,64},{64,96},{1,33},{33,65},{65,97},{2,34},{34,66},{66,9... | collective-permute-start | bytes 3145736 | tf_op jit(solution)/shard_map/ppermute | solution.py:20
  15.3 11.7 %collective-permute-done = bf16[2,1024,256]{1,2,0:T(8,128)(2,1)S(1)} collective-permute-done((bf16[2,1024,256]{1,2,0:T(8,128)(2,1)S(1)}, bf16[2,1024,256]{1,2,0:T(8,128)(2,1)S(1)}, u32[]{:S(2)}, u32[]{:S(2)}) %collective-permute-start) | collective-permute-done | bytes 1048608 | tf_op jit(solution)/shard_map/ppermute | solution.py:20
  27.0 1.0 copy-done.7
  28.0 5.9 %collective-permute-start.1 = (bf16[2,1024,256]{1,2,0:T(8,128)(2,1)S(1)}, bf16[2,1024,256]{1,2,0:T(8,128)(2,1)S(1)}, u32[]{:S(2)}, u32[]{:S(2)}) collective-permute-start(bf16[2,1024,256]{1,2,0:T(8,128)(2,1)S(1)} %collective-permute-done), channel_id=1, source_target_pairs={{0,32},{32,64},{64,96},{1,33},{33,65},{65,97},{2,34},{34,66},{66,9... | collective-permute-start | bytes 3145736 | tf_op jit(solution)/shard_map/ppermute | solution.py:20
  33.9 11.7 %collective-permute-done.1 = bf16[2,1024,256]{1,2,0:T(8,128)(2,1)S(1)} collective-permute-done((bf16[2,1024,256]{1,2,0:T(8,128)(2,1)S(1)}, bf16[2,1024,256]{1,2,0:T(8,128)(2,1)S(1)}, u32[]{:S(2)}, u32[]{:S(2)}) %collective-permute-start.1) | collective-permute-done | bytes 1048608 | tf_op jit(solution)/shard_map/ppermute | solution.py:20
  45.6 1.0 copy-done.9
  46.6 5.9 %collective-permute-start.2 = (bf16[2,1024,256]{1,2,0:T(8,128)(2,1)S(1)}, bf16[2,1024,256]{1,2,0:T(8,128)(2,1)}, u32[]{:S(2)}, u32[]{:S(2)}) collective-permute-start(bf16[2,1024,256]{1,2,0:T(8,128)(2,1)S(1)} %collective-permute-done.1), channel_id=1, source_target_pairs={{0,32},{32,64},{64,96},{1,33},{33,65},{65,97},{2,34},{34,66},{66,9... | collective-permute-start | bytes 3145736 | tf_op jit(solution)/shard_map/ppermute | solution.py:20
  52.5 22.1 %collective-permute-done.2 = bf16[2,1024,256]{1,2,0:T(8,128)(2,1)} collective-permute-done((bf16[2,1024,256]{1,2,0:T(8,128)(2,1)S(1)}, bf16[2,1024,256]{1,2,0:T(8,128)(2,1)}, u32[]{:S(2)}, u32[]{:S(2)}) %collective-permute-start.2) | collective-permute-done | bytes 1048608 | tf_op jit(solution)/shard_map/ppermute | solution.py:20
  74.7 0.0 all-gather.6.cloned.1.call-start
  74.7 0.7 all-gather.6.cloned.1.call-update
  75.4 0.0 all-gather.8.cloned.1.call-start
  75.5 0.1 collective-permute-start.4
  75.6 0.3 iota_compare_fusion
  75.9 1.8 fusion.3
  77.8 0.1 fusion.117
  77.9 1.4 bitcast_reduce_fusion.2
  79.3 1.0 fusion.116
  80.3 1.4 bitcast_reduce_fusion.1
  81.8 2.0 fusion.115
  83.8 1.4 bitcast_reduce_fusion
  85.3 3.8 %copy-done.2 = f32[2,1024,1024]{1,2,0:T(8,128)} copy-done((f32[2,1024,1024]{1,2,0:T(8,128)}, f32[2,1024,1024]{1,2,0:T(8,128)S(1)}, u32[]{:S(2)}) %copy-start.2) | copy-done | bytes 8388632
  89.0 2.1 fusion.10
  91.1 2.0 fusion.4
  93.1 4.0 %fusion.6 = (f32[2,1024]{1,0:T(2,128)S(1)}, f32[2,1024]{1,0:T(2,128)S(1)}) fusion(f32[2,1024,1024]{1,2,0:T(8,128)S(1)} %get-tuple-element.33, f32[2,1024]{1,0:T(2,128)S(1)} %get-tuple-element.16, pred[]{:T(512)S(6)} %ge.25, f32[2,1024]{1,0:T(2,128)S(1)} %get-tuple-element.15, f32[2,1024,1024]{1,2,0:T(8,128)S(1)} %get-tuple-element.31, pred[]{:T(512)S(6)} %ge.26), kind=kLoop, calls=%fused_computation.20 | loop fusion | flops 16773120 | bytes 16809986 | tf_op jit(solution)/shard_map/reduce_sum | solution.py:45
  97.2 4.2 %fusion.56 = f32[1024,2,128]{2,0,1:T(8,128)} fusion(f32[2,1024,1024]{1,2,0:T(8,128)S(1)} %get-tuple-element.35, f32[2,1024]{1,0:T(2,128)S(1)} %get-tuple-element.27, pred[1024,1024]{0,1:T(8,128)(4,1)S(1)} %iota_compare_fusion, f32[1024,2]{0,1:T(2,128)S(1)} %get-tuple-element.25, f32[1024,2]{0,1:T(2,128)S(1)} %get-tuple-element.26, ...), kind=kOutput, calls=%fused_computation.52 | convolution fusion | flops 545783808 | bytes 11034624 | tf_op jit(solution)/shard_map/hqk,khd->qhd/dot_general | solution.py:46
  101.4 5.8 %fusion.47 = f32[1024,2,128]{2,0,1:T(8,128)S(1)} fusion(f32[1024,2,128]{2,0,1:T(8,128)} %fusion.56, bf16[1024,2,128]{0,2,1:T(8,128)(2,1)S(1)} %bitcast.254, f32[2,1024,1024]{1,2,0:T(8,128)} %copy-done.3, f32[2,1024]{1,0:T(2,128)S(1)} %get-tuple-element.16, pred[]{:T(512)S(6)} %ge.25, f32[1024,2]{0,1:T(2,128)S(1)} %get-tuple-element.13), kind=kOutput, calls=%fused_computation.49 | convolution fusion | flops 545783808 | bytes 11026433 | tf_op jit(solution)/shard_map/hqk,khd->qhd/dot_general | solution.py:46
  107.2 4.7 %fusion.50 = f32[1024,2,128]{2,0,1:T(8,128)S(1)} fusion(f32[1024,2,128]{2,0,1:T(8,128)S(1)} %fusion.47, bf16[1024,2,128]{0,2,1:T(8,128)(2,1)S(1)} %bitcast.255, f32[2,1024,1024]{1,2,0:T(8,128)} %copy-done.4, f32[2,1024]{1,0:T(2,128)S(1)} %get-tuple-element.15, pred[]{:T(512)S(6)} %ge.26, f32[1024,2]{0,1:T(2,128)S(1)} %get-tuple-element.12), kind=kOutput, calls=%fused_computation.50 | convolution fusion | flops 545783808 | bytes 11026433 | tf_op jit(solution)/shard_map/hqk,khd->qhd/dot_general | solution.py:46
  111.9 2.3 divide_convert_fusion
  114.2 0.5 copy.47
  114.8 0.3 reshape_reshape.3
  115.1 1.7 collective-permute-start.3
  116.9 2.6 convolution_convert_fusion.1
  119.5 13.1 %collective-permute-done.4 = bf16[256,3584]{1,0:T(8,128)(2,1)S(1)} collective-permute-done((bf16[256,3584]{1,0:T(8,128)(2,1)}, bf16[256,3584]{1,0:T(8,128)(2,1)S(1)}, u32[]{:S(2)}, u32[]{:S(2)}) %collective-permute-start.4) | collective-permute-done | bytes 1835040 | tf_op jit(solution)/shard_map/ppermute | solution.py:79
  132.6 8.4 %collective-permute-done.3 = bf16[16,32,256]{2,1,0:T(8,128)(2,1)S(1)} collective-permute-done((bf16[16,32,256]{2,1,0:T(8,128)(2,1)S(1)}, bf16[16,32,256]{2,1,0:T(8,128)(2,1)S(1)}, u32[]{:S(2)}, u32[]{:S(2)}) %collective-permute-start.3) | collective-permute-done | bytes 262176 | tf_op jit(solution)/shard_map/ppermute | solution.py:83
  141.0 2.9 add_convert_fusion
  144.0 9.9 %all-to-all-start = ((bf16[16,32,3584]{2,1,0:T(8,128)(2,1)}), bf16[16,32,3584]{2,1,0:T(8,128)(2,1)}, u32[]{:S(2)}, u32[]{:S(2)}) async-start(bf16[16,32,3584]{2,1,0:T(8,128)(2,1)} %bitcast.242), calls=%async_computation | async-start | bytes 7340032 | tf_op jit(solution)/shard_map/all_to_all | solution.py:94
  153.9 0.1 copy.49
  153.9 0.1 eq.61
  154.0 0.1 reshape.115
  154.1 0.6 reduce-window.6
  154.7 0.2 slice_reduce_fusion
  154.9 0.1 fusion.93
  155.1 40.7 %all-to-all-done = bf16[16,32,3584]{2,1,0:T(8,128)(2,1)} async-done(((bf16[16,32,3584]{2,1,0:T(8,128)(2,1)}), bf16[16,32,3584]{2,1,0:T(8,128)(2,1)}, u32[]{:S(2)}, u32[]{:S(2)}) %all-to-all-start) | async-done | bytes 3670048 | tf_op jit(solution)/shard_map/all_to_all | solution.py:94
  195.8 2.6 convert_reduce_fusion.1
  198.4 0.2 multiply_reduce_fusion
  198.6 1.1 convolution_convert_fusion.2
  199.7 3.5 reshape.117
  203.2 31.4 %all_to_all.15 = bf16[32,8,4480]{2,1,0:T(8,128)(2,1)S(1)} all-to-all(bf16[32,8,4480]{2,1,0:T(8,128)(2,1)} %reshape.117), channel_id=1, replica_groups=mesh['ctx'=4,'exp_hi'=16,'exp_lo'=2] {'exp_hi','exp_lo'}, dimensions={0} | all-to-all | bytes 4587520 | tf_op jit(solution)/shard_map/all_to_all | solution.py:128
  234.7 3.5 reshape.118
  238.1 7.5 %fusion.118 = f32[320,1024]{1,0:T(8,128)} fusion(bf16[320,3584]{1,0:T(8,128)(2,1)} %reshape.118, bf16[3584,1024]{1,0:T(8,128)(2,1)} %all-gather.4.cloned.1.call-done), kind=kOutput, calls=%fused_computation.138 | convolution fusion | flops 2348810240 | bytes 10944512 | tf_op jit(solution)/shard_map/dot_general | solution.py:133
  245.7 7.9 %fusion.37 = bf16[320,1024]{1,0:T(8,128)(2,1)} fusion(bf16[320,3584]{1,0:T(8,128)(2,1)S(1)} %copy-done.5, bf16[3584,1024]{1,0:T(8,128)(2,1)} %all-gather.6.cloned.1.call-done, f32[320,1024]{1,0:T(8,128)} %fusion.118), kind=kOutput, calls=%fused_computation.45 | convolution fusion | flops 2350776320 | bytes 11599872 | tf_op jit(solution)/shard_map/dot_general | solution.py:134
  253.6 40.9 %all-gather.8.cloned.1.call-done = bf16[1024,3584]{1,0:T(8,128)(2,1)} async-done(((bf16[256,3584]{1,0:T(8,128)(2,1)}), bf16[1024,3584]{1,0:T(8,128)(2,1)}) %all-gather.8.cloned.1.call-update) | async-done | bytes 7340048 | tf_op jit(solution)/shard_map/all_gather | solution.py:131
  294.5 6.1 %convert_reduce_fusion = bf16[320,3584]{1,0:T(8,128)(2,1)S(1)} fusion(bf16[4,256,3584]{2,1,0:T(8,128)(2,1)} %bitcast.256, bf16[40,4,8,256]{3,2,1,0:T(8,128)(2,1)} %bitcast.257), kind=kOutput, calls=%fused_computation | convolution fusion | flops 2356838400 | bytes 10289152 | tf_op jit(solution)/shard_map/rqf,qfd->qrd/dot_general | solution.py:137
  300.6 3.5 reshape.121
  304.1 7.0 %all-to-all-start.2 = ((bf16[32,8,4480]{2,1,0:T(8,128)(2,1)}), bf16[32,8,4480]{2,1,0:T(8,128)(2,1)S(1)}, u32[]{:S(2)}, u32[]{:S(2)}) async-start(bf16[32,8,4480]{2,1,0:T(8,128)(2,1)} %reshape.121), calls=%async_computation.2 | async-start | bytes 4587520 | tf_op jit(solution)/shard_map/all_to_all | solution.py:148
  311.1 0.1 copy.48
  311.2 0.6 mul.119
  311.8 1.0 fusion.75
  312.8 29.3 %all-to-all-done.2 = bf16[32,8,4480]{2,1,0:T(8,128)(2,1)S(1)} async-done(((bf16[32,8,4480]{2,1,0:T(8,128)(2,1)}), bf16[32,8,4480]{2,1,0:T(8,128)(2,1)S(1)}, u32[]{:S(2)}, u32[]{:S(2)}) %all-to-all-start.2) | async-done | bytes 2293792 | tf_op jit(solution)/shard_map/all_to_all | solution.py:148
  342.1 3.5 reshape.122
  345.6 3.6 %fusion.12 = bf16[32,3584]{1,0:T(8,128)(2,1)} fusion(f32[32,320]{1,0:T(8,128)S(1)} %fusion.75, bf16[320,3584]{1,0:T(8,128)(2,1)} %reshape.122, f32[32,3584]{1,0:T(8,128)S(1)} %convert_reduce_fusion.1, bf16[32,3584]{1,0:T(8,128)(2,1)S(1)} %copy-done.6), kind=kOutput, calls=%fused_computation.30 | convolution fusion | flops 440860672 | bytes 3252224 | tf_op jit(solution)/shard_map/dot_general | solution.py:152
  (53 shorter events, 0.3 us)
Async XLA Ops:
  6.5 69.4 %copy-start = (bf16[1024,256]{1,0:T(8,128)(2,1)S(1)}, bf16[1024,256]{1,0:T(8,128)(2,1)}, u32[]{:S(2)}) copy-start(bf16[1024,256]{1,0:T(8,128)(2,1)} %param.11) | copy-start | bytes 1572868
  6.5 69.4 %copy-start.11 = (bf16[1024,256]{1,0:T(8,128)(2,1)S(1)}, bf16[1024,256]{1,0:T(8,128)(2,1)}, u32[]{:S(2)}) copy-start(bf16[1024,256]{1,0:T(8,128)(2,1)} %param.12) | copy-start | bytes 1572868
  6.5 231.6 %all-gather.4.cloned.1.call-start = ((), (), s32[]{:S(2)}) async-start(), calls=%async_computation.3 | async-start | bytes 9175040 | tf_op jit(solution)/shard_map/all_gather | solution.py:129
  9.2 17.8 %collective-permute-start = (bf16[2,1024,256]{1,2,0:T(8,128)(2,1)S(1)}, bf16[2,1024,256]{1,2,0:T(8,128)(2,1)S(1)}, u32[]{:S(2)}, u32[]{:S(2)}) collective-permute-start(bf16[2,1024,256]{1,2,0:T(8,128)(2,1)S(1)} %pad_maximum_fusion), channel_id=1, source_target_pairs={{0,32},{32,64},{64,96},{1,33},{33,65},{65,97},{2,34},{34,66},{66,9... | collective-permute-start | bytes 3145736 | tf_op jit(solution)/shard_map/ppermute | solution.py:20
  27.0 1.0 copy-start.7
  28.0 17.6 %collective-permute-start.1 = (bf16[2,1024,256]{1,2,0:T(8,128)(2,1)S(1)}, bf16[2,1024,256]{1,2,0:T(8,128)(2,1)S(1)}, u32[]{:S(2)}, u32[]{:S(2)}) collective-permute-start(bf16[2,1024,256]{1,2,0:T(8,128)(2,1)S(1)} %collective-permute-done), channel_id=1, source_target_pairs={{0,32},{32,64},{64,96},{1,33},{33,65},{65,97},{2,34},{34,66},{66,9... | collective-permute-start | bytes 3145736 | tf_op jit(solution)/shard_map/ppermute | solution.py:20
  45.6 1.0 copy-start.9
  46.6 28.0 %collective-permute-start.2 = (bf16[2,1024,256]{1,2,0:T(8,128)(2,1)S(1)}, bf16[2,1024,256]{1,2,0:T(8,128)(2,1)}, u32[]{:S(2)}, u32[]{:S(2)}) collective-permute-start(bf16[2,1024,256]{1,2,0:T(8,128)(2,1)S(1)} %collective-permute-done.1), channel_id=1, source_target_pairs={{0,32},{32,64},{64,96},{1,33},{33,65},{65,97},{2,34},{34,66},{66,9... | collective-permute-start | bytes 3145736 | tf_op jit(solution)/shard_map/ppermute | solution.py:20
  74.7 171.0 %all-gather.6.cloned.1.call-start = ((), (), s32[]{:S(2)}) async-start(), calls=%async_computation.4 | async-start | bytes 9175040 | tf_op jit(solution)/shard_map/all_gather | solution.py:130
  75.4 219.1 %all-gather.8.cloned.1.call-start = ((), (), s32[]{:S(2)}) async-start(), calls=%async_computation.5 | async-start | bytes 9175040 | tf_op jit(solution)/shard_map/all_gather | solution.py:131
  75.5 57.1 %collective-permute-start.4 = (bf16[256,3584]{1,0:T(8,128)(2,1)}, bf16[256,3584]{1,0:T(8,128)(2,1)S(1)}, u32[]{:S(2)}, u32[]{:S(2)}) collective-permute-start(bf16[256,3584]{1,0:T(8,128)(2,1)} %param.14), channel_id=1, source_target_pairs={{0,1},{1,0},{2,3},{3,2},{4,5},{5,4},{6,7},{7,6},{8,9},{9,8},{10,11... | collective-permute-start | bytes 5505032 | tf_op jit(solution)/shard_map/ppermute | solution.py:79
  75.6 2.2 copy-start.8
  77.8 1.5 copy-start.10
  79.3 13.8 %copy-start.3 = (f32[2,1024,1024]{1,2,0:T(8,128)}, f32[2,1024,1024]{1,2,0:T(8,128)S(1)}, u32[]{:S(2)}) copy-start(f32[2,1024,1024]{1,2,0:T(8,128)S(1)} %get-tuple-element.33) | copy-start | bytes 25165828
  81.7 11.4 %copy-start.4 = (f32[2,1024,1024]{1,2,0:T(8,128)}, f32[2,1024,1024]{1,2,0:T(8,128)S(1)}, u32[]{:S(2)}) copy-start(f32[2,1024,1024]{1,2,0:T(8,128)S(1)} %get-tuple-element.31) | copy-start | bytes 25165828
  85.2 3.8 %copy-start.2 = (f32[2,1024,1024]{1,2,0:T(8,128)}, f32[2,1024,1024]{1,2,0:T(8,128)S(1)}, u32[]{:S(2)}) copy-start(f32[2,1024,1024]{1,2,0:T(8,128)S(1)} %get-tuple-element.29) | copy-start | bytes 25165828
  93.1 4.1 %copy-start.12 = (bf16[1024,256]{1,0:T(8,128)(2,1)S(1)}, bf16[1024,256]{1,0:T(8,128)(2,1)}, u32[]{:S(2)}) copy-start(bf16[1024,256]{1,0:T(8,128)(2,1)} %param.13) | copy-start | bytes 1572868
  101.4 5.8 %copy-start.13 = (bf16[1,1024,256]{1,2,0:T(8,128)(2,1)S(1)}, bf16[1,1024,256]{1,2,0:T(8,128)(2,1)}, u32[]{:S(2)}) copy-start(bf16[1,1024,256]{1,2,0:T(8,128)(2,1)} %get-tuple-element.19) | copy-start | bytes 1572868
  101.4 10.5 %slice-start = ((s8[8388608]{0:T(1024)(128)(4,1)}), s8[4194304]{0:T(1024)(128)(4,1)S(1)}, s32[]{:S(2)}) async-start(s8[8388608]{0:T(1024)(128)(4,1)} %bitcast.240), calls=%async_computation.6 | async-start | bytes 8388608
  107.2 4.7 %slice-start.1 = ((s8[8388608]{0:T(1024)(128)(4,1)}), s8[4194304]{0:T(1024)(128)(4,1)S(1)}, s32[]{:S(2)}) async-start(s8[8388608]{0:T(1024)(128)(4,1)} %bitcast.240), calls=%async_computation.7 | async-start | bytes 8388608
  115.1 25.9 %collective-permute-start.3 = (bf16[16,32,256]{2,1,0:T(8,128)(2,1)S(1)}, bf16[16,32,256]{2,1,0:T(8,128)(2,1)S(1)}, u32[]{:S(2)}, u32[]{:S(2)}) collective-permute-start(bf16[16,32,256]{2,1,0:T(8,128)(2,1)S(1)} %get-tuple-element.23), channel_id=1, source_target_pairs={{0,1},{1,0},{2,3},{3,2},{4,5},{5,4},{6,7},{7,6},{8,9},{9,8},{10,11... | collective-permute-start | bytes 786440 | tf_op jit(solution)/shard_map/ppermute | solution.py:83
  141.0 12.8 %copy-start.17 = (s32[32,8]{0,1:T(8,128)S(1)}, s32[32,8]{0,1:T(8,128)}, u32[]{:S(2)}) copy-start(s32[32,8]{0,1:T(8,128)} %param.17) | copy-start | bytes 3076
  144.0 54.5 %copy-start.6 = (bf16[32,3584]{1,0:T(8,128)(2,1)S(1)}, bf16[32,3584]{1,0:T(8,128)(2,1)}, u32[]{:S(2)}) copy-start(bf16[32,3584]{1,0:T(8,128)(2,1)} %param.15) | copy-start | bytes 688132
  144.0 54.7 %copy-start.14 = (f32[3584]{0:T(1024)S(1)}, f32[3584]{0:T(1024)}, u32[]{:S(2)}) copy-start(f32[3584]{0:T(1024)} %param.16) | copy-start | bytes 43012
  144.0 51.8 %all-to-all-start = ((bf16[16,32,3584]{2,1,0:T(8,128)(2,1)}), bf16[16,32,3584]{2,1,0:T(8,128)(2,1)}, u32[]{:S(2)}, u32[]{:S(2)}) async-start(bf16[16,32,3584]{2,1,0:T(8,128)(2,1)} %bitcast.242), calls=%async_computation | async-start | bytes 7340032 | tf_op jit(solution)/shard_map/all_to_all | solution.py:94
  155.1 79.6 %copy-start.15 = (s32[256]{0:T(256)}, s32[256]{0:T(256)S(1)}, u32[]{:S(2)}) copy-start(s32[256]{0:T(256)S(1)} %get-tuple-element.36) | copy-start | bytes 3076
  155.1 79.6 %copy-start.16 = (s32[256]{0:T(256)}, s32[256]{0:T(256)S(1)}, u32[]{:S(2)}) copy-start(s32[256]{0:T(256)S(1)} %get-tuple-element.37) | copy-start | bytes 3076
  238.1 7.5 %copy-start.5 = (bf16[320,3584]{1,0:T(8,128)(2,1)S(1)}, bf16[320,3584]{1,0:T(8,128)(2,1)}, u32[]{:S(2)}) copy-start(bf16[320,3584]{1,0:T(8,128)(2,1)} %reshape.118) | copy-start | bytes 6881284
  294.5 16.6 %copy-start.18 = (f32[32,8]{0,1:T(8,128)S(1)}, f32[32,8]{0,1:T(8,128)}, u32[]{:S(2)}) copy-start(f32[32,8]{0,1:T(8,128)} %param.18) | copy-start | bytes 3076
  294.5 54.7 %copy-start.1 = (bf16[1024,256]{1,0:T(8,128)(2,1)S(1)}, bf16[1024,256]{1,0:T(8,128)(2,1)}, u32[]{:S(2)}) copy-start(bf16[1024,256]{1,0:T(8,128)(2,1)} %param.11) | copy-start | bytes 1572868
  304.1 38.0 %all-to-all-start.2 = ((bf16[32,8,4480]{2,1,0:T(8,128)(2,1)}), bf16[32,8,4480]{2,1,0:T(8,128)(2,1)S(1)}, u32[]{:S(2)}, u32[]{:S(2)}) async-start(bf16[32,8,4480]{2,1,0:T(8,128)(2,1)} %reshape.121), calls=%async_computation.2 | async-start | bytes 4587520 | tf_op jit(solution)/shard_map/all_to_all | solution.py:148
Sparse Core Ops, SparseCore 0:
  74.8 74.3 all-gather.3
  150.9 86.7 all-gather.5
  239.3 55.0 all-gather.7

commit v11 on v10

--- a/solution.py
+++ b/solution.py
@@ -9,6 +9,7 @@
 
 
 EXP = ("exp_hi", "exp_lo")
+CTX = ("ctx_hi", "ctx_lo")
 
 masked_score = -1e30
 norm_eps = 1e-06
@@ -26,8 +27,8 @@
     query_rows = queries.shape[0]
     head_count = queries.shape[1] // HD
     scaling = 1.0 / math.sqrt(HD)
-    ctx_where = lax.axis_index("ctx")
-    ctx_count = lax.axis_size("ctx")
+    ctx_where = lax.axis_index(CTX)
+    ctx_count = lax.axis_size(CTX)
 
     def attend(carried, query_heads, pair_block, visible):
         key_count = pair_block.shape[1]
@@ -62,7 +63,7 @@
     pair_block = jnp.stack([keys, values])
     carried = attend(initial, query_heads, pair_block, diag_mask)
     for step_index in range(1, ctx_count):
-        pair_block = from_behind(pair_block, "ctx", 1)
+        pair_block = from_behind(pair_block, CTX, 1)
         carried = attend(carried, query_heads, pair_block, ctx_where >= step_index)
     gate_local, up_local, down_local, _ = lax.optimization_barrier(
         (w_gate[0], w_up[0], w_down[0], pair_block)
@@ -126,9 +127,14 @@
         .reshape(experts, 8, capacity * width // 8)
     )
     received = lax.all_to_all(outgoing, EXP, split_axis=0, concat_axis=0, tiled=True)
-    gate_full = lax.all_gather(gate_local, "ctx", axis=1, tiled=True)
-    up_full = lax.all_gather(up_local, "ctx", axis=1, tiled=True)
-    down_full = lax.all_gather(down_local, "ctx", axis=0, tiled=True)
+    def gather_quarters(local, axis):
+        across = lax.ppermute(local, "ctx_hi", swap)
+        pair = jnp.concatenate([local, across], axis=axis)
+        return lax.all_gather(pair, "ctx_lo", axis=axis, tiled=True)
+
+    gate_full = gather_quarters(gate_local, 1)
+    up_full = gather_quarters(up_local, 1)
+    down_full = gather_quarters(down_local, 0)
     rows = received.reshape(experts * capacity, width)
     gate = jnp.dot(rows, gate_full, preferred_element_type=jnp.float32)
     upper = jnp.dot(rows, up_full, preferred_element_type=jnp.float32)
@@ -159,20 +165,20 @@
 
 def solution(mesh):
     in_specs = (
-        P("ctx", EXP),
-        P("ctx", EXP),
-        P("ctx", EXP),
+        P(CTX, EXP),
+        P(CTX, EXP),
+        P(CTX, EXP),
         P(EXP, None),
-        P(("ctx", *EXP), None),
+        P((*CTX, *EXP), None),
         P(),
-        P(("ctx", *EXP), None),
-        P(("ctx", *EXP), None),
-        P(EXP, None, "ctx"),
-        P(EXP, None, "ctx"),
-        P(EXP, "ctx", None),
+        P((*CTX, *EXP), None),
+        P((*CTX, *EXP), None),
+        P(EXP, None, CTX),
+        P(EXP, None, CTX),
+        P(EXP, CTX, None),
     )
-    out_specs = P(("ctx", *EXP), None)
-    split_mesh = Mesh(mesh.devices.reshape(mesh.devices.shape[0], -1, 2), ("ctx", *EXP))
+    out_specs = P((*CTX, *EXP), None)
+    split_mesh = Mesh(mesh.devices.reshape(2, -1, mesh.devices.shape[1] // 2, 2), (*CTX, *EXP))
     return jax.shard_map(
         per_device, mesh=split_mesh, in_specs=in_specs, out_specs=out_specs, check_vma=False
     )

time: 357 us -> 413 us (1.16)
  waiting for transfers between devices: 179 us -> 206 us
  other arithmetic: 12.1 us -> 29.4 us
  matrix products: 55.9 us -> 66.2 us
    ppermute x0 -> x3, waiting for transfers between devices: none -> 91.2 us  [gather_quarters(): across = lax.ppermute(local, 'ctx_hi', swap)]
    all_gather x3, waiting for transfers between devices: 40.9 us -> 0.01 us  [gather_quarters(): return lax.all_gather(pair, 'ctx_lo', axis=axis, tiled=True)]
    dot_general x4, matrix products: 6.18 us -> 21.3 us  [attend(): jnp.einsum('qhd,khd->hqk', query_heads, key_heads, preferred_element_type...]
    ppermute x1, waiting for transfers between devices: 13.1 us -> 0.01 us  [per_device(): partner_proj = lax.ppermute(out_proj, 'exp_lo', swap)]
    ppermute x3, waiting for transfers between devices: 45.6 us -> 35.2 us  [from_behind(): return lax.ppermute(shard, axis, pairs)]
    concatenate x0 -> x3, other arithmetic: none -> 9.95 us  [gather_quarters(): pair = jnp.concatenate([local, across], axis=axis)]
    reduce_sum x3, other arithmetic: 8.05 us -> 15.4 us  [attend(): total_new = total_old * factor + jnp.sum(expo_block, axis=2)]
    unnamed x46 -> x56, local copies, waits for them, and re-layouts: 8.6 us -> 5.23 us
  transfers between devices with their start and end apart: 10 -> 13, of which waited for: 8 -> 8; matrix products, arithmetic and copies ran while one was open for 20% -> 23% of each run, Pallas kernels for 0% -> 0%
where the time goes in v11:
time: 413 us; the launch traced here: 410 us
  waiting for transfers between devices  206 us (50%)
  matrix products  66.2 us (16%)
  starting transfers between devices  34.6 us (8%)
  blocking collectives  34.5 us (8%)
  other arithmetic  29.4 us (7%)
  local copies, waits for them, and re-layouts  25.1 us (6%)
  between operations  13.6 us (3%)
    ppermute x3, waiting for transfers between devices, gather_quarters(): across = lax.ppermute(local, 'ctx_hi', swap)  91.2 us
    all_to_all x1, waiting for transfers between devices, per_device(): lax.all_to_all(pair_term.reshape(hi_count, per_owner, pair_term.shape[1])...  43.1 us
    ppermute x3, waiting for transfers between devices, from_behind(): return lax.ppermute(shard, axis, pairs)  35.2 us
    all_to_all x1, blocking collectives, per_device(): lax.all_to_all(outgoing, EXP, split_axis=0, concat_axis=0, tiled=True)  34.5 us
    all_to_all x1, waiting for transfers between devices, per_device(): lax.all_to_all(expert_out, EXP, split_axis=0, concat_axis=0, tiled=True)  26 us
    dot_general x4, matrix products, attend(): jnp.einsum('qhd,khd->hqk', query_heads, key_heads, preferred_element_type...  21.3 us
    ppermute x3, starting transfers between devices, from_behind(): return lax.ppermute(shard, axis, pairs)  17.8 us
    reduce_sum x3, other arithmetic, attend(): total_new = total_old * factor + jnp.sum(expo_block, axis=2)  15.4 us
  transfers between devices with their start and end apart: 13, of which 8 were waited for; matrix products, arithmetic and copies ran while one was open for 23% of the time, Pallas kernels for 0%

profile of v11, /device:TPU:1, one launch (start us, length us, event | category | flops | bytes accessed | tf_op | source)
XLA Modules:
  0.0 409.6 jit_solution(7440705620149559127)
XLA Ops:
  6.5 1.3 copy.33
  7.8 1.2 copy.34
  9.1 0.1 pad_maximum_fusion.3
  9.2 6.0 %collective-permute-start = (bf16[2,1024,256]{1,2,0:T(8,128)(2,1)S(1)}, bf16[2,1024,256]{1,2,0:T(8,128)(2,1)S(1)}, u32[]{:S(2)}, u32[]{:S(2)}) collective-permute-start(bf16[2,1024,256]{1,2,0:T(8,128)(2,1)S(1)} %pad_maximum_fusion.3), channel_id=1, source_target_pairs={{0,32},{32,64},{64,96},{1,33},{33,65},{65,97},{2,34},{34,66},{66,9... | collective-permute-start | bytes 3145736 | tf_op jit(solution)/shard_map/ppermute | solution.py:21
  15.2 11.7 %collective-permute-done = bf16[2,1024,256]{1,2,0:T(8,128)(2,1)S(1)} collective-permute-done((bf16[2,1024,256]{1,2,0:T(8,128)(2,1)S(1)}, bf16[2,1024,256]{1,2,0:T(8,128)(2,1)S(1)}, u32[]{:S(2)}, u32[]{:S(2)}) %collective-permute-start) | collective-permute-done | bytes 1048608 | tf_op jit(solution)/shard_map/ppermute | solution.py:21
  27.0 5.9 %collective-permute-start.1 = (bf16[2,1024,256]{1,2,0:T(8,128)(2,1)S(1)}, bf16[2,1024,256]{1,2,0:T(8,128)(2,1)S(1)}, u32[]{:S(2)}, u32[]{:S(2)}) collective-permute-start(bf16[2,1024,256]{1,2,0:T(8,128)(2,1)S(1)} %collective-permute-done), channel_id=1, source_target_pairs={{0,32},{32,64},{64,96},{1,33},{33,65},{65,97},{2,34},{34,66},{66,9... | collective-permute-start | bytes 3145736 | tf_op jit(solution)/shard_map/ppermute | solution.py:21
  32.9 11.7 %collective-permute-done.1 = bf16[2,1024,256]{1,2,0:T(8,128)(2,1)S(1)} collective-permute-done((bf16[2,1024,256]{1,2,0:T(8,128)(2,1)S(1)}, bf16[2,1024,256]{1,2,0:T(8,128)(2,1)S(1)}, u32[]{:S(2)}, u32[]{:S(2)}) %collective-permute-start.1) | collective-permute-done | bytes 1048608 | tf_op jit(solution)/shard_map/ppermute | solution.py:21
  44.6 5.9 %collective-permute-start.2 = (bf16[2,1024,256]{1,2,0:T(8,128)(2,1)S(1)}, bf16[2,1024,256]{1,2,0:T(8,128)(2,1)S(1)}, u32[]{:S(2)}, u32[]{:S(2)}) collective-permute-start(bf16[2,1024,256]{1,2,0:T(8,128)(2,1)S(1)} %collective-permute-done.1), channel_id=1, source_target_pairs={{0,32},{32,64},{64,96},{1,33},{33,65},{65,97},{2,34},{34,66},{66,9... | collective-permute-start | bytes 3145736 | tf_op jit(solution)/shard_map/ppermute | solution.py:21
  50.5 11.7 %collective-permute-done.2 = bf16[2,1024,256]{1,2,0:T(8,128)(2,1)S(1)} collective-permute-done((bf16[2,1024,256]{1,2,0:T(8,128)(2,1)S(1)}, bf16[2,1024,256]{1,2,0:T(8,128)(2,1)S(1)}, u32[]{:S(2)}, u32[]{:S(2)}) %collective-permute-start.2) | collective-permute-done | bytes 1048608 | tf_op jit(solution)/shard_map/ppermute | solution.py:21
  62.2 1.0 copy-done.6
  63.2 42.4 %collective-permute-done.5 = bf16[3584,256]{1,0:T(8,128)(2,1)S(1)} collective-permute-done((bf16[3584,256]{1,0:T(8,128)(2,1)}, bf16[3584,256]{1,0:T(8,128)(2,1)S(1)}, u32[]{:S(2)}, u32[]{:S(2)}) %collective-permute-start.5) | collective-permute-done | bytes 1835040 | tf_op jit(solution)/shard_map/ppermute | solution.py:131
  105.6 3.6 pad_maximum_fusion
  109.2 0.4 collective-permute-start.4
  109.6 0.3 iota_compare_fusion
  110.0 6.1 %fusion.3 = (f32[2,1024]{1,0:T(2,128)S(1)}, f32[2,1024,1024]{1,2,0:T(8,128)}) fusion(pred[1024,1024]{0,1:T(8,128)(4,1)S(1)} %iota_compare_fusion, bf16[1024,256]{1,0:T(8,128)(2,1)} %param.12, bf16[1024,256]{1,0:T(8,128)(2,1)S(1)} %copy-done), kind=kOutput, calls=%fused_computation.15 | convolution fusion | flops 543160320 | bytes 10493952 | tf_op jit(solution)/shard_map/qhd,khd->hqk/dot_general | solution.py:38
  116.0 2.2 fusion.116
  118.2 5.7 %bitcast_reduce_fusion.2 = (f32[2,1024]{1,0:T(2,128)S(1)}, f32[2,1024,1024]{1,2,0:T(8,128)}) fusion(pred[]{:T(512)S(6)} %ge.25, bf16[1024,2,128]{0,2,1:T(8,128)(2,1)S(1)} %bitcast.247, bf16[1024,256]{1,0:T(8,128)(2,1)S(1)} %copy-done), kind=kOutput, calls=%fused_computation.8 | convolution fusion | flops 543160320 | bytes 9445377 | tf_op jit(solution)/shard_map/qhd,khd->hqk/dot_general | solution.py:38
  124.0 0.9 fusion.115
  124.8 4.9 %bitcast_reduce_fusion.1 = (f32[2,1024]{1,0:T(2,128)S(1)}, f32[2,1024,1024]{1,2,0:T(8,128)}) fusion(pred[]{:T(512)S(6)} %ge.26, bf16[1024,2,128]{0,2,1:T(8,128)(2,1)S(1)} %bitcast.248, bf16[1024,256]{1,0:T(8,128)(2,1)S(1)} %copy-done), kind=kOutput, calls=%fused_computation.5 | convolution fusion | flops 543160320 | bytes 9445377 | tf_op jit(solution)/shard_map/qhd,khd->hqk/dot_general | solution.py:38
  129.8 2.9 collective-permute-start.7
  132.7 0.9 fusion.114
  133.5 4.6 %bitcast_reduce_fusion = (f32[2,1024]{1,0:T(2,128)S(1)}, f32[2,1024,1024]{1,2,0:T(8,128)}) fusion(pred[]{:T(512)S(6)} %ge.27, bf16[1024,2,128]{0,2,1:T(8,128)(2,1)S(1)} %bitcast.249, bf16[1024,256]{1,0:T(8,128)(2,1)S(1)} %copy-done), kind=kOutput, calls=%fused_computation.2 | convolution fusion | flops 543160320 | bytes 9445377 | tf_op jit(solution)/shard_map/qhd,khd->hqk/dot_general | solution.py:38
  138.1 48.8 %collective-permute-done.6 = bf16[3584,256]{1,0:T(8,128)(2,1)S(1)} collective-permute-done((bf16[3584,256]{1,0:T(8,128)(2,1)S(1)}, bf16[3584,256]{1,0:T(8,128)(2,1)S(1)}, u32[]{:S(2)}, u32[]{:S(2)}) %collective-permute-start.6) | collective-permute-done | bytes 1835040 | tf_op jit(solution)/shard_map/ppermute | solution.py:131
  186.9 2.1 pad_maximum_fusion.1
  189.1 4.6 %fusion.10 = f32[2,1024]{1,0:T(2,128)S(1)} fusion(f32[2,1024,1024]{1,2,0:T(8,128)} %get-tuple-element.29, f32[2,1024]{1,0:T(2,128)S(1)} %get-tuple-element.14, pred[]{:T(512)S(6)} %ge.27), kind=kLoop, calls=%fused_computation.24 | loop fusion | flops 8386560 | bytes 8404993 | tf_op jit(solution)/shard_map/reduce_sum | solution.py:46
  193.7 4.6 %fusion.4 = f32[2,1024]{1,0:T(2,128)S(1)} fusion(f32[2,1024,1024]{1,2,0:T(8,128)} %get-tuple-element.35, f32[2,1024]{1,0:T(2,128)S(1)} %get-tuple-element.27, pred[1024,1024]{0,1:T(8,128)(4,1)S(1)} %iota_compare_fusion), kind=kLoop, calls=%fused_computation.18 | loop fusion | flops 8386560 | bytes 9453568 | tf_op jit(solution)/shard_map/reduce_sum | solution.py:46
  198.4 6.2 %fusion.6 = (f32[2,1024]{1,0:T(2,128)S(1)}, f32[2,1024]{1,0:T(2,128)S(1)}) fusion(f32[2,1024,1024]{1,2,0:T(8,128)S(1)} %bitcast.241, f32[2,1024]{1,0:T(2,128)S(1)} %get-tuple-element.16, pred[]{:T(512)S(6)} %ge.25, f32[2,1024]{1,0:T(2,128)S(1)} %get-tuple-element.15, f32[2,1024,1024]{1,2,0:T(8,128)} %get-tuple-element.31, pred[]{:T(512)S(6)} %ge.26), kind=kLoop, calls=%fused_computation.20 | loop fusion | flops 16773120 | bytes 16809986 | tf_op jit(solution)/shard_map/reduce_sum | solution.py:46
  204.6 6.5 %fusion.55 = f32[1024,2,128]{2,0,1:T(8,128)S(1)} fusion(f32[2,1024,1024]{1,2,0:T(8,128)} %get-tuple-element.35, f32[2,1024]{1,0:T(2,128)S(1)} %get-tuple-element.27, pred[1024,1024]{0,1:T(8,128)(4,1)S(1)} %iota_compare_fusion, f32[1024,2]{0,1:T(2,128)S(1)} %get-tuple-element.25, f32[1024,2]{0,1:T(2,128)S(1)} %get-tuple-element.26, ...), kind=kOutput, calls=%fused_computation.53 | convolution fusion | flops 545783808 | bytes 11034624 | tf_op jit(solution)/shard_map/hqk,khd->qhd/dot_general | solution.py:47
  211.2 2.2 fusion.46
  213.4 2.2 fusion.49
  215.7 0.1 copy-done.14
  215.8 1.3 slice-done.5
  217.1 2.3 divide_convert_fusion
  219.3 0.5 copy.47
  219.9 0.3 reshape_reshape.3
  220.3 1.4 collective-permute-start.3
  221.7 1.1 convolution_convert_fusion.1
  222.8 10.8 %collective-permute-done.3 = bf16[16,32,256]{2,1,0:T(8,128)(2,1)S(1)} collective-permute-done((bf16[16,32,256]{2,1,0:T(8,128)(2,1)S(1)}, bf16[16,32,256]{2,1,0:T(8,128)(2,1)S(1)}, u32[]{:S(2)}, u32[]{:S(2)}) %collective-permute-start.3) | collective-permute-done | bytes 262176 | tf_op jit(solution)/shard_map/ppermute | solution.py:84
  233.7 4.5 %add_convert_fusion = bf16[512,3584]{1,0:T(8,128)(2,1)} fusion(bf16[512,3584]{1,0:T(8,128)(2,1)S(1)} %convolution_convert_fusion.1, bf16[512,256]{1,0:T(8,128)(2,1)S(1)} %bitcast.257, bf16[256,3584]{1,0:T(8,128)(2,1)} %collective-permute-done.4), kind=kOutput, calls=%fused_computation.17 | convolution fusion | flops 948699136 | bytes 9437184 | tf_op jit(solution)/shard_map/dot_general | solution.py:91
  238.2 7.8 %all-to-all-start = ((bf16[16,32,3584]{2,1,0:T(8,128)(2,1)}), bf16[16,32,3584]{2,1,0:T(8,128)(2,1)}, u32[]{:S(2)}, u32[]{:S(2)}) async-start(bf16[16,32,3584]{2,1,0:T(8,128)(2,1)} %bitcast.246), calls=%async_computation | async-start | bytes 7340032 | tf_op jit(solution)/shard_map/all_to_all | solution.py:95
  246.1 4.2 %pad_maximum_fusion.2 = bf16[512,3584]{1,0:T(8,128)(2,1)} fusion(bf16[256,3584]{1,0:T(8,128)(2,1)} %collective-permute-done.7, bf16[256,3584]{1,0:T(8,128)(2,1)} %bitcast.30), kind=kLoop, calls=%fused_computation.42 | loop fusion | flops 7340032 | bytes 7340032 | tf_op jit(solution)/shard_map/concatenate | solution.py:132
  250.5 0.1 eq.61
  250.6 0.1 reshape.115
  250.7 0.6 reduce-window.6
  251.3 0.2 slice_reduce_fusion
  251.5 0.1 fusion.92
  251.6 43.1 %all-to-all-done = bf16[16,32,3584]{2,1,0:T(8,128)(2,1)} async-done(((bf16[16,32,3584]{2,1,0:T(8,128)(2,1)}), bf16[16,32,3584]{2,1,0:T(8,128)(2,1)}, u32[]{:S(2)}, u32[]{:S(2)}) %all-to-all-start) | async-done | bytes 3670048 | tf_op jit(solution)/shard_map/all_to_all | solution.py:95
  294.7 2.6 convert_reduce_fusion.1
  297.3 0.2 multiply_reduce_fusion
  297.5 1.1 convolution_convert_fusion.2
  298.6 3.5 reshape.117
  302.1 34.5 %all_to_all.15 = bf16[32,8,4480]{2,1,0:T(8,128)(2,1)S(1)} all-to-all(bf16[32,8,4480]{2,1,0:T(8,128)(2,1)} %reshape.117), channel_id=1, replica_groups=mesh['ctx_hi'=2,'ctx_lo'=2,'exp_hi'=16,'exp_lo'=2] {'exp_hi','exp_lo'}, dimensions={0} | all-to-all | bytes 4587520 | tf_op jit(solution)/shard_map/all_to_all | solution.py:129
  336.6 3.5 reshape.118
  340.1 7.5 %fusion.117 = f32[320,1024]{1,0:T(8,128)} fusion(bf16[320,3584]{1,0:T(8,128)(2,1)} %reshape.118, bf16[3584,1024]{1,0:T(8,128)(2,1)} %all-gather.4.cloned.1.call-done), kind=kOutput, calls=%fused_computation.140 | convolution fusion | flops 2348810240 | bytes 10944512 | tf_op jit(solution)/shard_map/dot_general | solution.py:139
  347.6 6.9 %multiply_convert_fusion = bf16[320,1024]{1,0:T(8,128)(2,1)} fusion(f32[320,1024]{1,0:T(8,128)} %fusion.117, bf16[320,3584]{1,0:T(8,128)(2,1)S(1)} %copy-done.2, bf16[3584,1024]{1,0:T(8,128)(2,1)} %all-gather.6.cloned.1.call-done), kind=kOutput, calls=%fused_computation.54 | convolution fusion | flops 2350776320 | bytes 11599872 | tf_op jit(solution)/shard_map/dot_general | solution.py:140
  354.5 6.1 %convert_reduce_fusion = bf16[320,3584]{1,0:T(8,128)(2,1)S(1)} fusion(bf16[4,256,3584]{2,1,0:T(8,128)(2,1)} %bitcast.261, bf16[40,4,8,256]{3,2,1,0:T(8,128)(2,1)} %bitcast.262), kind=kOutput, calls=%fused_computation | convolution fusion | flops 2356838400 | bytes 10289152 | tf_op jit(solution)/shard_map/rqf,qfd->qrd/dot_general | solution.py:143
  360.6 3.5 reshape.121
  364.1 4.2 %all-to-all-start.2 = ((bf16[32,8,4480]{2,1,0:T(8,128)(2,1)}), bf16[32,8,4480]{2,1,0:T(8,128)(2,1)S(1)}, u32[]{:S(2)}, u32[]{:S(2)}) async-start(bf16[32,8,4480]{2,1,0:T(8,128)(2,1)} %reshape.121), calls=%async_computation.2 | async-start | bytes 4587520 | tf_op jit(solution)/shard_map/all_to_all | solution.py:154
  368.3 0.1 copy.48
  368.4 0.7 mul.123
  369.1 1.0 fusion.74
  370.1 26.0 %all-to-all-done.2 = bf16[32,8,4480]{2,1,0:T(8,128)(2,1)S(1)} async-done(((bf16[32,8,4480]{2,1,0:T(8,128)(2,1)}), bf16[32,8,4480]{2,1,0:T(8,128)(2,1)S(1)}, u32[]{:S(2)}, u32[]{:S(2)}) %all-to-all-start.2) | async-done | bytes 2293792 | tf_op jit(solution)/shard_map/all_to_all | solution.py:154
  396.1 3.4 reshape.122
  399.5 3.6 fusion.12
  (74 shorter events, 0.6 us)
Async XLA Ops:
  6.5 103.4 %copy-start = (bf16[1024,256]{1,0:T(8,128)(2,1)S(1)}, bf16[1024,256]{1,0:T(8,128)(2,1)}, u32[]{:S(2)}) copy-start(bf16[1024,256]{1,0:T(8,128)(2,1)} %param.11) | copy-start | bytes 1572868
  6.5 333.6 %all-gather.4.cloned.1.call-start = ((), (), s32[]{:S(2)}) async-start(), calls=%async_computation.3 | async-start | bytes 11010048 | tf_op jit(solution)/shard_map/all_gather | solution.py:133
  9.2 17.8 %collective-permute-start = (bf16[2,1024,256]{1,2,0:T(8,128)(2,1)S(1)}, bf16[2,1024,256]{1,2,0:T(8,128)(2,1)S(1)}, u32[]{:S(2)}, u32[]{:S(2)}) collective-permute-start(bf16[2,1024,256]{1,2,0:T(8,128)(2,1)S(1)} %pad_maximum_fusion.3), channel_id=1, source_target_pairs={{0,32},{32,64},{64,96},{1,33},{33,65},{65,97},{2,34},{34,66},{66,9... | collective-permute-start | bytes 3145736 | tf_op jit(solution)/shard_map/ppermute | solution.py:21
  27.0 5.9 %copy-start.10 = (bf16[2,1024,256]{1,2,0:T(8,128)(2,1)}, bf16[2,1024,256]{1,2,0:T(8,128)(2,1)S(1)}, u32[]{:S(2)}) copy-start(bf16[2,1024,256]{1,2,0:T(8,128)(2,1)S(1)} %collective-permute-done) | copy-start | bytes 3145732
  27.0 17.6 %collective-permute-start.1 = (bf16[2,1024,256]{1,2,0:T(8,128)(2,1)S(1)}, bf16[2,1024,256]{1,2,0:T(8,128)(2,1)S(1)}, u32[]{:S(2)}, u32[]{:S(2)}) collective-permute-start(bf16[2,1024,256]{1,2,0:T(8,128)(2,1)S(1)} %collective-permute-done), channel_id=1, source_target_pairs={{0,32},{32,64},{64,96},{1,33},{33,65},{65,97},{2,34},{34,66},{66,9... | collective-permute-start | bytes 3145736 | tf_op jit(solution)/shard_map/ppermute | solution.py:21
  44.6 18.6 %copy-start.8 = (bf16[2,1024,256]{1,2,0:T(8,128)(2,1)}, bf16[2,1024,256]{1,2,0:T(8,128)(2,1)S(1)}, u32[]{:S(2)}) copy-start(bf16[2,1024,256]{1,2,0:T(8,128)(2,1)S(1)} %collective-permute-done.1) | copy-start | bytes 3145732
  44.6 17.6 %collective-permute-start.2 = (bf16[2,1024,256]{1,2,0:T(8,128)(2,1)S(1)}, bf16[2,1024,256]{1,2,0:T(8,128)(2,1)S(1)}, u32[]{:S(2)}, u32[]{:S(2)}) collective-permute-start(bf16[2,1024,256]{1,2,0:T(8,128)(2,1)S(1)} %collective-permute-done.1), channel_id=1, source_target_pairs={{0,32},{32,64},{64,96},{1,33},{33,65},{65,97},{2,34},{34,66},{66,9... | collective-permute-start | bytes 3145736 | tf_op jit(solution)/shard_map/ppermute | solution.py:21
  62.2 1.0 copy-start.6
  63.2 42.4 %collective-permute-start.5 = (bf16[3584,256]{1,0:T(8,128)(2,1)}, bf16[3584,256]{1,0:T(8,128)(2,1)S(1)}, u32[]{:S(2)}, u32[]{:S(2)}) collective-permute-start(bf16[3584,256]{1,0:T(8,128)(2,1)} %bitcast.252), channel_id=1, source_target_pairs={{0,64},{64,0},{1,65},{65,1},{2,66},{66,2},{3,67},{67,3},{4,68},{68... | collective-permute-start | bytes 5505032 | tf_op jit(solution)/shard_map/ppermute | solution.py:131
  109.2 9.0 %copy-start.4 = (bf16[1,3584,256]{2,1,0:T(8,128)(2,1)S(1)}, bf16[1,3584,256]{2,1,0:T(8,128)(2,1)}, u32[]{:S(2)}) copy-start(bf16[1,3584,256]{2,1,0:T(8,128)(2,1)} %param.20) | copy-start | bytes 5505028
  109.2 238.4 %all-gather.6.cloned.1.call-start = ((), (), s32[]{:S(2)}) async-start(), calls=%async_computation.4 | async-start | bytes 11010048 | tf_op jit(solution)/shard_map/all_gather | solution.py:133
  109.2 113.6 %collective-permute-start.4 = (bf16[256,3584]{1,0:T(8,128)(2,1)}, bf16[256,3584]{1,0:T(8,128)(2,1)}, u32[]{:S(2)}, u32[]{:S(2)}) collective-permute-start(bf16[256,3584]{1,0:T(8,128)(2,1)} %param.14), channel_id=1, source_target_pairs={{0,1},{1,0},{2,3},{3,2},{4,5},{5,4},{6,7},{7,6},{8,9},{9,8},{10,11... | collective-permute-start | bytes 5505032 | tf_op jit(solution)/shard_map/ppermute | solution.py:80
  116.0 7.9 %copy-start.9 = (bf16[2,1024,256]{1,2,0:T(8,128)(2,1)S(1)}, bf16[2,1024,256]{1,2,0:T(8,128)(2,1)}, u32[]{:S(2)}) copy-start(bf16[2,1024,256]{1,2,0:T(8,128)(2,1)} %copy-done.8) | copy-start | bytes 3145732
  118.2 68.7 %collective-permute-start.6 = (bf16[3584,256]{1,0:T(8,128)(2,1)S(1)}, bf16[3584,256]{1,0:T(8,128)(2,1)S(1)}, u32[]{:S(2)}, u32[]{:S(2)}) collective-permute-start(bf16[3584,256]{1,0:T(8,128)(2,1)S(1)} %bitcast.254), channel_id=1, source_target_pairs={{0,64},{64,0},{1,65},{65,1},{2,66},{66,2},{3,67},{67,3},{4,68},{68... | collective-permute-start | bytes 5505032 | tf_op jit(solution)/shard_map/ppermute | solution.py:131
  124.0 8.7 %copy-start.7 = (bf16[2,1024,256]{1,2,0:T(8,128)(2,1)S(1)}, bf16[2,1024,256]{1,2,0:T(8,128)(2,1)}, u32[]{:S(2)}) copy-start(bf16[2,1024,256]{1,2,0:T(8,128)(2,1)} %copy-done.6) | copy-start | bytes 3145732
  129.8 116.3 %collective-permute-start.7 = (bf16[256,3584]{1,0:T(8,128)(2,1)}, bf16[256,3584]{1,0:T(8,128)(2,1)}, u32[]{:S(2)}, u32[]{:S(2)}) collective-permute-start(bf16[256,3584]{1,0:T(8,128)(2,1)} %bitcast.30), channel_id=1, source_target_pairs={{0,64},{64,0},{1,65},{65,1},{2,66},{66,2},{3,67},{67,3},{4,68},{68... | collective-permute-start | bytes 5505032 | tf_op jit(solution)/shard_map/ppermute | solution.py:131
  189.1 9.3 %slice-start = ((s8[8388608]{0:T(1024)(128)(4,1)}), s8[4194304]{0:T(1024)(128)(4,1)S(1)}, s32[]{:S(2)}) async-start(s8[8388608]{0:T(1024)(128)(4,1)} %bitcast.240), calls=%async_computation.6 | async-start | bytes 8388608
  193.7 4.7 %slice-start.1 = ((s8[8388608]{0:T(1024)(128)(4,1)}), s8[4194304]{0:T(1024)(128)(4,1)S(1)}, s32[]{:S(2)}) async-start(s8[8388608]{0:T(1024)(128)(4,1)} %bitcast.240), calls=%async_computation.7 | async-start | bytes 8388608
  198.4 6.3 %copy-start.11 = (bf16[1024,256]{1,0:T(8,128)(2,1)S(1)}, bf16[1024,256]{1,0:T(8,128)(2,1)}, u32[]{:S(2)}) copy-start(bf16[1024,256]{1,0:T(8,128)(2,1)} %param.13) | copy-start | bytes 1572868
  204.6 8.8 %slice-start.2 = ((s8[8388608]{0:T(1024)(128)(4,1)}), s8[4194304]{0:T(1024)(128)(4,1)S(1)}, s32[]{:S(2)}) async-start(s8[8388608]{0:T(1024)(128)(4,1)} %bitcast.242), calls=%async_computation.8 | async-start | bytes 8388608
  204.6 6.5 %copy-start.12 = (bf16[1,1024,256]{1,2,0:T(8,128)(2,1)S(1)}, bf16[1,1024,256]{1,2,0:T(8,128)(2,1)}, u32[]{:S(2)}) copy-start(bf16[1,1024,256]{1,2,0:T(8,128)(2,1)} %get-tuple-element.21) | copy-start | bytes 1572868
  204.6 8.8 %slice-start.3 = ((s8[8388608]{0:T(1024)(128)(4,1)}), s8[4194304]{0:T(1024)(128)(4,1)S(1)}, s32[]{:S(2)}) async-start(s8[8388608]{0:T(1024)(128)(4,1)} %bitcast.242), calls=%async_computation.9 | async-start | bytes 8388608
  211.2 2.3 copy-start.13
  211.2 4.5 %slice-start.4 = ((s8[8388608]{0:T(1024)(128)(4,1)}), s8[4194304]{0:T(1024)(128)(4,1)S(1)}, s32[]{:S(2)}) async-start(s8[8388608]{0:T(1024)(128)(4,1)} %bitcast.244), calls=%async_computation.10 | async-start | bytes 8388608
  213.4 2.4 copy-start.14
  213.4 3.6 slice-start.5
  217.1 4.6 %copy-start.5 = (bf16[256,3584]{1,0:T(8,128)(2,1)S(1)}, bf16[256,3584]{1,0:T(8,128)(2,1)}, u32[]{:S(2)}) copy-start(bf16[256,3584]{1,0:T(8,128)(2,1)} %param.14) | copy-start | bytes 5505028
  220.3 13.4 %collective-permute-start.3 = (bf16[16,32,256]{2,1,0:T(8,128)(2,1)S(1)}, bf16[16,32,256]{2,1,0:T(8,128)(2,1)S(1)}, u32[]{:S(2)}, u32[]{:S(2)}) collective-permute-start(bf16[16,32,256]{2,1,0:T(8,128)(2,1)S(1)} %get-tuple-element.23), channel_id=1, source_target_pairs={{0,1},{1,0},{2,3},{3,2},{4,5},{5,4},{6,7},{7,6},{8,9},{9,8},{10,11... | collective-permute-start | bytes 786440 | tf_op jit(solution)/shard_map/ppermute | solution.py:84
  238.2 56.5 %all-to-all-start = ((bf16[16,32,3584]{2,1,0:T(8,128)(2,1)}), bf16[16,32,3584]{2,1,0:T(8,128)(2,1)}, u32[]{:S(2)}, u32[]{:S(2)}) async-start(bf16[16,32,3584]{2,1,0:T(8,128)(2,1)} %bitcast.246), calls=%async_computation | async-start | bytes 7340032 | tf_op jit(solution)/shard_map/all_to_all | solution.py:95
  246.0 4.4 %copy-start.18 = (s32[32,8]{0,1:T(8,128)S(1)}, s32[32,8]{0,1:T(8,128)}, u32[]{:S(2)}) copy-start(s32[32,8]{0,1:T(8,128)} %param.17) | copy-start | bytes 3076
  246.0 51.3 %copy-start.3 = (bf16[32,3584]{1,0:T(8,128)(2,1)S(1)}, bf16[32,3584]{1,0:T(8,128)(2,1)}, u32[]{:S(2)}) copy-start(bf16[32,3584]{1,0:T(8,128)(2,1)} %param.15) | copy-start | bytes 688132
  246.0 51.5 %copy-start.15 = (f32[3584]{0:T(1024)S(1)}, f32[3584]{0:T(1024)}, u32[]{:S(2)}) copy-start(f32[3584]{0:T(1024)} %param.16) | copy-start | bytes 43012
  246.1 108.4 %all-gather.8.cloned.1.call-start = ((), (), s32[]{:S(2)}) async-start(), calls=%async_computation.5 | async-start | bytes 11010048 | tf_op jit(solution)/shard_map/all_gather | solution.py:133
  251.6 85.0 %copy-start.16 = (s32[256]{0:T(256)}, s32[256]{0:T(256)S(1)}, u32[]{:S(2)}) copy-start(s32[256]{0:T(256)S(1)} %get-tuple-element.38) | copy-start | bytes 3076
  251.6 85.0 %copy-start.17 = (s32[256]{0:T(256)}, s32[256]{0:T(256)S(1)}, u32[]{:S(2)}) copy-start(s32[256]{0:T(256)S(1)} %get-tuple-element.39) | copy-start | bytes 3076
  340.1 7.5 %copy-start.2 = (bf16[320,3584]{1,0:T(8,128)(2,1)S(1)}, bf16[320,3584]{1,0:T(8,128)(2,1)}, u32[]{:S(2)}) copy-start(bf16[320,3584]{1,0:T(8,128)(2,1)} %reshape.118) | copy-start | bytes 6881284
  360.6 7.7 %copy-start.19 = (f32[32,8]{0,1:T(8,128)S(1)}, f32[32,8]{0,1:T(8,128)}, u32[]{:S(2)}) copy-start(f32[32,8]{0,1:T(8,128)} %param.18) | copy-start | bytes 3076
  360.6 42.5 %copy-start.1 = (bf16[1024,256]{1,0:T(8,128)(2,1)S(1)}, bf16[1024,256]{1,0:T(8,128)(2,1)}, u32[]{:S(2)}) copy-start(bf16[1024,256]{1,0:T(8,128)(2,1)} %param.11) | copy-start | bytes 1572868
  364.1 32.0 %all-to-all-start.2 = ((bf16[32,8,4480]{2,1,0:T(8,128)(2,1)}), bf16[32,8,4480]{2,1,0:T(8,128)(2,1)S(1)}, u32[]{:S(2)}, u32[]{:S(2)}) async-start(bf16[32,8,4480]{2,1,0:T(8,128)(2,1)} %reshape.121), calls=%async_computation.2 | async-start | bytes 4587520 | tf_op jit(solution)/shard_map/all_to_all | solution.py:154
Sparse Core Ops, SparseCore 0:
  109.3 22.4 all-gather.3
  189.2 29.3 all-gather.5
  250.5 22.6 all-gather.7

commit v12 on v10

--- a/solution.py
+++ b/solution.py
@@ -64,9 +64,8 @@
     for step_index in range(1, ctx_count):
         pair_block = from_behind(pair_block, "ctx", 1)
         carried = attend(carried, query_heads, pair_block, ctx_where >= step_index)
-    gate_local, up_local, down_local, _ = lax.optimization_barrier(
-        (w_gate[0], w_up[0], w_down[0], pair_block)
-    )
+    gate_local = w_gate[0]
+    up_local, down_local, _ = lax.optimization_barrier((w_up[0], w_down[0], pair_block))
     attended = (
         (carried[2] / carried[1].T[:, :, None])
         .astype(jnp.bfloat16)

time: 357 us -> 336 us (0.941)
  waiting for transfers between devices: 179 us -> 153 us
    all_gather x1, waiting for transfers between devices: 40.9 us -> 0.01 us  [per_device(): down_full = lax.all_gather(down_local, 'ctx', axis=0, tiled=True)]
    ppermute x3, waiting for transfers between devices: 45.6 us -> 75.9 us  [from_behind(): return lax.ppermute(shard, axis, pairs)]
    all_to_all x1, waiting for transfers between devices: 29.3 us -> 20.4 us  [per_device(): lax.all_to_all(expert_out, EXP, split_axis=0, concat_axis=0, tiled=True)]
    all_to_all x1, starting transfers between devices: 9.87 us -> 16.3 us  [per_device(): lax.all_to_all(pair_term.reshape(hi_count, per_owner, pair_term.shape[1])...]
    ppermute x1, waiting for transfers between devices: 13.1 us -> 6.96 us  [per_device(): partner_proj = lax.ppermute(out_proj, 'exp_lo', swap)]
  transfers between devices with their start and end apart: 10 -> 10, of which waited for: 8 -> 7; matrix products, arithmetic and copies ran while one was open for 20% -> 22% of each run, Pallas kernels for 0% -> 0%
where the time goes in v12:
time: 336 us; the launch traced here: 333 us
  waiting for transfers between devices  153 us (46%)
  matrix products  54.9 us (16%)
  starting transfers between devices  40 us (12%)
  blocking collectives  32 us (10%)
  local copies, waits for them, and re-layouts  26.9 us (8%)
  between operations  13.5 us (4%)
  other arithmetic  12.1 us (4%)
    ppermute x3, waiting for transfers between devices, from_behind(): return lax.ppermute(shard, axis, pairs)  75.9 us
    all_to_all x1, waiting for transfers between devices, per_device(): lax.all_to_all(pair_term.reshape(hi_count, per_owner, pair_term.shape[1])...  41 us
    all_to_all x1, blocking collectives, per_device(): lax.all_to_all(outgoing, EXP, split_axis=0, concat_axis=0, tiled=True)  32 us
    all_to_all x1, waiting for transfers between devices, per_device(): lax.all_to_all(expert_out, EXP, split_axis=0, concat_axis=0, tiled=True)  20.4 us
    ppermute x3, starting transfers between devices, from_behind(): return lax.ppermute(shard, axis, pairs)  17.8 us
    dot_general x4, matrix products, attend(): jnp.einsum('hqk,khd->qhd', expo_block.astype(jnp.bfloat16), value_heads,...  17 us
    all_to_all x1, starting transfers between devices, per_device(): lax.all_to_all(pair_term.reshape(hi_count, per_owner, pair_term.shape[1])...  16.3 us
    ppermute x1, waiting for transfers between devices, per_device(): lax.ppermute(lax.dynamic_index_in_dim(by_owner, 1 - lo_where, axis=1, kee...  8.32 us
  transfers between devices with their start and end apart: 10, of which 7 were waited for; matrix products, arithmetic and copies ran while one was open for 22% of the time, Pallas kernels for 0%

profile of v12, /device:TPU:1, one launch (start us, length us, event | category | flops | bytes accessed | tf_op | source)
XLA Modules:
  0.0 332.7 jit_solution(9755544627993506372)
XLA Ops:
  6.5 0.7 all-gather.9.cloned.1.call-update
  7.3 0.0 all-gather.5.cloned.1.call-start
  7.3 1.2 copy.33
  8.6 1.2 copy.34
  9.8 0.1 pad_maximum_fusion
  9.9 6.0 %collective-permute-start = (bf16[2,1024,256]{1,2,0:T(8,128)(2,1)S(1)}, bf16[2,1024,256]{1,2,0:T(8,128)(2,1)S(1)}, u32[]{:S(2)}, u32[]{:S(2)}) collective-permute-start(bf16[2,1024,256]{1,2,0:T(8,128)(2,1)S(1)} %pad_maximum_fusion), channel_id=1, source_target_pairs={{0,32},{32,64},{64,96},{1,33},{33,65},{65,97},{2,34},{34,66},{66,9... | collective-permute-start | bytes 3145736 | tf_op jit(solution)/shard_map/ppermute | solution.py:20
  16.0 18.6 %collective-permute-done = bf16[2,1024,256]{1,2,0:T(8,128)(2,1)S(1)} collective-permute-done((bf16[2,1024,256]{1,2,0:T(8,128)(2,1)S(1)}, bf16[2,1024,256]{1,2,0:T(8,128)(2,1)S(1)}, u32[]{:S(2)}, u32[]{:S(2)}) %collective-permute-start) | collective-permute-done | bytes 1048608 | tf_op jit(solution)/shard_map/ppermute | solution.py:20
  34.6 1.0 copy-done.7
  35.6 5.9 %collective-permute-start.1 = (bf16[2,1024,256]{1,2,0:T(8,128)(2,1)S(1)}, bf16[2,1024,256]{1,2,0:T(8,128)(2,1)S(1)}, u32[]{:S(2)}, u32[]{:S(2)}) collective-permute-start(bf16[2,1024,256]{1,2,0:T(8,128)(2,1)S(1)} %collective-permute-done), channel_id=1, source_target_pairs={{0,32},{32,64},{64,96},{1,33},{33,65},{65,97},{2,34},{34,66},{66,9... | collective-permute-start | bytes 3145736 | tf_op jit(solution)/shard_map/ppermute | solution.py:20
  41.5 34.3 %collective-permute-done.1 = bf16[2,1024,256]{1,2,0:T(8,128)(2,1)S(1)} collective-permute-done((bf16[2,1024,256]{1,2,0:T(8,128)(2,1)S(1)}, bf16[2,1024,256]{1,2,0:T(8,128)(2,1)S(1)}, u32[]{:S(2)}, u32[]{:S(2)}) %collective-permute-start.1) | collective-permute-done | bytes 1048608 | tf_op jit(solution)/shard_map/ppermute | solution.py:20
  75.8 1.0 copy-done.9
  76.8 5.9 %collective-permute-start.2 = (bf16[2,1024,256]{1,2,0:T(8,128)(2,1)S(1)}, bf16[2,1024,256]{1,2,0:T(8,128)(2,1)}, u32[]{:S(2)}, u32[]{:S(2)}) collective-permute-start(bf16[2,1024,256]{1,2,0:T(8,128)(2,1)S(1)} %collective-permute-done.1), channel_id=1, source_target_pairs={{0,32},{32,64},{64,96},{1,33},{33,65},{65,97},{2,34},{34,66},{66,9... | collective-permute-start | bytes 3145736 | tf_op jit(solution)/shard_map/ppermute | solution.py:20
  82.7 23.0 %collective-permute-done.2 = bf16[2,1024,256]{1,2,0:T(8,128)(2,1)} collective-permute-done((bf16[2,1024,256]{1,2,0:T(8,128)(2,1)S(1)}, bf16[2,1024,256]{1,2,0:T(8,128)(2,1)}, u32[]{:S(2)}, u32[]{:S(2)}) %collective-permute-start.2) | collective-permute-done | bytes 1048608 | tf_op jit(solution)/shard_map/ppermute | solution.py:20
  105.7 0.0 all-gather.5.cloned.1.call-update
  105.7 0.0 all-gather.7.cloned.1.call-start
  105.7 0.1 collective-permute-start.4
  105.8 0.3 iota_compare_fusion
  106.2 1.8 fusion.3
  108.0 0.1 fusion.119
  108.1 1.4 bitcast_reduce_fusion.2
  109.6 1.0 fusion.118
  110.6 1.4 bitcast_reduce_fusion.1
  112.0 2.1 fusion.117
  114.1 1.5 bitcast_reduce_fusion
  115.6 3.2 copy-done.2
  118.8 2.1 fusion.12
  120.8 2.0 fusion.6
  122.9 4.0 %fusion.8 = (f32[2,1024]{1,0:T(2,128)S(1)}, f32[2,1024]{1,0:T(2,128)S(1)}) fusion(f32[2,1024,1024]{1,2,0:T(8,128)S(1)} %get-tuple-element.31, f32[2,1024]{1,0:T(2,128)S(1)} %get-tuple-element.14, pred[]{:T(512)S(6)} %ge.25, f32[2,1024]{1,0:T(2,128)S(1)} %get-tuple-element.13, f32[2,1024,1024]{1,2,0:T(8,128)S(1)} %get-tuple-element.29, pred[]{:T(512)S(6)} %ge.26), kind=kLoop, calls=%fused_computation.22 | loop fusion | flops 16773120 | bytes 16809986 | tf_op jit(solution)/shard_map/reduce_sum | solution.py:45
  126.9 4.2 %fusion.58 = f32[1024,2,128]{2,0,1:T(8,128)} fusion(f32[2,1024,1024]{1,2,0:T(8,128)S(1)} %get-tuple-element.33, f32[2,1024]{1,0:T(2,128)S(1)} %get-tuple-element.25, pred[1024,1024]{0,1:T(8,128)(4,1)S(1)} %iota_compare_fusion, f32[1024,2]{0,1:T(2,128)S(1)} %get-tuple-element.23, f32[1024,2]{0,1:T(2,128)S(1)} %get-tuple-element.24, ...), kind=kOutput, calls=%fused_computation.54 | convolution fusion | flops 545783808 | bytes 11034624 | tf_op jit(solution)/shard_map/hqk,khd->qhd/dot_general | solution.py:46
  131.1 5.9 %fusion.49 = f32[1024,2,128]{2,0,1:T(8,128)S(1)} fusion(f32[1024,2,128]{2,0,1:T(8,128)} %fusion.58, bf16[1024,2,128]{0,2,1:T(8,128)(2,1)S(1)} %bitcast.254, f32[2,1024,1024]{1,2,0:T(8,128)} %copy-done.3, f32[2,1024]{1,0:T(2,128)S(1)} %get-tuple-element.14, pred[]{:T(512)S(6)} %ge.25, f32[1024,2]{0,1:T(2,128)S(1)} %get-tuple-element.11), kind=kOutput, calls=%fused_computation.51 | convolution fusion | flops 545783808 | bytes 11026433 | tf_op jit(solution)/shard_map/hqk,khd->qhd/dot_general | solution.py:46
  137.0 4.7 %fusion.52 = f32[1024,2,128]{2,0,1:T(8,128)S(1)} fusion(f32[1024,2,128]{2,0,1:T(8,128)S(1)} %fusion.49, bf16[1024,2,128]{0,2,1:T(8,128)(2,1)S(1)} %bitcast.255, f32[2,1024,1024]{1,2,0:T(8,128)} %copy-done.4, f32[2,1024]{1,0:T(2,128)S(1)} %get-tuple-element.13, pred[]{:T(512)S(6)} %ge.26, f32[1024,2]{0,1:T(2,128)S(1)} %get-tuple-element.10), kind=kOutput, calls=%fused_computation.52 | convolution fusion | flops 545783808 | bytes 11026433 | tf_op jit(solution)/shard_map/hqk,khd->qhd/dot_general | solution.py:46
  141.7 2.3 divide_convert_fusion
  144.0 0.5 copy.47
  144.6 0.3 reshape_reshape.3
  145.0 1.7 collective-permute-start.3
  146.7 2.6 convolution_convert_fusion.1
  149.3 7.0 %collective-permute-done.4 = bf16[256,3584]{1,0:T(8,128)(2,1)S(1)} collective-permute-done((bf16[256,3584]{1,0:T(8,128)(2,1)}, bf16[256,3584]{1,0:T(8,128)(2,1)S(1)}, u32[]{:S(2)}, u32[]{:S(2)}) %collective-permute-start.4) | collective-permute-done | bytes 1835040 | tf_op jit(solution)/shard_map/ppermute | solution.py:78
  156.3 8.3 %collective-permute-done.3 = bf16[16,32,256]{2,1,0:T(8,128)(2,1)S(1)} collective-permute-done((bf16[16,32,256]{2,1,0:T(8,128)(2,1)S(1)}, bf16[16,32,256]{2,1,0:T(8,128)(2,1)S(1)}, u32[]{:S(2)}, u32[]{:S(2)}) %collective-permute-start.3) | collective-permute-done | bytes 262176 | tf_op jit(solution)/shard_map/ppermute | solution.py:82
  164.6 2.9 add_convert_fusion
  167.5 16.3 %all-to-all-start = ((bf16[16,32,3584]{2,1,0:T(8,128)(2,1)}), bf16[16,32,3584]{2,1,0:T(8,128)(2,1)}, u32[]{:S(2)}, u32[]{:S(2)}) async-start(bf16[16,32,3584]{2,1,0:T(8,128)(2,1)} %bitcast.243), calls=%async_computation | async-start | bytes 7340032 | tf_op jit(solution)/shard_map/all_to_all | solution.py:93
  183.8 0.1 copy.49
  183.9 0.1 eq.61
  184.0 0.1 reshape.115
  184.1 0.6 reduce-window.6
  184.7 0.2 slice_reduce_fusion
  184.9 0.1 fusion.95
  185.0 41.0 %all-to-all-done = bf16[16,32,3584]{2,1,0:T(8,128)(2,1)} async-done(((bf16[16,32,3584]{2,1,0:T(8,128)(2,1)}), bf16[16,32,3584]{2,1,0:T(8,128)(2,1)}, u32[]{:S(2)}, u32[]{:S(2)}) %all-to-all-start) | async-done | bytes 3670048 | tf_op jit(solution)/shard_map/all_to_all | solution.py:93
  226.0 2.6 convert_reduce_fusion.1
  228.7 0.2 multiply_reduce_fusion
  228.9 1.1 convolution_convert_fusion.2
  229.9 3.5 %reshape.117 = bf16[32,8,4480]{2,1,0:T(8,128)(2,1)} reshape(bf16[320,3584]{1,0:T(8,128)(2,1)S(1)} %convolution_convert_fusion.2) | data formatting | bytes 4587520 | tf_op jit(solution)/shard_map/reshape | solution.py:125
  233.5 32.0 %all_to_all.15 = bf16[32,8,4480]{2,1,0:T(8,128)(2,1)S(1)} all-to-all(bf16[32,8,4480]{2,1,0:T(8,128)(2,1)} %reshape.117), channel_id=1, replica_groups=mesh['ctx'=4,'exp_hi'=16,'exp_lo'=2] {'exp_hi','exp_lo'}, dimensions={0} | all-to-all | bytes 4587520 | tf_op jit(solution)/shard_map/all_to_all | solution.py:127
  265.5 3.5 %reshape.118 = bf16[320,3584]{1,0:T(8,128)(2,1)} reshape(bf16[32,8,4480]{2,1,0:T(8,128)(2,1)S(1)} %all_to_all.15) | data formatting | bytes 4587520 | tf_op jit(solution)/shard_map/reshape | solution.py:131
  268.9 7.5 %fusion.4 = f32[320,1024]{1,0:T(8,128)} fusion(bf16[320,3584]{1,0:T(8,128)(2,1)} %reshape.118, bf16[1,3584,1024]{2,1,0:T(8,128)(2,1)} %all-gather.9.cloned.1.call-done), kind=kOutput, calls=%fused_computation.16 | convolution fusion | flops 2348810240 | bytes 10944512 | tf_op jit(solution)/shard_map/dot_general | solution.py:132
  276.4 6.9 %fusion.39 = bf16[320,1024]{1,0:T(8,128)(2,1)} fusion(bf16[320,3584]{1,0:T(8,128)(2,1)S(1)} %copy-done.5, bf16[3584,1024]{1,0:T(8,128)(2,1)} %all-gather.5.cloned.1.call-done, f32[320,1024]{1,0:T(8,128)} %fusion.4), kind=kOutput, calls=%fused_computation.47 | convolution fusion | flops 2350776320 | bytes 11599872 | tf_op jit(solution)/shard_map/dot_general | solution.py:133
  283.3 6.1 %convert_reduce_fusion = bf16[320,3584]{1,0:T(8,128)(2,1)S(1)} fusion(bf16[4,256,3584]{2,1,0:T(8,128)(2,1)} %bitcast.256, bf16[40,4,8,256]{3,2,1,0:T(8,128)(2,1)} %bitcast.257), kind=kOutput, calls=%fused_computation | convolution fusion | flops 2356838400 | bytes 10289152 | tf_op jit(solution)/shard_map/rqf,qfd->qrd/dot_general | solution.py:136
  289.4 3.5 %reshape.121 = bf16[32,8,4480]{2,1,0:T(8,128)(2,1)} reshape(bf16[320,3584]{1,0:T(8,128)(2,1)S(1)} %convert_reduce_fusion) | data formatting | bytes 4587520 | tf_op jit(solution)/shard_map/reshape | solution.py:145
  293.0 4.1 %all-to-all-start.2 = ((bf16[32,8,4480]{2,1,0:T(8,128)(2,1)}), bf16[32,8,4480]{2,1,0:T(8,128)(2,1)S(1)}, u32[]{:S(2)}, u32[]{:S(2)}) async-start(bf16[32,8,4480]{2,1,0:T(8,128)(2,1)} %reshape.121), calls=%async_computation.2 | async-start | bytes 4587520 | tf_op jit(solution)/shard_map/all_to_all | solution.py:147
  297.0 0.1 copy.48
  297.1 0.6 mul.119
  297.7 1.0 fusion.77
  298.7 20.4 %all-to-all-done.2 = bf16[32,8,4480]{2,1,0:T(8,128)(2,1)S(1)} async-done(((bf16[32,8,4480]{2,1,0:T(8,128)(2,1)}), bf16[32,8,4480]{2,1,0:T(8,128)(2,1)S(1)}, u32[]{:S(2)}, u32[]{:S(2)}) %all-to-all-start.2) | async-done | bytes 2293792 | tf_op jit(solution)/shard_map/all_to_all | solution.py:147
  319.1 3.5 %reshape.122 = bf16[320,3584]{1,0:T(8,128)(2,1)} reshape(bf16[32,8,4480]{2,1,0:T(8,128)(2,1)S(1)} %all-to-all-done.2) | data formatting | bytes 4587520 | tf_op jit(solution)/shard_map/reshape | solution.py:153
  322.6 3.6 %fusion.14 = bf16[32,3584]{1,0:T(8,128)(2,1)} fusion(f32[32,320]{1,0:T(8,128)S(1)} %fusion.77, bf16[320,3584]{1,0:T(8,128)(2,1)} %reshape.122, f32[32,3584]{1,0:T(8,128)S(1)} %convert_reduce_fusion.1, bf16[32,3584]{1,0:T(8,128)(2,1)S(1)} %copy-done.6), kind=kOutput, calls=%fused_computation.32 | convolution fusion | flops 440860672 | bytes 3252224 | tf_op jit(solution)/shard_map/dot_general | solution.py:151
  (53 shorter events, 0.3 us)
Async XLA Ops:
  6.5 99.6 %copy-start = (bf16[1024,256]{1,0:T(8,128)(2,1)S(1)}, bf16[1024,256]{1,0:T(8,128)(2,1)}, u32[]{:S(2)}) copy-start(bf16[1024,256]{1,0:T(8,128)(2,1)} %param.11) | copy-start | bytes 1572868
  6.5 99.6 %copy-start.11 = (bf16[1024,256]{1,0:T(8,128)(2,1)S(1)}, bf16[1024,256]{1,0:T(8,128)(2,1)}, u32[]{:S(2)}) copy-start(bf16[1024,256]{1,0:T(8,128)(2,1)} %param.12) | copy-start | bytes 1572868
  6.5 262.4 %all-gather.9.cloned.1.call-start = ((), (), s32[]{:S(2)}) async-start(), calls=%async_computation.5 | async-start | bytes 9175040 | tf_op jit(solution)/shard_map/all_gather | solution.py:128
  7.3 269.2 %all-gather.5.cloned.1.call-start = ((), (), s32[]{:S(2)}) async-start(), calls=%async_computation.3 | async-start | bytes 9175040 | tf_op jit(solution)/shard_map/all_gather | solution.py:129
  9.9 24.7 %collective-permute-start = (bf16[2,1024,256]{1,2,0:T(8,128)(2,1)S(1)}, bf16[2,1024,256]{1,2,0:T(8,128)(2,1)S(1)}, u32[]{:S(2)}, u32[]{:S(2)}) collective-permute-start(bf16[2,1024,256]{1,2,0:T(8,128)(2,1)S(1)} %pad_maximum_fusion), channel_id=1, source_target_pairs={{0,32},{32,64},{64,96},{1,33},{33,65},{65,97},{2,34},{34,66},{66,9... | collective-permute-start | bytes 3145736 | tf_op jit(solution)/shard_map/ppermute | solution.py:20
  34.6 1.0 copy-start.7
  35.6 40.2 %collective-permute-start.1 = (bf16[2,1024,256]{1,2,0:T(8,128)(2,1)S(1)}, bf16[2,1024,256]{1,2,0:T(8,128)(2,1)S(1)}, u32[]{:S(2)}, u32[]{:S(2)}) collective-permute-start(bf16[2,1024,256]{1,2,0:T(8,128)(2,1)S(1)} %collective-permute-done), channel_id=1, source_target_pairs={{0,32},{32,64},{64,96},{1,33},{33,65},{65,97},{2,34},{34,66},{66,9... | collective-permute-start | bytes 3145736 | tf_op jit(solution)/shard_map/ppermute | solution.py:20
  75.8 1.0 copy-start.9
  76.8 28.8 %collective-permute-start.2 = (bf16[2,1024,256]{1,2,0:T(8,128)(2,1)S(1)}, bf16[2,1024,256]{1,2,0:T(8,128)(2,1)}, u32[]{:S(2)}, u32[]{:S(2)}) collective-permute-start(bf16[2,1024,256]{1,2,0:T(8,128)(2,1)S(1)} %collective-permute-done.1), channel_id=1, source_target_pairs={{0,32},{32,64},{64,96},{1,33},{33,65},{65,97},{2,34},{34,66},{66,9... | collective-permute-start | bytes 3145736 | tf_op jit(solution)/shard_map/ppermute | solution.py:20
  105.7 177.6 %all-gather.7.cloned.1.call-start = ((), (), s32[]{:S(2)}) async-start(), calls=%async_computation.4 | async-start | bytes 9175040 | tf_op jit(solution)/shard_map/all_gather | solution.py:130
  105.7 50.5 %collective-permute-start.4 = (bf16[256,3584]{1,0:T(8,128)(2,1)}, bf16[256,3584]{1,0:T(8,128)(2,1)S(1)}, u32[]{:S(2)}, u32[]{:S(2)}) collective-permute-start(bf16[256,3584]{1,0:T(8,128)(2,1)} %param.14), channel_id=1, source_target_pairs={{0,1},{1,0},{2,3},{3,2},{4,5},{5,4},{6,7},{7,6},{8,9},{9,8},{10,11... | collective-permute-start | bytes 5505032 | tf_op jit(solution)/shard_map/ppermute | solution.py:78
  105.8 2.2 copy-start.8
  108.0 1.5 copy-start.10
  109.6 13.3 %copy-start.3 = (f32[2,1024,1024]{1,2,0:T(8,128)}, f32[2,1024,1024]{1,2,0:T(8,128)S(1)}, u32[]{:S(2)}) copy-start(f32[2,1024,1024]{1,2,0:T(8,128)S(1)} %get-tuple-element.31) | copy-start | bytes 25165828
  112.0 10.8 %copy-start.4 = (f32[2,1024,1024]{1,2,0:T(8,128)}, f32[2,1024,1024]{1,2,0:T(8,128)S(1)}, u32[]{:S(2)}) copy-start(f32[2,1024,1024]{1,2,0:T(8,128)S(1)} %get-tuple-element.29) | copy-start | bytes 25165828
  115.5 3.2 copy-start.2
  122.8 4.1 %copy-start.12 = (bf16[1024,256]{1,0:T(8,128)(2,1)S(1)}, bf16[1024,256]{1,0:T(8,128)(2,1)}, u32[]{:S(2)}) copy-start(bf16[1024,256]{1,0:T(8,128)(2,1)} %param.13) | copy-start | bytes 1572868
  131.1 5.9 %copy-start.13 = (bf16[1,1024,256]{1,2,0:T(8,128)(2,1)S(1)}, bf16[1,1024,256]{1,2,0:T(8,128)(2,1)}, u32[]{:S(2)}) copy-start(bf16[1,1024,256]{1,2,0:T(8,128)(2,1)} %get-tuple-element.17) | copy-start | bytes 1572868
  131.1 10.6 %slice-start = ((s8[8388608]{0:T(1024)(128)(4,1)}), s8[4194304]{0:T(1024)(128)(4,1)S(1)}, s32[]{:S(2)}) async-start(s8[8388608]{0:T(1024)(128)(4,1)} %bitcast.241), calls=%async_computation.6 | async-start | bytes 8388608
  137.0 4.7 %slice-start.1 = ((s8[8388608]{0:T(1024)(128)(4,1)}), s8[4194304]{0:T(1024)(128)(4,1)S(1)}, s32[]{:S(2)}) async-start(s8[8388608]{0:T(1024)(128)(4,1)} %bitcast.241), calls=%async_computation.7 | async-start | bytes 8388608
  145.0 19.6 %collective-permute-start.3 = (bf16[16,32,256]{2,1,0:T(8,128)(2,1)S(1)}, bf16[16,32,256]{2,1,0:T(8,128)(2,1)S(1)}, u32[]{:S(2)}, u32[]{:S(2)}) collective-permute-start(bf16[16,32,256]{2,1,0:T(8,128)(2,1)S(1)} %get-tuple-element.21), channel_id=1, source_target_pairs={{0,1},{1,0},{2,3},{3,2},{4,5},{5,4},{6,7},{7,6},{8,9},{9,8},{10,11... | collective-permute-start | bytes 786440 | tf_op jit(solution)/shard_map/ppermute | solution.py:82
  164.6 19.2 %copy-start.17 = (s32[32,8]{0,1:T(8,128)S(1)}, s32[32,8]{0,1:T(8,128)}, u32[]{:S(2)}) copy-start(s32[32,8]{0,1:T(8,128)} %param.17) | copy-start | bytes 3076
  167.5 61.1 %copy-start.6 = (bf16[32,3584]{1,0:T(8,128)(2,1)S(1)}, bf16[32,3584]{1,0:T(8,128)(2,1)}, u32[]{:S(2)}) copy-start(bf16[32,3584]{1,0:T(8,128)(2,1)} %param.15) | copy-start | bytes 688132
  167.5 61.3 %copy-start.14 = (f32[3584]{0:T(1024)S(1)}, f32[3584]{0:T(1024)}, u32[]{:S(2)}) copy-start(f32[3584]{0:T(1024)} %param.16) | copy-start | bytes 43012
  167.5 58.5 %all-to-all-start = ((bf16[16,32,3584]{2,1,0:T(8,128)(2,1)}), bf16[16,32,3584]{2,1,0:T(8,128)(2,1)}, u32[]{:S(2)}, u32[]{:S(2)}) async-start(bf16[16,32,3584]{2,1,0:T(8,128)(2,1)} %bitcast.243), calls=%async_computation | async-start | bytes 7340032 | tf_op jit(solution)/shard_map/all_to_all | solution.py:93
  185.0 80.4 %copy-start.15 = (s32[256]{0:T(256)}, s32[256]{0:T(256)S(1)}, u32[]{:S(2)}) copy-start(s32[256]{0:T(256)S(1)} %get-tuple-element.34) | copy-start | bytes 3076
  185.0 80.4 %copy-start.16 = (s32[256]{0:T(256)}, s32[256]{0:T(256)S(1)}, u32[]{:S(2)}) copy-start(s32[256]{0:T(256)S(1)} %get-tuple-element.35) | copy-start | bytes 3076
  268.9 7.5 %copy-start.5 = (bf16[320,3584]{1,0:T(8,128)(2,1)S(1)}, bf16[320,3584]{1,0:T(8,128)(2,1)}, u32[]{:S(2)}) copy-start(bf16[320,3584]{1,0:T(8,128)(2,1)} %reshape.118) | copy-start | bytes 6881284
  283.3 13.7 %copy-start.18 = (f32[32,8]{0,1:T(8,128)S(1)}, f32[32,8]{0,1:T(8,128)}, u32[]{:S(2)}) copy-start(f32[32,8]{0,1:T(8,128)} %param.18) | copy-start | bytes 3076
  283.3 42.8 %copy-start.1 = (bf16[1024,256]{1,0:T(8,128)(2,1)S(1)}, bf16[1024,256]{1,0:T(8,128)(2,1)}, u32[]{:S(2)}) copy-start(bf16[1024,256]{1,0:T(8,128)(2,1)} %param.11) | copy-start | bytes 1572868
  293.0 26.1 %all-to-all-start.2 = ((bf16[32,8,4480]{2,1,0:T(8,128)(2,1)}), bf16[32,8,4480]{2,1,0:T(8,128)(2,1)S(1)}, u32[]{:S(2)}, u32[]{:S(2)}) async-start(bf16[32,8,4480]{2,1,0:T(8,128)(2,1)} %reshape.121), calls=%async_computation.2 | async-start | bytes 4587520 | tf_op jit(solution)/shard_map/all_to_all | solution.py:147
Sparse Core Ops, SparseCore 0:
  9.0 69.0 all-gather.8
  105.8 73.2 all-gather.4
  180.8 88.2 all-gather.6

commit v13 on v12

--- a/solution.py
+++ b/solution.py
@@ -127,21 +127,26 @@
     received = lax.all_to_all(outgoing, EXP, split_axis=0, concat_axis=0, tiled=True)
     gate_full = lax.all_gather(gate_local, "ctx", axis=1, tiled=True)
     up_full = lax.all_gather(up_local, "ctx", axis=1, tiled=True)
-    down_full = lax.all_gather(down_local, "ctx", axis=0, tiled=True)
+    down_pieces = [down_local] + [
+        lax.ppermute(down_local, "ctx", [(i, (i + shift) % ctx_count) for i in range(ctx_count)])
+        for shift in range(1, ctx_count)
+    ]
     rows = received.reshape(experts * capacity, width)
     gate = jnp.dot(rows, gate_full, preferred_element_type=jnp.float32)
     upper = jnp.dot(rows, up_full, preferred_element_type=jnp.float32)
     act_all = (jax.nn.silu(gate) * upper).astype(jnp.bfloat16)
     quarter = w_down.shape[1]
-    quarter_terms = jnp.einsum(
-        "rqf,qfd->qrd",
-        act_all.reshape(experts * capacity, ctx_count, quarter),
-        down_full.reshape(ctx_count, quarter, width),
-        preferred_element_type=jnp.float32,
-    ).astype(jnp.bfloat16)
+    act_quarters = act_all.reshape(experts * capacity, ctx_count, quarter)
+    expert_sum = jnp.zeros((experts * capacity, width), jnp.float32)
+    for piece_index, piece in enumerate(down_pieces):
+        act_piece = lax.dynamic_index_in_dim(
+            act_quarters, (ctx_where - piece_index) % ctx_count, axis=1, keepdims=False
+        )
+        expert_sum = expert_sum + jnp.dot(
+            act_piece, piece, preferred_element_type=jnp.float32
+        ).astype(jnp.bfloat16).astype(jnp.float32)
     expert_out = (
-        jnp.sum(quarter_terms.astype(jnp.float32), axis=0)
-        .astype(jnp.bfloat16)
+        expert_sum.astype(jnp.bfloat16)
         .reshape(experts, 8, capacity * width // 8)
     )
     returned = lax.all_to_all(expert_out, EXP, split_axis=0, concat_axis=0, tiled=True)

time: 336 us -> 393 us (1.17)
  the two profiles are of different devices: /device:TPU:1 before, /device:TPU:7 now
where the time goes in v13:
time: 393 us; the launch traced here: 386 us
  waiting for transfers between devices  165 us (42%)
  starting transfers between devices  91 us (23%)
  matrix products  67.1 us (17%)
  local copies, waits for them, and re-layouts  32.1 us (8%)
  other arithmetic  16.1 us (4%)
  between operations  14.4 us (4%)
    ppermute x3, starting transfers between devices, per_device(): lax.ppermute(down_local, 'ctx', [(i, (i + shift) % ctx_count) for i in ra...  60.3 us
    ppermute x3, waiting for transfers between devices, per_device(): lax.ppermute(down_local, 'ctx', [(i, (i + shift) % ctx_count) for i in ra...  59.1 us
    ppermute x3, waiting for transfers between devices, from_behind(): return lax.ppermute(shard, axis, pairs)  53.6 us
    all_to_all x1, waiting for transfers between devices, per_device(): lax.all_to_all(pair_term.reshape(hi_count, per_owner, pair_term.shape[1])...  29.4 us
    all_to_all x1, waiting for transfers between devices, per_device(): lax.all_to_all(expert_out, EXP, split_axis=0, concat_axis=0, tiled=True)  21.1 us
    dot_general x4, matrix products, attend(): jnp.einsum('qhd,khd->hqk', query_heads, key_heads, preferred_element_type...  17.6 us
    dot_general x4, matrix products, attend(): jnp.einsum('hqk,khd->qhd', expo_block.astype(jnp.bfloat16), value_heads,...  14.7 us
    reduce_sum x3, other arithmetic, attend(): total_new = total_old * factor + jnp.sum(expo_block, axis=2)  12.1 us
  transfers between devices with their start and end apart: 13, of which 8 were waited for; matrix products, arithmetic and copies ran while one was open for 26% of the time, Pallas kernels for 0%

profile of v13, /device:TPU:7, one launch (start us, length us, event | category | flops | bytes accessed | tf_op | source)
XLA Modules:
  0.0 385.8 jit_solution(1072573858528645113)
XLA Ops:
  6.5 0.7 all-gather.6.cloned.1.call-update
  7.3 1.2 copy.32
  8.6 1.2 copy.33
  9.8 0.1 pad_maximum_fusion
  9.9 1.3 collective-permute-start
  11.2 3.6 collective-permute-done
  14.8 1.3 collective-permute-start.1
  16.1 0.6 collective-permute-start.4
  16.7 0.3 iota_compare_fusion
  17.0 7.0 %fusion.3 = (f32[2,1024]{1,0:T(2,128)S(1)}, f32[2,1024,1024]{1,2,0:T(8,128)}) fusion(pred[1024,1024]{0,1:T(8,128)(4,1)S(1)} %iota_compare_fusion, bf16[1024,256]{1,0:T(8,128)(2,1)} %param.12, bf16[1024,256]{1,0:T(8,128)(2,1)S(1)} %copy-done), kind=kOutput, calls=%fused_computation.14 | convolution fusion | flops 543160320 | bytes 10493952 | tf_op jit(solution)/shard_map/qhd,khd->hqk/dot_general | solution.py:37
  24.1 2.3 fusion.125
  26.3 11.2 %collective-permute-done.1 = bf16[2,1024,256]{1,2,0:T(8,128)(2,1)} collective-permute-done((bf16[2,1024,256]{1,2,0:T(8,128)(2,1)}, bf16[2,1024,256]{1,2,0:T(8,128)(2,1)}, u32[]{:S(2)}, u32[]{:S(2)}) %collective-permute-start.1) | collective-permute-done | bytes 1048608 | tf_op jit(solution)/shard_map/ppermute | solution.py:20
  37.5 1.3 collective-permute-start.2
  38.8 4.6 %bitcast_reduce_fusion.2 = (f32[2,1024]{1,0:T(2,128)S(1)}, f32[2,1024,1024]{1,2,0:T(8,128)}) fusion(pred[]{:T(512)S(6)} %ge.25, bf16[1024,2,128]{0,2,1:T(8,128)(2,1)S(1)} %bitcast.258, bf16[1024,256]{1,0:T(8,128)(2,1)S(1)} %copy-done), kind=kOutput, calls=%fused_computation.7 | convolution fusion | flops 543160320 | bytes 9445377 | tf_op jit(solution)/shard_map/qhd,khd->hqk/dot_general | solution.py:37
  43.4 2.1 fusion.124
  45.5 4.6 %bitcast_reduce_fusion.1 = (f32[2,1024]{1,0:T(2,128)S(1)}, f32[2,1024,1024]{1,2,0:T(8,128)}) fusion(pred[]{:T(512)S(6)} %ge.26, bf16[1024,2,128]{0,2,1:T(8,128)(2,1)S(1)} %bitcast.260, bf16[1024,256]{1,0:T(8,128)(2,1)S(1)} %copy-done), kind=kOutput, calls=%fused_computation.4 | convolution fusion | flops 543160320 | bytes 9445377 | tf_op jit(solution)/shard_map/qhd,khd->hqk/dot_general | solution.py:37
  50.0 38.9 %collective-permute-done.2 = bf16[2,1024,256]{1,2,0:T(8,128)(2,1)} collective-permute-done((bf16[2,1024,256]{1,2,0:T(8,128)(2,1)}, bf16[2,1024,256]{1,2,0:T(8,128)(2,1)}, u32[]{:S(2)}, u32[]{:S(2)}) %collective-permute-start.2) | collective-permute-done | bytes 1048608 | tf_op jit(solution)/shard_map/ppermute | solution.py:20
  88.9 2.1 fusion.123
  91.1 1.4 bitcast_reduce_fusion
  92.5 4.0 %copy-done.2 = f32[2,1024,1024]{1,2,0:T(8,128)} copy-done((f32[2,1024,1024]{1,2,0:T(8,128)}, f32[2,1024,1024]{1,2,0:T(8,128)S(1)}, u32[]{:S(2)}) %copy-start.2) | copy-done | bytes 8388632
  96.5 2.2 fusion.12
  98.8 2.0 fusion.6
  100.8 7.9 %fusion.8 = (f32[2,1024]{1,0:T(2,128)S(1)}, f32[2,1024]{1,0:T(2,128)S(1)}) fusion(f32[2,1024,1024]{1,2,0:T(8,128)} %get-tuple-element.35, f32[2,1024]{1,0:T(2,128)S(1)} %get-tuple-element.14, pred[]{:T(512)S(6)} %ge.25, f32[2,1024]{1,0:T(2,128)S(1)} %get-tuple-element.13, f32[2,1024,1024]{1,2,0:T(8,128)} %get-tuple-element.33, pred[]{:T(512)S(6)} %ge.26), kind=kLoop, calls=%fused_computation.21 | loop fusion | flops 16773120 | bytes 16809986 | tf_op jit(solution)/shard_map/reduce_sum | solution.py:45
  108.8 5.5 %fusion.66 = f32[1024,2,128]{2,0,1:T(8,128)S(1)} fusion(f32[2,1024,1024]{1,2,0:T(8,128)} %get-tuple-element.37, f32[2,1024]{1,0:T(2,128)S(1)} %get-tuple-element.29, pred[1024,1024]{0,1:T(8,128)(4,1)S(1)} %iota_compare_fusion, f32[1024,2]{0,1:T(2,128)S(1)} %get-tuple-element.27, f32[1024,2]{0,1:T(2,128)S(1)} %get-tuple-element.28, ...), kind=kOutput, calls=%fused_computation.65 | convolution fusion | flops 545783808 | bytes 11034624 | tf_op jit(solution)/shard_map/hqk,khd->qhd/dot_general | solution.py:46
  114.4 4.7 %fusion.57 = f32[1024,2,128]{2,0,1:T(8,128)S(1)} fusion(f32[1024,2,128]{2,0,1:T(8,128)S(1)} %fusion.66, bf16[1024,2,128]{0,2,1:T(8,128)(2,1)S(1)} %bitcast.270, f32[2,1024,1024]{1,2,0:T(8,128)} %get-tuple-element.35, f32[2,1024]{1,0:T(2,128)S(1)} %get-tuple-element.14, pred[]{:T(512)S(6)} %ge.25, f32[1024,2]{0,1:T(2,128)S(1)} %get-tuple-element.11), kind=kOutput, calls=%fused_computation.62 | convolution fusion | flops 545783808 | bytes 11026433 | tf_op jit(solution)/shard_map/hqk,khd->qhd/dot_general | solution.py:46
  119.2 2.2 fusion.60
  121.4 2.3 divide_convert_fusion
  123.7 0.5 copy.46
  124.2 0.3 reshape_reshape.3
  124.6 3.3 collective-permute-start.3
  128.0 2.6 convolution_convert_fusion.1
  130.6 1.1 collective-permute-done.3
  131.7 3.0 add_convert_fusion
  134.7 9.9 %all-to-all-start = ((bf16[16,32,3584]{2,1,0:T(8,128)(2,1)}), bf16[16,32,3584]{2,1,0:T(8,128)(2,1)}, u32[]{:S(2)}, u32[]{:S(2)}) async-start(bf16[16,32,3584]{2,1,0:T(8,128)(2,1)} %bitcast.255), calls=%async_computation | async-start | bytes 7340032 | tf_op jit(solution)/shard_map/all_to_all | solution.py:93
  144.9 0.6 reduce-window.6
  145.5 0.2 slice_reduce_fusion
  145.8 0.1 fusion.101
  145.9 29.4 %all-to-all-done = bf16[16,32,3584]{2,1,0:T(8,128)(2,1)} async-done(((bf16[16,32,3584]{2,1,0:T(8,128)(2,1)}), bf16[16,32,3584]{2,1,0:T(8,128)(2,1)}, u32[]{:S(2)}, u32[]{:S(2)}) %all-to-all-start) | async-done | bytes 3670048 | tf_op jit(solution)/shard_map/all_to_all | solution.py:93
  175.3 2.6 convert_reduce_fusion
  177.9 0.2 multiply_reduce_fusion
  178.1 1.1 convolution_convert_fusion.6
  179.2 3.5 reshape.114
  182.7 5.2 %all-to-all-start.1 = ((bf16[32,8,4480]{2,1,0:T(8,128)(2,1)}), bf16[32,8,4480]{2,1,0:T(8,128)(2,1)S(1)}, u32[]{:S(2)}, u32[]{:S(2)}) async-start(bf16[32,8,4480]{2,1,0:T(8,128)(2,1)} %reshape.114), calls=%async_computation.1 | async-start | bytes 4587520 | tf_op jit(solution)/shard_map/all_to_all | solution.py:127
  188.0 12.6 %collective-permute-start.5 = (bf16[256,3584]{1,0:T(8,128)(2,1)}, bf16[256,3584]{1,0:T(8,128)(2,1)}, u32[]{:S(2)}, u32[]{:S(2)}) collective-permute-start(bf16[256,3584]{1,0:T(8,128)(2,1)} %bitcast.263), channel_id=1, source_target_pairs={{0,32},{32,64},{64,96},{96,0},{1,33},{33,65},{65,97},{97,1},{2,34}... | collective-permute-start | bytes 5505032 | tf_op jit(solution)/shard_map/ppermute | solution.py:131
  200.6 44.7 %collective-permute-start.7 = (bf16[256,3584]{1,0:T(8,128)(2,1)}, bf16[256,3584]{1,0:T(8,128)(2,1)}, u32[]{:S(2)}, u32[]{:S(2)}) collective-permute-start(bf16[256,3584]{1,0:T(8,128)(2,1)} %bitcast.264), channel_id=1, source_target_pairs={{0,96},{32,0},{64,32},{96,64},{1,97},{33,1},{65,33},{97,65},{2,98}... | collective-permute-start | bytes 5505032 | tf_op jit(solution)/shard_map/ppermute | solution.py:131
  245.2 3.0 collective-permute-start.6
  248.2 3.4 reshape.115
  251.7 7.6 %fusion.4 = f32[320,1024]{1,0:T(8,128)} fusion(bf16[320,3584]{1,0:T(8,128)(2,1)} %reshape.115, bf16[1,3584,1024]{2,1,0:T(8,128)(2,1)} %all-gather.6.cloned.1.call-done), kind=kOutput, calls=%fused_computation.15 | convolution fusion | flops 2348810240 | bytes 10944512 | tf_op jit(solution)/shard_map/dot_general | solution.py:135
  259.3 6.9 %fusion.47 = bf16[320,1024]{1,0:T(8,128)(2,1)} fusion(bf16[320,3584]{1,0:T(8,128)(2,1)S(1)} %copy-done.3, bf16[3584,1024]{1,0:T(8,128)(2,1)} %all-gather.4.cloned.1.call-done, f32[320,1024]{1,0:T(8,128)} %fusion.4), kind=kOutput, calls=%fused_computation.58 | convolution fusion | flops 2350776320 | bytes 11599872 | tf_op jit(solution)/shard_map/dot_general | solution.py:136
  266.1 1.8 reshape.116
  267.9 1.4 constant_dynamic-slice_fusion.1
  269.3 2.3 fusion.21
  271.6 13.2 %collective-permute-done.7 = bf16[256,3584]{1,0:T(8,128)(2,1)} collective-permute-done((bf16[256,3584]{1,0:T(8,128)(2,1)}, bf16[256,3584]{1,0:T(8,128)(2,1)}, u32[]{:S(2)}, u32[]{:S(2)}) %collective-permute-start.7) | collective-permute-done | bytes 1835040 | tf_op jit(solution)/shard_map/ppermute | solution.py:131
  284.8 2.3 fusion.14
  287.1 2.3 fusion.20
  289.3 45.8 %collective-permute-done.6 = bf16[256,3584]{1,0:T(8,128)(2,1)} collective-permute-done((bf16[256,3584]{1,0:T(8,128)(2,1)}, bf16[256,3584]{1,0:T(8,128)(2,1)}, u32[]{:S(2)}, u32[]{:S(2)}) %collective-permute-start.6) | collective-permute-done | bytes 1835040 | tf_op jit(solution)/shard_map/ppermute | solution.py:131
  335.2 2.3 fusion.18
  337.5 3.5 reshape.117
  340.9 7.8 %all-to-all-start.2 = ((bf16[32,8,4480]{2,1,0:T(8,128)(2,1)}), bf16[32,8,4480]{2,1,0:T(8,128)(2,1)S(1)}, u32[]{:S(2)}, u32[]{:S(2)}) async-start(bf16[32,8,4480]{2,1,0:T(8,128)(2,1)} %reshape.117), calls=%async_computation.2 | async-start | bytes 4587520 | tf_op jit(solution)/shard_map/all_to_all | solution.py:152
  348.8 0.6 mul.119
  349.4 1.0 fusion.83
  350.4 21.1 %all-to-all-done.2 = bf16[32,8,4480]{2,1,0:T(8,128)(2,1)S(1)} async-done(((bf16[32,8,4480]{2,1,0:T(8,128)(2,1)}), bf16[32,8,4480]{2,1,0:T(8,128)(2,1)S(1)}, u32[]{:S(2)}, u32[]{:S(2)}) %all-to-all-start.2) | async-done | bytes 2293792 | tf_op jit(solution)/shard_map/all_to_all | solution.py:152
  371.5 3.4 reshape.118
  375.0 3.6 fusion.22
  (62 shorter events, 0.7 us)
Async XLA Ops:
  6.5 10.5 %copy-start = (bf16[1024,256]{1,0:T(8,128)(2,1)S(1)}, bf16[1024,256]{1,0:T(8,128)(2,1)}, u32[]{:S(2)}) copy-start(bf16[1024,256]{1,0:T(8,128)(2,1)} %param.11) | copy-start | bytes 1572868
  6.5 245.1 %all-gather.6.cloned.1.call-start = ((), (), s32[]{:S(2)}) async-start(), calls=%async_computation.4 | async-start | bytes 9175040 | tf_op jit(solution)/shard_map/all_gather | solution.py:128
  7.3 252.0 %all-gather.4.cloned.1.call-start = ((), (), s32[]{:S(2)}) async-start(), calls=%async_computation.3 | async-start | bytes 9175040 | tf_op jit(solution)/shard_map/all_gather | solution.py:129
  9.9 4.9 %collective-permute-start = (bf16[2,1024,256]{1,2,0:T(8,128)(2,1)S(1)}, bf16[2,1024,256]{1,2,0:T(8,128)(2,1)}, u32[]{:S(2)}, u32[]{:S(2)}) collective-permute-start(bf16[2,1024,256]{1,2,0:T(8,128)(2,1)S(1)} %pad_maximum_fusion), channel_id=1, source_target_pairs={{0,32},{32,64},{64,96},{1,33},{33,65},{65,97},{2,34},{34,66},{66,9... | collective-permute-start | bytes 3145736 | tf_op jit(solution)/shard_map/ppermute | solution.py:20
  14.8 22.7 %collective-permute-start.1 = (bf16[2,1024,256]{1,2,0:T(8,128)(2,1)}, bf16[2,1024,256]{1,2,0:T(8,128)(2,1)}, u32[]{:S(2)}, u32[]{:S(2)}) collective-permute-start(bf16[2,1024,256]{1,2,0:T(8,128)(2,1)} %collective-permute-done), channel_id=1, source_target_pairs={{0,32},{32,64},{64,96},{1,33},{33,65},{65,97},{2,34},{34,66},{66,9... | collective-permute-start | bytes 3145736 | tf_op jit(solution)/shard_map/ppermute | solution.py:20
  16.1 114.5 %collective-permute-start.4 = (bf16[256,3584]{1,0:T(8,128)(2,1)}, bf16[256,3584]{1,0:T(8,128)(2,1)S(1)}, u32[]{:S(2)}, u32[]{:S(2)}) collective-permute-start(bf16[256,3584]{1,0:T(8,128)(2,1)} %param.14), channel_id=1, source_target_pairs={{0,1},{1,0},{2,3},{3,2},{4,5},{5,4},{6,7},{7,6},{8,9},{9,8},{10,11... | collective-permute-start | bytes 5505032 | tf_op jit(solution)/shard_map/ppermute | solution.py:78
  37.5 51.4 %collective-permute-start.2 = (bf16[2,1024,256]{1,2,0:T(8,128)(2,1)}, bf16[2,1024,256]{1,2,0:T(8,128)(2,1)}, u32[]{:S(2)}, u32[]{:S(2)}) collective-permute-start(bf16[2,1024,256]{1,2,0:T(8,128)(2,1)} %collective-permute-done.1), channel_id=1, source_target_pairs={{0,32},{32,64},{64,96},{1,33},{33,65},{65,97},{2,34},{34,66},{66,9... | collective-permute-start | bytes 3145736 | tf_op jit(solution)/shard_map/ppermute | solution.py:20
  91.0 7.7 %slice-start.4 = ((s8[8388608]{0:T(1024)(128)(4,1)}), s8[4194304]{0:T(1024)(128)(4,1)S(1)}, s32[]{:S(2)}) async-start(s8[8388608]{0:T(1024)(128)(4,1)} %bitcast.256), calls=%async_computation.9 | async-start | bytes 8388608
  91.0 7.7 %slice-start.5 = ((s8[8388608]{0:T(1024)(128)(4,1)}), s8[4194304]{0:T(1024)(128)(4,1)S(1)}, s32[]{:S(2)}) async-start(s8[8388608]{0:T(1024)(128)(4,1)} %bitcast.256), calls=%async_computation.10 | async-start | bytes 8388608
  92.5 4.0 %copy-start.2 = (f32[2,1024,1024]{1,2,0:T(8,128)}, f32[2,1024,1024]{1,2,0:T(8,128)S(1)}, u32[]{:S(2)}) copy-start(f32[2,1024,1024]{1,2,0:T(8,128)S(1)} %get-tuple-element.31) | copy-start | bytes 25165828
  100.8 8.0 %copy-start.5 = (bf16[1024,256]{1,0:T(8,128)(2,1)S(1)}, bf16[1024,256]{1,0:T(8,128)(2,1)}, u32[]{:S(2)}) copy-start(bf16[1024,256]{1,0:T(8,128)(2,1)} %param.13) | copy-start | bytes 1572868
  100.8 18.3 %slice-start = ((s8[8388608]{0:T(1024)(128)(4,1)}), s8[4194304]{0:T(1024)(128)(4,1)S(1)}, s32[]{:S(2)}) async-start(s8[8388608]{0:T(1024)(128)(4,1)} %bitcast.251), calls=%async_computation.5 | async-start | bytes 8388608
  108.8 5.6 %copy-start.6 = (bf16[1,1024,256]{1,2,0:T(8,128)(2,1)S(1)}, bf16[1,1024,256]{1,2,0:T(8,128)(2,1)}, u32[]{:S(2)}) copy-start(bf16[1,1024,256]{1,2,0:T(8,128)(2,1)} %get-tuple-element.19) | copy-start | bytes 1572868
  108.8 10.3 %slice-start.1 = ((s8[8388608]{0:T(1024)(128)(4,1)}), s8[4194304]{0:T(1024)(128)(4,1)S(1)}, s32[]{:S(2)}) async-start(s8[8388608]{0:T(1024)(128)(4,1)} %bitcast.251), calls=%async_computation.6 | async-start | bytes 8388608
  114.4 4.7 %copy-start.7 = (bf16[1,1024,256]{1,2,0:T(8,128)(2,1)S(1)}, bf16[1,1024,256]{1,2,0:T(8,128)(2,1)}, u32[]{:S(2)}) copy-start(bf16[1,1024,256]{1,2,0:T(8,128)(2,1)} %get-tuple-element.17) | copy-start | bytes 1572868
  114.4 7.0 %slice-start.2 = ((s8[8388608]{0:T(1024)(128)(4,1)}), s8[4194304]{0:T(1024)(128)(4,1)S(1)}, s32[]{:S(2)}) async-start(s8[8388608]{0:T(1024)(128)(4,1)} %bitcast.253), calls=%async_computation.7 | async-start | bytes 8388608
  119.1 2.3 slice-start.3
  119.1 2.2 copy-start.8
  124.6 7.1 %collective-permute-start.3 = (bf16[16,32,256]{2,1,0:T(8,128)(2,1)S(1)}, bf16[16,32,256]{2,1,0:T(8,128)(2,1)S(1)}, u32[]{:S(2)}, u32[]{:S(2)}) collective-permute-start(bf16[16,32,256]{2,1,0:T(8,128)(2,1)S(1)} %get-tuple-element.25), channel_id=1, source_target_pairs={{0,1},{1,0},{2,3},{3,2},{4,5},{5,4},{6,7},{7,6},{8,9},{9,8},{10,11... | collective-permute-start | bytes 786440 | tf_op jit(solution)/shard_map/ppermute | solution.py:82
  134.7 9.9 %copy-start.12 = (s32[32,8]{0,1:T(8,128)S(1)}, s32[32,8]{0,1:T(8,128)}, u32[]{:S(2)}) copy-start(s32[32,8]{0,1:T(8,128)} %param.17) | copy-start | bytes 3076
  134.7 43.2 %copy-start.4 = (bf16[32,3584]{1,0:T(8,128)(2,1)S(1)}, bf16[32,3584]{1,0:T(8,128)(2,1)}, u32[]{:S(2)}) copy-start(bf16[32,3584]{1,0:T(8,128)(2,1)} %param.15) | copy-start | bytes 688132
  134.7 43.4 %copy-start.9 = (f32[3584]{0:T(1024)S(1)}, f32[3584]{0:T(1024)}, u32[]{:S(2)}) copy-start(f32[3584]{0:T(1024)} %param.16) | copy-start | bytes 43012
  134.7 40.6 %all-to-all-start = ((bf16[16,32,3584]{2,1,0:T(8,128)(2,1)}), bf16[16,32,3584]{2,1,0:T(8,128)(2,1)}, u32[]{:S(2)}, u32[]{:S(2)}) async-start(bf16[16,32,3584]{2,1,0:T(8,128)(2,1)} %bitcast.255), calls=%async_computation | async-start | bytes 7340032 | tf_op jit(solution)/shard_map/all_to_all | solution.py:93
  145.9 36.8 %copy-start.10 = (s32[256]{0:T(256)}, s32[256]{0:T(256)S(1)}, u32[]{:S(2)}) copy-start(s32[256]{0:T(256)S(1)} %get-tuple-element.38) | copy-start | bytes 3076
  145.9 36.8 %copy-start.11 = (s32[256]{0:T(256)}, s32[256]{0:T(256)S(1)}, u32[]{:S(2)}) copy-start(s32[256]{0:T(256)S(1)} %get-tuple-element.39) | copy-start | bytes 3076
  182.7 65.5 %all-to-all-start.1 = ((bf16[32,8,4480]{2,1,0:T(8,128)(2,1)}), bf16[32,8,4480]{2,1,0:T(8,128)(2,1)S(1)}, u32[]{:S(2)}, u32[]{:S(2)}) async-start(bf16[32,8,4480]{2,1,0:T(8,128)(2,1)} %reshape.114), calls=%async_computation.1 | async-start | bytes 4587520 | tf_op jit(solution)/shard_map/all_to_all | solution.py:127
  188.0 99.1 %collective-permute-start.5 = (bf16[256,3584]{1,0:T(8,128)(2,1)}, bf16[256,3584]{1,0:T(8,128)(2,1)}, u32[]{:S(2)}, u32[]{:S(2)}) collective-permute-start(bf16[256,3584]{1,0:T(8,128)(2,1)} %bitcast.263), channel_id=1, source_target_pairs={{0,32},{32,64},{64,96},{96,0},{1,33},{33,65},{65,97},{97,1},{2,34}... | collective-permute-start | bytes 5505032 | tf_op jit(solution)/shard_map/ppermute | solution.py:131
  200.6 84.2 %collective-permute-start.7 = (bf16[256,3584]{1,0:T(8,128)(2,1)}, bf16[256,3584]{1,0:T(8,128)(2,1)}, u32[]{:S(2)}, u32[]{:S(2)}) collective-permute-start(bf16[256,3584]{1,0:T(8,128)(2,1)} %bitcast.264), channel_id=1, source_target_pairs={{0,96},{32,0},{64,32},{96,64},{1,97},{33,1},{65,33},{97,65},{2,98}... | collective-permute-start | bytes 5505032 | tf_op jit(solution)/shard_map/ppermute | solution.py:131
  245.2 90.0 %collective-permute-start.6 = (bf16[256,3584]{1,0:T(8,128)(2,1)}, bf16[256,3584]{1,0:T(8,128)(2,1)}, u32[]{:S(2)}, u32[]{:S(2)}) collective-permute-start(bf16[256,3584]{1,0:T(8,128)(2,1)} %bitcast.265), channel_id=1, source_target_pairs={{0,64},{32,96},{64,0},{96,32},{1,65},{33,97},{65,1},{97,33},{2,66}... | collective-permute-start | bytes 5505032 | tf_op jit(solution)/shard_map/ppermute | solution.py:131
  251.7 7.6 %copy-start.3 = (bf16[320,3584]{1,0:T(8,128)(2,1)S(1)}, bf16[320,3584]{1,0:T(8,128)(2,1)}, u32[]{:S(2)}) copy-start(bf16[320,3584]{1,0:T(8,128)(2,1)} %reshape.115) | copy-start | bytes 6881284
  337.4 11.3 %copy-start.13 = (f32[32,8]{0,1:T(8,128)S(1)}, f32[32,8]{0,1:T(8,128)}, u32[]{:S(2)}) copy-start(f32[32,8]{0,1:T(8,128)} %param.18) | copy-start | bytes 3076
  340.9 30.6 %all-to-all-start.2 = ((bf16[32,8,4480]{2,1,0:T(8,128)(2,1)}), bf16[32,8,4480]{2,1,0:T(8,128)(2,1)S(1)}, u32[]{:S(2)}, u32[]{:S(2)}) async-start(bf16[32,8,4480]{2,1,0:T(8,128)(2,1)} %reshape.117), calls=%async_computation.2 | async-start | bytes 4587520 | tf_op jit(solution)/shard_map/all_to_all | solution.py:152
  348.7 29.8 %copy-start.1 = (bf16[1024,256]{1,0:T(8,128)(2,1)S(1)}, bf16[1024,256]{1,0:T(8,128)(2,1)}, u32[]{:S(2)}) copy-start(bf16[1024,256]{1,0:T(8,128)(2,1)} %param.11) | copy-start | bytes 1572868
Sparse Core Ops, SparseCore 0:
  9.0 88.4 all-gather.5
  100.9 101.0 all-gather.3

commit v14 on v12

--- a/solution.py
+++ b/solution.py
@@ -126,8 +126,11 @@
     )
     received = lax.all_to_all(outgoing, EXP, split_axis=0, concat_axis=0, tiled=True)
     gate_full = lax.all_gather(gate_local, "ctx", axis=1, tiled=True)
-    up_full = lax.all_gather(up_local, "ctx", axis=1, tiled=True)
-    down_full = lax.all_gather(down_local, "ctx", axis=0, tiled=True)
+    up_down = lax.all_gather(
+        jnp.stack([up_local, down_local.reshape(up_local.shape)]), "ctx", axis=0, tiled=False
+    )
+    up_full = jnp.concatenate(list(up_down[:, 0]), axis=1)
+    down_full = up_down[:, 1].reshape(ctx_count * down_local.shape[0], down_local.shape[1])
     rows = received.reshape(experts * capacity, width)
     gate = jnp.dot(rows, gate_full, preferred_element_type=jnp.float32)
     upper = jnp.dot(rows, up_full, preferred_element_type=jnp.float32)

time: 336 us -> 356 us (1.060)
  local copies, waits for them, and re-layouts: 26.9 us -> 53.3 us
  waiting for transfers between devices: 153 us -> 135 us
  other arithmetic: 12.1 us -> 20.1 us
  starting transfers between devices: 40 us -> 45.3 us
  blocking collectives: 32 us -> 28.3 us
    another operation x1 -> x4, local copies, waits for them, and re-layouts: 0.01 us -> 24.2 us  [the longest x1 14.2 us: per_device(): down_full.reshape(ctx_count, quarter, width)]
    ppermute x1, starting transfers between devices: 1.7 us -> 12.9 us  [per_device(): lax.ppermute(lax.dynamic_index_in_dim(by_owner, 1 - lo_where, axis=1, kee...]
    ppermute x3, waiting for transfers between devices: 75.9 us -> 68.1 us  [from_behind(): return lax.ppermute(shard, axis, pairs)]
    ppermute x1, waiting for transfers between devices: 6.96 us -> 0.01 us  [per_device(): partner_proj = lax.ppermute(out_proj, 'exp_lo', swap)]
    all_to_all x1, starting transfers between devices: 16.3 us -> 10.4 us  [per_device(): lax.all_to_all(pair_term.reshape(hi_count, per_owner, pair_term.shape[1])...]
    all_to_all x1, waiting for transfers between devices: 41 us -> 36.2 us  [per_device(): lax.all_to_all(pair_term.reshape(hi_count, per_owner, pair_term.shape[1])...]
    reduce_sum x3, other arithmetic: 8.05 us -> 12.4 us  [attend(): total_new = total_old * factor + jnp.sum(expo_block, axis=2)]
    another operation x2 -> x3, other arithmetic: 0.63 us -> 4.3 us  [the longest x1 3.68 us: per_device(): jnp.stack([up_local, down_local.reshape(up_local.shape)])]
  transfers between devices with their start and end apart: 10 -> 9, of which waited for: 7 -> 6; matrix products, arithmetic and copies ran while one was open for 22% -> 23% of each run, Pallas kernels for 0% -> 0%
where the time goes in v14:
time: 356 us; the launch traced here: 352 us
  waiting for transfers between devices  135 us (38%)
  matrix products  55.6 us (16%)
  local copies, waits for them, and re-layouts  53.3 us (15%)
  starting transfers between devices  45.3 us (13%)
  blocking collectives  28.3 us (8%)
  other arithmetic  20.1 us (6%)
  between operations  14 us (4%)
    ppermute x3, waiting for transfers between devices, from_behind(): return lax.ppermute(shard, axis, pairs)  68.1 us
    all_to_all x1, waiting for transfers between devices, per_device(): lax.all_to_all(pair_term.reshape(hi_count, per_owner, pair_term.shape[1])...  36.2 us
    all_to_all x1, blocking collectives, per_device(): lax.all_to_all(outgoing, EXP, split_axis=0, concat_axis=0, tiled=True)  28.3 us
    all_to_all x1, waiting for transfers between devices, per_device(): lax.all_to_all(expert_out, EXP, split_axis=0, concat_axis=0, tiled=True)  23 us
    dot_general x4, matrix products, attend(): jnp.einsum('hqk,khd->qhd', expo_block.astype(jnp.bfloat16), value_heads,...  18.2 us
    ppermute x3, starting transfers between devices, from_behind(): return lax.ppermute(shard, axis, pairs)  17.8 us
    another operation x1, local copies, waits for them, and re-layouts, per_device(): down_full.reshape(ctx_count, quarter, width)  14.2 us
    ppermute x1, starting transfers between devices, per_device(): lax.ppermute(lax.dynamic_index_in_dim(by_owner, 1 - lo_where, axis=1, kee...  12.9 us
  transfers between devices with their start and end apart: 9, of which 6 were waited for; matrix products, arithmetic and copies ran while one was open for 23% of the time, Pallas kernels for 0%

profile of v14, /device:TPU:1, one launch (start us, length us, event | category | flops | bytes accessed | tf_op | source)
XLA Modules:
  0.0 352.0 jit_solution(12650937195677415483)
XLA Ops:
  6.5 0.7 all-gather.5.cloned.1.call-update
  7.3 0.0 all-gather.7.cloned.1.call-start
  7.3 1.2 copy.59
  8.6 1.2 copy.60
  9.8 0.1 pad_maximum_fusion.1
  9.9 6.0 %collective-permute-start = (bf16[2,1024,256]{1,2,0:T(8,128)(2,1)S(1)}, bf16[2,1024,256]{1,2,0:T(8,128)(2,1)S(1)}, u32[]{:S(2)}, u32[]{:S(2)}) collective-permute-start(bf16[2,1024,256]{1,2,0:T(8,128)(2,1)S(1)} %pad_maximum_fusion.1), channel_id=1, source_target_pairs={{0,32},{32,64},{64,96},{1,33},{33,65},{65,97},{2,34},{34,66},{66,9... | collective-permute-start | bytes 3145736 | tf_op jit(solution)/shard_map/ppermute | solution.py:20
  16.0 18.6 %collective-permute-done = bf16[2,1024,256]{1,2,0:T(8,128)(2,1)S(1)} collective-permute-done((bf16[2,1024,256]{1,2,0:T(8,128)(2,1)S(1)}, bf16[2,1024,256]{1,2,0:T(8,128)(2,1)S(1)}, u32[]{:S(2)}, u32[]{:S(2)}) %collective-permute-start) | collective-permute-done | bytes 1048608 | tf_op jit(solution)/shard_map/ppermute | solution.py:20
  34.6 5.9 %collective-permute-start.1 = (bf16[2,1024,256]{1,2,0:T(8,128)(2,1)S(1)}, bf16[2,1024,256]{1,2,0:T(8,128)(2,1)S(1)}, u32[]{:S(2)}, u32[]{:S(2)}) collective-permute-start(bf16[2,1024,256]{1,2,0:T(8,128)(2,1)S(1)} %collective-permute-done), channel_id=1, source_target_pairs={{0,32},{32,64},{64,96},{1,33},{33,65},{65,97},{2,34},{34,66},{66,9... | collective-permute-start | bytes 3145736 | tf_op jit(solution)/shard_map/ppermute | solution.py:20
  40.5 34.3 %collective-permute-done.1 = bf16[2,1024,256]{1,2,0:T(8,128)(2,1)S(1)} collective-permute-done((bf16[2,1024,256]{1,2,0:T(8,128)(2,1)S(1)}, bf16[2,1024,256]{1,2,0:T(8,128)(2,1)S(1)}, u32[]{:S(2)}, u32[]{:S(2)}) %collective-permute-start.1) | collective-permute-done | bytes 1048608 | tf_op jit(solution)/shard_map/ppermute | solution.py:20
  74.8 5.9 %collective-permute-start.2 = (bf16[2,1024,256]{1,2,0:T(8,128)(2,1)S(1)}, bf16[2,1024,256]{1,2,0:T(8,128)(2,1)S(1)}, u32[]{:S(2)}, u32[]{:S(2)}) collective-permute-start(bf16[2,1024,256]{1,2,0:T(8,128)(2,1)S(1)} %collective-permute-done.1), channel_id=1, source_target_pairs={{0,32},{32,64},{64,96},{1,33},{33,65},{65,97},{2,34},{34,66},{66,9... | collective-permute-start | bytes 3145736 | tf_op jit(solution)/shard_map/ppermute | solution.py:20
  80.7 15.2 %collective-permute-done.2 = bf16[2,1024,256]{1,2,0:T(8,128)(2,1)S(1)} collective-permute-done((bf16[2,1024,256]{1,2,0:T(8,128)(2,1)S(1)}, bf16[2,1024,256]{1,2,0:T(8,128)(2,1)S(1)}, u32[]{:S(2)}, u32[]{:S(2)}) %collective-permute-start.2) | collective-permute-done | bytes 1048608 | tf_op jit(solution)/shard_map/ppermute | solution.py:20
  95.9 1.0 copy-done.6
  96.9 3.8 %stack_reshape.3 = bf16[1,3584,256]{2,1,0:T(8,128)(2,1)S(1)} reshape(bf16[256,3584]{1,0:T(8,128)(2,1)} %bitcast.263) | data formatting | bytes 3670016 | tf_op jit(solution)/shard_map/stack;reshape | solution.py:130
  100.7 3.7 %pad_maximum_fusion = bf16[2,3584,256]{2,1,0:T(8,128)(2,1)} fusion(bf16[1,3584,256]{2,1,0:T(8,128)(2,1)S(1)} %stack_reshape.3, bf16[1,3584,256]{2,1,0:T(8,128)(2,1)} %param.20), kind=kLoop, calls=%fused_computation.51 | loop fusion | flops 1835008 | bytes 7340032 | tf_op jit(solution)/shard_map/stack | solution.py:130
  104.4 0.1 collective-permute-start.4
  104.5 0.3 iota_compare_fusion
  104.8 5.1 %fusion.3 = (f32[2,1024]{1,0:T(2,128)S(1)}, f32[2,1024,1024]{1,2,0:T(8,128)}) fusion(pred[1024,1024]{0,1:T(8,128)(4,1)S(1)} %iota_compare_fusion, bf16[1024,256]{1,0:T(8,128)(2,1)S(1)} %copy-done.11, bf16[1024,256]{1,0:T(8,128)(2,1)S(1)} %copy-done), kind=kOutput, calls=%fused_computation.15 | convolution fusion | flops 543160320 | bytes 10493952 | tf_op jit(solution)/shard_map/qhd,khd->hqk/dot_general | solution.py:37
  109.9 2.2 fusion.133
  112.1 1.4 bitcast_reduce_fusion.2
  113.5 0.9 fusion.132
  114.4 1.4 bitcast_reduce_fusion.1
  115.8 0.1 fusion.131
  115.9 1.4 bitcast_reduce_fusion
  117.4 2.3 fusion.20
  119.7 6.0 %fusion.14 = f32[2,1024]{1,0:T(2,128)S(1)} fusion(f32[2,1024,1024]{1,2,0:T(8,128)} %get-tuple-element.37, f32[2,1024]{1,0:T(2,128)S(1)} %get-tuple-element.29, pred[1024,1024]{0,1:T(8,128)(4,1)S(1)} %iota_compare_fusion), kind=kLoop, calls=%fused_computation.29 | loop fusion | flops 8386560 | bytes 9453568 | tf_op jit(solution)/shard_map/reduce_sum | solution.py:45
  125.8 4.0 %fusion.16 = (f32[2,1024]{1,0:T(2,128)S(1)}, f32[2,1024]{1,0:T(2,128)S(1)}) fusion(f32[2,1024,1024]{1,2,0:T(8,128)S(1)} %get-tuple-element.35, f32[2,1024]{1,0:T(2,128)S(1)} %get-tuple-element.14, pred[]{:T(512)S(6)} %ge.25, f32[2,1024]{1,0:T(2,128)S(1)} %get-tuple-element.13, f32[2,1024,1024]{1,2,0:T(8,128)S(1)} %get-tuple-element.33, pred[]{:T(512)S(6)} %ge.26), kind=kLoop, calls=%fused_computation.31 | loop fusion | flops 16773120 | bytes 16809986 | tf_op jit(solution)/shard_map/reduce_sum | solution.py:45
  129.9 7.6 %fusion.71 = f32[1024,2,128]{2,0,1:T(8,128)} fusion(f32[2,1024,1024]{1,2,0:T(8,128)} %get-tuple-element.37, f32[2,1024]{1,0:T(2,128)S(1)} %get-tuple-element.29, pred[1024,1024]{0,1:T(8,128)(4,1)S(1)} %iota_compare_fusion, f32[1024,2]{0,1:T(2,128)S(1)} %get-tuple-element.27, f32[1024,2]{0,1:T(2,128)S(1)} %get-tuple-element.28, ...), kind=kOutput, calls=%fused_computation.68 | convolution fusion | flops 545783808 | bytes 11034624 | tf_op jit(solution)/shard_map/hqk,khd->qhd/dot_general | solution.py:46
  137.5 3.6 %fusion.62 = f32[1024,2,128]{2,0,1:T(8,128)S(1)} fusion(f32[1024,2,128]{2,0,1:T(8,128)} %fusion.71, bf16[1024,2,128]{0,2,1:T(8,128)(2,1)} %bitcast.267, f32[2,1024,1024]{1,2,0:T(8,128)S(1)} %get-tuple-element.35, f32[2,1024]{1,0:T(2,128)S(1)} %get-tuple-element.14, pred[]{:T(512)S(6)} %ge.25, f32[1024,2]{0,1:T(2,128)S(1)} %get-tuple-element.11), kind=kOutput, calls=%fused_computation.65 | convolution fusion | flops 545783808 | bytes 11026433 | tf_op jit(solution)/shard_map/hqk,khd->qhd/dot_general | solution.py:46
  141.1 4.7 %fusion.65 = f32[1024,2,128]{2,0,1:T(8,128)S(1)} fusion(f32[1024,2,128]{2,0,1:T(8,128)S(1)} %fusion.62, bf16[1024,2,128]{0,2,1:T(8,128)(2,1)S(1)} %bitcast.268, f32[2,1024,1024]{1,2,0:T(8,128)} %copy-done.2, f32[2,1024]{1,0:T(2,128)S(1)} %get-tuple-element.13, pred[]{:T(512)S(6)} %ge.26, f32[1024,2]{0,1:T(2,128)S(1)} %get-tuple-element.10), kind=kOutput, calls=%fused_computation.66 | convolution fusion | flops 545783808 | bytes 11026433 | tf_op jit(solution)/shard_map/hqk,khd->qhd/dot_general | solution.py:46
  145.8 2.3 divide_convert_fusion
  148.1 0.5 copy.73
  148.6 0.3 reshape_reshape.3
  149.0 12.9 %collective-permute-start.3 = (bf16[16,32,256]{2,1,0:T(8,128)(2,1)S(1)}, bf16[16,32,256]{2,1,0:T(8,128)(2,1)S(1)}, u32[]{:S(2)}, u32[]{:S(2)}) collective-permute-start(bf16[16,32,256]{2,1,0:T(8,128)(2,1)S(1)} %get-tuple-element.25), channel_id=1, source_target_pairs={{0,1},{1,0},{2,3},{3,2},{4,5},{5,4},{6,7},{7,6},{8,9},{9,8},{10,11... | collective-permute-start | bytes 786440 | tf_op jit(solution)/shard_map/ppermute | solution.py:82
  161.9 2.6 convolution_convert_fusion.1
  164.6 7.3 %collective-permute-done.3 = bf16[16,32,256]{2,1,0:T(8,128)(2,1)S(1)} collective-permute-done((bf16[16,32,256]{2,1,0:T(8,128)(2,1)S(1)}, bf16[16,32,256]{2,1,0:T(8,128)(2,1)S(1)}, u32[]{:S(2)}, u32[]{:S(2)}) %collective-permute-start.3) | collective-permute-done | bytes 262176 | tf_op jit(solution)/shard_map/ppermute | solution.py:82
  171.9 3.0 add_convert_fusion
  174.8 10.4 %all-to-all-start = ((bf16[16,32,3584]{2,1,0:T(8,128)(2,1)}), bf16[16,32,3584]{2,1,0:T(8,128)(2,1)}, u32[]{:S(2)}, u32[]{:S(2)}) async-start(bf16[16,32,3584]{2,1,0:T(8,128)(2,1)} %bitcast.255), calls=%async_computation | async-start | bytes 7340032 | tf_op jit(solution)/shard_map/all_to_all | solution.py:93
  185.3 0.1 copy.75
  185.3 0.1 eq.61
  185.4 0.1 reshape.120
  185.5 0.6 reduce-window.6
  186.1 0.2 slice_reduce_fusion
  186.3 0.1 fusion.108
  186.5 36.2 %all-to-all-done = bf16[16,32,3584]{2,1,0:T(8,128)(2,1)} async-done(((bf16[16,32,3584]{2,1,0:T(8,128)(2,1)}), bf16[16,32,3584]{2,1,0:T(8,128)(2,1)}, u32[]{:S(2)}, u32[]{:S(2)}) %all-to-all-start) | async-done | bytes 3670048 | tf_op jit(solution)/shard_map/all_to_all | solution.py:93
  222.7 2.6 convert_reduce_fusion.1
  225.3 0.2 multiply_reduce_fusion
  225.5 1.1 convolution_convert_fusion.2
  226.5 3.5 reshape.122
  230.0 28.3 %all_to_all.15 = bf16[32,8,4480]{2,1,0:T(8,128)(2,1)S(1)} all-to-all(bf16[32,8,4480]{2,1,0:T(8,128)(2,1)} %reshape.122), channel_id=1, replica_groups=mesh['ctx'=4,'exp_hi'=16,'exp_lo'=2] {'exp_hi','exp_lo'}, dimensions={0} | all-to-all | bytes 4587520 | tf_op jit(solution)/shard_map/all_to_all | solution.py:127
  258.4 3.4 reshape.123
  261.8 7.4 %fusion.12 = f32[320,1024]{1,0:T(8,128)} fusion(bf16[320,3584]{1,0:T(8,128)(2,1)} %reshape.123, bf16[1,3584,1024]{2,1,0:T(8,128)(2,1)} %all-gather.5.cloned.1.call-done), kind=kOutput, calls=%fused_computation.25 | convolution fusion | flops 2348810240 | bytes 10944512 | tf_op jit(solution)/shard_map/dot_general | solution.py:135
  269.2 6.3 %slice_bitcast_fusion.4 = (bf16[3584,256]{1,0:T(8,128)(2,1)}, bf16[3584,256]{1,0:T(8,128)(2,1)}, bf16[3584,256]{1,0:T(8,128)(2,1)}, bf16[3584,256]{1,0:T(8,128)(2,1)}) fusion(bf16[4,2,3584,256]{3,2,1,0:T(8,128)(2,1)} %bitcast.256), kind=kLoop, calls=%fused_computation.55 | loop fusion | bytes 14680064 | tf_op jit(solution)/shard_map/unstack | solution.py:132
  275.5 6.5 %slice_bitcast_fusion = bf16[4,1,3584,256]{3,2,0,1:T(8,128)(2,1)} fusion(bf16[4,2,3584,256]{3,2,1,0:T(8,128)(2,1)} %bitcast.257), kind=kLoop, calls=%fused_computation.16 | loop fusion | bytes 14680064
  282.0 14.2 %reshape_reshape_squeeze.3 = bf16[4,256,3584]{2,1,0:T(8,128)(2,1)} reshape(bf16[4,1,3584,256]{3,2,0,1:T(8,128)(2,1)} %slice_bitcast_fusion) | data formatting | bytes 14680064 | tf_op jit(solution)/shard_map/reshape;reshape;squeeze | solution.py:142
  296.2 6.8 %fusion.50 = bf16[320,1024]{1,0:T(8,128)(2,1)S(1)} fusion(bf16[320,3584]{1,0:T(8,128)(2,1)S(1)} %copy-done.4, bf16[3584,256]{1,0:T(8,128)(2,1)} %get-tuple-element.16, bf16[3584,256]{1,0:T(8,128)(2,1)} %get-tuple-element.17, bf16[3584,256]{1,0:T(8,128)(2,1)} %get-tuple-element.18, bf16[3584,256]{1,0:T(8,128)(2,1)} %get-tuple-element.15, f32[320,1024]{1,0:T(8,128)} %fusion.12), kind=kOutput, calls=%fused_computation.61 | convolution fusion | flops 2380136448 | bytes 11599872 | tf_op jit(solution)/shard_map/dot_general | solution.py:136
  303.0 2.6 convert_reduce_fusion
  305.6 3.5 reshape.125
  309.1 4.1 %all-to-all-start.2 = ((bf16[32,8,4480]{2,1,0:T(8,128)(2,1)}), bf16[32,8,4480]{2,1,0:T(8,128)(2,1)S(1)}, u32[]{:S(2)}, u32[]{:S(2)}) async-start(bf16[32,8,4480]{2,1,0:T(8,128)(2,1)} %reshape.125), calls=%async_computation.2 | async-start | bytes 4587520 | tf_op jit(solution)/shard_map/all_to_all | solution.py:150
  313.2 0.1 copy.74
  313.3 0.6 mul.119
  313.9 1.0 fusion.90
  314.9 23.0 %all-to-all-done.2 = bf16[32,8,4480]{2,1,0:T(8,128)(2,1)S(1)} async-done(((bf16[32,8,4480]{2,1,0:T(8,128)(2,1)}), bf16[32,8,4480]{2,1,0:T(8,128)(2,1)S(1)}, u32[]{:S(2)}, u32[]{:S(2)}) %all-to-all-start.2) | async-done | bytes 2293792 | tf_op jit(solution)/shard_map/all_to_all | solution.py:150
  338.0 3.4 reshape.126
  341.4 3.6 %fusion.22 = bf16[32,3584]{1,0:T(8,128)(2,1)} fusion(f32[32,320]{1,0:T(8,128)S(1)} %fusion.90, bf16[320,3584]{1,0:T(8,128)(2,1)} %reshape.126, f32[32,3584]{1,0:T(8,128)S(1)} %convert_reduce_fusion.1, bf16[32,3584]{1,0:T(8,128)(2,1)S(1)} %copy-done.5), kind=kOutput, calls=%fused_computation.41 | convolution fusion | flops 440860672 | bytes 3252224 | tf_op jit(solution)/shard_map/dot_general | solution.py:154
  (50 shorter events, 0.3 us)
Async XLA Ops:
  6.5 98.3 %copy-start = (bf16[1024,256]{1,0:T(8,128)(2,1)S(1)}, bf16[1024,256]{1,0:T(8,128)(2,1)}, u32[]{:S(2)}) copy-start(bf16[1024,256]{1,0:T(8,128)(2,1)} %param.11) | copy-start | bytes 1572868
  6.5 255.3 %all-gather.5.cloned.1.call-start = ((), (), s32[]{:S(2)}) async-start(), calls=%async_computation.3 | async-start | bytes 9175040 | tf_op jit(solution)/shard_map/all_gather | solution.py:128
  7.3 262.0 %all-gather.7.cloned.1.call-start = ((), (), s32[]{:S(2)}) async-start(), calls=%async_computation.4 | async-start | bytes 18350080 | tf_op jit(solution)/shard_map/all_gather | solution.py:129
  9.9 24.7 %collective-permute-start = (bf16[2,1024,256]{1,2,0:T(8,128)(2,1)S(1)}, bf16[2,1024,256]{1,2,0:T(8,128)(2,1)S(1)}, u32[]{:S(2)}, u32[]{:S(2)}) collective-permute-start(bf16[2,1024,256]{1,2,0:T(8,128)(2,1)S(1)} %pad_maximum_fusion.1), channel_id=1, source_target_pairs={{0,32},{32,64},{64,96},{1,33},{33,65},{65,97},{2,34},{34,66},{66,9... | collective-permute-start | bytes 3145736 | tf_op jit(solution)/shard_map/ppermute | solution.py:20
  34.6 5.9 %copy-start.8 = (bf16[2,1024,256]{1,2,0:T(8,128)(2,1)}, bf16[2,1024,256]{1,2,0:T(8,128)(2,1)S(1)}, u32[]{:S(2)}) copy-start(bf16[2,1024,256]{1,2,0:T(8,128)(2,1)S(1)} %collective-permute-done) | copy-start | bytes 3145732
  34.6 40.2 %collective-permute-start.1 = (bf16[2,1024,256]{1,2,0:T(8,128)(2,1)S(1)}, bf16[2,1024,256]{1,2,0:T(8,128)(2,1)S(1)}, u32[]{:S(2)}, u32[]{:S(2)}) collective-permute-start(bf16[2,1024,256]{1,2,0:T(8,128)(2,1)S(1)} %collective-permute-done), channel_id=1, source_target_pairs={{0,32},{32,64},{64,96},{1,33},{33,65},{65,97},{2,34},{34,66},{66,9... | collective-permute-start | bytes 3145736 | tf_op jit(solution)/shard_map/ppermute | solution.py:20
  74.8 21.1 %copy-start.9 = (bf16[2,1024,256]{1,2,0:T(8,128)(2,1)}, bf16[2,1024,256]{1,2,0:T(8,128)(2,1)S(1)}, u32[]{:S(2)}) copy-start(bf16[2,1024,256]{1,2,0:T(8,128)(2,1)S(1)} %collective-permute-done.1) | copy-start | bytes 3145732
  74.8 21.1 %collective-permute-start.2 = (bf16[2,1024,256]{1,2,0:T(8,128)(2,1)S(1)}, bf16[2,1024,256]{1,2,0:T(8,128)(2,1)S(1)}, u32[]{:S(2)}, u32[]{:S(2)}) collective-permute-start(bf16[2,1024,256]{1,2,0:T(8,128)(2,1)S(1)} %collective-permute-done.1), channel_id=1, source_target_pairs={{0,32},{32,64},{64,96},{1,33},{33,65},{65,97},{2,34},{34,66},{66,9... | collective-permute-start | bytes 3145736 | tf_op jit(solution)/shard_map/ppermute | solution.py:20
  95.9 1.0 copy-start.6
  96.9 7.9 %copy-start.11 = (bf16[1024,256]{1,0:T(8,128)(2,1)S(1)}, bf16[1024,256]{1,0:T(8,128)(2,1)}, u32[]{:S(2)}) copy-start(bf16[1024,256]{1,0:T(8,128)(2,1)} %param.12) | copy-start | bytes 1572868
  104.4 60.2 %collective-permute-start.4 = (bf16[256,3584]{1,0:T(8,128)(2,1)}, bf16[256,3584]{1,0:T(8,128)(2,1)S(1)}, u32[]{:S(2)}, u32[]{:S(2)}) collective-permute-start(bf16[256,3584]{1,0:T(8,128)(2,1)} %param.14), channel_id=1, source_target_pairs={{0,1},{1,0},{2,3},{3,2},{4,5},{5,4},{6,7},{7,6},{8,9},{9,8},{10,11... | collective-permute-start | bytes 5505032 | tf_op jit(solution)/shard_map/ppermute | solution.py:78
  109.9 3.6 %copy-start.10 = (bf16[2,1024,256]{1,2,0:T(8,128)(2,1)S(1)}, bf16[2,1024,256]{1,2,0:T(8,128)(2,1)}, u32[]{:S(2)}) copy-start(bf16[2,1024,256]{1,2,0:T(8,128)(2,1)} %copy-done.9) | copy-start | bytes 3145732
  113.5 2.3 copy-start.7
  115.8 10.0 %copy-start.2 = (f32[2,1024,1024]{1,2,0:T(8,128)}, f32[2,1024,1024]{1,2,0:T(8,128)S(1)}, u32[]{:S(2)}) copy-start(f32[2,1024,1024]{1,2,0:T(8,128)S(1)} %get-tuple-element.33) | copy-start | bytes 25165828
  125.8 4.1 %copy-start.12 = (bf16[1024,256]{1,0:T(8,128)(2,1)S(1)}, bf16[1024,256]{1,0:T(8,128)(2,1)}, u32[]{:S(2)}) copy-start(bf16[1024,256]{1,0:T(8,128)(2,1)} %param.13) | copy-start | bytes 1572868
  137.5 3.6 %copy-start.13 = (bf16[1,1024,256]{1,2,0:T(8,128)(2,1)S(1)}, bf16[1,1024,256]{1,2,0:T(8,128)(2,1)}, u32[]{:S(2)}) copy-start(bf16[1,1024,256]{1,2,0:T(8,128)(2,1)} %get-tuple-element.21) | copy-start | bytes 1572868
  149.0 22.9 %collective-permute-start.3 = (bf16[16,32,256]{2,1,0:T(8,128)(2,1)S(1)}, bf16[16,32,256]{2,1,0:T(8,128)(2,1)S(1)}, u32[]{:S(2)}, u32[]{:S(2)}) collective-permute-start(bf16[16,32,256]{2,1,0:T(8,128)(2,1)S(1)} %get-tuple-element.25), channel_id=1, source_target_pairs={{0,1},{1,0},{2,3},{3,2},{4,5},{5,4},{6,7},{7,6},{8,9},{9,8},{10,11... | collective-permute-start | bytes 786440 | tf_op jit(solution)/shard_map/ppermute | solution.py:82
  171.9 13.4 %copy-start.17 = (s32[32,8]{0,1:T(8,128)S(1)}, s32[32,8]{0,1:T(8,128)}, u32[]{:S(2)}) copy-start(s32[32,8]{0,1:T(8,128)} %param.17) | copy-start | bytes 3076
  174.8 50.4 %copy-start.5 = (bf16[32,3584]{1,0:T(8,128)(2,1)S(1)}, bf16[32,3584]{1,0:T(8,128)(2,1)}, u32[]{:S(2)}) copy-start(bf16[32,3584]{1,0:T(8,128)(2,1)} %param.15) | copy-start | bytes 688132
  174.8 50.6 %copy-start.14 = (f32[3584]{0:T(1024)S(1)}, f32[3584]{0:T(1024)}, u32[]{:S(2)}) copy-start(f32[3584]{0:T(1024)} %param.16) | copy-start | bytes 43012
  174.8 47.8 %all-to-all-start = ((bf16[16,32,3584]{2,1,0:T(8,128)(2,1)}), bf16[16,32,3584]{2,1,0:T(8,128)(2,1)}, u32[]{:S(2)}, u32[]{:S(2)}) async-start(bf16[16,32,3584]{2,1,0:T(8,128)(2,1)} %bitcast.255), calls=%async_computation | async-start | bytes 7340032 | tf_op jit(solution)/shard_map/all_to_all | solution.py:93
  186.5 71.9 %copy-start.15 = (s32[256]{0:T(256)}, s32[256]{0:T(256)S(1)}, u32[]{:S(2)}) copy-start(s32[256]{0:T(256)S(1)} %get-tuple-element.38) | copy-start | bytes 3076
  186.5 71.9 %copy-start.16 = (s32[256]{0:T(256)}, s32[256]{0:T(256)S(1)}, u32[]{:S(2)}) copy-start(s32[256]{0:T(256)S(1)} %get-tuple-element.39) | copy-start | bytes 3076
  282.0 14.2 %copy-start.4 = (bf16[320,3584]{1,0:T(8,128)(2,1)S(1)}, bf16[320,3584]{1,0:T(8,128)(2,1)}, u32[]{:S(2)}) copy-start(bf16[320,3584]{1,0:T(8,128)(2,1)} %reshape.123) | copy-start | bytes 6881284
  296.2 6.8 %copy-start.3 = (bf16[4,256,3584]{2,1,0:T(8,128)(2,1)S(1)}, bf16[4,256,3584]{2,1,0:T(8,128)(2,1)}, u32[]{:S(2)}) copy-start(bf16[4,256,3584]{2,1,0:T(8,128)(2,1)} %reshape_reshape_squeeze.3) | copy-start | bytes 22020100
  305.6 7.6 %copy-start.18 = (f32[32,8]{0,1:T(8,128)S(1)}, f32[32,8]{0,1:T(8,128)}, u32[]{:S(2)}) copy-start(f32[32,8]{0,1:T(8,128)} %param.18) | copy-start | bytes 3076
  305.6 39.3 %copy-start.1 = (bf16[1024,256]{1,0:T(8,128)(2,1)S(1)}, bf16[1024,256]{1,0:T(8,128)(2,1)}, u32[]{:S(2)}) copy-start(bf16[1024,256]{1,0:T(8,128)(2,1)} %param.11) | copy-start | bytes 1572868
  309.1 28.8 %all-to-all-start.2 = ((bf16[32,8,4480]{2,1,0:T(8,128)(2,1)}), bf16[32,8,4480]{2,1,0:T(8,128)(2,1)S(1)}, u32[]{:S(2)}, u32[]{:S(2)}) async-start(bf16[32,8,4480]{2,1,0:T(8,128)(2,1)} %reshape.125), calls=%async_computation.2 | async-start | bytes 4587520 | tf_op jit(solution)/shard_map/all_to_all | solution.py:150
Sparse Core Ops, SparseCore 0:
  9.0 69.0 all-gather.4
  104.5 114.2 all-gather.6

commit v15 on v12

--- a/solution.py
+++ b/solution.py
@@ -65,7 +65,8 @@
         pair_block = from_behind(pair_block, "ctx", 1)
         carried = attend(carried, query_heads, pair_block, ctx_where >= step_index)
     gate_local = w_gate[0]
-    up_local, down_local, _ = lax.optimization_barrier((w_up[0], w_down[0], pair_block))
+    up_local = w_up[0]
+    down_local, _ = lax.optimization_barrier((w_down[0], pair_block))
     attended = (
         (carried[2] / carried[1].T[:, :, None])
         .astype(jnp.bfloat16)

time: 336 us -> 373 us (1.11)
  the two profiles are of different devices: /device:TPU:1 before, /device:TPU:6 now
where the time goes in v15:
time: 373 us; the launch traced here: 372 us
  waiting for transfers between devices  185 us (50%)
  matrix products  65.7 us (18%)
  blocking collectives  32.6 us (9%)
  starting transfers between devices  32.5 us (9%)
  local copies, waits for them, and re-layouts  28.3 us (8%)
  other arithmetic  15.2 us (4%)
  between operations  13.5 us (4%)
    ppermute x3, waiting for transfers between devices, from_behind(): return lax.ppermute(shard, axis, pairs)  125 us
    all_to_all x1, blocking collectives, per_device(): lax.all_to_all(outgoing, EXP, split_axis=0, concat_axis=0, tiled=True)  32.6 us
    all_to_all x1, waiting for transfers between devices, per_device(): lax.all_to_all(pair_term.reshape(hi_count, per_owner, pair_term.shape[1])...  30.6 us
    all_to_all x1, waiting for transfers between devices, per_device(): lax.all_to_all(expert_out, EXP, split_axis=0, concat_axis=0, tiled=True)  18.4 us
    dot_general x4, matrix products, attend(): jnp.einsum('hqk,khd->qhd', expo_block.astype(jnp.bfloat16), value_heads,...  17 us
    dot_general x4, matrix products, attend(): jnp.einsum('qhd,khd->hqk', query_heads, key_heads, preferred_element_type...  16.7 us
    all_to_all x1, starting transfers between devices, per_device(): lax.all_to_all(pair_term.reshape(hi_count, per_owner, pair_term.shape[1])...  11.6 us
    reduce_sum x3, other arithmetic, attend(): total_new = total_old * factor + jnp.sum(expo_block, axis=2)  11.2 us
  transfers between devices with their start and end apart: 10, of which 6 were waited for; matrix products, arithmetic and copies ran while one was open for 24% of the time, Pallas kernels for 0%

profile of v15, /device:TPU:6, one launch (start us, length us, event | category | flops | bytes accessed | tf_op | source)
XLA Modules:
  0.0 372.3 jit_solution(12553352048751211303)
XLA Ops:
  6.5 0.7 all-gather.8.cloned.1.call-update
  7.3 0.0 all-gather.10.cloned.1.call-start
  7.3 0.7 all-gather.10.cloned.1.call-update
  8.0 0.0 all-gather.6.cloned.1.call-start
  8.1 1.2 copy.33
  9.3 1.2 copy.34
  10.6 0.1 pad_maximum_fusion
  10.7 1.9 collective-permute-start
  12.6 22.1 %collective-permute-done = bf16[2,1024,256]{1,2,0:T(8,128)(2,1)} collective-permute-done((bf16[2,1024,256]{1,2,0:T(8,128)(2,1)S(1)}, bf16[2,1024,256]{1,2,0:T(8,128)(2,1)}, u32[]{:S(2)}, u32[]{:S(2)}) %collective-permute-start) | collective-permute-done | bytes 1048608 | tf_op jit(solution)/shard_map/ppermute | solution.py:20
  34.7 1.9 collective-permute-start.1
  36.6 3.0 collective-permute-start.4
  39.6 0.3 iota_compare_fusion
  40.0 6.1 %fusion.3 = (f32[2,1024]{1,0:T(2,128)S(1)}, f32[2,1024,1024]{1,2,0:T(8,128)}) fusion(pred[1024,1024]{0,1:T(8,128)(4,1)S(1)} %iota_compare_fusion, bf16[1024,256]{1,0:T(8,128)(2,1)} %param.12, bf16[1024,256]{1,0:T(8,128)(2,1)S(1)} %copy-done), kind=kOutput, calls=%fused_computation.15 | convolution fusion | flops 543160320 | bytes 10493952 | tf_op jit(solution)/shard_map/qhd,khd->hqk/dot_general | solution.py:37
  46.1 2.1 fusion.126
  48.1 38.0 %collective-permute-done.1 = bf16[2,1024,256]{1,2,0:T(8,128)(2,1)} collective-permute-done((bf16[2,1024,256]{1,2,0:T(8,128)(2,1)}, bf16[2,1024,256]{1,2,0:T(8,128)(2,1)}, u32[]{:S(2)}, u32[]{:S(2)}) %collective-permute-start.1) | collective-permute-done | bytes 1048608 | tf_op jit(solution)/shard_map/ppermute | solution.py:20
  86.1 1.9 collective-permute-start.2
  88.0 4.6 %bitcast_reduce_fusion.2 = (f32[2,1024]{1,0:T(2,128)S(1)}, f32[2,1024,1024]{1,2,0:T(8,128)}) fusion(pred[]{:T(512)S(6)} %ge.25, bf16[1024,2,128]{0,2,1:T(8,128)(2,1)S(1)} %bitcast.255, bf16[1024,256]{1,0:T(8,128)(2,1)S(1)} %copy-done), kind=kOutput, calls=%fused_computation.8 | convolution fusion | flops 543160320 | bytes 9445377 | tf_op jit(solution)/shard_map/qhd,khd->hqk/dot_general | solution.py:37
  92.6 2.1 fusion.125
  94.7 4.6 %bitcast_reduce_fusion.1 = (f32[2,1024]{1,0:T(2,128)S(1)}, f32[2,1024,1024]{1,2,0:T(8,128)}) fusion(pred[]{:T(512)S(6)} %ge.26, bf16[1024,2,128]{0,2,1:T(8,128)(2,1)S(1)} %bitcast.257, bf16[1024,256]{1,0:T(8,128)(2,1)S(1)} %copy-done), kind=kOutput, calls=%fused_computation.5 | convolution fusion | flops 543160320 | bytes 9445377 | tf_op jit(solution)/shard_map/qhd,khd->hqk/dot_general | solution.py:37
  99.2 64.9 %collective-permute-done.2 = bf16[2,1024,256]{1,2,0:T(8,128)(2,1)} collective-permute-done((bf16[2,1024,256]{1,2,0:T(8,128)(2,1)}, bf16[2,1024,256]{1,2,0:T(8,128)(2,1)}, u32[]{:S(2)}, u32[]{:S(2)}) %collective-permute-start.2) | collective-permute-done | bytes 1048608 | tf_op jit(solution)/shard_map/ppermute | solution.py:20
  164.1 2.1 fusion.124
  166.3 1.4 bitcast_reduce_fusion
  167.7 3.2 copy-done.2
  171.0 2.1 fusion.14
  173.0 5.2 %fusion.8 = f32[2,1024]{1,0:T(2,128)S(1)} fusion(f32[2,1024,1024]{1,2,0:T(8,128)} %get-tuple-element.31, f32[2,1024]{1,0:T(2,128)S(1)} %get-tuple-element.23, pred[1024,1024]{0,1:T(8,128)(4,1)S(1)} %iota_compare_fusion), kind=kLoop, calls=%fused_computation.22 | loop fusion | flops 8386560 | bytes 9453568 | tf_op jit(solution)/shard_map/reduce_sum | solution.py:45
  178.3 0.3 slice-done.1
  178.5 4.0 %fusion.10 = (f32[2,1024]{1,0:T(2,128)S(1)}, f32[2,1024]{1,0:T(2,128)S(1)}) fusion(f32[2,1024,1024]{1,2,0:T(8,128)S(1)} %bitcast.249, f32[2,1024]{1,0:T(2,128)S(1)} %get-tuple-element.12, pred[]{:T(512)S(6)} %ge.25, f32[2,1024]{1,0:T(2,128)S(1)} %get-tuple-element.11, f32[2,1024,1024]{1,2,0:T(8,128)S(1)} %bitcast.247, pred[]{:T(512)S(6)} %ge.26), kind=kLoop, calls=%fused_computation.24 | loop fusion | flops 16773120 | bytes 16809986 | tf_op jit(solution)/shard_map/reduce_sum | solution.py:45
  182.6 4.2 %fusion.65 = f32[1024,2,128]{2,0,1:T(8,128)} fusion(f32[2,1024,1024]{1,2,0:T(8,128)S(1)} %bitcast.254, f32[2,1024]{1,0:T(2,128)S(1)} %get-tuple-element.23, pred[1024,1024]{0,1:T(8,128)(4,1)S(1)} %iota_compare_fusion, f32[1024,2]{0,1:T(2,128)S(1)} %get-tuple-element.21, f32[1024,2]{0,1:T(2,128)S(1)} %get-tuple-element.22, bf16[1024,256]{1,0:T(8,128)(2,1)S(1)} %copy-done.5), kind=kOutput, calls=%fused_computation.56 | convolution fusion | flops 545783808 | bytes 11034624 | tf_op jit(solution)/shard_map/hqk,khd->qhd/dot_general | solution.py:46
  186.8 0.0 all-gather.6.cloned.1.call-update
  186.8 5.9 %fusion.56 = f32[1024,2,128]{2,0,1:T(8,128)S(1)} fusion(f32[1024,2,128]{2,0,1:T(8,128)} %fusion.65, bf16[1024,2,128]{0,2,1:T(8,128)(2,1)} %bitcast.263, f32[2,1024,1024]{1,2,0:T(8,128)} %get-tuple-element.29, f32[2,1024]{1,0:T(2,128)S(1)} %get-tuple-element.12, pred[]{:T(512)S(6)} %ge.25, f32[1024,2]{0,1:T(2,128)S(1)} %get-tuple-element.9), kind=kOutput, calls=%fused_computation.53 | convolution fusion | flops 545783808 | bytes 11026433 | tf_op jit(solution)/shard_map/hqk,khd->qhd/dot_general | solution.py:46
  192.7 4.7 %fusion.59 = f32[1024,2,128]{2,0,1:T(8,128)S(1)} fusion(f32[1024,2,128]{2,0,1:T(8,128)S(1)} %fusion.56, bf16[1024,2,128]{0,2,1:T(8,128)(2,1)S(1)} %bitcast.264, f32[2,1024,1024]{1,2,0:T(8,128)} %get-tuple-element.27, f32[2,1024]{1,0:T(2,128)S(1)} %get-tuple-element.11, pred[]{:T(512)S(6)} %ge.26, f32[1024,2]{0,1:T(2,128)S(1)} %get-tuple-element.8), kind=kOutput, calls=%fused_computation.54 | convolution fusion | flops 545783808 | bytes 11026433 | tf_op jit(solution)/shard_map/hqk,khd->qhd/dot_general | solution.py:46
  197.5 0.1 slice-done.5
  197.5 2.3 divide_convert_fusion
  199.8 0.5 copy.47
  200.4 0.3 reshape_reshape.3
  200.7 3.0 collective-permute-start.3
  203.8 2.9 convolution_convert_fusion.1
  206.7 9.1 %collective-permute-done.3 = bf16[16,32,256]{2,1,0:T(8,128)(2,1)S(1)} collective-permute-done((bf16[16,32,256]{2,1,0:T(8,128)(2,1)S(1)}, bf16[16,32,256]{2,1,0:T(8,128)(2,1)S(1)}, u32[]{:S(2)}, u32[]{:S(2)}) %collective-permute-start.3) | collective-permute-done | bytes 262176 | tf_op jit(solution)/shard_map/ppermute | solution.py:83
  215.7 3.0 add_convert_fusion
  218.7 11.6 %all-to-all-start = ((bf16[16,32,3584]{2,1,0:T(8,128)(2,1)}), bf16[16,32,3584]{2,1,0:T(8,128)(2,1)}, u32[]{:S(2)}, u32[]{:S(2)}) async-start(bf16[16,32,3584]{2,1,0:T(8,128)(2,1)} %bitcast.252), calls=%async_computation | async-start | bytes 7340032 | tf_op jit(solution)/shard_map/all_to_all | solution.py:94
  230.4 0.1 copy.49
  230.5 0.1 eq.61
  230.5 0.1 reshape.115
  230.6 0.6 reduce-window.6
  231.2 0.2 slice_reduce_fusion
  231.5 0.1 fusion.102
  231.6 30.6 %all-to-all-done = bf16[16,32,3584]{2,1,0:T(8,128)(2,1)} async-done(((bf16[16,32,3584]{2,1,0:T(8,128)(2,1)}), bf16[16,32,3584]{2,1,0:T(8,128)(2,1)}, u32[]{:S(2)}, u32[]{:S(2)}) %all-to-all-start) | async-done | bytes 3670048 | tf_op jit(solution)/shard_map/all_to_all | solution.py:94
  262.2 2.6 convert_reduce_fusion.1
  264.8 0.2 multiply_reduce_fusion
  265.0 1.1 convolution_convert_fusion.2
  266.1 3.5 reshape.117
  269.6 32.6 %all_to_all.15 = bf16[32,8,4480]{2,1,0:T(8,128)(2,1)S(1)} all-to-all(bf16[32,8,4480]{2,1,0:T(8,128)(2,1)} %reshape.117), channel_id=1, replica_groups=mesh['ctx'=4,'exp_hi'=16,'exp_lo'=2] {'exp_hi','exp_lo'}, dimensions={0} | all-to-all | bytes 4587520 | tf_op jit(solution)/shard_map/all_to_all | solution.py:128
  302.1 3.4 reshape.118
  305.6 7.5 %fusion.6 = f32[320,1024]{1,0:T(8,128)} fusion(bf16[320,3584]{1,0:T(8,128)(2,1)} %reshape.118, bf16[1,3584,1024]{2,1,0:T(8,128)(2,1)} %all-gather.8.cloned.1.call-done), kind=kOutput, calls=%fused_computation.18 | convolution fusion | flops 2348810240 | bytes 10944512 | tf_op jit(solution)/shard_map/dot_general | solution.py:133
  313.1 6.9 %fusion.44 = bf16[320,1024]{1,0:T(8,128)(2,1)} fusion(bf16[320,3584]{1,0:T(8,128)(2,1)S(1)} %copy-done.3, bf16[1,3584,1024]{2,1,0:T(8,128)(2,1)} %all-gather.10.cloned.1.call-done, f32[320,1024]{1,0:T(8,128)} %fusion.6), kind=kOutput, calls=%fused_computation.49 | convolution fusion | flops 2350776320 | bytes 11599872 | tf_op jit(solution)/shard_map/dot_general | solution.py:134
  320.0 6.1 %convert_reduce_fusion = bf16[320,3584]{1,0:T(8,128)(2,1)S(1)} fusion(bf16[4,256,3584]{2,1,0:T(8,128)(2,1)} %bitcast.266, bf16[40,4,8,256]{3,2,1,0:T(8,128)(2,1)} %bitcast.267), kind=kOutput, calls=%fused_computation | convolution fusion | flops 2356838400 | bytes 10289152 | tf_op jit(solution)/shard_map/rqf,qfd->qrd/dot_general | solution.py:137
  326.1 3.5 reshape.121
  329.6 9.0 %all-to-all-start.2 = ((bf16[32,8,4480]{2,1,0:T(8,128)(2,1)}), bf16[32,8,4480]{2,1,0:T(8,128)(2,1)S(1)}, u32[]{:S(2)}, u32[]{:S(2)}) async-start(bf16[32,8,4480]{2,1,0:T(8,128)(2,1)} %reshape.121), calls=%async_computation.2 | async-start | bytes 4587520 | tf_op jit(solution)/shard_map/all_to_all | solution.py:148
  338.6 0.1 copy.48
  338.7 0.6 mul.119
  339.3 1.0 fusion.84
  340.3 18.4 %all-to-all-done.2 = bf16[32,8,4480]{2,1,0:T(8,128)(2,1)S(1)} async-done(((bf16[32,8,4480]{2,1,0:T(8,128)(2,1)}), bf16[32,8,4480]{2,1,0:T(8,128)(2,1)S(1)}, u32[]{:S(2)}, u32[]{:S(2)}) %all-to-all-start.2) | async-done | bytes 2293792 | tf_op jit(solution)/shard_map/all_to_all | solution.py:148
  358.7 3.4 reshape.122
  362.2 3.6 fusion.16
  (56 shorter events, 0.3 us)
Async XLA Ops:
  6.5 33.4 %copy-start = (bf16[1024,256]{1,0:T(8,128)(2,1)S(1)}, bf16[1024,256]{1,0:T(8,128)(2,1)}, u32[]{:S(2)}) copy-start(bf16[1024,256]{1,0:T(8,128)(2,1)} %param.11) | copy-start | bytes 1572868
  6.5 299.0 %all-gather.8.cloned.1.call-start = ((), (), s32[]{:S(2)}) async-start(), calls=%async_computation.4 | async-start | bytes 9175040 | tf_op jit(solution)/shard_map/all_gather | solution.py:129
  7.3 305.8 %all-gather.10.cloned.1.call-start = ((), (), s32[]{:S(2)}) async-start(), calls=%async_computation.5 | async-start | bytes 9175040 | tf_op jit(solution)/shard_map/all_gather | solution.py:130
  8.0 312.0 %all-gather.6.cloned.1.call-start = ((), (), s32[]{:S(2)}) async-start(), calls=%async_computation.3 | async-start | bytes 9175040 | tf_op jit(solution)/shard_map/all_gather | solution.py:131
  10.7 24.1 %collective-permute-start = (bf16[2,1024,256]{1,2,0:T(8,128)(2,1)S(1)}, bf16[2,1024,256]{1,2,0:T(8,128)(2,1)}, u32[]{:S(2)}, u32[]{:S(2)}) collective-permute-start(bf16[2,1024,256]{1,2,0:T(8,128)(2,1)S(1)} %pad_maximum_fusion), channel_id=1, source_target_pairs={{0,32},{32,64},{64,96},{1,33},{33,65},{65,97},{2,34},{34,66},{66,9... | collective-permute-start | bytes 3145736 | tf_op jit(solution)/shard_map/ppermute | solution.py:20
  34.7 51.4 %collective-permute-start.1 = (bf16[2,1024,256]{1,2,0:T(8,128)(2,1)}, bf16[2,1024,256]{1,2,0:T(8,128)(2,1)}, u32[]{:S(2)}, u32[]{:S(2)}) collective-permute-start(bf16[2,1024,256]{1,2,0:T(8,128)(2,1)} %collective-permute-done), channel_id=1, source_target_pairs={{0,32},{32,64},{64,96},{1,33},{33,65},{65,97},{2,34},{34,66},{66,9... | collective-permute-start | bytes 3145736 | tf_op jit(solution)/shard_map/ppermute | solution.py:20
  36.6 170.0 %collective-permute-start.4 = (bf16[256,3584]{1,0:T(8,128)(2,1)}, bf16[256,3584]{1,0:T(8,128)(2,1)S(1)}, u32[]{:S(2)}, u32[]{:S(2)}) collective-permute-start(bf16[256,3584]{1,0:T(8,128)(2,1)} %param.14), channel_id=1, source_target_pairs={{0,1},{1,0},{2,3},{3,2},{4,5},{5,4},{6,7},{7,6},{8,9},{9,8},{10,11... | collective-permute-start | bytes 5505032 | tf_op jit(solution)/shard_map/ppermute | solution.py:79
  86.1 78.0 %collective-permute-start.2 = (bf16[2,1024,256]{1,2,0:T(8,128)(2,1)}, bf16[2,1024,256]{1,2,0:T(8,128)(2,1)}, u32[]{:S(2)}, u32[]{:S(2)}) collective-permute-start(bf16[2,1024,256]{1,2,0:T(8,128)(2,1)} %collective-permute-done.1), channel_id=1, source_target_pairs={{0,32},{32,64},{64,96},{1,33},{33,65},{65,97},{2,34},{34,66},{66,9... | collective-permute-start | bytes 3145736 | tf_op jit(solution)/shard_map/ppermute | solution.py:20
  166.3 12.0 %slice-start.2 = ((s8[8388608]{0:T(1024)(128)(4,1)}), s8[4194304]{0:T(1024)(128)(4,1)S(1)}, s32[]{:S(2)}) async-start(s8[8388608]{0:T(1024)(128)(4,1)} %bitcast.248), calls=%async_computation.8 | async-start | bytes 8388608
  167.7 3.2 copy-start.2
  170.9 7.3 %slice-start = ((s8[8388608]{0:T(1024)(128)(4,1)}), s8[4194304]{0:T(1024)(128)(4,1)S(1)}, s32[]{:S(2)}) async-start(s8[8388608]{0:T(1024)(128)(4,1)} %bitcast.246), calls=%async_computation.6 | async-start | bytes 8388608
  170.9 7.3 %slice-start.3 = ((s8[8388608]{0:T(1024)(128)(4,1)}), s8[4194304]{0:T(1024)(128)(4,1)S(1)}, s32[]{:S(2)}) async-start(s8[8388608]{0:T(1024)(128)(4,1)} %bitcast.248), calls=%async_computation.9 | async-start | bytes 8388608
  173.0 5.5 %slice-start.1 = ((s8[8388608]{0:T(1024)(128)(4,1)}), s8[4194304]{0:T(1024)(128)(4,1)S(1)}, s32[]{:S(2)}) async-start(s8[8388608]{0:T(1024)(128)(4,1)} %bitcast.246), calls=%async_computation.7 | async-start | bytes 8388608
  173.0 9.5 %slice-start.6 = ((s8[8388608]{0:T(1024)(128)(4,1)}), s8[4194304]{0:T(1024)(128)(4,1)S(1)}, s32[]{:S(2)}) async-start(s8[8388608]{0:T(1024)(128)(4,1)} %bitcast.253), calls=%async_computation.12 | async-start | bytes 8388608
  178.5 4.1 %slice-start.7 = ((s8[8388608]{0:T(1024)(128)(4,1)}), s8[4194304]{0:T(1024)(128)(4,1)S(1)}, s32[]{:S(2)}) async-start(s8[8388608]{0:T(1024)(128)(4,1)} %bitcast.253), calls=%async_computation.13 | async-start | bytes 8388608
  178.5 4.1 %copy-start.5 = (bf16[1024,256]{1,0:T(8,128)(2,1)S(1)}, bf16[1024,256]{1,0:T(8,128)(2,1)}, u32[]{:S(2)}) copy-start(bf16[1024,256]{1,0:T(8,128)(2,1)} %param.13) | copy-start | bytes 1572868
  186.8 6.0 %copy-start.6 = (bf16[1,1024,256]{1,2,0:T(8,128)(2,1)S(1)}, bf16[1,1024,256]{1,2,0:T(8,128)(2,1)}, u32[]{:S(2)}) copy-start(bf16[1,1024,256]{1,2,0:T(8,128)(2,1)} %get-tuple-element.15) | copy-start | bytes 1572868
  186.8 10.7 %slice-start.4 = ((s8[8388608]{0:T(1024)(128)(4,1)}), s8[4194304]{0:T(1024)(128)(4,1)S(1)}, s32[]{:S(2)}) async-start(s8[8388608]{0:T(1024)(128)(4,1)} %bitcast.250), calls=%async_computation.10 | async-start | bytes 8388608
  192.7 4.7 %copy-start.7 = (bf16[1,1024,256]{1,2,0:T(8,128)(2,1)S(1)}, bf16[1,1024,256]{1,2,0:T(8,128)(2,1)}, u32[]{:S(2)}) copy-start(bf16[1,1024,256]{1,2,0:T(8,128)(2,1)} %get-tuple-element.13) | copy-start | bytes 1572868
  192.7 4.8 %slice-start.5 = ((s8[8388608]{0:T(1024)(128)(4,1)}), s8[4194304]{0:T(1024)(128)(4,1)S(1)}, s32[]{:S(2)}) async-start(s8[8388608]{0:T(1024)(128)(4,1)} %bitcast.250), calls=%async_computation.11 | async-start | bytes 8388608
  200.7 15.0 %collective-permute-start.3 = (bf16[16,32,256]{2,1,0:T(8,128)(2,1)S(1)}, bf16[16,32,256]{2,1,0:T(8,128)(2,1)S(1)}, u32[]{:S(2)}, u32[]{:S(2)}) collective-permute-start(bf16[16,32,256]{2,1,0:T(8,128)(2,1)S(1)} %get-tuple-element.19), channel_id=1, source_target_pairs={{0,1},{1,0},{2,3},{3,2},{4,5},{5,4},{6,7},{7,6},{8,9},{9,8},{10,11... | collective-permute-start | bytes 786440 | tf_op jit(solution)/shard_map/ppermute | solution.py:83
  215.7 14.6 %copy-start.11 = (s32[32,8]{0,1:T(8,128)S(1)}, s32[32,8]{0,1:T(8,128)}, u32[]{:S(2)}) copy-start(s32[32,8]{0,1:T(8,128)} %param.17) | copy-start | bytes 3076
  218.7 46.1 %copy-start.4 = (bf16[32,3584]{1,0:T(8,128)(2,1)S(1)}, bf16[32,3584]{1,0:T(8,128)(2,1)}, u32[]{:S(2)}) copy-start(bf16[32,3584]{1,0:T(8,128)(2,1)} %param.15) | copy-start | bytes 688132
  218.7 46.3 %copy-start.8 = (f32[3584]{0:T(1024)S(1)}, f32[3584]{0:T(1024)}, u32[]{:S(2)}) copy-start(f32[3584]{0:T(1024)} %param.16) | copy-start | bytes 43012
  218.7 43.5 %all-to-all-start = ((bf16[16,32,3584]{2,1,0:T(8,128)(2,1)}), bf16[16,32,3584]{2,1,0:T(8,128)(2,1)}, u32[]{:S(2)}, u32[]{:S(2)}) async-start(bf16[16,32,3584]{2,1,0:T(8,128)(2,1)} %bitcast.252), calls=%async_computation | async-start | bytes 7340032 | tf_op jit(solution)/shard_map/all_to_all | solution.py:94
  231.6 70.5 %copy-start.9 = (s32[256]{0:T(256)}, s32[256]{0:T(256)S(1)}, u32[]{:S(2)}) copy-start(s32[256]{0:T(256)S(1)} %get-tuple-element.32) | copy-start | bytes 3076
  231.6 70.5 %copy-start.10 = (s32[256]{0:T(256)}, s32[256]{0:T(256)S(1)}, u32[]{:S(2)}) copy-start(s32[256]{0:T(256)S(1)} %get-tuple-element.33) | copy-start | bytes 3076
  305.6 7.6 %copy-start.3 = (bf16[320,3584]{1,0:T(8,128)(2,1)S(1)}, bf16[320,3584]{1,0:T(8,128)(2,1)}, u32[]{:S(2)}) copy-start(bf16[320,3584]{1,0:T(8,128)(2,1)} %reshape.118) | copy-start | bytes 6881284
  320.0 18.6 %copy-start.12 = (f32[32,8]{0,1:T(8,128)S(1)}, f32[32,8]{0,1:T(8,128)}, u32[]{:S(2)}) copy-start(f32[32,8]{0,1:T(8,128)} %param.18) | copy-start | bytes 3076
  320.0 45.8 %copy-start.1 = (bf16[1024,256]{1,0:T(8,128)(2,1)S(1)}, bf16[1024,256]{1,0:T(8,128)(2,1)}, u32[]{:S(2)}) copy-start(bf16[1024,256]{1,0:T(8,128)(2,1)} %param.11) | copy-start | bytes 1572868
  329.6 29.2 %all-to-all-start.2 = ((bf16[32,8,4480]{2,1,0:T(8,128)(2,1)}), bf16[32,8,4480]{2,1,0:T(8,128)(2,1)S(1)}, u32[]{:S(2)}, u32[]{:S(2)}) async-start(bf16[32,8,4480]{2,1,0:T(8,128)(2,1)} %reshape.121), calls=%async_computation.2 | async-start | bytes 4587520 | tf_op jit(solution)/shard_map/all_to_all | solution.py:148
Sparse Core Ops, SparseCore 0:
  9.0 87.2 all-gather.7
  97.9 76.2 all-gather.9
  186.9 73.7 all-gather.5
